TPU v7x, 32 devices: a whole 2x2x4 slice. The times are simulated.
32 devices in a mesh: groups: 2 (over y), tgt: 4 (over z), inner: 2 (over x), sub: 2 (over core).
Axes of the slice: x: 2, y: 2, z: 4, core: 2. Of those that a mesh axis runs over, the one named last changes fastest.
Arguments:
- density: bfloat16 [4096, 1024], P(('tgt', 'inner', 'sub'), 'groups'), parts along dimension 1, may hold values from -6 to 6
- cluster_basis: bfloat16 [32, 32, 256], P(('groups', 'tgt', 'inner', 'sub')), parts along dimension 0, may hold values from -0.375 to 0.375
- near_blocks: bfloat16 [8, 4, 8, 256, 256], P(('groups', 'tgt'), ('inner', 'sub')), parts along dimension 0, may hold values from -0.25 to 0.25
- near_pairs: int32 [8, 4, 8, 2], P(('groups', 'tgt'), ('inner', 'sub')), parts along dimension 0, may hold values from 0 to 3, as said below
- near_count: int32 [8, 4], P(('groups', 'tgt'), ('inner', 'sub')), parts along dimension 0, may hold values from 4 to 8, as said below
- coupling: bfloat16 [8, 4, 128, 128], P(('groups', 'tgt'), ('inner', 'sub')), parts along dimension 0, may hold values from -0.5 to 0.5
Outputs:
- potential: bfloat16 [4096, 1024], P(('tgt', 'inner', 'sub'), 'groups'), parts along dimension 1
There are 2 independent parts, one for each index of `groups`. A program takes and returns all parts, laid end to end along the dimension named above; each array names one. Nothing has to cross between parts.
Inputs may be any that keep to these rules, and one draw needn't show every extreme that they name: `near_pairs`: within one device's slots the pairs are distinct; the first column is below 4, the second below 4. Only the first near_count slots of a device are live; some device is full in every draw.
All inputs are finite; a program needn't handle non-finite values.
Results may differ from a plain program's by a relative error of at most 0.015.
Values may be sent and summed in bfloat16 or wider, within the bound.
No kernel may reach another device: no remote copies, remote signals or barrier semaphores. Data moves between devices by JAX's collectives and lax.ppermute only.
A program may use at most 64 MiB of HBM per device.

v0:
```python
import jax
import jax.numpy as jnp
from jax import lax
from jax.sharding import PartitionSpec as P


def on_device(density, cluster_basis, near_blocks, near_pairs, near_count, coupling):
    width = cluster_basis.shape[2]
    rank_size = cluster_basis.shape[1]
    rhs_count = density.shape[1]
    tgt_count = lax.axis_size("tgt")
    inner_count = lax.axis_size(("inner", "sub"))
    gathered, basis_all = (
        lax.all_gather(density, "tgt", axis=0, tiled=True),
        lax.all_gather(cluster_basis, "tgt", axis=0, tiled=True),
    )
    sources = gathered.reshape(tgt_count, width, rhs_count)
    projected = jnp.einsum(
        "srb,sbn->srn", basis_all, sources, preferred_element_type=jnp.float32
    ).astype(jnp.bfloat16)
    pair_list = near_pairs[0, 0]
    live_count = near_count[0, 0]
    tiles = near_blocks[0, 0]

    def add_block(slot_index, partial_value):
        target_local = pair_list[slot_index, 0]
        source_local = pair_list[slot_index, 1]
        source_tile = lax.dynamic_index_in_dim(sources, source_local, 0, False)
        block_tile = lax.dynamic_index_in_dim(tiles, slot_index, 0, False)
        block_term = jnp.dot(block_tile, source_tile, preferred_element_type=jnp.float32)
        target_row = lax.dynamic_index_in_dim(partial_value, target_local, 0, False)
        return lax.dynamic_update_index_in_dim(
            partial_value, target_row + block_term, target_local, 0
        )

    partial_value = lax.fori_loop(
        0, live_count, add_block, jnp.zeros((inner_count, width, rhs_count), jnp.float32)
    )
    rounded = lax.optimization_barrier(partial_value.astype(jnp.bfloat16)).astype(jnp.float32)
    near_sum = lax.psum_scatter(
        rounded.astype(jnp.bfloat16), ("inner", "sub"), scatter_dimension=0, tiled=True
    ).astype(jnp.float32)
    slot_count = pair_list.shape[0]
    flat_pairs = pair_list[:, 0] * tgt_count + pair_list[:, 1]
    live_slots = jnp.arange(slot_count) < live_count
    hit_table = (flat_pairs[:, None] == jnp.arange(inner_count * tgt_count)[None, :]) & live_slots[
        :, None
    ]
    keep_mask = (
        (1.0 - jnp.any(hit_table, axis=0).astype(jnp.float32))
        .reshape(inner_count, 1, tgt_count, 1)
        .astype(jnp.bfloat16)
    )
    masked = coupling[0, 0].reshape(inner_count, rank_size, tgt_count, rank_size) * keep_mask
    coeffs = jnp.dot(
        masked.reshape(inner_count * rank_size, tgt_count * rank_size),
        projected.reshape(tgt_count * rank_size, rhs_count),
        preferred_element_type=jnp.float32,
    )
    totals = lax.psum(coeffs.astype(jnp.bfloat16), ("inner", "sub")).astype(jnp.float32)
    own_coeffs = lax.dynamic_slice_in_dim(
        totals, lax.axis_index(("inner", "sub")) * rank_size, rank_size, 0
    )
    far_rows = jnp.einsum(
        "rb,rn->bn",
        cluster_basis[0],
        own_coeffs.astype(jnp.bfloat16),
        preferred_element_type=jnp.float32,
    )
    return (near_sum[0] + far_rows).astype(jnp.bfloat16)


def solution(mesh):
    in_specs = (
        P(("tgt", "inner", "sub"), "groups"),
        P(("groups", "tgt", "inner", "sub"), None, None),
        P(("groups", "tgt"), ("inner", "sub"), None, None, None),
        P(("groups", "tgt"), ("inner", "sub"), None, None),
        P(("groups", "tgt"), ("inner", "sub")),
        P(("groups", "tgt"), ("inner", "sub"), None, None),
    )
    out_specs = P(("tgt", "inner", "sub"), "groups")
    return jax.shard_map(
        on_device, mesh=mesh, in_specs=in_specs, out_specs=out_specs, check_vma=False
    )
```

profile of v0, /device:TPU:0, one launch (start us, length us, event | category | flops | bytes accessed | tf_op | source)
XLA Modules:
  0.0 133.4 jit_solution(1353661432246515566)
XLA Ops:
  6.5 0.0 all-gather.2.cloned.1.call-start
  6.5 0.7 all-gather.2.cloned.1.call-update
  7.3 0.0 all-reduce.2.cloned.1.call-start
  8.0 0.8 add_bitcast_fusion
  8.7 0.1 fusion.13
  8.8 0.0 copy-start.1
  8.8 0.1 convert_element_type.44
  8.9 0.1 mul.25
  9.0 0.1 mul.26
  9.2 15.2 %all_gather.7 = bf16[4,32,256]{2,1,0:T(8,128)(2,1)S(1)} all-gather(bf16[1,32,256]{2,1,0:T(8,128)(2,1)} %param.9), channel_id=1, replica_groups=mesh['groups'=2,'tgt'=4,'inner'=2,'sub'=2] {'tgt'}, dimensions={0}, use_global_device_ids=true | all-gather | bytes 81920 | tf_op jit(solution)/shard_map/all_gather | solution.py:15
  24.4 15.4 %all-gather.2.cloned.1.call-done = bf16[1024,512]{1,0:T(8,128)(2,1)} async-done(((bf16[256,512]{1,0:T(8,128)(2,1)}), bf16[1024,512]{1,0:T(8,128)(2,1)}) %all-gather.2.cloned.1.call-update) | async-done | bytes 1048592 | tf_op jit(solution)/shard_map/all_gather | solution.py:14
  39.7 1.5 %convolution_convert_fusion = bf16[4,32,512]{2,1,0:T(8,128)(2,1)S(1)} fusion(bf16[4,32,256]{2,1,0:T(8,128)(2,1)S(1)} %all_gather.7, bf16[4,256,512]{2,1,0:T(8,128)(2,1)} %bitcast.50), kind=kOutput, calls=%fused_computation.14 | convolution fusion | flops 33619968 | bytes 1245184 | tf_op jit(solution)/shard_map/srb,sbn->srn/dot_general | solution.py:18
  41.2 1.6 %convolution_convert_fusion.1 = bf16[128,512]{1,0:T(8,128)(2,1)} fusion(bf16[128,512]{1,0:T(8,128)(2,1)S(1)} %bitcast.52, bf16[1,1,128,128]{3,2,1,0:T(8,128)(2,1)} %param.13, bf16[1,1,128,128]{3,2,1,0:T(8,128)(2,1)S(1)} %mul.26), kind=kOutput, calls=%fused_computation.15 | convolution fusion | flops 16859136 | bytes 327680 | tf_op jit(solution)/shard_map/dot_general | solution.py:55
  42.9 0.0 all-reduce.2.cloned.1.call-update
  42.9 0.0 reduce-scatter.2.cloned.1.call-start
  42.9 0.2 broadcast_in_dim.10.clone
  43.1 0.0 copy-done.1
  43.1 35.9 %while.10 = (s32[]{:T(128)}, f32[4,256,512]{1,2,0:T(8,128)S(1)}, s32[]{:T(128)}, s32[8,2]{0,1:T(2,128)S(1)}, bf16[8,256,256]{2,1,0:T(8,128)(2,1)}, /*index=5*/bf...) while((s32[]{:T(128)}, f32[4,256,512]{1,2,0:T(8,128)S(1)}, s32[]{:T(128)}, ...), condition=%wide.region_1.2_spmd, body=%wide.region_0.1_spmd.sunk | while | flops 67239944 | bytes 5636343 | solution.py:36
  43.8 0.7 constant_dynamic-slice_fusion.5
  46.4 0.2 copy.18
  48.6 1.2 fusion.23
  49.9 0.2 copy.19
  50.8 0.7 constant_dynamic-slice_fusion.5
  53.4 0.2 copy.18
  55.7 1.3 fusion.23
  56.9 0.2 copy.19
  57.9 0.7 constant_dynamic-slice_fusion.5
  60.5 0.2 copy.18
  62.7 1.3 fusion.23
  64.0 0.2 copy.19
  64.9 0.7 constant_dynamic-slice_fusion.5
  67.5 0.2 copy.18
  69.8 1.3 fusion.23
  71.0 0.2 copy.19
  72.0 0.7 constant_dynamic-slice_fusion.5
  74.6 0.2 copy.18
  76.8 1.3 fusion.23
  78.1 0.2 copy.19
  79.0 0.0 copy-start
  79.0 1.1 convert_element_type.41
  80.1 0.0 reduce-scatter.2.cloned.1.call-update
  80.1 0.0 all-reduce.2.cloned.1.call-done
  80.1 44.6 %reduce-scatter.2.cloned.1.call-done = bf16[1,256,512]{1,2,0:T(8,128)(2,1)} async-done(((bf16[4,256,512]{1,2,0:T(8,128)(2,1)}), bf16[1,256,512]{1,2,0:T(8,128)(2,1)}) %reduce-scatter.2.cloned.1.call-update) | async-done | bytes 262160 | tf_op jit(solution)/shard_map/reduce_scatter | solution.py:40
  124.8 0.0 copy-done
  124.8 1.2 fusion.7
  126.0 0.8 copy.12
  (12 shorter events, 0.4 us)
Async XLA Ops:
  6.5 33.2 %all-gather.2.cloned.1.call-start = ((), (), s32[]{:S(2)}) async-start(), calls=%async_computation.1 | async-start | bytes 1310720 | tf_op jit(solution)/shard_map/all_gather | solution.py:14
  7.3 72.9 %all-reduce.2.cloned.1.call-start = ((), (), s32[]{:S(2)}) async-start(), calls=%async_computation.3 | async-start | bytes 262144 | tf_op jit(solution)/shard_map/psum | solution.py:60
  8.8 34.3 %copy-start.1 = (s32[1,1,8,2]{2,3,1,0:T(2,128)S(1)}, s32[1,1,8,2]{2,3,1,0:T(2,128)}, u32[]{:S(2)}) copy-start(s32[1,1,8,2]{2,3,1,0:T(2,128)} %param.11) | copy-start | bytes 196
  42.9 81.9 %reduce-scatter.2.cloned.1.call-start = ((), (), s32[]{:S(2)}) async-start(), calls=%async_computation.2 | async-start | bytes 1310720 | tf_op jit(solution)/shard_map/reduce_scatter | solution.py:40
  79.0 45.8 %copy-start = (bf16[1,32,256]{2,1,0:T(8,128)(2,1)S(1)}, bf16[1,32,256]{2,1,0:T(8,128)(2,1)}, u32[]{:S(2)}) copy-start(bf16[1,32,256]{2,1,0:T(8,128)(2,1)} %param.9) | copy-start | bytes 49156
Sparse Core Ops, SparseCore 0:
  8.9 30.8 all-gather.1
  43.0 31.3 all-reduce.1
  80.2 44.5 reduce-scatter.1
where the time goes:
time: 135 us; the launch traced here: 133 us
  waiting for transfers between devices  60.8 us (45%)
  loops' own time  24 us (18%)
  blocking collectives  15.2 us (11%)
  between operations  13.8 us (10%)
  matrix products  10.6 us (8%)
  local copies, waits for them, and re-layouts  6.99 us (5%)
  other arithmetic  1.93 us (1%)
    reduce_scatter x1, waiting for transfers between devices, on_device(): lax.psum_scatter(rounded.astype(jnp.bfloat16), ('inner', 'sub'), scatter_...  44.6 us
    another operation x1, loops' own time, on_device(): lax.fori_loop(0, live_count, add_block, jnp.zeros((inner_count, width, rh...  24 us
    all_gather x1, waiting for transfers between devices, on_device(): lax.all_gather(density, 'tgt', axis=0, tiled=True)  15.4 us
    all_gather x1, blocking collectives, on_device(): lax.all_gather(cluster_basis, 'tgt', axis=0, tiled=True)  15.2 us
    dot_general x5, matrix products, add_block(): jnp.dot(block_tile, source_tile, preferred_element_type=jnp.float32)  6.27 us
    dynamic_slice x5, local copies, waits for them, and re-layouts, add_block(): source_local = pair_list[slot_index, 1]  3.28 us
  transfers between devices with their start and end apart: 3, of which 2 were waited for; matrix products, arithmetic and copies ran while one was open for 11% of the time, Pallas kernels for 0%

commit v1 on v0

v1 whole, which is shorter than its diff:
```python
import jax
import jax.numpy as jnp
from jax import lax
from jax.experimental import pallas as pl
from jax.experimental.pallas import tpu as pltpu
from jax.sharding import PartitionSpec as P


def _near_far_kernel(pairs_ref, count_ref, tiles_ref, gathered_ref, masked_ref, out_ref, acc_ref):
    slot = pl.program_id(0)
    slot_total = pl.num_programs(0)
    inner_count, width, _ = acc_ref.shape
    tgt_count = gathered_ref.shape[0]
    rank_size = gathered_ref.shape[1] - width

    @pl.when(slot == 0)
    def _():
        acc_ref[...] = jnp.zeros_like(acc_ref)

    @pl.when(slot < count_ref[0])
    def _():
        target = jnp.clip(pairs_ref[2 * slot], 0, inner_count - 1)
        source = jnp.clip(pairs_ref[2 * slot + 1], 0, tgt_count - 1)
        term = jnp.dot(
            tiles_ref[...], gathered_ref[source, :width, :], preferred_element_type=jnp.float32
        )
        acc_ref[target] += term

    @pl.when(slot == slot_total - 1)
    def _():
        out_ref[:, :width, :] = acc_ref[...].astype(out_ref.dtype)
        coeffs = jnp.zeros((inner_count * rank_size, out_ref.shape[2]), jnp.float32)
        for source in range(tgt_count):
            coeffs += jnp.dot(
                masked_ref[source],
                gathered_ref[source, width:, :],
                preferred_element_type=jnp.float32,
            )
        out_ref[:, width:, :] = coeffs.reshape(inner_count, rank_size, -1).astype(out_ref.dtype)


def _near_far(pairs_flat, count, tiles, gathered, masked_t, inner_count):
    slot_count, width, _ = tiles.shape
    tgt_count, rows, rhs_count = gathered.shape

    def tile_index(k, pairs, cnt):
        return (jnp.maximum(jnp.minimum(k, cnt[0] - 1), 0), 0, 0)

    grid_spec = pltpu.PrefetchScalarGridSpec(
        num_scalar_prefetch=2,
        grid=(slot_count,),
        in_specs=[
            pl.BlockSpec((None, width, width), tile_index),
            pl.BlockSpec((tgt_count, rows, rhs_count), lambda k, p, c: (0, 0, 0)),
            pl.BlockSpec(masked_t.shape, lambda k, p, c: (0, 0, 0)),
        ],
        out_specs=pl.BlockSpec((inner_count, rows, rhs_count), lambda k, p, c: (0, 0, 0)),
        scratch_shapes=[pltpu.VMEM((inner_count, width, rhs_count), jnp.float32)],
    )
    return pl.pallas_call(
        _near_far_kernel,
        grid_spec=grid_spec,
        out_shape=jax.ShapeDtypeStruct((inner_count, rows, rhs_count), jnp.bfloat16),
        compiler_params=pltpu.CompilerParams(
            dimension_semantics=("arbitrary",), vmem_limit_bytes=100 * 1024 * 1024 // 2
        ),
    )(pairs_flat, count, tiles, gathered, masked_t)


def _epilogue_kernel(reduced_ref, basis_ref, out_ref):
    width = out_ref.shape[0]
    near = reduced_ref[0, :width, :].astype(jnp.float32)
    coeffs = reduced_ref[0, width:, :]
    far = lax.dot_general(
        basis_ref[0], coeffs, (((0,), (0,)), ((), ())), preferred_element_type=jnp.float32
    )
    out_ref[...] = (near + far).astype(out_ref.dtype)


def _epilogue(reduced, basis):
    width = basis.shape[2]
    return pl.pallas_call(
        _epilogue_kernel,
        out_shape=jax.ShapeDtypeStruct((width, reduced.shape[2]), jnp.bfloat16),
    )(reduced, basis)


def on_device(density, cluster_basis, near_blocks, near_pairs, near_count, coupling):
    width = cluster_basis.shape[2]
    rank_size = cluster_basis.shape[1]
    tgt_count = lax.axis_size("tgt")
    inner_count = lax.axis_size(("inner", "sub"))
    own_projected = jnp.dot(
        cluster_basis[0], density, preferred_element_type=jnp.float32
    ).astype(jnp.bfloat16)
    send = jnp.concatenate([density, own_projected], axis=0)
    gathered = lax.all_gather(send, "tgt", axis=0, tiled=False)

    pair_list = near_pairs[0, 0]
    live_count = near_count[0, 0]
    slot_count = pair_list.shape[0]
    flat_pairs = pair_list[:, 0] * tgt_count + pair_list[:, 1]
    live_slots = jnp.arange(slot_count) < live_count
    hit_table = (flat_pairs[:, None] == jnp.arange(inner_count * tgt_count)[None, :]) & live_slots[
        :, None
    ]
    keep_mask = (
        (1.0 - jnp.any(hit_table, axis=0).astype(jnp.float32))
        .reshape(inner_count, 1, tgt_count, 1)
        .astype(jnp.bfloat16)
    )
    masked = coupling[0, 0].reshape(inner_count, rank_size, tgt_count, rank_size) * keep_mask
    masked_t = masked.transpose(2, 0, 1, 3).reshape(tgt_count, inner_count * rank_size, rank_size)

    partial = _near_far(
        pair_list.reshape(-1), live_count.reshape(1), near_blocks[0, 0], gathered, masked_t,
        inner_count,
    )
    reduced = lax.psum_scatter(partial, ("inner", "sub"), scatter_dimension=0, tiled=True)
    return _epilogue(reduced, cluster_basis)


def solution(mesh):
    in_specs = (
        P(("tgt", "inner", "sub"), "groups"),
        P(("groups", "tgt", "inner", "sub"), None, None),
        P(("groups", "tgt"), ("inner", "sub"), None, None, None),
        P(("groups", "tgt"), ("inner", "sub"), None, None),
        P(("groups", "tgt"), ("inner", "sub")),
        P(("groups", "tgt"), ("inner", "sub"), None, None),
    )
    out_specs = P(("tgt", "inner", "sub"), "groups")
    return jax.shard_map(
        on_device, mesh=mesh, in_specs=in_specs, out_specs=out_specs, check_vma=False
    )
```

time: 135 us -> 81.9 us (0.61); the launches traced: 133 us -> 81.8 us
  loops' own time: 24 us -> 0 us
  blocking collectives: 15.2 us -> 0 us
  matrix products: 10.6 us -> 1.2 us
  Pallas kernels: 0 us -> 6.04 us
  local copies, waits for them, and re-layouts: 6.99 us -> 1.75 us
  waiting for transfers between devices: 60.8 us -> 56.8 us
    another operation x1 -> x0, loops' own time: 24 us -> none  [on_device(): lax.fori_loop(0, live_count, add_block, jnp.zeros((inner_count, width, rh...]
    reduce_scatter x1, waiting for transfers between devices: 44.6 us -> 25 us  [on_device(): lax.psum_scatter(partial, ('inner', 'sub'), scatter_dimension=0, tiled=True)]
    all_gather x1, waiting for transfers between devices: 15.4 us -> 31.7 us  [on_device(): gathered = lax.all_gather(send, 'tgt', axis=0, tiled=False)]
    all_gather x1 -> x0, blocking collectives: 15.2 us -> none  [on_device(): lax.all_gather(cluster_basis, 'tgt', axis=0, tiled=True)]
    dot_general x8 -> x1, matrix products: 10.6 us -> 1.2 us  [on_device(): jnp.dot(cluster_basis[0], density, preferred_element_type=jnp.float32)]
    pallas_call x0 -> x2, Pallas kernels: none -> 6.04 us  [the longest x1 4.12 us: _near_far(): pl.pallas_call(_near_far_kernel, grid_spec=grid_spec, out_shape=jax.Shape...]
    dynamic_slice x15 -> x0, local copies, waits for them, and re-layouts: 4.47 us -> none  [the longest x5 3.28 us: add_block(): source_local = pair_list[slot_index, 1]]
    concatenate x0 -> x1, other arithmetic: none -> 1.71 us  [on_device(): send = jnp.concatenate([density, own_projected], axis=0)]
  transfers between devices with their start and end apart: 3 -> 2, of which waited for: 2 -> 2; matrix products, arithmetic and copies ran while one was open for 11% -> 1% of each run, Pallas kernels for 0% -> 0%
where the time goes in v1:
time: 81.9 us; the launch traced here: 81.8 us
  waiting for transfers between devices  56.8 us (69%)
  between operations  14.1 us (17%)
  Pallas kernels  6.04 us (7%)
  other arithmetic  1.91 us (2%)
  local copies, waits for them, and re-layouts  1.75 us (2%)
  matrix products  1.2 us (1%)
    all_gather x1, waiting for transfers between devices, on_device(): gathered = lax.all_gather(send, 'tgt', axis=0, tiled=False)  31.7 us
    reduce_scatter x1, waiting for transfers between devices, on_device(): lax.psum_scatter(partial, ('inner', 'sub'), scatter_dimension=0, tiled=True)  25 us
    pallas_call x1, Pallas kernels, _near_far(): pl.pallas_call(_near_far_kernel, grid_spec=grid_spec, out_shape=jax.Shape...  4.12 us
    pallas_call x1, Pallas kernels, _epilogue(): pl.pallas_call(_epilogue_kernel, out_shape=jax.ShapeDtypeStruct((width, r...  1.92 us
    concatenate x1, other arithmetic, on_device(): send = jnp.concatenate([density, own_projected], axis=0)  1.71 us
  transfers between devices with their start and end apart: 2, of which 2 were waited for; matrix products, arithmetic and copies ran while one was open for 1% of the time, Pallas kernels for 0%

profile of v1, /device:TPU:0, one launch (start us, length us, event | category | flops | bytes accessed | tf_op | source)
XLA Modules:
  0.0 81.8 jit_solution(10817492045208757904)
XLA Ops:
  6.5 0.0 copy-start.3
  6.5 0.0 copy-start.2
  6.5 0.0 copy-start.1
  6.5 0.0 all-gather.3.cloned.1.call-start
  6.5 1.2 %convolution_convert_fusion = bf16[32,512]{1,0:T(8,128)(2,1)S(1)} fusion(bf16[256,512]{1,0:T(8,128)(2,1)} %param.6, bf16[1,32,256]{2,1,0:T(8,128)(2,1)} %basis_ref.1), kind=kOutput, calls=%fused_computation | convolution fusion | flops 8404992 | bytes 311296 | tf_op jit(solution)/shard_map/dot_general | solution.py:93
  7.7 1.7 %pad_maximum_fusion = bf16[288,512]{1,0:T(8,128)(2,1)} fusion(bf16[32,512]{1,0:T(8,128)(2,1)S(1)} %convolution_convert_fusion, bf16[256,512]{1,0:T(8,128)(2,1)} %param.6), kind=kLoop, calls=%fused_computation.1 | loop fusion | flops 589824 | bytes 589824 | tf_op jit(solution)/shard_map/concatenate | solution.py:96
  9.5 0.0 all-gather.3.cloned.1.call-update
  9.5 0.0 reduce-scatter.2.cloned.1.call-start
  10.2 0.0 copy-done.3
  10.2 0.1 copy.13
  10.3 0.1 fusion.2
  10.4 0.1 convert_element_type.26
  10.5 0.1 copy.14
  10.6 0.1 reshape_squeeze.9.pairs_ref
  10.7 0.0 copy-done.2
  10.7 0.1 reshape_squeeze.11
  10.8 0.1 copy_multiply_fusion
  10.9 31.7 %all-gather.3.cloned.1.call-done = bf16[1152,512]{1,0:T(8,128)(2,1)} async-done(((bf16[288,512]{1,0:T(8,128)(2,1)}), bf16[1152,512]{1,0:T(8,128)(2,1)}) %all-gather.3.cloned.1.call-update) | async-done | bytes 1179664 | tf_op jit(solution)/shard_map/all_gather | solution.py:97
  42.6 0.0 copy-done.1
  42.6 0.0 copy-start
  42.6 1.3 %copy-done = bf16[1152,512]{1,0:T(8,128)(2,1)S(1)} copy-done((bf16[1152,512]{1,0:T(8,128)(2,1)S(1)}, bf16[1152,512]{1,0:T(8,128)(2,1)}, u32[]{:S(2)}) %copy-start) | copy-done | bytes 1179672
  43.9 4.1 %shard_map.64 = bf16[4,288,512]{2,1,0:T(8,128)(2,1)} custom-call(s32[16]{0:T(128)S(1)} %reshape_squeeze.9.pairs_ref, s32[1]{0:T(128)} %bitcast.18.count_ref, bf16[8,256,256]{2,1,0:T(8,128)(2,1)S(1)} %bitcast.21, bf16[4,288,512]{2,1,0:T(8,128)(2,1)S(1)} %bitcast.20, bf16[4,128,32]{2,1,0:T(8,128)(2,1)S(1)} %bitcast.22), custom_call_target="tpu_custom_call" | custom-call | tf_op jit(solution)/shard_map/pallas_call | solution.py:60
  48.0 0.0 reduce-scatter.2.cloned.1.call-update
  48.0 25.0 %reduce-scatter.2.cloned.1.call-done.reduced_ref = bf16[1,288,512]{2,1,0:T(8,128)(2,1)} async-done(((bf16[4,288,512]{2,1,0:T(8,128)(2,1)}), bf16[1,288,512]{2,1,0:T(8,128)(2,1)}) %reduce-scatter.2.cloned.1.call-update) | async-done | bytes 294928 | tf_op jit(solution)/shard_map/reduce_scatter | solution.py:119
  73.0 1.9 %shard_map.65 = bf16[256,512]{1,0:T(8,128)(2,1)} custom-call(bf16[1,288,512]{2,1,0:T(8,128)(2,1)} %reduce-scatter.2.cloned.1.call-done.reduced_ref, bf16[1,32,256]{2,1,0:T(8,128)(2,1)} %basis_ref.1), custom_call_target="tpu_custom_call" | custom-call | tf_op jit(solution)/shard_map/pallas_call | solution.py:82
  (3 shorter events, 0.0 us)
Async XLA Ops:
  6.5 3.6 %copy-start.3 = (s32[1,1,8,2]{2,3,1,0:T(2,128)S(1)}, s32[1,1,8,2]{2,3,1,0:T(2,128)}, u32[]{:S(2)}) copy-start(s32[1,1,8,2]{2,3,1,0:T(2,128)} %param.9) | copy-start | bytes 196
  6.5 4.1 %copy-start.2 = (bf16[1,1,128,128]{3,2,1,0:T(8,128)(2,1)S(1)}, bf16[1,1,128,128]{3,2,1,0:T(8,128)(2,1)}, u32[]{:S(2)}) copy-start(bf16[1,1,128,128]{3,2,1,0:T(8,128)(2,1)} %param.11) | copy-start | bytes 98308
  6.5 36.1 %copy-start.1 = (bf16[1,1,8,256,256]{4,3,2,1,0:T(8,128)(2,1)S(1)}, bf16[1,1,8,256,256]{4,3,2,1,0:T(8,128)(2,1)}, u32[]{:S(2)}) copy-start(bf16[1,1,8,256,256]{4,3,2,1,0:T(8,128)(2,1)} %param.8) | copy-start | bytes 3145732
  6.5 36.1 %all-gather.3.cloned.1.call-start = ((), (), s32[]{:S(2)}) async-start(), calls=%async_computation.2 | async-start | bytes 1474560 | tf_op jit(solution)/shard_map/all_gather | solution.py:97
  9.5 63.6 %reduce-scatter.2.cloned.1.call-start = ((), (), s32[]{:S(2)}) async-start(), calls=%async_computation.1 | async-start | bytes 1474560 | tf_op jit(solution)/shard_map/reduce_scatter | solution.py:119
  42.6 1.3 %copy-start = (bf16[1152,512]{1,0:T(8,128)(2,1)S(1)}, bf16[1152,512]{1,0:T(8,128)(2,1)}, u32[]{:S(2)}) copy-start(bf16[1152,512]{1,0:T(8,128)(2,1)} %all-gather.3.cloned.1.call-done) | copy-start | bytes 3538948
Sparse Core Ops, SparseCore 0:
  9.6 32.9 all-gather.2
  48.2 24.8 reduce-scatter.1

commit v2 on v1

v2 whole, which is shorter than its diff:
```python
import jax
import jax.numpy as jnp
from jax import lax
from jax.experimental import pallas as pl
from jax.experimental.pallas import tpu as pltpu
from jax.sharding import PartitionSpec as P


def _near_far_kernel(
    pairs_ref, count_ref, place_ref, tiles_ref, stack_ref, masked_ref, mine_ref, theirs_ref, acc_ref
):
    slot = pl.program_id(0)
    slot_total = pl.num_programs(0)
    inner_count, width, rhs_count = acc_ref.shape
    tgt_count = masked_ref.shape[0]
    rank_size = masked_ref.shape[2]
    half_rank = rank_size // 2
    sub_count = 2
    own_tgt = place_ref[0]
    own_sub = place_ref[1]

    @pl.when(slot == 0)
    def _():
        acc_ref[...] = jnp.zeros_like(acc_ref)

    @pl.when(slot < count_ref[0])
    def _():
        target = jnp.clip(pairs_ref[2 * slot], 0, inner_count - 1)
        source = jnp.clip(pairs_ref[2 * slot + 1], 0, tgt_count - 1)
        term = jnp.dot(
            tiles_ref[...],
            stack_ref[source - own_tgt + tgt_count - 1, :width, :],
            preferred_element_type=jnp.float32,
        )
        acc_ref[target] += term

    @pl.when(slot == slot_total - 1)
    def _():
        coeffs = jnp.zeros((inner_count * rank_size, rhs_count), jnp.float32)
        for source in range(tgt_count):
            block = stack_ref[source - own_tgt + tgt_count - 1]
            dens = block[:width, :]
            packed = block[width:, :]
            top = jnp.dot(packed[:, :width], dens, preferred_element_type=jnp.float32)
            bottom = jnp.dot(packed[:, width:], dens, preferred_element_type=jnp.float32)
            projected = jnp.concatenate([top, bottom], axis=0).astype(jnp.bfloat16)
            coeffs += jnp.dot(masked_ref[source], projected, preferred_element_type=jnp.float32)
        coeffs = coeffs.astype(jnp.bfloat16)

        def write(first_ref, second_ref):
            for target in range(inner_count):
                dest = first_ref if target % sub_count == 0 else second_ref
                row = target // sub_count
                dest[row, :width, :] = acc_ref[target].astype(dest.dtype)
                dest[row, width:, :] = coeffs[target * rank_size : (target + 1) * rank_size]

        @pl.when(own_sub == 0)
        def _():
            write(mine_ref, theirs_ref)

        @pl.when(own_sub != 0)
        def _():
            write(theirs_ref, mine_ref)


def _near_far(pairs_flat, count, place, tiles, stack, masked_t, inner_count, rank_size):
    slot_count, width, _ = tiles.shape
    stack_count, rows, rhs_count = stack.shape
    half_count = inner_count // 2
    out_rows = width + rank_size

    def tile_index(k, pairs, cnt, place):
        return (jnp.maximum(jnp.minimum(k, cnt[0] - 1), 0), 0, 0)

    whole = lambda k, p, c, q: (0, 0, 0)
    grid_spec = pltpu.PrefetchScalarGridSpec(
        num_scalar_prefetch=3,
        grid=(slot_count,),
        in_specs=[
            pl.BlockSpec((None, width, width), tile_index),
            pl.BlockSpec(stack.shape, whole),
            pl.BlockSpec(masked_t.shape, whole),
        ],
        out_specs=[
            pl.BlockSpec((half_count, out_rows, rhs_count), whole),
            pl.BlockSpec((half_count, out_rows, rhs_count), whole),
        ],
        scratch_shapes=[pltpu.VMEM((inner_count, width, rhs_count), jnp.float32)],
    )
    out = jax.ShapeDtypeStruct((half_count, out_rows, rhs_count), jnp.bfloat16)
    return pl.pallas_call(
        _near_far_kernel,
        grid_spec=grid_spec,
        out_shape=[out, out],
        compiler_params=pltpu.CompilerParams(
            dimension_semantics=("arbitrary",), vmem_limit_bytes=56 * 1024 * 1024
        ),
    )(pairs_flat, count, place, tiles, stack, masked_t)


def _epilogue_kernel(total_ref, basis_ref, out_ref):
    width = out_ref.shape[0]
    near = total_ref[:width, :]
    coeffs = total_ref[width:, :].astype(jnp.bfloat16)
    far = lax.dot_general(
        basis_ref[0], coeffs, (((0,), (0,)), ((), ())), preferred_element_type=jnp.float32
    )
    out_ref[...] = (near + far).astype(out_ref.dtype)


def _epilogue(total, basis):
    width = basis.shape[2]
    return pl.pallas_call(
        _epilogue_kernel,
        out_shape=jax.ShapeDtypeStruct((width, total.shape[1]), jnp.bfloat16),
    )(total, basis)


def _line_gather(payload, axis):
    n = lax.axis_size(axis)
    up_pairs = [(i, i + 1) for i in range(n - 1)]
    down_pairs = [(i + 1, i) for i in range(n - 1)]
    ups, downs = [], []
    up, down = payload, payload
    for _ in range(n - 1):
        up = lax.ppermute(up, axis, up_pairs)
        down = lax.ppermute(down, axis, down_pairs)
        ups.append(up)
        downs.append(down)
    return jnp.stack(ups[::-1] + [payload] + downs)


def _ring_reduce_scatter(blocks, axis):
    n = lax.axis_size(axis)
    if n == 1:
        return blocks[0]
    me = lax.axis_index(axis)
    ring = [(i, (i + 1) % n) for i in range(n)]
    carry = lax.dynamic_index_in_dim(blocks, jnp.mod(me - 1, n), 0, False)
    for step in range(n - 1):
        arrived = lax.ppermute(carry.astype(jnp.bfloat16), axis, ring)
        own = lax.dynamic_index_in_dim(blocks, jnp.mod(me - 2 - step, n), 0, False)
        carry = arrived.astype(jnp.float32) + own
    return carry


def on_device(density, cluster_basis, near_blocks, near_pairs, near_count, coupling):
    width = cluster_basis.shape[2]
    rank_size = cluster_basis.shape[1]
    rhs_count = density.shape[1]
    tgt_count = lax.axis_size("tgt")
    inner_count = lax.axis_size(("inner", "sub"))
    assert lax.axis_size("sub") == 2 and 2 * width == rhs_count and rank_size % 2 == 0
    basis = cluster_basis[0]
    half_rank = rank_size // 2
    packed = jnp.concatenate([basis[:half_rank], basis[half_rank:]], axis=1)
    payload = jnp.concatenate([density, packed], axis=0)
    stack = _line_gather(payload, "tgt")

    pair_list = near_pairs[0, 0]
    live_count = near_count[0, 0]
    slot_count = pair_list.shape[0]
    flat_pairs = pair_list[:, 0] * tgt_count + pair_list[:, 1]
    live_slots = jnp.arange(slot_count) < live_count
    hit_table = (flat_pairs[:, None] == jnp.arange(inner_count * tgt_count)[None, :]) & live_slots[
        :, None
    ]
    keep_mask = (
        (1.0 - jnp.any(hit_table, axis=0).astype(jnp.float32))
        .reshape(inner_count, 1, tgt_count, 1)
        .astype(jnp.bfloat16)
    )
    masked = coupling[0, 0].reshape(inner_count, rank_size, tgt_count, rank_size) * keep_mask
    masked_t = masked.transpose(2, 0, 1, 3).reshape(tgt_count, inner_count * rank_size, rank_size)

    place = jnp.stack([lax.axis_index("tgt"), lax.axis_index("sub")]).astype(jnp.int32)
    mine, theirs = _near_far(
        pair_list.reshape(-1), live_count.reshape(1), place, near_blocks[0, 0], stack, masked_t,
        inner_count, rank_size,
    )
    arrived = lax.ppermute(theirs, "sub", [(0, 1), (1, 0)])
    stage = mine.astype(jnp.float32) + arrived.astype(jnp.float32)
    total = _ring_reduce_scatter(stage, "inner")
    return _epilogue(total, cluster_basis)


def solution(mesh):
    in_specs = (
        P(("tgt", "inner", "sub"), "groups"),
        P(("groups", "tgt", "inner", "sub"), None, None),
        P(("groups", "tgt"), ("inner", "sub"), None, None, None),
        P(("groups", "tgt"), ("inner", "sub"), None, None),
        P(("groups", "tgt"), ("inner", "sub")),
        P(("groups", "tgt"), ("inner", "sub"), None, None),
    )
    out_specs = P(("tgt", "inner", "sub"), "groups")
    return jax.shard_map(
        on_device, mesh=mesh, in_specs=in_specs, out_specs=out_specs, check_vma=False
    )
```

time: 81.9 us -> 63.2 us (0.77)
  waiting for transfers between devices: 56.8 us -> 23.3 us
  starting transfers between devices: 0.04 us -> 19.4 us
  between operations: 14.1 us -> 0.82 us
  other arithmetic: 1.91 us -> 5.36 us
  Pallas kernels: 6.04 us -> 9.15 us
  local copies, waits for them, and re-layouts: 1.75 us -> 4.62 us
  matrix products: 1.2 us -> 0 us
    all_gather x1 -> x0, waiting for transfers between devices: 31.7 us -> none  [on_device(): gathered = lax.all_gather(send, 'tgt', axis=0, tiled=False)]
    reduce_scatter x1 -> x0, waiting for transfers between devices: 25 us -> none  [on_device(): lax.psum_scatter(partial, ('inner', 'sub'), scatter_dimension=0, tiled=True)]
    ppermute x0 -> x8, waiting for transfers between devices: none -> 23.3 us  [the longest x1 7.31 us: _ring_reduce_scatter(): arrived = lax.ppermute(carry.astype(jnp.bfloat16), axis, ring)]
    ppermute x0 -> x8, starting transfers between devices: none -> 19.4 us  [the longest x3 13.8 us: _line_gather(): up = lax.ppermute(up, axis, up_pairs)]
    pallas_call x2, Pallas kernels: 6.04 us -> 9.15 us  [the longest x1 7.14 us: _near_far(): pl.pallas_call(_near_far_kernel, grid_spec=grid_spec, out_shape=[out, out...]
    add x0 -> x2, other arithmetic: none -> 2.12 us  [the longest x1 1.22 us: on_device(): stage = mine.astype(jnp.float32) + arrived.astype(jnp.float32)]
    dot_general x1 -> x0, matrix products: 1.2 us -> none  [on_device(): jnp.dot(cluster_basis[0], density, preferred_element_type=jnp.float32)]
    unnamed x9 -> x10, local copies, waits for them, and re-layouts: 1.36 us -> 2.15 us
  transfers between devices with their start and end apart: 2 -> 8, of which waited for: 2 -> 5; matrix products, arithmetic and copies ran while one was open for 1% -> 8% of each run, Pallas kernels for 0% -> 0%
where the time goes in v2:
time: 63.2 us; the launch traced here: 62.6 us
  waiting for transfers between devices  23.3 us (37%)
  starting transfers between devices  19.4 us (31%)
  Pallas kernels  9.15 us (14%)
  other arithmetic  5.36 us (8%)
  local copies, waits for them, and re-layouts  4.62 us (7%)
  between operations  0.82 us (1%)
    ppermute x3, starting transfers between devices, _line_gather(): up = lax.ppermute(up, axis, up_pairs)  13.8 us
    ppermute x1, waiting for transfers between devices, _ring_reduce_scatter(): arrived = lax.ppermute(carry.astype(jnp.bfloat16), axis, ring)  7.31 us
    pallas_call x1, Pallas kernels, _near_far(): pl.pallas_call(_near_far_kernel, grid_spec=grid_spec, out_shape=[out, out...  7.14 us
    ppermute x3, waiting for transfers between devices, _line_gather(): down = lax.ppermute(down, axis, down_pairs)  6.96 us
    ppermute x3, waiting for transfers between devices, _line_gather(): up = lax.ppermute(up, axis, up_pairs)  6.79 us
    ppermute x3, starting transfers between devices, _line_gather(): down = lax.ppermute(down, axis, down_pairs)  3.86 us
    ppermute x1, waiting for transfers between devices, on_device(): arrived = lax.ppermute(theirs, 'sub', [(0, 1), (1, 0)])  2.21 us
    unnamed x10, local copies, waits for them, and re-layouts  2.15 us
  transfers between devices with their start and end apart: 8, of which 5 were waited for; matrix products, arithmetic and copies ran while one was open for 8% of the time, Pallas kernels for 0%

profile of v2, /device:TPU:0, one launch (start us, length us, event | category | flops | bytes accessed | tf_op | source)
XLA Modules:
  0.0 62.6 jit_solution(12989415820277839006)
XLA Ops:
  0.0 0.0 copy-start.1
  0.0 0.8 %slice_bitcast_fusion.1 = (bf16[16,256]{1,0:T(8,128)(2,1)S(1)}, bf16[16,256]{1,0:T(8,128)(2,1)S(1)}) fusion(bf16[1,32,256]{2,1,0:T(8,128)(2,1)} %basis_ref.1), kind=kLoop, calls=%fused_computation.14 | loop fusion | bytes 32768 | tf_op jit(solution)/shard_map/slice | solution.py:156
  0.8 1.0 %maximum_maximum_fusion = bf16[272,512]{1,0:T(8,128)(2,1)S(1)} fusion(bf16[16,256]{1,0:T(8,128)(2,1)S(1)} %get-tuple-element.10, bf16[16,256]{1,0:T(8,128)(2,1)S(1)} %get-tuple-element.9, bf16[256,512]{1,0:T(8,128)(2,1)} %param.6), kind=kLoop, calls=%fused_computation.4 | loop fusion | flops 835584 | bytes 557056 | tf_op jit(solution)/shard_map/concatenate | solution.py:157
  1.7 5.0 %collective-permute-start = (bf16[272,512]{1,0:T(8,128)(2,1)S(1)}, bf16[272,512]{1,0:T(8,128)(2,1)S(1)}, u32[]{:S(2)}, u32[]{:S(2)}) collective-permute-start(bf16[272,512]{1,0:T(8,128)(2,1)S(1)} %maximum_maximum_fusion), channel_id=1, source_target_pairs={{0,4},{4,8},{8,12},{1,5},{5,9},{9,13},{2,6},{6,10},{10,14},{3,7},{... | collective-permute-start | bytes 835592 | tf_op jit(solution)/shard_map/ppermute | solution.py:126
  6.7 1.3 %collective-permute-start.3 = (bf16[272,512]{1,0:T(8,128)(2,1)S(1)}, bf16[272,512]{1,0:T(8,128)(2,1)S(1)}, u32[]{:S(2)}, u32[]{:S(2)}) collective-permute-start(bf16[272,512]{1,0:T(8,128)(2,1)S(1)} %maximum_maximum_fusion), channel_id=1, source_target_pairs={{4,0},{8,4},{12,8},{5,1},{9,5},{13,9},{6,2},{10,6},{14,10},{7,3},{... | collective-permute-start | bytes 835592 | tf_op jit(solution)/shard_map/ppermute | solution.py:127
  8.7 0.8 %add_bitcast_fusion = s32[8]{0:T(128)S(1)} fusion(s32[8,2]{0,1:T(2,128)} %bitcast.41), kind=kLoop, calls=%fused_computation.21 | loop fusion | flops 16 | bytes 96 | tf_op jit(solution)/shard_map/eq | solution.py:165
  9.4 3.2 %collective-permute-done = bf16[272,512]{1,0:T(8,128)(2,1)S(1)} collective-permute-done((bf16[272,512]{1,0:T(8,128)(2,1)S(1)}, bf16[272,512]{1,0:T(8,128)(2,1)S(1)}, u32[]{:S(2)}, u32[]{:S(2)}) %collective-permute-start) | collective-permute-done | bytes 278560 | tf_op jit(solution)/shard_map/ppermute | solution.py:126
  12.6 4.4 %collective-permute-start.1 = (bf16[272,512]{1,0:T(8,128)(2,1)S(1)}, bf16[272,512]{1,0:T(8,128)(2,1)S(1)}, u32[]{:S(2)}, u32[]{:S(2)}) collective-permute-start(bf16[272,512]{1,0:T(8,128)(2,1)S(1)} %collective-permute-done), channel_id=1, source_target_pairs={{0,4},{4,8},{8,12},{1,5},{5,9},{9,13},{2,6},{6,10},{10,14},{3,7},{... | collective-permute-start | bytes 835592 | tf_op jit(solution)/shard_map/ppermute | solution.py:126
  17.0 0.1 fusion.2
  17.1 0.0 collective-permute-done.3
  17.1 1.3 %collective-permute-start.4 = (bf16[272,512]{1,0:T(8,128)(2,1)S(1)}, bf16[272,512]{1,0:T(8,128)(2,1)S(1)}, u32[]{:S(2)}, u32[]{:S(2)}) collective-permute-start(bf16[272,512]{1,0:T(8,128)(2,1)S(1)} %collective-permute-done.3), channel_id=1, source_target_pairs={{4,0},{8,4},{12,8},{5,1},{9,5},{13,9},{6,2},{10,6},{14,10},{7,3},{... | collective-permute-start | bytes 835592 | tf_op jit(solution)/shard_map/ppermute | solution.py:127
  18.4 3.6 %collective-permute-done.1 = bf16[272,512]{1,0:T(8,128)(2,1)S(1)} collective-permute-done((bf16[272,512]{1,0:T(8,128)(2,1)S(1)}, bf16[272,512]{1,0:T(8,128)(2,1)S(1)}, u32[]{:S(2)}, u32[]{:S(2)}) %collective-permute-start.1) | collective-permute-done | bytes 278560 | tf_op jit(solution)/shard_map/ppermute | solution.py:126
  22.0 4.4 %collective-permute-start.2 = (bf16[272,512]{1,0:T(8,128)(2,1)S(1)}, bf16[272,512]{1,0:T(8,128)(2,1)S(1)}, u32[]{:S(2)}, u32[]{:S(2)}) collective-permute-start(bf16[272,512]{1,0:T(8,128)(2,1)S(1)} %collective-permute-done.1), channel_id=1, source_target_pairs={{0,4},{4,8},{8,12},{1,5},{5,9},{9,13},{2,6},{6,10},{10,14},{3,7},{... | collective-permute-start | bytes 835592 | tf_op jit(solution)/shard_map/ppermute | solution.py:126
  26.4 0.6 %pad_add_fusion.place_ref = s32[2]{0:T(128)} fusion(s32[1]{0:T(128)} %bitcast.2, s32[1]{0:T(128)} %bitcast.1), kind=kLoop, calls=%fused_computation.18 | loop fusion | flops 2 | bytes 16 | tf_op jit(solution)/shard_map/stack | solution.py:176
  27.1 0.8 %copy.13 = s32[1,1,8,2]{3,2,1,0:T(8,128)S(1)} copy(s32[1,1,8,2]{2,3,1,0:T(2,128)} %param.9) | data formatting | bytes 128 | tf_op args[3]
  27.8 0.1 convert_element_type.37
  27.9 0.1 copy.14
  28.0 0.9 %reshape_squeeze.11 = bf16[4,32,4,32]{3,2,1,0:T(4,128)(2,1)S(1)} reshape(bf16[1,1,128,128]{3,2,1,0:T(8,128)(2,1)} %param.11) | data formatting | bytes 65536 | tf_op jit(solution)/shard_map/reshape;squeeze | solution.py:173
  28.9 0.6 reshape_squeeze.9.pairs_ref
  29.5 0.7 %copy_multiply_fusion = bf16[4,32,4,32]{3,1,0,2:T(8,128)(2,1)} fusion(bf16[4,32,4,32]{3,2,1,0:T(4,128)(2,1)S(1)} %reshape_squeeze.11, bf16[4,4]{0,1:T(4,128)(2,1)S(1)} %copy.14), kind=kLoop, calls=%fused_computation.12 | loop fusion | flops 16384 | bytes 65568 | tf_op jit(solution)/shard_map/mul | solution.py:173
  30.2 0.0 collective-permute-done.4
  30.2 1.3 %collective-permute-start.5 = (bf16[272,512]{1,0:T(8,128)(2,1)S(1)}, bf16[272,512]{1,0:T(8,128)(2,1)S(1)}, u32[]{:S(2)}, u32[]{:S(2)}) collective-permute-start(bf16[272,512]{1,0:T(8,128)(2,1)S(1)} %collective-permute-done.4), channel_id=1, source_target_pairs={{4,0},{8,4},{12,8},{5,1},{9,5},{13,9},{6,2},{10,6},{14,10},{7,3},{... | collective-permute-start | bytes 835592 | tf_op jit(solution)/shard_map/ppermute | solution.py:127
  31.5 0.0 collective-permute-done.2
  31.6 0.0 copy-done.1
  31.7 7.0 %collective-permute-done.5 = bf16[272,512]{1,0:T(8,128)(2,1)S(1)} collective-permute-done((bf16[272,512]{1,0:T(8,128)(2,1)S(1)}, bf16[272,512]{1,0:T(8,128)(2,1)S(1)}, u32[]{:S(2)}, u32[]{:S(2)}) %collective-permute-start.5) | collective-permute-done | bytes 278560 | tf_op jit(solution)/shard_map/ppermute | solution.py:127
  38.7 0.0 copy-start
  38.7 1.3 %copy-done = bf16[7,272,512]{2,1,0:T(8,128)(2,1)} copy-done((bf16[7,272,512]{2,1,0:T(8,128)(2,1)}, bf16[7,272,512]{2,1,0:T(8,128)(2,1)S(1)}, u32[]{:S(2)}) %copy-start) | copy-done | bytes 1949720
  40.0 7.1 %shard_map.64 = (bf16[2,288,512]{2,1,0:T(8,128)(2,1)}, bf16[2,288,512]{2,1,0:T(8,128)(2,1)}) custom-call(s32[16]{0:T(128)} %reshape_squeeze.9.pairs_ref, s32[1]{0:T(128)} %bitcast.37.count_ref, s32[2]{0:T(128)} %pad_add_fusion.place_ref, bf16[8,256,256]{2,1,0:T(8,128)(2,1)} %bitcast.39, bf16[7,272,512]{2,1,0:T(8,128)(2,1)} %copy-done, ...), custom_call_target="tpu_custom_call" | custom-call | tf_op jit(solution)/shard_map/pallas_call | solution.py:91
  47.1 0.0 collective-permute-start.6
  47.1 2.2 %collective-permute-done.6 = bf16[2,288,512]{2,1,0:T(8,128)(2,1)S(1)} collective-permute-done((bf16[2,288,512]{2,1,0:T(8,128)(2,1)}, bf16[2,288,512]{2,1,0:T(8,128)(2,1)S(1)}, u32[]{:S(2)}, u32[]{:S(2)}) %collective-permute-start.6) | collective-permute-done | bytes 589856 | tf_op jit(solution)/shard_map/ppermute | solution.py:181
  49.3 1.2 %convert_add_fusion = f32[2,288,512]{2,1,0:T(8,128)S(1)} fusion(bf16[2,288,512]{2,1,0:T(8,128)(2,1)S(1)} %collective-permute-done.6, bf16[2,288,512]{2,1,0:T(8,128)(2,1)} %get-tuple-element.7), kind=kLoop, calls=%fused_computation | loop fusion | flops 884736 | bytes 2359296 | tf_op jit(solution)/shard_map/add | solution.py:182
  50.6 1.8 %collective-permute-start.7 = (bf16[288,512]{1,0:T(8,128)(2,1)S(1)}, bf16[288,512]{1,0:T(8,128)(2,1)S(1)}, u32[]{:S(2)}, u32[]{:S(2)}) collective-permute-start(bf16[288,512]{1,0:T(8,128)(2,1)S(1)} %fusion), channel_id=1, source_target_pairs={{0,2},{2,0},{1,3},{3,1},{4,6},{6,4},{5,7},{7,5},{8,10},{10,8},{9,1... | collective-permute-start | bytes 884744 | tf_op jit(solution)/shard_map/ppermute | solution.py:141
  52.4 7.3 %collective-permute-done.7 = bf16[288,512]{1,0:T(8,128)(2,1)S(1)} collective-permute-done((bf16[288,512]{1,0:T(8,128)(2,1)S(1)}, bf16[288,512]{1,0:T(8,128)(2,1)S(1)}, u32[]{:S(2)}, u32[]{:S(2)}) %collective-permute-start.7) | collective-permute-done | bytes 294944 | tf_op jit(solution)/shard_map/ppermute | solution.py:141
  59.7 0.9 %bitcast_add_fusion.total_ref = f32[288,512]{1,0:T(8,128)} fusion(f32[2,288,512]{2,1,0:T(8,128)S(1)} %convert_add_fusion, s32[]{:T(128)S(6)} %select_n.21, bf16[288,512]{1,0:T(8,128)(2,1)S(1)} %collective-permute-done.7), kind=kLoop, calls=%fused_computation.1 | loop fusion | flops 294912 | bytes 1474564 | tf_op jit(solution)/shard_map/add | solution.py:143
  60.6 2.0 %shard_map.65 = bf16[256,512]{1,0:T(8,128)(2,1)} custom-call(f32[288,512]{1,0:T(8,128)} %bitcast_add_fusion.total_ref, bf16[1,32,256]{2,1,0:T(8,128)(2,1)} %basis_ref.1), custom_call_target="tpu_custom_call" | custom-call | tf_op jit(solution)/shard_map/pallas_call | solution.py:113
  (10 shorter events, 0.2 us)
Async XLA Ops:
  0.0 31.6 %copy-start.1 = (bf16[256,512]{1,0:T(8,128)(2,1)S(1)}, bf16[256,512]{1,0:T(8,128)(2,1)}, u32[]{:S(2)}) copy-start(bf16[256,512]{1,0:T(8,128)(2,1)} %param.6) | copy-start | bytes 786436
  1.7 10.9 %collective-permute-start = (bf16[272,512]{1,0:T(8,128)(2,1)S(1)}, bf16[272,512]{1,0:T(8,128)(2,1)S(1)}, u32[]{:S(2)}, u32[]{:S(2)}) collective-permute-start(bf16[272,512]{1,0:T(8,128)(2,1)S(1)} %maximum_maximum_fusion), channel_id=1, source_target_pairs={{0,4},{4,8},{8,12},{1,5},{5,9},{9,13},{2,6},{6,10},{10,14},{3,7},{... | collective-permute-start | bytes 835592 | tf_op jit(solution)/shard_map/ppermute | solution.py:126
  6.7 10.4 %collective-permute-start.3 = (bf16[272,512]{1,0:T(8,128)(2,1)S(1)}, bf16[272,512]{1,0:T(8,128)(2,1)S(1)}, u32[]{:S(2)}, u32[]{:S(2)}) collective-permute-start(bf16[272,512]{1,0:T(8,128)(2,1)S(1)} %maximum_maximum_fusion), channel_id=1, source_target_pairs={{4,0},{8,4},{12,8},{5,1},{9,5},{13,9},{6,2},{10,6},{14,10},{7,3},{... | collective-permute-start | bytes 835592 | tf_op jit(solution)/shard_map/ppermute | solution.py:127
  12.6 9.4 %collective-permute-start.1 = (bf16[272,512]{1,0:T(8,128)(2,1)S(1)}, bf16[272,512]{1,0:T(8,128)(2,1)S(1)}, u32[]{:S(2)}, u32[]{:S(2)}) collective-permute-start(bf16[272,512]{1,0:T(8,128)(2,1)S(1)} %collective-permute-done), channel_id=1, source_target_pairs={{0,4},{4,8},{8,12},{1,5},{5,9},{9,13},{2,6},{6,10},{10,14},{3,7},{... | collective-permute-start | bytes 835592 | tf_op jit(solution)/shard_map/ppermute | solution.py:126
  17.1 13.1 %collective-permute-start.4 = (bf16[272,512]{1,0:T(8,128)(2,1)S(1)}, bf16[272,512]{1,0:T(8,128)(2,1)S(1)}, u32[]{:S(2)}, u32[]{:S(2)}) collective-permute-start(bf16[272,512]{1,0:T(8,128)(2,1)S(1)} %collective-permute-done.3), channel_id=1, source_target_pairs={{4,0},{8,4},{12,8},{5,1},{9,5},{13,9},{6,2},{10,6},{14,10},{7,3},{... | collective-permute-start | bytes 835592 | tf_op jit(solution)/shard_map/ppermute | solution.py:127
  22.0 9.5 %collective-permute-start.2 = (bf16[272,512]{1,0:T(8,128)(2,1)S(1)}, bf16[272,512]{1,0:T(8,128)(2,1)S(1)}, u32[]{:S(2)}, u32[]{:S(2)}) collective-permute-start(bf16[272,512]{1,0:T(8,128)(2,1)S(1)} %collective-permute-done.1), channel_id=1, source_target_pairs={{0,4},{4,8},{8,12},{1,5},{5,9},{9,13},{2,6},{6,10},{10,14},{3,7},{... | collective-permute-start | bytes 835592 | tf_op jit(solution)/shard_map/ppermute | solution.py:126
  30.2 8.4 %collective-permute-start.5 = (bf16[272,512]{1,0:T(8,128)(2,1)S(1)}, bf16[272,512]{1,0:T(8,128)(2,1)S(1)}, u32[]{:S(2)}, u32[]{:S(2)}) collective-permute-start(bf16[272,512]{1,0:T(8,128)(2,1)S(1)} %collective-permute-done.4), channel_id=1, source_target_pairs={{4,0},{8,4},{12,8},{5,1},{9,5},{13,9},{6,2},{10,6},{14,10},{7,3},{... | collective-permute-start | bytes 835592 | tf_op jit(solution)/shard_map/ppermute | solution.py:127
  38.7 1.3 %copy-start = (bf16[7,272,512]{2,1,0:T(8,128)(2,1)}, bf16[7,272,512]{2,1,0:T(8,128)(2,1)S(1)}, u32[]{:S(2)}) copy-start(bf16[7,272,512]{2,1,0:T(8,128)(2,1)S(1)} %bitcast_dynamic-update-slice_fusion.stack_ref) | copy-start | bytes 5849092
  47.1 2.2 %collective-permute-start.6 = (bf16[2,288,512]{2,1,0:T(8,128)(2,1)}, bf16[2,288,512]{2,1,0:T(8,128)(2,1)S(1)}, u32[]{:S(2)}, u32[]{:S(2)}) collective-permute-start(bf16[2,288,512]{2,1,0:T(8,128)(2,1)} %get-tuple-element.8), channel_id=1, source_target_pairs={{0,1},{1,0},{2,3},{3,2},{4,5},{5,4},{6,7},{7,6},{8,9},{9,8},{10,11... | collective-permute-start | bytes 1769480 | tf_op jit(solution)/shard_map/ppermute | solution.py:181
  50.6 9.1 %collective-permute-start.7 = (bf16[288,512]{1,0:T(8,128)(2,1)S(1)}, bf16[288,512]{1,0:T(8,128)(2,1)S(1)}, u32[]{:S(2)}, u32[]{:S(2)}) collective-permute-start(bf16[288,512]{1,0:T(8,128)(2,1)S(1)} %fusion), channel_id=1, source_target_pairs={{0,2},{2,0},{1,3},{3,1},{4,6},{6,4},{5,7},{7,5},{8,10},{10,8},{9,1... | collective-permute-start | bytes 884744 | tf_op jit(solution)/shard_map/ppermute | solution.py:141

commit v3 on v2

--- a/solution.py
+++ b/solution.py
@@ -7,14 +7,22 @@
 
 
 def _near_far_kernel(
-    pairs_ref, count_ref, place_ref, tiles_ref, stack_ref, masked_ref, mine_ref, theirs_ref, acc_ref
+    pairs_ref,
+    count_ref,
+    place_ref,
+    tiles_ref,
+    stack_ref,
+    basis_ref,
+    masked_ref,
+    mine_ref,
+    theirs_ref,
+    acc_ref,
 ):
     slot = pl.program_id(0)
     slot_total = pl.num_programs(0)
     inner_count, width, rhs_count = acc_ref.shape
     tgt_count = masked_ref.shape[0]
     rank_size = masked_ref.shape[2]
-    half_rank = rank_size // 2
     sub_count = 2
     own_tgt = place_ref[0]
     own_sub = place_ref[1]
@@ -38,12 +46,10 @@
     def _():
         coeffs = jnp.zeros((inner_count * rank_size, rhs_count), jnp.float32)
         for source in range(tgt_count):
-            block = stack_ref[source - own_tgt + tgt_count - 1]
-            dens = block[:width, :]
-            packed = block[width:, :]
-            top = jnp.dot(packed[:, :width], dens, preferred_element_type=jnp.float32)
-            bottom = jnp.dot(packed[:, width:], dens, preferred_element_type=jnp.float32)
-            projected = jnp.concatenate([top, bottom], axis=0).astype(jnp.bfloat16)
+            offset = source - own_tgt + tgt_count - 1
+            projected = jnp.dot(
+                basis_ref[offset], stack_ref[offset, :width, :], preferred_element_type=jnp.float32
+            ).astype(jnp.bfloat16)
             coeffs += jnp.dot(masked_ref[source], projected, preferred_element_type=jnp.float32)
         coeffs = coeffs.astype(jnp.bfloat16)
 
@@ -63,7 +69,7 @@
             write(theirs_ref, mine_ref)
 
 
-def _near_far(pairs_flat, count, place, tiles, stack, masked_t, inner_count, rank_size):
+def _near_far(pairs_flat, count, place, tiles, stack, basis_stack, masked_t, inner_count, rank_size):
     slot_count, width, _ = tiles.shape
     stack_count, rows, rhs_count = stack.shape
     half_count = inner_count // 2
@@ -79,6 +85,7 @@
         in_specs=[
             pl.BlockSpec((None, width, width), tile_index),
             pl.BlockSpec(stack.shape, whole),
+            pl.BlockSpec(basis_stack.shape, whole),
             pl.BlockSpec(masked_t.shape, whole),
         ],
         out_specs=[
@@ -95,39 +102,45 @@
         compiler_params=pltpu.CompilerParams(
             dimension_semantics=("arbitrary",), vmem_limit_bytes=56 * 1024 * 1024
         ),
-    )(pairs_flat, count, place, tiles, stack, masked_t)
-
-
-def _epilogue_kernel(total_ref, basis_ref, out_ref):
+    )(pairs_flat, count, place, tiles, stack, basis_stack, masked_t)
+
+
+def _epilogue_kernel(*refs):
+    basis_ref, total_refs, out_ref = refs[0], refs[1:-1], refs[-1]
     width = out_ref.shape[0]
-    near = total_ref[:width, :]
-    coeffs = total_ref[width:, :].astype(jnp.bfloat16)
-    far = lax.dot_general(
-        basis_ref[0], coeffs, (((0,), (0,)), ((), ())), preferred_element_type=jnp.float32
-    )
-    out_ref[...] = (near + far).astype(out_ref.dtype)
-
-
-def _epilogue(total, basis):
+    for index, total_ref in enumerate(total_refs):
+        cols = total_ref.shape[1]
+        near = total_ref[:width, :]
+        coeffs = total_ref[width:, :].astype(jnp.bfloat16)
+        far = lax.dot_general(
+            basis_ref[0], coeffs, (((0,), (0,)), ((), ())), preferred_element_type=jnp.float32
+        )
+        out_ref[:, index * cols : (index + 1) * cols] = (near + far).astype(out_ref.dtype)
+
+
+def _epilogue(totals, basis):
     width = basis.shape[2]
+    cols = sum(total.shape[1] for total in totals)
     return pl.pallas_call(
         _epilogue_kernel,
-        out_shape=jax.ShapeDtypeStruct((width, total.shape[1]), jnp.bfloat16),
-    )(total, basis)
-
-
-def _line_gather(payload, axis):
+        out_shape=jax.ShapeDtypeStruct((width, cols), jnp.bfloat16),
+    )(basis, *totals)
+
+
+def _line_gather(payload, axis, ties=()):
     n = lax.axis_size(axis)
     up_pairs = [(i, i + 1) for i in range(n - 1)]
     down_pairs = [(i + 1, i) for i in range(n - 1)]
     ups, downs = [], []
     up, down = payload, payload
-    for _ in range(n - 1):
+    for step in range(n - 1):
+        if step < len(ties) and ties[step]:
+            up, down = lax.optimization_barrier((up, down) + tuple(ties[step]))[:2]
         up = lax.ppermute(up, axis, up_pairs)
         down = lax.ppermute(down, axis, down_pairs)
         ups.append(up)
         downs.append(down)
-    return jnp.stack(ups[::-1] + [payload] + downs)
+    return jnp.stack(ups[::-1] + [payload] + downs), (up, down)
 
 
 def _ring_reduce_scatter(blocks, axis):
@@ -150,12 +163,10 @@
     rhs_count = density.shape[1]
     tgt_count = lax.axis_size("tgt")
     inner_count = lax.axis_size(("inner", "sub"))
-    assert lax.axis_size("sub") == 2 and 2 * width == rhs_count and rank_size % 2 == 0
+    assert lax.axis_size("sub") == 2 and 2 * width == rhs_count
     basis = cluster_basis[0]
-    half_rank = rank_size // 2
-    packed = jnp.concatenate([basis[:half_rank], basis[half_rank:]], axis=1)
-    payload = jnp.concatenate([density, packed], axis=0)
-    stack = _line_gather(payload, "tgt")
+    chunk_count = 2
+    cols = rhs_count // chunk_count
 
     pair_list = near_pairs[0, 0]
     live_count = near_count[0, 0]
@@ -172,16 +183,29 @@
     )
     masked = coupling[0, 0].reshape(inner_count, rank_size, tgt_count, rank_size) * keep_mask
     masked_t = masked.transpose(2, 0, 1, 3).reshape(tgt_count, inner_count * rank_size, rank_size)
-
     place = jnp.stack([lax.axis_index("tgt"), lax.axis_index("sub")]).astype(jnp.int32)
-    mine, theirs = _near_far(
-        pair_list.reshape(-1), live_count.reshape(1), place, near_blocks[0, 0], stack, masked_t,
-        inner_count, rank_size,
-    )
-    arrived = lax.ppermute(theirs, "sub", [(0, 1), (1, 0)])
-    stage = mine.astype(jnp.float32) + arrived.astype(jnp.float32)
-    total = _ring_reduce_scatter(stage, "inner")
-    return _epilogue(total, cluster_basis)
+
+    totals = []
+    basis_stack = None
+    previous = None
+    for chunk in range(chunk_count):
+        piece = density[:, chunk * cols : (chunk + 1) * cols]
+        if chunk == 0:
+            stack, last_round = _line_gather(jnp.concatenate([piece, basis], axis=0), "tgt")
+            basis_stack = stack[:, width:, :]
+        else:
+            ties = (previous[0], previous[1], previous[2])
+            stack, last_round = _line_gather(piece, "tgt", ties)
+            stack = lax.optimization_barrier((stack, previous[3]))[0]
+        mine, theirs = _near_far(
+            pair_list.reshape(-1), live_count.reshape(1), place, near_blocks[0, 0], stack,
+            basis_stack, masked_t, inner_count, rank_size,
+        )
+        arrived = lax.ppermute(theirs, "sub", [(0, 1), (1, 0)])
+        stage = mine.astype(jnp.float32) + arrived.astype(jnp.float32)
+        totals.append(_ring_reduce_scatter(stage, "inner"))
+        previous = (tuple(last_round), (mine, theirs), (stage,), totals[-1])
+    return _epilogue(totals, cluster_basis)
 
 
 def solution(mesh):

time: 63.2 us -> 89.4 us (1.41)
  starting transfers between devices: 19.4 us -> 34.1 us
  waiting for transfers between devices: 23.3 us -> 28.9 us
  Pallas kernels: 9.15 us -> 14.4 us
    ppermute x3 -> x6, waiting for transfers between devices: 6.96 us -> 18.6 us  [_line_gather(): down = lax.ppermute(down, axis, down_pairs)]
    ppermute x3 -> x6, starting transfers between devices: 13.8 us -> 22.8 us  [_line_gather(): up = lax.ppermute(up, axis, up_pairs)]
    pallas_call x1 -> x2, Pallas kernels: 7.14 us -> 12.4 us  [_near_far(): pl.pallas_call(_near_far_kernel, grid_spec=grid_spec, out_shape=[out, out...]
    ppermute x3 -> x6, starting transfers between devices: 3.86 us -> 7.72 us  [_line_gather(): down = lax.ppermute(down, axis, down_pairs)]
    ppermute x3 -> x6, waiting for transfers between devices: 6.79 us -> 3.62 us  [_line_gather(): up = lax.ppermute(up, axis, up_pairs)]
    ppermute x1 -> x2, waiting for transfers between devices: 7.31 us -> 4.82 us  [_ring_reduce_scatter(): arrived = lax.ppermute(carry.astype(jnp.bfloat16), axis, ring)]
    ppermute x1 -> x2, starting transfers between devices: 1.8 us -> 3.52 us  [_ring_reduce_scatter(): arrived = lax.ppermute(carry.astype(jnp.bfloat16), axis, ring)]
    concatenate x1, other arithmetic: 0.97 us -> 0.01 us  [on_device(): jnp.concatenate([piece, basis], axis=0)]
  transfers between devices with their start and end apart: 8 -> 16, of which waited for: 5 -> 10; matrix products, arithmetic and copies ran while one was open for 8% -> 4% of each run, Pallas kernels for 0% -> 0%
where the time goes in v3:
time: 89.4 us; the launch traced here: 88.6 us
  starting transfers between devices  34.1 us (38%)
  waiting for transfers between devices  28.9 us (32%)
  Pallas kernels  14.4 us (16%)
  other arithmetic  5.13 us (6%)
  local copies, waits for them, and re-layouts  5.04 us (6%)
  between operations  1.03 us (1%)
    ppermute x6, starting transfers between devices, _line_gather(): up = lax.ppermute(up, axis, up_pairs)  22.8 us
    ppermute x6, waiting for transfers between devices, _line_gather(): down = lax.ppermute(down, axis, down_pairs)  18.6 us
    pallas_call x2, Pallas kernels, _near_far(): pl.pallas_call(_near_far_kernel, grid_spec=grid_spec, out_shape=[out, out...  12.4 us
    ppermute x6, starting transfers between devices, _line_gather(): down = lax.ppermute(down, axis, down_pairs)  7.72 us
    ppermute x2, waiting for transfers between devices, _ring_reduce_scatter(): arrived = lax.ppermute(carry.astype(jnp.bfloat16), axis, ring)  4.82 us
    ppermute x6, waiting for transfers between devices, _line_gather(): up = lax.ppermute(up, axis, up_pairs)  3.62 us
    ppermute x2, starting transfers between devices, _ring_reduce_scatter(): arrived = lax.ppermute(carry.astype(jnp.bfloat16), axis, ring)  3.52 us
    unnamed x24, local copies, waits for them, and re-layouts  2.32 us
  transfers between devices with their start and end apart: 16, of which 10 were waited for; matrix products, arithmetic and copies ran while one was open for 4% of the time, Pallas kernels for 0%

profile of v3, /device:TPU:0, one launch (start us, length us, event | category | flops | bytes accessed | tf_op | source)
XLA Modules:
  0.0 88.6 jit_solution(6471180626588638683)
XLA Ops:
  0.0 0.0 copy-start.3
  0.0 1.0 %fusion.4 = (bf16[256,256]{1,0:T(8,128)(2,1)S(1)}, bf16[256,256]{1,0:T(8,128)(2,1)S(1)}) fusion(bf16[256,512]{1,0:T(8,128)(2,1)} %param.6), kind=kLoop, calls=%fused_computation.31 | loop fusion | bytes 524288 | tf_op jit(solution)/shard_map/slice | solution.py:192
  1.0 0.0 copy-done.3
  1.0 0.0 copy-start.4
  1.0 5.0 %collective-permute-start = (bf16[288,256]{1,0:T(8,128)(2,1)S(1)}, bf16[288,256]{1,0:T(8,128)(2,1)S(1)}, u32[]{:S(2)}, u32[]{:S(2)}) collective-permute-start(bf16[288,256]{1,0:T(8,128)(2,1)S(1)} %pad_maximum_fusion), channel_id=1, source_target_pairs={{0,4},{4,8},{8,12},{1,5},{5,9},{9,13},{2,6},{6,10},{10,14},{3,7},{... | collective-permute-start | bytes 442376 | tf_op jit(solution)/shard_map/ppermute | solution.py:139
  6.0 1.3 %collective-permute-start.3 = (bf16[288,256]{1,0:T(8,128)(2,1)S(1)}, bf16[288,256]{1,0:T(8,128)(2,1)S(1)}, u32[]{:S(2)}, u32[]{:S(2)}) collective-permute-start(bf16[288,256]{1,0:T(8,128)(2,1)S(1)} %pad_maximum_fusion), channel_id=1, source_target_pairs={{4,0},{8,4},{12,8},{5,1},{9,5},{13,9},{6,2},{10,6},{14,10},{7,3},{... | collective-permute-start | bytes 442376 | tf_op jit(solution)/shard_map/ppermute | solution.py:140
  8.0 0.0 copy-start.5
  8.0 0.7 copy-done.5
  8.7 0.0 copy-done.4
  8.7 0.1 reshape_squeeze.13
  8.8 0.1 fusion.3
  8.9 0.2 collective-permute-done
  9.1 4.4 %collective-permute-start.1 = (bf16[288,256]{1,0:T(8,128)(2,1)S(1)}, bf16[288,256]{1,0:T(8,128)(2,1)S(1)}, u32[]{:S(2)}, u32[]{:S(2)}) collective-permute-start(bf16[288,256]{1,0:T(8,128)(2,1)S(1)} %collective-permute-done), channel_id=1, source_target_pairs={{0,4},{4,8},{8,12},{1,5},{5,9},{9,13},{2,6},{6,10},{10,14},{3,7},{... | collective-permute-start | bytes 442376 | tf_op jit(solution)/shard_map/ppermute | solution.py:139
  13.5 0.1 convert_element_type.52
  13.6 0.1 copy.14
  13.7 0.0 collective-permute-done.3
  13.7 1.3 %collective-permute-start.4 = (bf16[288,256]{1,0:T(8,128)(2,1)S(1)}, bf16[288,256]{1,0:T(8,128)(2,1)S(1)}, u32[]{:S(2)}, u32[]{:S(2)}) collective-permute-start(bf16[288,256]{1,0:T(8,128)(2,1)S(1)} %collective-permute-done.3), channel_id=1, source_target_pairs={{4,0},{8,4},{12,8},{5,1},{9,5},{13,9},{6,2},{10,6},{14,10},{7,3},{... | collective-permute-start | bytes 442376 | tf_op jit(solution)/shard_map/ppermute | solution.py:140
  15.0 1.1 %collective-permute-done.1 = bf16[288,256]{1,0:T(8,128)(2,1)S(1)} collective-permute-done((bf16[288,256]{1,0:T(8,128)(2,1)S(1)}, bf16[288,256]{1,0:T(8,128)(2,1)S(1)}, u32[]{:S(2)}, u32[]{:S(2)}) %collective-permute-start.1) | collective-permute-done | bytes 147488 | tf_op jit(solution)/shard_map/ppermute | solution.py:139
  16.1 4.4 %collective-permute-start.2 = (bf16[288,256]{1,0:T(8,128)(2,1)S(1)}, bf16[288,256]{1,0:T(8,128)(2,1)S(1)}, u32[]{:S(2)}, u32[]{:S(2)}) collective-permute-start(bf16[288,256]{1,0:T(8,128)(2,1)S(1)} %collective-permute-done.1), channel_id=1, source_target_pairs={{0,4},{4,8},{8,12},{1,5},{5,9},{9,13},{2,6},{6,10},{10,14},{3,7},{... | collective-permute-start | bytes 442376 | tf_op jit(solution)/shard_map/ppermute | solution.py:139
  20.5 0.7 copy_multiply_fusion
  21.3 0.1 copy.13
  21.3 0.7 reshape_squeeze.11.pairs_ref
  22.0 0.6 pad_add_fusion.place_ref
  22.6 0.0 collective-permute-done.4
  22.6 1.3 %collective-permute-start.5 = (bf16[288,256]{1,0:T(8,128)(2,1)S(1)}, bf16[288,256]{1,0:T(8,128)(2,1)S(1)}, u32[]{:S(2)}, u32[]{:S(2)}) collective-permute-start(bf16[288,256]{1,0:T(8,128)(2,1)S(1)} %collective-permute-done.4), channel_id=1, source_target_pairs={{4,0},{8,4},{12,8},{5,1},{9,5},{13,9},{6,2},{10,6},{14,10},{7,3},{... | collective-permute-start | bytes 442376 | tf_op jit(solution)/shard_map/ppermute | solution.py:140
  23.9 0.0 collective-permute-done.2
  24.0 5.6 %collective-permute-done.5 = bf16[288,256]{1,0:T(8,128)(2,1)S(1)} collective-permute-done((bf16[288,256]{1,0:T(8,128)(2,1)S(1)}, bf16[288,256]{1,0:T(8,128)(2,1)S(1)}, u32[]{:S(2)}, u32[]{:S(2)}) %collective-permute-start.5) | collective-permute-done | bytes 147488 | tf_op jit(solution)/shard_map/ppermute | solution.py:140
  29.7 0.0 copy-start
  29.7 0.7 slice.20.basis_ref
  30.4 0.3 copy-done
  30.7 6.2 %shard_map.64 = (bf16[2,288,256]{2,1,0:T(8,128)(2,1)}, bf16[2,288,256]{2,1,0:T(8,128)(2,1)}) custom-call(s32[16]{0:T(128)} %reshape_squeeze.11.pairs_ref, s32[1]{0:T(128)} %bitcast.52.count_ref, s32[2]{0:T(128)} %pad_add_fusion.place_ref, bf16[8,256,256]{2,1,0:T(8,128)(2,1)} %bitcast.55, bf16[7,288,256]{2,1,0:T(8,128)(2,1)} %copy-done, ...), custom_call_target="tpu_custom_call" | custom-call | tf_op jit(solution)/shard_map/pallas_call | solution.py:98
  36.9 0.0 collective-permute-start.6
  36.9 3.5 %collective-permute-start.8 = (bf16[256,256]{1,0:T(8,128)(2,1)S(1)}, bf16[256,256]{1,0:T(8,128)(2,1)S(1)}, u32[]{:S(2)}, u32[]{:S(2)}) collective-permute-start(bf16[256,256]{1,0:T(8,128)(2,1)S(1)} %get-tuple-element.19), channel_id=1, source_target_pairs={{0,4},{4,8},{8,12},{1,5},{5,9},{9,13},{2,6},{6,10},{10,14},{3,7},{... | collective-permute-start | bytes 393224 | tf_op jit(solution)/shard_map/ppermute | solution.py:139
  40.4 1.3 %collective-permute-start.9 = (bf16[256,256]{1,0:T(8,128)(2,1)S(1)}, bf16[256,256]{1,0:T(8,128)(2,1)S(1)}, u32[]{:S(2)}, u32[]{:S(2)}) collective-permute-start(bf16[256,256]{1,0:T(8,128)(2,1)S(1)} %get-tuple-element.19), channel_id=1, source_target_pairs={{4,0},{8,4},{12,8},{5,1},{9,5},{13,9},{6,2},{10,6},{14,10},{7,3},{... | collective-permute-start | bytes 393224 | tf_op jit(solution)/shard_map/ppermute | solution.py:140
  41.7 2.1 %collective-permute-done.8 = bf16[256,256]{1,0:T(8,128)(2,1)S(1)} collective-permute-done((bf16[256,256]{1,0:T(8,128)(2,1)S(1)}, bf16[256,256]{1,0:T(8,128)(2,1)S(1)}, u32[]{:S(2)}, u32[]{:S(2)}) %collective-permute-start.8) | collective-permute-done | bytes 131104 | tf_op jit(solution)/shard_map/ppermute | solution.py:139
  43.8 4.1 %collective-permute-done.9 = bf16[256,256]{1,0:T(8,128)(2,1)S(1)} collective-permute-done((bf16[256,256]{1,0:T(8,128)(2,1)S(1)}, bf16[256,256]{1,0:T(8,128)(2,1)S(1)}, u32[]{:S(2)}, u32[]{:S(2)}) %collective-permute-start.9) | collective-permute-done | bytes 131104 | tf_op jit(solution)/shard_map/ppermute | solution.py:140
  47.9 3.5 %collective-permute-start.10 = (bf16[256,256]{1,0:T(8,128)(2,1)S(1)}, bf16[256,256]{1,0:T(8,128)(2,1)S(1)}, u32[]{:S(2)}, u32[]{:S(2)}) collective-permute-start(bf16[256,256]{1,0:T(8,128)(2,1)S(1)} %collective-permute-done.8), channel_id=1, source_target_pairs={{0,4},{4,8},{8,12},{1,5},{5,9},{9,13},{2,6},{6,10},{10,14},{3,7},{... | collective-permute-start | bytes 393224 | tf_op jit(solution)/shard_map/ppermute | solution.py:139
  51.4 1.3 %collective-permute-start.11 = (bf16[256,256]{1,0:T(8,128)(2,1)S(1)}, bf16[256,256]{1,0:T(8,128)(2,1)S(1)}, u32[]{:S(2)}, u32[]{:S(2)}) collective-permute-start(bf16[256,256]{1,0:T(8,128)(2,1)S(1)} %collective-permute-done.9), channel_id=1, source_target_pairs={{4,0},{8,4},{12,8},{5,1},{9,5},{13,9},{6,2},{10,6},{14,10},{7,3},{... | collective-permute-start | bytes 393224 | tf_op jit(solution)/shard_map/ppermute | solution.py:140
  52.7 0.0 collective-permute-done.6
  52.7 1.0 %convert_add_fusion.1 = f32[2,288,256]{2,1,0:T(8,128)S(1)} fusion(bf16[2,288,256]{2,1,0:T(8,128)(2,1)S(1)} %collective-permute-done.6, bf16[2,288,256]{2,1,0:T(8,128)(2,1)} %get-tuple-element.16), kind=kLoop, calls=%fused_computation.1 | loop fusion | flops 442368 | bytes 1179648 | tf_op jit(solution)/shard_map/add | solution.py:205
  53.8 0.1 collective-permute-done.10
  53.9 4.4 %collective-permute-done.11 = bf16[256,256]{1,0:T(8,128)(2,1)S(1)} collective-permute-done((bf16[256,256]{1,0:T(8,128)(2,1)S(1)}, bf16[256,256]{1,0:T(8,128)(2,1)S(1)}, u32[]{:S(2)}, u32[]{:S(2)}) %collective-permute-start.11) | collective-permute-done | bytes 131104 | tf_op jit(solution)/shard_map/ppermute | solution.py:140
  58.3 2.2 %collective-permute-start.12 = (bf16[256,256]{1,0:T(8,128)(2,1)S(1)}, bf16[256,256]{1,0:T(8,128)(2,1)S(1)}, u32[]{:S(2)}, u32[]{:S(2)}) collective-permute-start(bf16[256,256]{1,0:T(8,128)(2,1)S(1)} %collective-permute-done.10), channel_id=1, source_target_pairs={{0,4},{4,8},{8,12},{1,5},{5,9},{9,13},{2,6},{6,10},{10,14},{3,7},{... | collective-permute-start | bytes 393224 | tf_op jit(solution)/shard_map/ppermute | solution.py:139
  60.5 2.4 %collective-permute-start.7 = (bf16[288,256]{1,0:T(8,128)(2,1)S(1)}, bf16[288,256]{1,0:T(8,128)(2,1)S(1)}, u32[]{:S(2)}, u32[]{:S(2)}) collective-permute-start(bf16[288,256]{1,0:T(8,128)(2,1)S(1)} %fusion), channel_id=1, source_target_pairs={{0,2},{2,0},{1,3},{3,1},{4,6},{6,4},{5,7},{7,5},{8,10},{10,8},{9,1... | collective-permute-start | bytes 442376 | tf_op jit(solution)/shard_map/ppermute | solution.py:154
  62.9 1.3 %collective-permute-start.13 = (bf16[256,256]{1,0:T(8,128)(2,1)S(1)}, bf16[256,256]{1,0:T(8,128)(2,1)S(1)}, u32[]{:S(2)}, u32[]{:S(2)}) collective-permute-start(bf16[256,256]{1,0:T(8,128)(2,1)S(1)} %collective-permute-done.11), channel_id=1, source_target_pairs={{4,0},{8,4},{12,8},{5,1},{9,5},{13,9},{6,2},{10,6},{14,10},{7,3},{... | collective-permute-start | bytes 393224 | tf_op jit(solution)/shard_map/ppermute | solution.py:140
  64.2 0.0 collective-permute-done.12
  64.2 0.0 copy-start.2
  64.3 0.9 %copy-done.2 = bf16[256,512]{1,0:T(8,128)(2,1)S(1)} copy-done((bf16[256,512]{1,0:T(8,128)(2,1)S(1)}, bf16[256,512]{1,0:T(8,128)(2,1)}, u32[]{:S(2)}) %copy-start.2) | copy-done | bytes 262168
  65.3 4.5 %collective-permute-done.13 = bf16[256,256]{1,0:T(8,128)(2,1)S(1)} collective-permute-done((bf16[256,256]{1,0:T(8,128)(2,1)S(1)}, bf16[256,256]{1,0:T(8,128)(2,1)S(1)}, u32[]{:S(2)}, u32[]{:S(2)}) %collective-permute-start.13) | collective-permute-done | bytes 131104 | tf_op jit(solution)/shard_map/ppermute | solution.py:140
  69.8 0.0 copy-start.1
  69.8 0.0 collective-permute-done.7
  69.8 0.8 bitcast_add_fusion.1.refs_1_
  70.6 0.2 copy-done.1
  70.8 6.2 %shard_map.65 = (bf16[2,288,256]{2,1,0:T(8,128)(2,1)}, bf16[2,288,256]{2,1,0:T(8,128)(2,1)}) custom-call(s32[16]{0:T(128)} %reshape_squeeze.11.pairs_ref, s32[1]{0:T(128)} %bitcast.53.count_ref, s32[2]{0:T(128)} %pad_add_fusion.place_ref, bf16[8,256,256]{2,1,0:T(8,128)(2,1)} %bitcast.56, bf16[7,256,256]{2,1,0:T(8,128)(2,1)} %copy-done.1, ...), custom_call_target="tpu_custom_call" | custom-call | tf_op jit(solution)/shard_map/pallas_call | solution.py:98
  77.0 0.0 collective-permute-start.14
  77.0 1.8 %collective-permute-done.14 = bf16[2,288,256]{2,1,0:T(8,128)(2,1)S(1)} collective-permute-done((bf16[2,288,256]{2,1,0:T(8,128)(2,1)}, bf16[2,288,256]{2,1,0:T(8,128)(2,1)S(1)}, u32[]{:S(2)}, u32[]{:S(2)}) %collective-permute-start.14) | collective-permute-done | bytes 294944 | tf_op jit(solution)/shard_map/ppermute | solution.py:204
  78.8 1.0 %convert_add_fusion = f32[2,288,256]{2,1,0:T(8,128)S(1)} fusion(bf16[2,288,256]{2,1,0:T(8,128)(2,1)S(1)} %collective-permute-done.14, bf16[2,288,256]{2,1,0:T(8,128)(2,1)} %get-tuple-element.25), kind=kLoop, calls=%fused_computation | loop fusion | flops 442368 | bytes 1179648 | tf_op jit(solution)/shard_map/add | solution.py:205
  79.9 1.1 %collective-permute-start.15 = (bf16[288,256]{1,0:T(8,128)(2,1)S(1)}, bf16[288,256]{1,0:T(8,128)(2,1)S(1)}, u32[]{:S(2)}, u32[]{:S(2)}) collective-permute-start(bf16[288,256]{1,0:T(8,128)(2,1)S(1)} %fusion.1), channel_id=1, source_target_pairs={{0,2},{2,0},{1,3},{3,1},{4,6},{6,4},{5,7},{7,5},{8,10},{10,8},{9,1... | collective-permute-start | bytes 442376 | tf_op jit(solution)/shard_map/ppermute | solution.py:154
  81.0 4.8 %collective-permute-done.15 = bf16[288,256]{1,0:T(8,128)(2,1)S(1)} collective-permute-done((bf16[288,256]{1,0:T(8,128)(2,1)S(1)}, bf16[288,256]{1,0:T(8,128)(2,1)S(1)}, u32[]{:S(2)}, u32[]{:S(2)}) %collective-permute-start.15) | collective-permute-done | bytes 147488 | tf_op jit(solution)/shard_map/ppermute | solution.py:154
  85.8 0.7 bitcast_add_fusion.refs_2_
  86.6 2.0 %shard_map.66 = bf16[256,512]{1,0:T(8,128)(2,1)} custom-call(bf16[1,32,256]{2,1,0:T(8,128)(2,1)} %refs_0_.1, f32[288,256]{1,0:T(8,128)} %bitcast_add_fusion.1.refs_1_, f32[288,256]{1,0:T(8,128)} %bitcast_add_fusion.refs_2_), custom_call_target="tpu_custom_call" | custom-call | tf_op jit(solution)/shard_map/pallas_call | solution.py:124
  (20 shorter events, 0.2 us)
Async XLA Ops:
  0.0 1.0 %copy-start.3 = (bf16[1,32,256]{2,1,0:T(8,128)(2,1)S(1)}, bf16[1,32,256]{2,1,0:T(8,128)(2,1)}, u32[]{:S(2)}) copy-start(bf16[1,32,256]{2,1,0:T(8,128)(2,1)} %refs_0_.1) | copy-start | bytes 49156
  1.0 7.6 %copy-start.4 = (bf16[1,1,128,128]{3,2,1,0:T(8,128)(2,1)S(1)}, bf16[1,1,128,128]{3,2,1,0:T(8,128)(2,1)}, u32[]{:S(2)}) copy-start(bf16[1,1,128,128]{3,2,1,0:T(8,128)(2,1)} %param.11) | copy-start | bytes 98308
  1.0 8.1 %collective-permute-start = (bf16[288,256]{1,0:T(8,128)(2,1)S(1)}, bf16[288,256]{1,0:T(8,128)(2,1)S(1)}, u32[]{:S(2)}, u32[]{:S(2)}) collective-permute-start(bf16[288,256]{1,0:T(8,128)(2,1)S(1)} %pad_maximum_fusion), channel_id=1, source_target_pairs={{0,4},{4,8},{8,12},{1,5},{5,9},{9,13},{2,6},{6,10},{10,14},{3,7},{... | collective-permute-start | bytes 442376 | tf_op jit(solution)/shard_map/ppermute | solution.py:139
  6.0 7.7 %collective-permute-start.3 = (bf16[288,256]{1,0:T(8,128)(2,1)S(1)}, bf16[288,256]{1,0:T(8,128)(2,1)S(1)}, u32[]{:S(2)}, u32[]{:S(2)}) collective-permute-start(bf16[288,256]{1,0:T(8,128)(2,1)S(1)} %pad_maximum_fusion), channel_id=1, source_target_pairs={{4,0},{8,4},{12,8},{5,1},{9,5},{13,9},{6,2},{10,6},{14,10},{7,3},{... | collective-permute-start | bytes 442376 | tf_op jit(solution)/shard_map/ppermute | solution.py:140
  8.0 0.7 copy-start.5
  9.1 7.0 %collective-permute-start.1 = (bf16[288,256]{1,0:T(8,128)(2,1)S(1)}, bf16[288,256]{1,0:T(8,128)(2,1)S(1)}, u32[]{:S(2)}, u32[]{:S(2)}) collective-permute-start(bf16[288,256]{1,0:T(8,128)(2,1)S(1)} %collective-permute-done), channel_id=1, source_target_pairs={{0,4},{4,8},{8,12},{1,5},{5,9},{9,13},{2,6},{6,10},{10,14},{3,7},{... | collective-permute-start | bytes 442376 | tf_op jit(solution)/shard_map/ppermute | solution.py:139
  13.7 8.9 %collective-permute-start.4 = (bf16[288,256]{1,0:T(8,128)(2,1)S(1)}, bf16[288,256]{1,0:T(8,128)(2,1)S(1)}, u32[]{:S(2)}, u32[]{:S(2)}) collective-permute-start(bf16[288,256]{1,0:T(8,128)(2,1)S(1)} %collective-permute-done.3), channel_id=1, source_target_pairs={{4,0},{8,4},{12,8},{5,1},{9,5},{13,9},{6,2},{10,6},{14,10},{7,3},{... | collective-permute-start | bytes 442376 | tf_op jit(solution)/shard_map/ppermute | solution.py:140
  16.1 7.8 %collective-permute-start.2 = (bf16[288,256]{1,0:T(8,128)(2,1)S(1)}, bf16[288,256]{1,0:T(8,128)(2,1)S(1)}, u32[]{:S(2)}, u32[]{:S(2)}) collective-permute-start(bf16[288,256]{1,0:T(8,128)(2,1)S(1)} %collective-permute-done.1), channel_id=1, source_target_pairs={{0,4},{4,8},{8,12},{1,5},{5,9},{9,13},{2,6},{6,10},{10,14},{3,7},{... | collective-permute-start | bytes 442376 | tf_op jit(solution)/shard_map/ppermute | solution.py:139
  22.6 7.0 %collective-permute-start.5 = (bf16[288,256]{1,0:T(8,128)(2,1)S(1)}, bf16[288,256]{1,0:T(8,128)(2,1)S(1)}, u32[]{:S(2)}, u32[]{:S(2)}) collective-permute-start(bf16[288,256]{1,0:T(8,128)(2,1)S(1)} %collective-permute-done.4), channel_id=1, source_target_pairs={{4,0},{8,4},{12,8},{5,1},{9,5},{13,9},{6,2},{10,6},{14,10},{7,3},{... | collective-permute-start | bytes 442376 | tf_op jit(solution)/shard_map/ppermute | solution.py:140
  29.7 1.0 %copy-start = (bf16[7,288,256]{2,1,0:T(8,128)(2,1)}, bf16[7,288,256]{2,1,0:T(8,128)(2,1)S(1)}, u32[]{:S(2)}) copy-start(bf16[7,288,256]{2,1,0:T(8,128)(2,1)S(1)} %bitcast_dynamic-update-slice_fusion.stack_ref) | copy-start | bytes 3096580
  36.9 15.8 %collective-permute-start.6 = (bf16[2,288,256]{2,1,0:T(8,128)(2,1)}, bf16[2,288,256]{2,1,0:T(8,128)(2,1)S(1)}, u32[]{:S(2)}, u32[]{:S(2)}) collective-permute-start(bf16[2,288,256]{2,1,0:T(8,128)(2,1)} %get-tuple-element.17), channel_id=1, source_target_pairs={{0,1},{1,0},{2,3},{3,2},{4,5},{5,4},{6,7},{7,6},{8,9},{9,8},{10,11... | collective-permute-start | bytes 884744 | tf_op jit(solution)/shard_map/ppermute | solution.py:204
  36.9 6.9 %collective-permute-start.8 = (bf16[256,256]{1,0:T(8,128)(2,1)S(1)}, bf16[256,256]{1,0:T(8,128)(2,1)S(1)}, u32[]{:S(2)}, u32[]{:S(2)}) collective-permute-start(bf16[256,256]{1,0:T(8,128)(2,1)S(1)} %get-tuple-element.19), channel_id=1, source_target_pairs={{0,4},{4,8},{8,12},{1,5},{5,9},{9,13},{2,6},{6,10},{10,14},{3,7},{... | collective-permute-start | bytes 393224 | tf_op jit(solution)/shard_map/ppermute | solution.py:139
  40.4 7.5 %collective-permute-start.9 = (bf16[256,256]{1,0:T(8,128)(2,1)S(1)}, bf16[256,256]{1,0:T(8,128)(2,1)S(1)}, u32[]{:S(2)}, u32[]{:S(2)}) collective-permute-start(bf16[256,256]{1,0:T(8,128)(2,1)S(1)} %get-tuple-element.19), channel_id=1, source_target_pairs={{4,0},{8,4},{12,8},{5,1},{9,5},{13,9},{6,2},{10,6},{14,10},{7,3},{... | collective-permute-start | bytes 393224 | tf_op jit(solution)/shard_map/ppermute | solution.py:140
  47.9 6.0 %collective-permute-start.10 = (bf16[256,256]{1,0:T(8,128)(2,1)S(1)}, bf16[256,256]{1,0:T(8,128)(2,1)S(1)}, u32[]{:S(2)}, u32[]{:S(2)}) collective-permute-start(bf16[256,256]{1,0:T(8,128)(2,1)S(1)} %collective-permute-done.8), channel_id=1, source_target_pairs={{0,4},{4,8},{8,12},{1,5},{5,9},{9,13},{2,6},{6,10},{10,14},{3,7},{... | collective-permute-start | bytes 393224 | tf_op jit(solution)/shard_map/ppermute | solution.py:139
  51.4 6.9 %collective-permute-start.11 = (bf16[256,256]{1,0:T(8,128)(2,1)S(1)}, bf16[256,256]{1,0:T(8,128)(2,1)S(1)}, u32[]{:S(2)}, u32[]{:S(2)}) collective-permute-start(bf16[256,256]{1,0:T(8,128)(2,1)S(1)} %collective-permute-done.9), channel_id=1, source_target_pairs={{4,0},{8,4},{12,8},{5,1},{9,5},{13,9},{6,2},{10,6},{14,10},{7,3},{... | collective-permute-start | bytes 393224 | tf_op jit(solution)/shard_map/ppermute | solution.py:140
  58.3 5.9 %collective-permute-start.12 = (bf16[256,256]{1,0:T(8,128)(2,1)S(1)}, bf16[256,256]{1,0:T(8,128)(2,1)S(1)}, u32[]{:S(2)}, u32[]{:S(2)}) collective-permute-start(bf16[256,256]{1,0:T(8,128)(2,1)S(1)} %collective-permute-done.10), channel_id=1, source_target_pairs={{0,4},{4,8},{8,12},{1,5},{5,9},{9,13},{2,6},{6,10},{10,14},{3,7},{... | collective-permute-start | bytes 393224 | tf_op jit(solution)/shard_map/ppermute | solution.py:139
  60.5 9.3 %collective-permute-start.7 = (bf16[288,256]{1,0:T(8,128)(2,1)S(1)}, bf16[288,256]{1,0:T(8,128)(2,1)S(1)}, u32[]{:S(2)}, u32[]{:S(2)}) collective-permute-start(bf16[288,256]{1,0:T(8,128)(2,1)S(1)} %fusion), channel_id=1, source_target_pairs={{0,2},{2,0},{1,3},{3,1},{4,6},{6,4},{5,7},{7,5},{8,10},{10,8},{9,1... | collective-permute-start | bytes 442376 | tf_op jit(solution)/shard_map/ppermute | solution.py:154
  62.9 6.8 %collective-permute-start.13 = (bf16[256,256]{1,0:T(8,128)(2,1)S(1)}, bf16[256,256]{1,0:T(8,128)(2,1)S(1)}, u32[]{:S(2)}, u32[]{:S(2)}) collective-permute-start(bf16[256,256]{1,0:T(8,128)(2,1)S(1)} %collective-permute-done.11), channel_id=1, source_target_pairs={{4,0},{8,4},{12,8},{5,1},{9,5},{13,9},{6,2},{10,6},{14,10},{7,3},{... | collective-permute-start | bytes 393224 | tf_op jit(solution)/shard_map/ppermute | solution.py:140
  64.2 1.0 %copy-start.2 = (bf16[256,512]{1,0:T(8,128)(2,1)S(1)}, bf16[256,512]{1,0:T(8,128)(2,1)}, u32[]{:S(2)}) copy-start(bf16[256,512]{1,0:T(8,128)(2,1)} %param.6) | copy-start | bytes 786436
  69.8 1.0 %copy-start.1 = (bf16[7,256,256]{2,1,0:T(8,128)(2,1)}, bf16[7,256,256]{2,1,0:T(8,128)(2,1)S(1)}, u32[]{:S(2)}) copy-start(bf16[7,256,256]{2,1,0:T(8,128)(2,1)S(1)} %bitcast_dynamic-update-slice_fusion.7.stack_ref) | copy-start | bytes 2752516
  77.0 1.8 %collective-permute-start.14 = (bf16[2,288,256]{2,1,0:T(8,128)(2,1)}, bf16[2,288,256]{2,1,0:T(8,128)(2,1)S(1)}, u32[]{:S(2)}, u32[]{:S(2)}) collective-permute-start(bf16[2,288,256]{2,1,0:T(8,128)(2,1)} %get-tuple-element.26), channel_id=1, source_target_pairs={{0,1},{1,0},{2,3},{3,2},{4,5},{5,4},{6,7},{7,6},{8,9},{9,8},{10,11... | collective-permute-start | bytes 884744 | tf_op jit(solution)/shard_map/ppermute | solution.py:204
  79.9 6.0 %collective-permute-start.15 = (bf16[288,256]{1,0:T(8,128)(2,1)S(1)}, bf16[288,256]{1,0:T(8,128)(2,1)S(1)}, u32[]{:S(2)}, u32[]{:S(2)}) collective-permute-start(bf16[288,256]{1,0:T(8,128)(2,1)S(1)} %fusion.1), channel_id=1, source_target_pairs={{0,2},{2,0},{1,3},{3,1},{4,6},{6,4},{5,7},{7,5},{8,10},{10,8},{9,1... | collective-permute-start | bytes 442376 | tf_op jit(solution)/shard_map/ppermute | solution.py:154

commit v4 on v2

--- a/solution.py
+++ b/solution.py
@@ -118,11 +118,11 @@
 
 def _line_gather(payload, axis):
     n = lax.axis_size(axis)
-    up_pairs = [(i, i + 1) for i in range(n - 1)]
-    down_pairs = [(i + 1, i) for i in range(n - 1)]
     ups, downs = [], []
     up, down = payload, payload
-    for _ in range(n - 1):
+    for step in range(n - 1):
+        up_pairs = [(i, i + 1) for i in range(step, n - 1)]
+        down_pairs = [(i + 1, i) for i in range(n - 1 - step)]
         up = lax.ppermute(up, axis, up_pairs)
         down = lax.ppermute(down, axis, down_pairs)
         ups.append(up)

time: 63.2 us -> 59.7 us (0.945); the launches traced: 62.6 us -> 59.9 us
  starting transfers between devices: 19.4 us -> 11.7 us
  waiting for transfers between devices: 23.3 us -> 26.9 us
  Pallas kernels: 9.15 us -> 10.5 us
    ppermute x3, starting transfers between devices: 13.8 us -> 6.32 us  [_line_gather(): up = lax.ppermute(up, axis, up_pairs)]
    ppermute x3, waiting for transfers between devices: 6.96 us -> 14 us  [_line_gather(): down = lax.ppermute(down, axis, down_pairs)]
    ppermute x3, waiting for transfers between devices: 6.79 us -> 3.16 us  [_line_gather(): up = lax.ppermute(up, axis, up_pairs)]
    pallas_call x1, Pallas kernels: 7.14 us -> 8.45 us  [_near_far(): pl.pallas_call(_near_far_kernel, grid_spec=grid_spec, out_shape=[out, out...]
  transfers between devices with their start and end apart: 8 -> 8, of which waited for: 5 -> 6; matrix products, arithmetic and copies ran while one was open for 8% -> 8% of each run, Pallas kernels for 0% -> 0%
where the time goes in v4:
time: 59.7 us; the launch traced here: 59.9 us
  waiting for transfers between devices  26.9 us (45%)
  starting transfers between devices  11.7 us (20%)
  Pallas kernels  10.5 us (18%)
  other arithmetic  5.36 us (9%)
  local copies, waits for them, and re-layouts  4.62 us (8%)
  between operations  0.82 us (1%)
    ppermute x3, waiting for transfers between devices, _line_gather(): down = lax.ppermute(down, axis, down_pairs)  14 us
    pallas_call x1, Pallas kernels, _near_far(): pl.pallas_call(_near_far_kernel, grid_spec=grid_spec, out_shape=[out, out...  8.45 us
    ppermute x1, waiting for transfers between devices, _ring_reduce_scatter(): arrived = lax.ppermute(carry.astype(jnp.bfloat16), axis, ring)  7.54 us
    ppermute x3, starting transfers between devices, _line_gather(): up = lax.ppermute(up, axis, up_pairs)  6.32 us
    ppermute x3, starting transfers between devices, _line_gather(): down = lax.ppermute(down, axis, down_pairs)  3.85 us
    ppermute x3, waiting for transfers between devices, _line_gather(): up = lax.ppermute(up, axis, up_pairs)  3.16 us
    ppermute x1, waiting for transfers between devices, on_device(): arrived = lax.ppermute(theirs, 'sub', [(0, 1), (1, 0)])  2.21 us
    unnamed x10, local copies, waits for them, and re-layouts  2.15 us
  transfers between devices with their start and end apart: 8, of which 6 were waited for; matrix products, arithmetic and copies ran while one was open for 8% of the time, Pallas kernels for 0%

profile of v4, /device:TPU:0, one launch (start us, length us, event | category | flops | bytes accessed | tf_op | source)
XLA Modules:
  0.0 59.9 jit_solution(9515953214733057155)
XLA Ops:
  0.0 0.0 copy-start.1
  0.0 0.8 %slice_bitcast_fusion.1 = (bf16[16,256]{1,0:T(8,128)(2,1)S(1)}, bf16[16,256]{1,0:T(8,128)(2,1)S(1)}) fusion(bf16[1,32,256]{2,1,0:T(8,128)(2,1)} %basis_ref.1), kind=kLoop, calls=%fused_computation.14 | loop fusion | bytes 32768 | tf_op jit(solution)/shard_map/slice | solution.py:156
  0.8 1.0 %maximum_maximum_fusion = bf16[272,512]{1,0:T(8,128)(2,1)S(1)} fusion(bf16[16,256]{1,0:T(8,128)(2,1)S(1)} %get-tuple-element.10, bf16[16,256]{1,0:T(8,128)(2,1)S(1)} %get-tuple-element.9, bf16[256,512]{1,0:T(8,128)(2,1)} %param.6), kind=kLoop, calls=%fused_computation.4 | loop fusion | flops 835584 | bytes 557056 | tf_op jit(solution)/shard_map/concatenate | solution.py:157
  1.7 5.0 %collective-permute-start = (bf16[272,512]{1,0:T(8,128)(2,1)S(1)}, bf16[272,512]{1,0:T(8,128)(2,1)S(1)}, u32[]{:S(2)}, u32[]{:S(2)}) collective-permute-start(bf16[272,512]{1,0:T(8,128)(2,1)S(1)} %maximum_maximum_fusion), channel_id=1, source_target_pairs={{0,4},{4,8},{8,12},{1,5},{5,9},{9,13},{2,6},{6,10},{10,14},{3,7},{... | collective-permute-start | bytes 835592 | tf_op jit(solution)/shard_map/ppermute | solution.py:126
  6.7 1.3 %collective-permute-start.3 = (bf16[272,512]{1,0:T(8,128)(2,1)S(1)}, bf16[272,512]{1,0:T(8,128)(2,1)S(1)}, u32[]{:S(2)}, u32[]{:S(2)}) collective-permute-start(bf16[272,512]{1,0:T(8,128)(2,1)S(1)} %maximum_maximum_fusion), channel_id=1, source_target_pairs={{4,0},{8,4},{12,8},{5,1},{9,5},{13,9},{6,2},{10,6},{14,10},{7,3},{... | collective-permute-start | bytes 835592 | tf_op jit(solution)/shard_map/ppermute | solution.py:127
  8.7 0.8 %add_bitcast_fusion = s32[8]{0:T(128)S(1)} fusion(s32[8,2]{0,1:T(2,128)} %bitcast.41), kind=kLoop, calls=%fused_computation.21 | loop fusion | flops 16 | bytes 96 | tf_op jit(solution)/shard_map/eq | solution.py:165
  9.4 3.2 %collective-permute-done = bf16[272,512]{1,0:T(8,128)(2,1)S(1)} collective-permute-done((bf16[272,512]{1,0:T(8,128)(2,1)S(1)}, bf16[272,512]{1,0:T(8,128)(2,1)S(1)}, u32[]{:S(2)}, u32[]{:S(2)}) %collective-permute-start) | collective-permute-done | bytes 278560 | tf_op jit(solution)/shard_map/ppermute | solution.py:126
  12.6 0.7 %collective-permute-start.1 = (bf16[272,512]{1,0:T(8,128)(2,1)S(1)}, bf16[272,512]{1,0:T(8,128)(2,1)S(1)}, u32[]{:S(2)}, u32[]{:S(2)}) collective-permute-start(bf16[272,512]{1,0:T(8,128)(2,1)S(1)} %collective-permute-done), channel_id=1, source_target_pairs={{4,8},{8,12},{5,9},{9,13},{6,10},{10,14},{7,11},{11,15},{20,24},{2... | collective-permute-start | bytes 835592 | tf_op jit(solution)/shard_map/ppermute | solution.py:126
  13.3 0.1 fusion.2
  13.4 3.4 %collective-permute-done.3 = bf16[272,512]{1,0:T(8,128)(2,1)S(1)} collective-permute-done((bf16[272,512]{1,0:T(8,128)(2,1)S(1)}, bf16[272,512]{1,0:T(8,128)(2,1)S(1)}, u32[]{:S(2)}, u32[]{:S(2)}) %collective-permute-start.3) | collective-permute-done | bytes 278560 | tf_op jit(solution)/shard_map/ppermute | solution.py:127
  16.7 1.3 %collective-permute-start.4 = (bf16[272,512]{1,0:T(8,128)(2,1)S(1)}, bf16[272,512]{1,0:T(8,128)(2,1)S(1)}, u32[]{:S(2)}, u32[]{:S(2)}) collective-permute-start(bf16[272,512]{1,0:T(8,128)(2,1)S(1)} %collective-permute-done.3), channel_id=1, source_target_pairs={{4,0},{8,4},{5,1},{9,5},{6,2},{10,6},{7,3},{11,7},{20,16},{24,20},... | collective-permute-start | bytes 835592 | tf_op jit(solution)/shard_map/ppermute | solution.py:127
  18.0 0.0 collective-permute-done.1
  18.0 0.7 %collective-permute-start.2 = (bf16[272,512]{1,0:T(8,128)(2,1)S(1)}, bf16[272,512]{1,0:T(8,128)(2,1)S(1)}, u32[]{:S(2)}, u32[]{:S(2)}) collective-permute-start(bf16[272,512]{1,0:T(8,128)(2,1)S(1)} %collective-permute-done.1), channel_id=1, source_target_pairs={{8,12},{9,13},{10,14},{11,15},{24,28},{25,29},{26,30},{27,31}} | collective-permute-start | bytes 835592 | tf_op jit(solution)/shard_map/ppermute | solution.py:126
  18.7 0.6 %pad_add_fusion.place_ref = s32[2]{0:T(128)} fusion(s32[1]{0:T(128)} %bitcast.2, s32[1]{0:T(128)} %bitcast.1), kind=kLoop, calls=%fused_computation.18 | loop fusion | flops 2 | bytes 16 | tf_op jit(solution)/shard_map/stack | solution.py:176
  19.4 0.8 %copy.13 = s32[1,1,8,2]{3,2,1,0:T(8,128)S(1)} copy(s32[1,1,8,2]{2,3,1,0:T(2,128)} %param.9) | data formatting | bytes 128 | tf_op args[3]
  20.1 0.1 convert_element_type.37
  20.2 0.1 copy.14
  20.3 0.9 %reshape_squeeze.11 = bf16[4,32,4,32]{3,2,1,0:T(4,128)(2,1)S(1)} reshape(bf16[1,1,128,128]{3,2,1,0:T(8,128)(2,1)} %param.11) | data formatting | bytes 65536 | tf_op jit(solution)/shard_map/reshape;squeeze | solution.py:173
  21.2 0.6 reshape_squeeze.9.pairs_ref
  21.8 0.7 %copy_multiply_fusion = bf16[4,32,4,32]{3,1,0,2:T(8,128)(2,1)} fusion(bf16[4,32,4,32]{3,2,1,0:T(4,128)(2,1)S(1)} %reshape_squeeze.11, bf16[4,4]{0,1:T(4,128)(2,1)S(1)} %copy.14), kind=kLoop, calls=%fused_computation.12 | loop fusion | flops 16384 | bytes 65568 | tf_op jit(solution)/shard_map/mul | solution.py:173
  22.5 3.6 %collective-permute-done.4 = bf16[272,512]{1,0:T(8,128)(2,1)S(1)} collective-permute-done((bf16[272,512]{1,0:T(8,128)(2,1)S(1)}, bf16[272,512]{1,0:T(8,128)(2,1)S(1)}, u32[]{:S(2)}, u32[]{:S(2)}) %collective-permute-start.4) | collective-permute-done | bytes 278560 | tf_op jit(solution)/shard_map/ppermute | solution.py:127
  26.1 1.3 %collective-permute-start.5 = (bf16[272,512]{1,0:T(8,128)(2,1)S(1)}, bf16[272,512]{1,0:T(8,128)(2,1)S(1)}, u32[]{:S(2)}, u32[]{:S(2)}) collective-permute-start(bf16[272,512]{1,0:T(8,128)(2,1)S(1)} %collective-permute-done.4), channel_id=1, source_target_pairs={{4,0},{5,1},{6,2},{7,3},{20,16},{21,17},{22,18},{23,19}} | collective-permute-start | bytes 835592 | tf_op jit(solution)/shard_map/ppermute | solution.py:127
  27.4 0.0 collective-permute-done.2
  27.5 0.0 copy-done.1
  27.6 7.0 %collective-permute-done.5 = bf16[272,512]{1,0:T(8,128)(2,1)S(1)} collective-permute-done((bf16[272,512]{1,0:T(8,128)(2,1)S(1)}, bf16[272,512]{1,0:T(8,128)(2,1)S(1)}, u32[]{:S(2)}, u32[]{:S(2)}) %collective-permute-start.5) | collective-permute-done | bytes 278560 | tf_op jit(solution)/shard_map/ppermute | solution.py:127
  34.6 0.0 copy-start
  34.6 1.3 %copy-done = bf16[7,272,512]{2,1,0:T(8,128)(2,1)} copy-done((bf16[7,272,512]{2,1,0:T(8,128)(2,1)}, bf16[7,272,512]{2,1,0:T(8,128)(2,1)S(1)}, u32[]{:S(2)}) %copy-start) | copy-done | bytes 1949720
  35.9 8.5 %shard_map.64 = (bf16[2,288,512]{2,1,0:T(8,128)(2,1)}, bf16[2,288,512]{2,1,0:T(8,128)(2,1)}) custom-call(s32[16]{0:T(128)} %reshape_squeeze.9.pairs_ref, s32[1]{0:T(128)} %bitcast.37.count_ref, s32[2]{0:T(128)} %pad_add_fusion.place_ref, bf16[8,256,256]{2,1,0:T(8,128)(2,1)} %bitcast.39, bf16[7,272,512]{2,1,0:T(8,128)(2,1)} %copy-done, ...), custom_call_target="tpu_custom_call" | custom-call | tf_op jit(solution)/shard_map/pallas_call | solution.py:91
  44.4 0.0 collective-permute-start.6
  44.4 2.2 %collective-permute-done.6 = bf16[2,288,512]{2,1,0:T(8,128)(2,1)S(1)} collective-permute-done((bf16[2,288,512]{2,1,0:T(8,128)(2,1)}, bf16[2,288,512]{2,1,0:T(8,128)(2,1)S(1)}, u32[]{:S(2)}, u32[]{:S(2)}) %collective-permute-start.6) | collective-permute-done | bytes 589856 | tf_op jit(solution)/shard_map/ppermute | solution.py:181
  46.6 1.2 %convert_add_fusion = f32[2,288,512]{2,1,0:T(8,128)S(1)} fusion(bf16[2,288,512]{2,1,0:T(8,128)(2,1)S(1)} %collective-permute-done.6, bf16[2,288,512]{2,1,0:T(8,128)(2,1)} %get-tuple-element.7), kind=kLoop, calls=%fused_computation | loop fusion | flops 884736 | bytes 2359296 | tf_op jit(solution)/shard_map/add | solution.py:182
  47.9 1.6 %collective-permute-start.7 = (bf16[288,512]{1,0:T(8,128)(2,1)S(1)}, bf16[288,512]{1,0:T(8,128)(2,1)S(1)}, u32[]{:S(2)}, u32[]{:S(2)}) collective-permute-start(bf16[288,512]{1,0:T(8,128)(2,1)S(1)} %fusion), channel_id=1, source_target_pairs={{0,2},{2,0},{1,3},{3,1},{4,6},{6,4},{5,7},{7,5},{8,10},{10,8},{9,1... | collective-permute-start | bytes 884744 | tf_op jit(solution)/shard_map/ppermute | solution.py:141
  49.4 7.5 %collective-permute-done.7 = bf16[288,512]{1,0:T(8,128)(2,1)S(1)} collective-permute-done((bf16[288,512]{1,0:T(8,128)(2,1)S(1)}, bf16[288,512]{1,0:T(8,128)(2,1)S(1)}, u32[]{:S(2)}, u32[]{:S(2)}) %collective-permute-start.7) | collective-permute-done | bytes 294944 | tf_op jit(solution)/shard_map/ppermute | solution.py:141
  57.0 0.9 %bitcast_add_fusion.total_ref = f32[288,512]{1,0:T(8,128)} fusion(f32[2,288,512]{2,1,0:T(8,128)S(1)} %convert_add_fusion, s32[]{:T(128)S(6)} %select_n.21, bf16[288,512]{1,0:T(8,128)(2,1)S(1)} %collective-permute-done.7), kind=kLoop, calls=%fused_computation.1 | loop fusion | flops 294912 | bytes 1474564 | tf_op jit(solution)/shard_map/add | solution.py:143
  57.9 2.0 %shard_map.65 = bf16[256,512]{1,0:T(8,128)(2,1)} custom-call(f32[288,512]{1,0:T(8,128)} %bitcast_add_fusion.total_ref, bf16[1,32,256]{2,1,0:T(8,128)(2,1)} %basis_ref.1), custom_call_target="tpu_custom_call" | custom-call | tf_op jit(solution)/shard_map/pallas_call | solution.py:113
  (10 shorter events, 0.2 us)
Async XLA Ops:
  0.0 27.5 %copy-start.1 = (bf16[256,512]{1,0:T(8,128)(2,1)S(1)}, bf16[256,512]{1,0:T(8,128)(2,1)}, u32[]{:S(2)}) copy-start(bf16[256,512]{1,0:T(8,128)(2,1)} %param.6) | copy-start | bytes 786436
  1.7 10.9 %collective-permute-start = (bf16[272,512]{1,0:T(8,128)(2,1)S(1)}, bf16[272,512]{1,0:T(8,128)(2,1)S(1)}, u32[]{:S(2)}, u32[]{:S(2)}) collective-permute-start(bf16[272,512]{1,0:T(8,128)(2,1)S(1)} %maximum_maximum_fusion), channel_id=1, source_target_pairs={{0,4},{4,8},{8,12},{1,5},{5,9},{9,13},{2,6},{6,10},{10,14},{3,7},{... | collective-permute-start | bytes 835592 | tf_op jit(solution)/shard_map/ppermute | solution.py:126
  6.7 10.0 %collective-permute-start.3 = (bf16[272,512]{1,0:T(8,128)(2,1)S(1)}, bf16[272,512]{1,0:T(8,128)(2,1)S(1)}, u32[]{:S(2)}, u32[]{:S(2)}) collective-permute-start(bf16[272,512]{1,0:T(8,128)(2,1)S(1)} %maximum_maximum_fusion), channel_id=1, source_target_pairs={{4,0},{8,4},{12,8},{5,1},{9,5},{13,9},{6,2},{10,6},{14,10},{7,3},{... | collective-permute-start | bytes 835592 | tf_op jit(solution)/shard_map/ppermute | solution.py:127
  12.6 5.4 %collective-permute-start.1 = (bf16[272,512]{1,0:T(8,128)(2,1)S(1)}, bf16[272,512]{1,0:T(8,128)(2,1)S(1)}, u32[]{:S(2)}, u32[]{:S(2)}) collective-permute-start(bf16[272,512]{1,0:T(8,128)(2,1)S(1)} %collective-permute-done), channel_id=1, source_target_pairs={{4,8},{8,12},{5,9},{9,13},{6,10},{10,14},{7,11},{11,15},{20,24},{2... | collective-permute-start | bytes 835592 | tf_op jit(solution)/shard_map/ppermute | solution.py:126
  16.7 9.4 %collective-permute-start.4 = (bf16[272,512]{1,0:T(8,128)(2,1)S(1)}, bf16[272,512]{1,0:T(8,128)(2,1)S(1)}, u32[]{:S(2)}, u32[]{:S(2)}) collective-permute-start(bf16[272,512]{1,0:T(8,128)(2,1)S(1)} %collective-permute-done.3), channel_id=1, source_target_pairs={{4,0},{8,4},{5,1},{9,5},{6,2},{10,6},{7,3},{11,7},{20,16},{24,20},... | collective-permute-start | bytes 835592 | tf_op jit(solution)/shard_map/ppermute | solution.py:127
  18.0 9.4 %collective-permute-start.2 = (bf16[272,512]{1,0:T(8,128)(2,1)S(1)}, bf16[272,512]{1,0:T(8,128)(2,1)S(1)}, u32[]{:S(2)}, u32[]{:S(2)}) collective-permute-start(bf16[272,512]{1,0:T(8,128)(2,1)S(1)} %collective-permute-done.1), channel_id=1, source_target_pairs={{8,12},{9,13},{10,14},{11,15},{24,28},{25,29},{26,30},{27,31}} | collective-permute-start | bytes 835592 | tf_op jit(solution)/shard_map/ppermute | solution.py:126
  26.1 8.5 %collective-permute-start.5 = (bf16[272,512]{1,0:T(8,128)(2,1)S(1)}, bf16[272,512]{1,0:T(8,128)(2,1)S(1)}, u32[]{:S(2)}, u32[]{:S(2)}) collective-permute-start(bf16[272,512]{1,0:T(8,128)(2,1)S(1)} %collective-permute-done.4), channel_id=1, source_target_pairs={{4,0},{5,1},{6,2},{7,3},{20,16},{21,17},{22,18},{23,19}} | collective-permute-start | bytes 835592 | tf_op jit(solution)/shard_map/ppermute | solution.py:127
  34.6 1.3 %copy-start = (bf16[7,272,512]{2,1,0:T(8,128)(2,1)}, bf16[7,272,512]{2,1,0:T(8,128)(2,1)S(1)}, u32[]{:S(2)}) copy-start(bf16[7,272,512]{2,1,0:T(8,128)(2,1)S(1)} %bitcast_dynamic-update-slice_fusion.stack_ref) | copy-start | bytes 5849092
  44.4 2.2 %collective-permute-start.6 = (bf16[2,288,512]{2,1,0:T(8,128)(2,1)}, bf16[2,288,512]{2,1,0:T(8,128)(2,1)S(1)}, u32[]{:S(2)}, u32[]{:S(2)}) collective-permute-start(bf16[2,288,512]{2,1,0:T(8,128)(2,1)} %get-tuple-element.8), channel_id=1, source_target_pairs={{0,1},{1,0},{2,3},{3,2},{4,5},{5,4},{6,7},{7,6},{8,9},{9,8},{10,11... | collective-permute-start | bytes 1769480 | tf_op jit(solution)/shard_map/ppermute | solution.py:181
  47.9 9.1 %collective-permute-start.7 = (bf16[288,512]{1,0:T(8,128)(2,1)S(1)}, bf16[288,512]{1,0:T(8,128)(2,1)S(1)}, u32[]{:S(2)}, u32[]{:S(2)}) collective-permute-start(bf16[288,512]{1,0:T(8,128)(2,1)S(1)} %fusion), channel_id=1, source_target_pairs={{0,2},{2,0},{1,3},{3,1},{4,6},{6,4},{5,7},{7,5},{8,10},{10,8},{9,1... | collective-permute-start | bytes 884744 | tf_op jit(solution)/shard_map/ppermute | solution.py:141

commit v5 on v4

--- a/solution.py
+++ b/solution.py
@@ -7,52 +7,51 @@
 
 
 def _near_far_kernel(
-    pairs_ref, count_ref, place_ref, tiles_ref, stack_ref, masked_ref, mine_ref, theirs_ref, acc_ref
+    pairs_ref, count_ref, place_ref, tiles_ref, source_ref, packed_ref, masked_ref,
+    mine_ref, theirs_ref, acc_ref, coeff_ref,
 ):
-    slot = pl.program_id(0)
-    slot_total = pl.num_programs(0)
+    step = pl.program_id(0)
+    step_total = pl.num_programs(0)
     inner_count, width, rhs_count = acc_ref.shape
     tgt_count = masked_ref.shape[0]
     rank_size = masked_ref.shape[2]
+    slot_count = step_total - tgt_count
     half_rank = rank_size // 2
     sub_count = 2
     own_tgt = place_ref[0]
     own_sub = place_ref[1]
 
-    @pl.when(slot == 0)
+    @pl.when(step == 0)
     def _():
         acc_ref[...] = jnp.zeros_like(acc_ref)
-
-    @pl.when(slot < count_ref[0])
-    def _():
-        target = jnp.clip(pairs_ref[2 * slot], 0, inner_count - 1)
-        source = jnp.clip(pairs_ref[2 * slot + 1], 0, tgt_count - 1)
-        term = jnp.dot(
-            tiles_ref[...],
-            stack_ref[source - own_tgt + tgt_count - 1, :width, :],
-            preferred_element_type=jnp.float32,
-        )
+        coeff_ref[...] = jnp.zeros_like(coeff_ref)
+
+    @pl.when(step < jnp.minimum(count_ref[0], slot_count))
+    def _():
+        target = jnp.clip(pairs_ref[2 * step], 0, inner_count - 1)
+        term = jnp.dot(tiles_ref[...], source_ref[...], preferred_element_type=jnp.float32)
         acc_ref[target] += term
 
-    @pl.when(slot == slot_total - 1)
-    def _():
-        coeffs = jnp.zeros((inner_count * rank_size, rhs_count), jnp.float32)
-        for source in range(tgt_count):
-            block = stack_ref[source - own_tgt + tgt_count - 1]
-            dens = block[:width, :]
-            packed = block[width:, :]
-            top = jnp.dot(packed[:, :width], dens, preferred_element_type=jnp.float32)
-            bottom = jnp.dot(packed[:, width:], dens, preferred_element_type=jnp.float32)
-            projected = jnp.concatenate([top, bottom], axis=0).astype(jnp.bfloat16)
-            coeffs += jnp.dot(masked_ref[source], projected, preferred_element_type=jnp.float32)
-        coeffs = coeffs.astype(jnp.bfloat16)
-
+    @pl.when(step >= slot_count)
+    def _():
+        source = step - slot_count
+        packed = packed_ref[source - own_tgt + tgt_count - 1]
+        dens = source_ref[...]
+        top = jnp.dot(packed[:, :width], dens, preferred_element_type=jnp.float32)
+        bottom = jnp.dot(packed[:, width:], dens, preferred_element_type=jnp.float32)
+        projected = jnp.concatenate([top, bottom], axis=0).astype(jnp.bfloat16)
+        coeff_ref[...] += jnp.dot(masked_ref[source], projected, preferred_element_type=jnp.float32)
+
+    @pl.when(step == step_total - 1)
+    def _():
         def write(first_ref, second_ref):
             for target in range(inner_count):
                 dest = first_ref if target % sub_count == 0 else second_ref
                 row = target // sub_count
                 dest[row, :width, :] = acc_ref[target].astype(dest.dtype)
-                dest[row, width:, :] = coeffs[target * rank_size : (target + 1) * rank_size]
+                dest[row, width:, :] = coeff_ref[
+                    target * rank_size : (target + 1) * rank_size
+                ].astype(dest.dtype)
 
         @pl.when(own_sub == 0)
         def _():
@@ -66,26 +65,42 @@
 def _near_far(pairs_flat, count, place, tiles, stack, masked_t, inner_count, rank_size):
     slot_count, width, _ = tiles.shape
     stack_count, rows, rhs_count = stack.shape
+    tgt_count = masked_t.shape[0]
+    half_rank = rank_size // 2
     half_count = inner_count // 2
     out_rows = width + rank_size
 
+    def last_slot(k, cnt):
+        return jnp.maximum(jnp.minimum(jnp.minimum(k, cnt[0] - 1), slot_count - 1), 0)
+
     def tile_index(k, pairs, cnt, place):
-        return (jnp.maximum(jnp.minimum(k, cnt[0] - 1), 0), 0, 0)
+        return (last_slot(k, cnt), 0, 0)
+
+    def source_index(k, pairs, cnt, place):
+        near_source = jnp.clip(pairs[2 * last_slot(k, cnt) + 1], 0, tgt_count - 1)
+        source = jnp.where(k < slot_count, near_source, k - slot_count)
+        return (source - place[0] + tgt_count - 1, 0, 0)
 
     whole = lambda k, p, c, q: (0, 0, 0)
     grid_spec = pltpu.PrefetchScalarGridSpec(
         num_scalar_prefetch=3,
-        grid=(slot_count,),
+        grid=(slot_count + tgt_count,),
         in_specs=[
             pl.BlockSpec((None, width, width), tile_index),
-            pl.BlockSpec(stack.shape, whole),
+            pl.BlockSpec((None, width, rhs_count), source_index),
+            pl.BlockSpec(
+                (stack_count, half_rank, rhs_count), lambda k, p, c, q: (0, width // half_rank, 0)
+            ),
             pl.BlockSpec(masked_t.shape, whole),
         ],
         out_specs=[
             pl.BlockSpec((half_count, out_rows, rhs_count), whole),
             pl.BlockSpec((half_count, out_rows, rhs_count), whole),
         ],
-        scratch_shapes=[pltpu.VMEM((inner_count, width, rhs_count), jnp.float32)],
+        scratch_shapes=[
+            pltpu.VMEM((inner_count, width, rhs_count), jnp.float32),
+            pltpu.VMEM((inner_count * rank_size, rhs_count), jnp.float32),
+        ],
     )
     out = jax.ShapeDtypeStruct((half_count, out_rows, rhs_count), jnp.bfloat16)
     return pl.pallas_call(
@@ -95,25 +110,28 @@
         compiler_params=pltpu.CompilerParams(
             dimension_semantics=("arbitrary",), vmem_limit_bytes=56 * 1024 * 1024
         ),
-    )(pairs_flat, count, place, tiles, stack, masked_t)
-
-
-def _epilogue_kernel(total_ref, basis_ref, out_ref):
+    )(pairs_flat, count, place, tiles, stack, stack, masked_t)
+
+
+def _epilogue_kernel(basis_ref, *refs):
+    piece_refs, out_ref = refs[:-1], refs[-1]
     width = out_ref.shape[0]
-    near = total_ref[:width, :]
-    coeffs = total_ref[width:, :].astype(jnp.bfloat16)
+    total = piece_refs[0][...].astype(jnp.float32)
+    for piece_ref in piece_refs[1:]:
+        total += piece_ref[...].astype(jnp.float32)
+    coeffs = total[width:, :].astype(jnp.bfloat16)
     far = lax.dot_general(
         basis_ref[0], coeffs, (((0,), (0,)), ((), ())), preferred_element_type=jnp.float32
     )
-    out_ref[...] = (near + far).astype(out_ref.dtype)
-
-
-def _epilogue(total, basis):
+    out_ref[...] = (total[:width, :] + far).astype(out_ref.dtype)
+
+
+def _epilogue(pieces, basis):
     width = basis.shape[2]
     return pl.pallas_call(
         _epilogue_kernel,
-        out_shape=jax.ShapeDtypeStruct((width, total.shape[1]), jnp.bfloat16),
-    )(total, basis)
+        out_shape=jax.ShapeDtypeStruct((width, pieces[0].shape[1]), jnp.bfloat16),
+    )(basis, *pieces)
 
 
 def _line_gather(payload, axis):
@@ -179,9 +197,22 @@
         inner_count, rank_size,
     )
     arrived = lax.ppermute(theirs, "sub", [(0, 1), (1, 0)])
-    stage = mine.astype(jnp.float32) + arrived.astype(jnp.float32)
-    total = _ring_reduce_scatter(stage, "inner")
-    return _epilogue(total, cluster_basis)
+    if lax.axis_size("inner") == 2:
+        me = lax.axis_index("inner")
+        send = (
+            lax.dynamic_index_in_dim(mine, 1 - me, 0, False).astype(jnp.float32)
+            + lax.dynamic_index_in_dim(arrived, 1 - me, 0, False).astype(jnp.float32)
+        ).astype(jnp.bfloat16)
+        back = lax.ppermute(send, "inner", [(0, 1), (1, 0)])
+        pieces = (
+            lax.dynamic_index_in_dim(mine, me, 0, False),
+            lax.dynamic_index_in_dim(arrived, me, 0, False),
+            back,
+        )
+    else:
+        stage = mine.astype(jnp.float32) + arrived.astype(jnp.float32)
+        pieces = (_ring_reduce_scatter(stage, "inner"),)
+    return _epilogue(pieces, cluster_basis)
 
 
 def solution(mesh):

time: 59.7 us -> 62 us (1.039); the launches traced: 59.9 us -> 61.6 us
  local copies, waits for them, and re-layouts: 4.62 us -> 7.79 us
  waiting for transfers between devices: 26.9 us -> 24.5 us
  Pallas kernels: 10.5 us -> 12.5 us
  other arithmetic: 5.36 us -> 4.21 us
    squeeze x0 -> x2, local copies, waits for them, and re-layouts: none -> 2.43 us  [the longest x1 1.69 us: on_device(): lax.dynamic_index_in_dim(mine, me, 0, False)]
    ppermute x1, waiting for transfers between devices: 7.54 us -> 5.13 us  [on_device(): back = lax.ppermute(send, 'inner', [(0, 1), (1, 0)])]
    add x2 -> x0, other arithmetic: 2.12 us -> none  [the longest x1 1.22 us: on_device(): stage = mine.astype(jnp.float32) + arrived.astype(jnp.float32)]
    pallas_call x1, Pallas kernels: 8.45 us -> 10.4 us  [_near_far(): pl.pallas_call(_near_far_kernel, grid_spec=grid_spec, out_shape=[out, out...]
    convert_element_type x0 -> x1, other arithmetic: none -> 1.04 us  [on_device(): send = (lax.dynamic_index_in_dim(mine, 1 - me, 0, False).astype(jnp.float...]
    unnamed x10 -> x12, local copies, waits for them, and re-layouts: 2.15 us -> 2.86 us
  transfers between devices with their start and end apart: 8 -> 8, of which waited for: 6 -> 6; matrix products, arithmetic and copies ran while one was open for 8% -> 12% of each run, Pallas kernels for 0% -> 0%
where the time goes in v5:
time: 62 us; the launch traced here: 61.6 us
  waiting for transfers between devices  24.5 us (40%)
  Pallas kernels  12.5 us (20%)
  starting transfers between devices  11.7 us (19%)
  local copies, waits for them, and re-layouts  7.79 us (13%)
  other arithmetic  4.21 us (7%)
  between operations  0.81 us (1%)
    ppermute x3, waiting for transfers between devices, _line_gather(): down = lax.ppermute(down, axis, down_pairs)  14 us
    pallas_call x1, Pallas kernels, _near_far(): pl.pallas_call(_near_far_kernel, grid_spec=grid_spec, out_shape=[out, out...  10.4 us
    ppermute x3, starting transfers between devices, _line_gather(): up = lax.ppermute(up, axis, up_pairs)  6.32 us
    ppermute x1, waiting for transfers between devices, on_device(): back = lax.ppermute(send, 'inner', [(0, 1), (1, 0)])  5.13 us
    ppermute x3, starting transfers between devices, _line_gather(): down = lax.ppermute(down, axis, down_pairs)  3.85 us
    ppermute x3, waiting for transfers between devices, _line_gather(): up = lax.ppermute(up, axis, up_pairs)  3.16 us
    unnamed x12, local copies, waits for them, and re-layouts  2.86 us
    ppermute x1, waiting for transfers between devices, on_device(): arrived = lax.ppermute(theirs, 'sub', [(0, 1), (1, 0)])  2.21 us
  transfers between devices with their start and end apart: 8, of which 6 were waited for; matrix products, arithmetic and copies ran while one was open for 12% of the time, Pallas kernels for 0%

profile of v5, /device:TPU:0, one launch (start us, length us, event | category | flops | bytes accessed | tf_op | source)
XLA Modules:
  0.0 61.6 jit_solution(7353042030396162195)
XLA Ops:
  0.0 0.0 copy-start.1
  0.0 0.8 %slice_bitcast_fusion.1 = (bf16[16,256]{1,0:T(8,128)(2,1)S(1)}, bf16[16,256]{1,0:T(8,128)(2,1)S(1)}) fusion(bf16[1,32,256]{2,1,0:T(8,128)(2,1)} %basis_ref.1), kind=kLoop, calls=%fused_computation.14 | loop fusion | bytes 32768 | tf_op jit(solution)/shard_map/slice | solution.py:174
  0.8 1.0 %maximum_maximum_fusion = bf16[272,512]{1,0:T(8,128)(2,1)S(1)} fusion(bf16[16,256]{1,0:T(8,128)(2,1)S(1)} %get-tuple-element.10, bf16[16,256]{1,0:T(8,128)(2,1)S(1)} %get-tuple-element.9, bf16[256,512]{1,0:T(8,128)(2,1)} %param.6), kind=kLoop, calls=%fused_computation.4 | loop fusion | flops 835584 | bytes 557056 | tf_op jit(solution)/shard_map/concatenate | solution.py:175
  1.7 5.0 %collective-permute-start = (bf16[272,512]{1,0:T(8,128)(2,1)S(1)}, bf16[272,512]{1,0:T(8,128)(2,1)S(1)}, u32[]{:S(2)}, u32[]{:S(2)}) collective-permute-start(bf16[272,512]{1,0:T(8,128)(2,1)S(1)} %maximum_maximum_fusion), channel_id=1, source_target_pairs={{0,4},{4,8},{8,12},{1,5},{5,9},{9,13},{2,6},{6,10},{10,14},{3,7},{... | collective-permute-start | bytes 835592 | tf_op jit(solution)/shard_map/ppermute | solution.py:144
  6.7 1.3 %collective-permute-start.3 = (bf16[272,512]{1,0:T(8,128)(2,1)S(1)}, bf16[272,512]{1,0:T(8,128)(2,1)S(1)}, u32[]{:S(2)}, u32[]{:S(2)}) collective-permute-start(bf16[272,512]{1,0:T(8,128)(2,1)S(1)} %maximum_maximum_fusion), channel_id=1, source_target_pairs={{4,0},{8,4},{12,8},{5,1},{9,5},{13,9},{6,2},{10,6},{14,10},{7,3},{... | collective-permute-start | bytes 835592 | tf_op jit(solution)/shard_map/ppermute | solution.py:145
  8.7 0.8 %add_bitcast_fusion = s32[8]{0:T(128)S(1)} fusion(s32[8,2]{0,1:T(2,128)} %bitcast.43), kind=kLoop, calls=%fused_computation.21 | loop fusion | flops 16 | bytes 96 | tf_op jit(solution)/shard_map/eq | solution.py:183
  9.4 3.2 %collective-permute-done = bf16[272,512]{1,0:T(8,128)(2,1)S(1)} collective-permute-done((bf16[272,512]{1,0:T(8,128)(2,1)S(1)}, bf16[272,512]{1,0:T(8,128)(2,1)S(1)}, u32[]{:S(2)}, u32[]{:S(2)}) %collective-permute-start) | collective-permute-done | bytes 278560 | tf_op jit(solution)/shard_map/ppermute | solution.py:144
  12.6 0.7 %collective-permute-start.1 = (bf16[272,512]{1,0:T(8,128)(2,1)S(1)}, bf16[272,512]{1,0:T(8,128)(2,1)S(1)}, u32[]{:S(2)}, u32[]{:S(2)}) collective-permute-start(bf16[272,512]{1,0:T(8,128)(2,1)S(1)} %collective-permute-done), channel_id=1, source_target_pairs={{4,8},{8,12},{5,9},{9,13},{6,10},{10,14},{7,11},{11,15},{20,24},{2... | collective-permute-start | bytes 835592 | tf_op jit(solution)/shard_map/ppermute | solution.py:144
  13.3 0.1 fusion.2
  13.4 3.4 %collective-permute-done.3 = bf16[272,512]{1,0:T(8,128)(2,1)S(1)} collective-permute-done((bf16[272,512]{1,0:T(8,128)(2,1)S(1)}, bf16[272,512]{1,0:T(8,128)(2,1)S(1)}, u32[]{:S(2)}, u32[]{:S(2)}) %collective-permute-start.3) | collective-permute-done | bytes 278560 | tf_op jit(solution)/shard_map/ppermute | solution.py:145
  16.7 1.3 %collective-permute-start.4 = (bf16[272,512]{1,0:T(8,128)(2,1)S(1)}, bf16[272,512]{1,0:T(8,128)(2,1)S(1)}, u32[]{:S(2)}, u32[]{:S(2)}) collective-permute-start(bf16[272,512]{1,0:T(8,128)(2,1)S(1)} %collective-permute-done.3), channel_id=1, source_target_pairs={{4,0},{8,4},{5,1},{9,5},{6,2},{10,6},{7,3},{11,7},{20,16},{24,20},... | collective-permute-start | bytes 835592 | tf_op jit(solution)/shard_map/ppermute | solution.py:145
  18.0 0.0 collective-permute-done.1
  18.0 0.7 %collective-permute-start.2 = (bf16[272,512]{1,0:T(8,128)(2,1)S(1)}, bf16[272,512]{1,0:T(8,128)(2,1)S(1)}, u32[]{:S(2)}, u32[]{:S(2)}) collective-permute-start(bf16[272,512]{1,0:T(8,128)(2,1)S(1)} %collective-permute-done.1), channel_id=1, source_target_pairs={{8,12},{9,13},{10,14},{11,15},{24,28},{25,29},{26,30},{27,31}} | collective-permute-start | bytes 835592 | tf_op jit(solution)/shard_map/ppermute | solution.py:144
  18.7 0.6 pad_add_fusion.place_ref
  19.3 0.8 %copy.13 = s32[1,1,8,2]{3,2,1,0:T(8,128)S(1)} copy(s32[1,1,8,2]{2,3,1,0:T(2,128)} %param.9) | data formatting | bytes 128 | tf_op args[3]
  20.0 0.1 convert_element_type.36
  20.1 0.1 copy.14
  20.2 0.9 %reshape_squeeze.11 = bf16[4,32,4,32]{3,2,1,0:T(4,128)(2,1)S(1)} reshape(bf16[1,1,128,128]{3,2,1,0:T(8,128)(2,1)} %param.11) | data formatting | bytes 65536 | tf_op jit(solution)/shard_map/reshape;squeeze | solution.py:191
  21.1 0.7 %reshape_squeeze.9.pairs_ref = s32[16]{0:T(128)} reshape(s32[1,1,8,2]{3,2,1,0:T(8,128)S(1)} %copy.13) | data formatting | bytes 128 | tf_op jit(solution)/shard_map/reshape;squeeze | solution.py:196
  21.8 0.7 %copy_multiply_fusion = bf16[4,32,4,32]{3,1,0,2:T(8,128)(2,1)} fusion(bf16[4,32,4,32]{3,2,1,0:T(4,128)(2,1)S(1)} %reshape_squeeze.11, bf16[4,4]{0,1:T(4,128)(2,1)S(1)} %copy.14), kind=kLoop, calls=%fused_computation.12 | loop fusion | flops 16384 | bytes 65568 | tf_op jit(solution)/shard_map/mul | solution.py:191
  22.5 3.6 %collective-permute-done.4 = bf16[272,512]{1,0:T(8,128)(2,1)S(1)} collective-permute-done((bf16[272,512]{1,0:T(8,128)(2,1)S(1)}, bf16[272,512]{1,0:T(8,128)(2,1)S(1)}, u32[]{:S(2)}, u32[]{:S(2)}) %collective-permute-start.4) | collective-permute-done | bytes 278560 | tf_op jit(solution)/shard_map/ppermute | solution.py:145
  26.1 1.3 %collective-permute-start.5 = (bf16[272,512]{1,0:T(8,128)(2,1)S(1)}, bf16[272,512]{1,0:T(8,128)(2,1)S(1)}, u32[]{:S(2)}, u32[]{:S(2)}) collective-permute-start(bf16[272,512]{1,0:T(8,128)(2,1)S(1)} %collective-permute-done.4), channel_id=1, source_target_pairs={{4,0},{5,1},{6,2},{7,3},{20,16},{21,17},{22,18},{23,19}} | collective-permute-start | bytes 835592 | tf_op jit(solution)/shard_map/ppermute | solution.py:145
  27.4 0.0 collective-permute-done.2
  27.5 0.0 copy-done.1
  27.6 7.0 %collective-permute-done.5 = bf16[272,512]{1,0:T(8,128)(2,1)S(1)} collective-permute-done((bf16[272,512]{1,0:T(8,128)(2,1)S(1)}, bf16[272,512]{1,0:T(8,128)(2,1)S(1)}, u32[]{:S(2)}, u32[]{:S(2)}) %collective-permute-start.5) | collective-permute-done | bytes 278560 | tf_op jit(solution)/shard_map/ppermute | solution.py:145
  34.6 0.0 copy-start
  34.6 1.3 %copy-done = bf16[7,272,512]{2,1,0:T(8,128)(2,1)} copy-done((bf16[7,272,512]{2,1,0:T(8,128)(2,1)}, bf16[7,272,512]{2,1,0:T(8,128)(2,1)S(1)}, u32[]{:S(2)}) %copy-start) | copy-done | bytes 1949720
  35.9 10.4 %shard_map.64 = (bf16[2,288,512]{2,1,0:T(8,128)(2,1)}, bf16[2,288,512]{2,1,0:T(8,128)(2,1)}) custom-call(s32[16]{0:T(128)} %reshape_squeeze.9.pairs_ref, s32[1]{0:T(128)} %bitcast.39.count_ref, s32[2]{0:T(128)} %pad_add_fusion.place_ref, bf16[8,256,256]{2,1,0:T(8,128)(2,1)} %bitcast.41, bf16[7,272,512]{2,1,0:T(8,128)(2,1)} %copy-done, ...), custom_call_target="tpu_custom_call" | custom-call | tf_op jit(solution)/shard_map/pallas_call | solution.py:106
  46.3 0.0 collective-permute-start.6
  46.4 2.2 %collective-permute-done.6 = bf16[2,288,512]{2,1,0:T(8,128)(2,1)S(1)} collective-permute-done((bf16[2,288,512]{2,1,0:T(8,128)(2,1)}, bf16[2,288,512]{2,1,0:T(8,128)(2,1)S(1)}, u32[]{:S(2)}, u32[]{:S(2)}) %collective-permute-start.6) | collective-permute-done | bytes 589856 | tf_op jit(solution)/shard_map/ppermute | solution.py:199
  48.6 1.0 %fusion = bf16[288,512]{1,0:T(8,128)(2,1)S(1)} fusion(bf16[2,288,512]{2,1,0:T(8,128)(2,1)S(1)} %collective-permute-done.6, s32[]{:T(128)S(6)} %select_n.10, bf16[2,288,512]{2,1,0:T(8,128)(2,1)} %get-tuple-element.7), kind=kLoop, calls=%fused_computation.1 | loop fusion | flops 589824 | bytes 884740 | tf_op jit(solution)/shard_map/convert_element_type | solution.py:205
  49.6 1.5 %collective-permute-start.7 = (bf16[288,512]{1,0:T(8,128)(2,1)S(1)}, bf16[288,512]{1,0:T(8,128)(2,1)S(1)}, u32[]{:S(2)}, u32[]{:S(2)}) collective-permute-start(bf16[288,512]{1,0:T(8,128)(2,1)S(1)} %fusion), channel_id=1, source_target_pairs={{0,2},{2,0},{1,3},{3,1},{4,6},{6,4},{5,7},{7,5},{8,10},{10,8},{9,1... | collective-permute-start | bytes 884744 | tf_op jit(solution)/shard_map/ppermute | solution.py:206
  51.1 1.7 %dynamic-slice_bitcast_fusion.1.refs_0_ = bf16[288,512]{1,0:T(8,128)(2,1)} fusion(bf16[2,288,512]{2,1,0:T(8,128)(2,1)} %get-tuple-element.7, s32[]{:T(128)S(6)} %select_n.9), kind=kLoop, calls=%fused_computation.3 | loop fusion | bytes 589828 | tf_op jit(solution)/shard_map/jit(dynamic_index_in_dim)/squeeze | solution.py:208
  52.8 0.7 %dynamic-slice_bitcast_fusion.refs_1_ = bf16[288,512]{1,0:T(8,128)(2,1)} fusion(bf16[2,288,512]{2,1,0:T(8,128)(2,1)S(1)} %collective-permute-done.6, s32[]{:T(128)S(6)} %select_n.9), kind=kLoop, calls=%fused_computation.2 | loop fusion | bytes 589828 | tf_op jit(solution)/shard_map/jit(dynamic_index_in_dim)/squeeze | solution.py:209
  53.6 5.1 %collective-permute-done.7.refs_2_ = bf16[288,512]{1,0:T(8,128)(2,1)S(1)} collective-permute-done((bf16[288,512]{1,0:T(8,128)(2,1)S(1)}, bf16[288,512]{1,0:T(8,128)(2,1)S(1)}, u32[]{:S(2)}, u32[]{:S(2)}) %collective-permute-start.7) | collective-permute-done | bytes 294944 | tf_op jit(solution)/shard_map/ppermute | solution.py:206
  58.7 0.0 copy-start.2
  58.7 0.7 %copy-done.2 = bf16[288,512]{1,0:T(8,128)(2,1)} copy-done((bf16[288,512]{1,0:T(8,128)(2,1)}, bf16[288,512]{1,0:T(8,128)(2,1)S(1)}, u32[]{:S(2)}) %copy-start.2) | copy-done | bytes 294936
  59.4 2.1 %shard_map.65 = bf16[256,512]{1,0:T(8,128)(2,1)} custom-call(bf16[1,32,256]{2,1,0:T(8,128)(2,1)} %basis_ref.1, bf16[288,512]{1,0:T(8,128)(2,1)} %dynamic-slice_bitcast_fusion.1.refs_0_, bf16[288,512]{1,0:T(8,128)(2,1)} %dynamic-slice_bitcast_fusion.refs_1_, bf16[288,512]{1,0:T(8,128)(2,1)} %copy-done.2), custom_call_target="tpu_custom_call" | custom-call | tf_op jit(solution)/shard_map/pallas_call | solution.py:131
  (9 shorter events, 0.2 us)
Async XLA Ops:
  0.0 27.5 %copy-start.1 = (bf16[256,512]{1,0:T(8,128)(2,1)S(1)}, bf16[256,512]{1,0:T(8,128)(2,1)}, u32[]{:S(2)}) copy-start(bf16[256,512]{1,0:T(8,128)(2,1)} %param.6) | copy-start | bytes 786436
  1.7 10.9 %collective-permute-start = (bf16[272,512]{1,0:T(8,128)(2,1)S(1)}, bf16[272,512]{1,0:T(8,128)(2,1)S(1)}, u32[]{:S(2)}, u32[]{:S(2)}) collective-permute-start(bf16[272,512]{1,0:T(8,128)(2,1)S(1)} %maximum_maximum_fusion), channel_id=1, source_target_pairs={{0,4},{4,8},{8,12},{1,5},{5,9},{9,13},{2,6},{6,10},{10,14},{3,7},{... | collective-permute-start | bytes 835592 | tf_op jit(solution)/shard_map/ppermute | solution.py:144
  6.7 10.0 %collective-permute-start.3 = (bf16[272,512]{1,0:T(8,128)(2,1)S(1)}, bf16[272,512]{1,0:T(8,128)(2,1)S(1)}, u32[]{:S(2)}, u32[]{:S(2)}) collective-permute-start(bf16[272,512]{1,0:T(8,128)(2,1)S(1)} %maximum_maximum_fusion), channel_id=1, source_target_pairs={{4,0},{8,4},{12,8},{5,1},{9,5},{13,9},{6,2},{10,6},{14,10},{7,3},{... | collective-permute-start | bytes 835592 | tf_op jit(solution)/shard_map/ppermute | solution.py:145
  12.6 5.4 %collective-permute-start.1 = (bf16[272,512]{1,0:T(8,128)(2,1)S(1)}, bf16[272,512]{1,0:T(8,128)(2,1)S(1)}, u32[]{:S(2)}, u32[]{:S(2)}) collective-permute-start(bf16[272,512]{1,0:T(8,128)(2,1)S(1)} %collective-permute-done), channel_id=1, source_target_pairs={{4,8},{8,12},{5,9},{9,13},{6,10},{10,14},{7,11},{11,15},{20,24},{2... | collective-permute-start | bytes 835592 | tf_op jit(solution)/shard_map/ppermute | solution.py:144
  16.7 9.4 %collective-permute-start.4 = (bf16[272,512]{1,0:T(8,128)(2,1)S(1)}, bf16[272,512]{1,0:T(8,128)(2,1)S(1)}, u32[]{:S(2)}, u32[]{:S(2)}) collective-permute-start(bf16[272,512]{1,0:T(8,128)(2,1)S(1)} %collective-permute-done.3), channel_id=1, source_target_pairs={{4,0},{8,4},{5,1},{9,5},{6,2},{10,6},{7,3},{11,7},{20,16},{24,20},... | collective-permute-start | bytes 835592 | tf_op jit(solution)/shard_map/ppermute | solution.py:145
  18.0 9.4 %collective-permute-start.2 = (bf16[272,512]{1,0:T(8,128)(2,1)S(1)}, bf16[272,512]{1,0:T(8,128)(2,1)S(1)}, u32[]{:S(2)}, u32[]{:S(2)}) collective-permute-start(bf16[272,512]{1,0:T(8,128)(2,1)S(1)} %collective-permute-done.1), channel_id=1, source_target_pairs={{8,12},{9,13},{10,14},{11,15},{24,28},{25,29},{26,30},{27,31}} | collective-permute-start | bytes 835592 | tf_op jit(solution)/shard_map/ppermute | solution.py:144
  26.1 8.5 %collective-permute-start.5 = (bf16[272,512]{1,0:T(8,128)(2,1)S(1)}, bf16[272,512]{1,0:T(8,128)(2,1)S(1)}, u32[]{:S(2)}, u32[]{:S(2)}) collective-permute-start(bf16[272,512]{1,0:T(8,128)(2,1)S(1)} %collective-permute-done.4), channel_id=1, source_target_pairs={{4,0},{5,1},{6,2},{7,3},{20,16},{21,17},{22,18},{23,19}} | collective-permute-start | bytes 835592 | tf_op jit(solution)/shard_map/ppermute | solution.py:145
  34.6 1.3 %copy-start = (bf16[7,272,512]{2,1,0:T(8,128)(2,1)}, bf16[7,272,512]{2,1,0:T(8,128)(2,1)S(1)}, u32[]{:S(2)}) copy-start(bf16[7,272,512]{2,1,0:T(8,128)(2,1)S(1)} %bitcast_dynamic-update-slice_fusion.source_ref.packed_ref) | copy-start | bytes 5849092
  46.3 2.2 %collective-permute-start.6 = (bf16[2,288,512]{2,1,0:T(8,128)(2,1)}, bf16[2,288,512]{2,1,0:T(8,128)(2,1)S(1)}, u32[]{:S(2)}, u32[]{:S(2)}) collective-permute-start(bf16[2,288,512]{2,1,0:T(8,128)(2,1)} %get-tuple-element.8), channel_id=1, source_target_pairs={{0,1},{1,0},{2,3},{3,2},{4,5},{5,4},{6,7},{7,6},{8,9},{9,8},{10,11... | collective-permute-start | bytes 1769480 | tf_op jit(solution)/shard_map/ppermute | solution.py:199
  49.6 9.1 %collective-permute-start.7 = (bf16[288,512]{1,0:T(8,128)(2,1)S(1)}, bf16[288,512]{1,0:T(8,128)(2,1)S(1)}, u32[]{:S(2)}, u32[]{:S(2)}) collective-permute-start(bf16[288,512]{1,0:T(8,128)(2,1)S(1)} %fusion), channel_id=1, source_target_pairs={{0,2},{2,0},{1,3},{3,1},{4,6},{6,4},{5,7},{7,5},{8,10},{10,8},{9,1... | collective-permute-start | bytes 884744 | tf_op jit(solution)/shard_map/ppermute | solution.py:206
  58.7 0.7 %copy-start.2 = (bf16[288,512]{1,0:T(8,128)(2,1)}, bf16[288,512]{1,0:T(8,128)(2,1)S(1)}, u32[]{:S(2)}) copy-start(bf16[288,512]{1,0:T(8,128)(2,1)S(1)} %collective-permute-done.7.refs_2_) | copy-start | bytes 884740

commit v6 on v4

--- a/solution.py
+++ b/solution.py
@@ -88,12 +88,19 @@
         scratch_shapes=[pltpu.VMEM((inner_count, width, rhs_count), jnp.float32)],
     )
     out = jax.ShapeDtypeStruct((half_count, out_rows, rhs_count), jnp.bfloat16)
+    block_bytes = 2 * (
+        width * width * tiles.dtype.itemsize
+        + stack.size * stack.dtype.itemsize
+        + masked_t.size * masked_t.dtype.itemsize
+        + 2 * half_count * out_rows * rhs_count * 2
+    )
+    vmem_bytes = block_bytes + inner_count * width * rhs_count * 4 + (4 << 20)
     return pl.pallas_call(
         _near_far_kernel,
         grid_spec=grid_spec,
         out_shape=[out, out],
         compiler_params=pltpu.CompilerParams(
-            dimension_semantics=("arbitrary",), vmem_limit_bytes=56 * 1024 * 1024
+            dimension_semantics=("arbitrary",), vmem_limit_bytes=int(vmem_bytes)
         ),
     )(pairs_flat, count, place, tiles, stack, masked_t)
 

time: 59.7 us -> 52.9 us (0.89); the launches traced: 59.9 us -> 52.4 us
  Pallas kernels: 10.5 us -> 5.28 us
  other arithmetic: 5.36 us -> 3.09 us
  local copies, waits for them, and re-layouts: 4.62 us -> 2.83 us
  waiting for transfers between devices: 26.9 us -> 28.1 us
  starting transfers between devices: 11.7 us -> 12.3 us
    pallas_call x1, Pallas kernels: 8.45 us -> 3.26 us  [_near_far(): pl.pallas_call(_near_far_kernel, grid_spec=grid_spec, out_shape=[out, out...]
    ppermute x3, waiting for transfers between devices: 14 us -> 15.7 us  [_line_gather(): down = lax.ppermute(down, axis, down_pairs)]
    unnamed x10, local copies, waits for them, and re-layouts: 2.15 us -> 0.87 us
    add x1, other arithmetic: 1.22 us -> 0.17 us  [on_device(): stage = mine.astype(jnp.float32) + arrived.astype(jnp.float32)]
    mul x1, other arithmetic: 0.74 us -> 0.09 us  [on_device(): coupling[0, 0].reshape(inner_count, rank_size, tgt_count, rank_size)]
  transfers between devices with their start and end apart: 8 -> 8, of which waited for: 6 -> 6; matrix products, arithmetic and copies ran while one was open for 8% -> 6% of each run, Pallas kernels for 0% -> 0%
where the time goes in v6:
time: 52.9 us; the launch traced here: 52.4 us
  waiting for transfers between devices  28.1 us (53%)
  starting transfers between devices  12.3 us (23%)
  Pallas kernels  5.28 us (10%)
  other arithmetic  3.09 us (6%)
  local copies, waits for them, and re-layouts  2.83 us (5%)
  between operations  0.88 us (2%)
    ppermute x3, waiting for transfers between devices, _line_gather(): down = lax.ppermute(down, axis, down_pairs)  15.7 us
    ppermute x1, waiting for transfers between devices, _ring_reduce_scatter(): arrived = lax.ppermute(carry.astype(jnp.bfloat16), axis, ring)  7.31 us
    ppermute x3, starting transfers between devices, _line_gather(): up = lax.ppermute(up, axis, up_pairs)  6.32 us
    ppermute x3, starting transfers between devices, _line_gather(): down = lax.ppermute(down, axis, down_pairs)  3.85 us
    pallas_call x1, Pallas kernels, _near_far(): pl.pallas_call(_near_far_kernel, grid_spec=grid_spec, out_shape=[out, out...  3.26 us
    ppermute x3, waiting for transfers between devices, _line_gather(): up = lax.ppermute(up, axis, up_pairs)  3.16 us
    pallas_call x1, Pallas kernels, _epilogue(): pl.pallas_call(_epilogue_kernel, out_shape=jax.ShapeDtypeStruct((width, t...  2.02 us
    ppermute x1, starting transfers between devices, _ring_reduce_scatter(): arrived = lax.ppermute(carry.astype(jnp.bfloat16), axis, ring)  2.02 us
  transfers between devices with their start and end apart: 8, of which 6 were waited for; matrix products, arithmetic and copies ran while one was open for 6% of the time, Pallas kernels for 0%

profile of v6, /device:TPU:0, one launch (start us, length us, event | category | flops | bytes accessed | tf_op | source)
XLA Modules:
  0.0 52.4 jit_solution(5692682006527029234)
XLA Ops:
  0.0 0.0 copy-start.1
  0.0 0.8 %slice_bitcast_fusion.1 = (bf16[16,256]{1,0:T(8,128)(2,1)S(1)}, bf16[16,256]{1,0:T(8,128)(2,1)S(1)}) fusion(bf16[1,32,256]{2,1,0:T(8,128)(2,1)} %basis_ref.1), kind=kLoop, calls=%fused_computation.14 | loop fusion | bytes 32768 | tf_op jit(solution)/shard_map/slice | solution.py:163
  0.8 1.0 %maximum_maximum_fusion = bf16[272,512]{1,0:T(8,128)(2,1)S(1)} fusion(bf16[16,256]{1,0:T(8,128)(2,1)S(1)} %get-tuple-element.10, bf16[16,256]{1,0:T(8,128)(2,1)S(1)} %get-tuple-element.9, bf16[256,512]{1,0:T(8,128)(2,1)} %param.6), kind=kLoop, calls=%fused_computation.4 | loop fusion | flops 835584 | bytes 557056 | tf_op jit(solution)/shard_map/concatenate | solution.py:164
  1.7 5.0 %collective-permute-start = (bf16[272,512]{1,0:T(8,128)(2,1)S(1)}, bf16[272,512]{1,0:T(8,128)(2,1)S(1)}, u32[]{:S(2)}, u32[]{:S(2)}) collective-permute-start(bf16[272,512]{1,0:T(8,128)(2,1)S(1)} %maximum_maximum_fusion), channel_id=1, source_target_pairs={{0,4},{4,8},{8,12},{1,5},{5,9},{9,13},{2,6},{6,10},{10,14},{3,7},{... | collective-permute-start | bytes 835592 | tf_op jit(solution)/shard_map/ppermute | solution.py:133
  6.7 1.3 %collective-permute-start.3 = (bf16[272,512]{1,0:T(8,128)(2,1)S(1)}, bf16[272,512]{1,0:T(8,128)(2,1)S(1)}, u32[]{:S(2)}, u32[]{:S(2)}) collective-permute-start(bf16[272,512]{1,0:T(8,128)(2,1)S(1)} %maximum_maximum_fusion), channel_id=1, source_target_pairs={{4,0},{8,4},{12,8},{5,1},{9,5},{13,9},{6,2},{10,6},{14,10},{7,3},{... | collective-permute-start | bytes 835592 | tf_op jit(solution)/shard_map/ppermute | solution.py:134
  8.7 0.8 %add_bitcast_fusion = s32[8]{0:T(128)S(1)} fusion(s32[8,2]{0,1:T(2,128)} %bitcast.41), kind=kLoop, calls=%fused_computation.21 | loop fusion | flops 16 | bytes 96 | tf_op jit(solution)/shard_map/eq | solution.py:172
  9.4 3.2 %collective-permute-done = bf16[272,512]{1,0:T(8,128)(2,1)S(1)} collective-permute-done((bf16[272,512]{1,0:T(8,128)(2,1)S(1)}, bf16[272,512]{1,0:T(8,128)(2,1)S(1)}, u32[]{:S(2)}, u32[]{:S(2)}) %collective-permute-start) | collective-permute-done | bytes 278560 | tf_op jit(solution)/shard_map/ppermute | solution.py:133
  12.6 0.7 %collective-permute-start.1 = (bf16[272,512]{1,0:T(8,128)(2,1)S(1)}, bf16[272,512]{1,0:T(8,128)(2,1)S(1)}, u32[]{:S(2)}, u32[]{:S(2)}) collective-permute-start(bf16[272,512]{1,0:T(8,128)(2,1)S(1)} %collective-permute-done), channel_id=1, source_target_pairs={{4,8},{8,12},{5,9},{9,13},{6,10},{10,14},{7,11},{11,15},{20,24},{2... | collective-permute-start | bytes 835592 | tf_op jit(solution)/shard_map/ppermute | solution.py:133
  13.3 0.1 fusion.2
  13.4 3.4 %collective-permute-done.3 = bf16[272,512]{1,0:T(8,128)(2,1)S(1)} collective-permute-done((bf16[272,512]{1,0:T(8,128)(2,1)S(1)}, bf16[272,512]{1,0:T(8,128)(2,1)S(1)}, u32[]{:S(2)}, u32[]{:S(2)}) %collective-permute-start.3) | collective-permute-done | bytes 278560 | tf_op jit(solution)/shard_map/ppermute | solution.py:134
  16.7 1.3 %collective-permute-start.4 = (bf16[272,512]{1,0:T(8,128)(2,1)S(1)}, bf16[272,512]{1,0:T(8,128)(2,1)S(1)}, u32[]{:S(2)}, u32[]{:S(2)}) collective-permute-start(bf16[272,512]{1,0:T(8,128)(2,1)S(1)} %collective-permute-done.3), channel_id=1, source_target_pairs={{4,0},{8,4},{5,1},{9,5},{6,2},{10,6},{7,3},{11,7},{20,16},{24,20},... | collective-permute-start | bytes 835592 | tf_op jit(solution)/shard_map/ppermute | solution.py:134
  18.0 0.0 collective-permute-done.1
  18.0 0.7 %collective-permute-start.2 = (bf16[272,512]{1,0:T(8,128)(2,1)S(1)}, bf16[272,512]{1,0:T(8,128)(2,1)S(1)}, u32[]{:S(2)}, u32[]{:S(2)}) collective-permute-start(bf16[272,512]{1,0:T(8,128)(2,1)S(1)} %collective-permute-done.1), channel_id=1, source_target_pairs={{8,12},{9,13},{10,14},{11,15},{24,28},{25,29},{26,30},{27,31}} | collective-permute-start | bytes 835592 | tf_op jit(solution)/shard_map/ppermute | solution.py:133
  18.7 0.1 pad_add_fusion.place_ref
  18.8 0.8 %copy.13 = s32[1,1,8,2]{3,2,1,0:T(8,128)S(1)} copy(s32[1,1,8,2]{2,3,1,0:T(2,128)} %param.9) | data formatting | bytes 128 | tf_op args[3]
  19.5 0.1 convert_element_type.37
  19.6 0.1 copy.14
  19.7 0.9 %reshape_squeeze.11 = bf16[4,32,4,32]{3,2,1,0:T(4,128)(2,1)S(1)} reshape(bf16[1,1,128,128]{3,2,1,0:T(8,128)(2,1)} %param.11) | data formatting | bytes 65536 | tf_op jit(solution)/shard_map/reshape;squeeze | solution.py:180
  20.6 0.1 reshape_squeeze.9.pairs_ref
  20.7 0.1 copy_multiply_fusion
  20.8 0.0 copy-start
  20.8 5.3 %collective-permute-done.4 = bf16[272,512]{1,0:T(8,128)(2,1)S(1)} collective-permute-done((bf16[272,512]{1,0:T(8,128)(2,1)S(1)}, bf16[272,512]{1,0:T(8,128)(2,1)S(1)}, u32[]{:S(2)}, u32[]{:S(2)}) %collective-permute-start.4) | collective-permute-done | bytes 278560 | tf_op jit(solution)/shard_map/ppermute | solution.py:134
  26.1 1.3 %collective-permute-start.5 = (bf16[272,512]{1,0:T(8,128)(2,1)S(1)}, bf16[272,512]{1,0:T(8,128)(2,1)S(1)}, u32[]{:S(2)}, u32[]{:S(2)}) collective-permute-start(bf16[272,512]{1,0:T(8,128)(2,1)S(1)} %collective-permute-done.4), channel_id=1, source_target_pairs={{4,0},{5,1},{6,2},{7,3},{20,16},{21,17},{22,18},{23,19}} | collective-permute-start | bytes 835592 | tf_op jit(solution)/shard_map/ppermute | solution.py:134
  27.4 0.0 collective-permute-done.2
  27.5 0.0 copy-done.1
  27.6 7.0 %collective-permute-done.5 = bf16[272,512]{1,0:T(8,128)(2,1)S(1)} collective-permute-done((bf16[272,512]{1,0:T(8,128)(2,1)S(1)}, bf16[272,512]{1,0:T(8,128)(2,1)S(1)}, u32[]{:S(2)}, u32[]{:S(2)}) %collective-permute-start.5) | collective-permute-done | bytes 278560 | tf_op jit(solution)/shard_map/ppermute | solution.py:134
  34.6 0.0 copy-done
  34.6 3.3 %shard_map.64 = (bf16[2,288,512]{2,1,0:T(8,128)(2,1)S(1)}, bf16[2,288,512]{2,1,0:T(8,128)(2,1)S(1)}) custom-call(s32[16]{0:T(128)S(1)} %reshape_squeeze.9.pairs_ref, s32[1]{0:T(128)} %bitcast.37.count_ref, s32[2]{0:T(128)S(1)} %pad_add_fusion.place_ref, bf16[8,256,256]{2,1,0:T(8,128)(2,1)S(1)} %bitcast.39, ...), custom_call_target="tpu_custom_call" | custom-call | tf_op jit(solution)/shard_map/pallas_call | solution.py:98
  37.9 0.1 collective-permute-start.6
  38.0 2.0 %collective-permute-done.6 = bf16[2,288,512]{2,1,0:T(8,128)(2,1)S(1)} collective-permute-done((bf16[2,288,512]{2,1,0:T(8,128)(2,1)S(1)}, bf16[2,288,512]{2,1,0:T(8,128)(2,1)S(1)}, u32[]{:S(2)}, u32[]{:S(2)}) %collective-permute-start.6) | collective-permute-done | bytes 589856 | tf_op jit(solution)/shard_map/ppermute | solution.py:188
  40.0 0.2 convert_add_fusion
  40.2 2.0 %collective-permute-start.7 = (bf16[288,512]{1,0:T(8,128)(2,1)S(1)}, bf16[288,512]{1,0:T(8,128)(2,1)S(1)}, u32[]{:S(2)}, u32[]{:S(2)}) collective-permute-start(bf16[288,512]{1,0:T(8,128)(2,1)S(1)} %fusion), channel_id=1, source_target_pairs={{0,2},{2,0},{1,3},{3,1},{4,6},{6,4},{5,7},{7,5},{8,10},{10,8},{9,1... | collective-permute-start | bytes 884744 | tf_op jit(solution)/shard_map/ppermute | solution.py:148
  42.2 7.3 %collective-permute-done.7 = bf16[288,512]{1,0:T(8,128)(2,1)S(1)} collective-permute-done((bf16[288,512]{1,0:T(8,128)(2,1)S(1)}, bf16[288,512]{1,0:T(8,128)(2,1)S(1)}, u32[]{:S(2)}, u32[]{:S(2)}) %collective-permute-start.7) | collective-permute-done | bytes 294944 | tf_op jit(solution)/shard_map/ppermute | solution.py:148
  49.5 0.9 %bitcast_add_fusion.total_ref = f32[288,512]{1,0:T(8,128)} fusion(f32[2,288,512]{2,1,0:T(8,128)S(1)} %convert_add_fusion, s32[]{:T(128)S(6)} %select_n.21, bf16[288,512]{1,0:T(8,128)(2,1)S(1)} %collective-permute-done.7), kind=kLoop, calls=%fused_computation.1 | loop fusion | flops 294912 | bytes 1474564 | tf_op jit(solution)/shard_map/add | solution.py:150
  50.4 2.0 %shard_map.65 = bf16[256,512]{1,0:T(8,128)(2,1)} custom-call(f32[288,512]{1,0:T(8,128)} %bitcast_add_fusion.total_ref, bf16[1,32,256]{2,1,0:T(8,128)(2,1)} %basis_ref.1), custom_call_target="tpu_custom_call" | custom-call | tf_op jit(solution)/shard_map/pallas_call | solution.py:120
  (10 shorter events, 0.2 us)
Async XLA Ops:
  0.0 27.5 %copy-start.1 = (bf16[256,512]{1,0:T(8,128)(2,1)S(1)}, bf16[256,512]{1,0:T(8,128)(2,1)}, u32[]{:S(2)}) copy-start(bf16[256,512]{1,0:T(8,128)(2,1)} %param.6) | copy-start | bytes 786436
  1.7 10.9 %collective-permute-start = (bf16[272,512]{1,0:T(8,128)(2,1)S(1)}, bf16[272,512]{1,0:T(8,128)(2,1)S(1)}, u32[]{:S(2)}, u32[]{:S(2)}) collective-permute-start(bf16[272,512]{1,0:T(8,128)(2,1)S(1)} %maximum_maximum_fusion), channel_id=1, source_target_pairs={{0,4},{4,8},{8,12},{1,5},{5,9},{9,13},{2,6},{6,10},{10,14},{3,7},{... | collective-permute-start | bytes 835592 | tf_op jit(solution)/shard_map/ppermute | solution.py:133
  6.7 10.0 %collective-permute-start.3 = (bf16[272,512]{1,0:T(8,128)(2,1)S(1)}, bf16[272,512]{1,0:T(8,128)(2,1)S(1)}, u32[]{:S(2)}, u32[]{:S(2)}) collective-permute-start(bf16[272,512]{1,0:T(8,128)(2,1)S(1)} %maximum_maximum_fusion), channel_id=1, source_target_pairs={{4,0},{8,4},{12,8},{5,1},{9,5},{13,9},{6,2},{10,6},{14,10},{7,3},{... | collective-permute-start | bytes 835592 | tf_op jit(solution)/shard_map/ppermute | solution.py:134
  12.6 5.4 %collective-permute-start.1 = (bf16[272,512]{1,0:T(8,128)(2,1)S(1)}, bf16[272,512]{1,0:T(8,128)(2,1)S(1)}, u32[]{:S(2)}, u32[]{:S(2)}) collective-permute-start(bf16[272,512]{1,0:T(8,128)(2,1)S(1)} %collective-permute-done), channel_id=1, source_target_pairs={{4,8},{8,12},{5,9},{9,13},{6,10},{10,14},{7,11},{11,15},{20,24},{2... | collective-permute-start | bytes 835592 | tf_op jit(solution)/shard_map/ppermute | solution.py:133
  16.7 9.4 %collective-permute-start.4 = (bf16[272,512]{1,0:T(8,128)(2,1)S(1)}, bf16[272,512]{1,0:T(8,128)(2,1)S(1)}, u32[]{:S(2)}, u32[]{:S(2)}) collective-permute-start(bf16[272,512]{1,0:T(8,128)(2,1)S(1)} %collective-permute-done.3), channel_id=1, source_target_pairs={{4,0},{8,4},{5,1},{9,5},{6,2},{10,6},{7,3},{11,7},{20,16},{24,20},... | collective-permute-start | bytes 835592 | tf_op jit(solution)/shard_map/ppermute | solution.py:134
  18.0 9.4 %collective-permute-start.2 = (bf16[272,512]{1,0:T(8,128)(2,1)S(1)}, bf16[272,512]{1,0:T(8,128)(2,1)S(1)}, u32[]{:S(2)}, u32[]{:S(2)}) collective-permute-start(bf16[272,512]{1,0:T(8,128)(2,1)S(1)} %collective-permute-done.1), channel_id=1, source_target_pairs={{8,12},{9,13},{10,14},{11,15},{24,28},{25,29},{26,30},{27,31}} | collective-permute-start | bytes 835592 | tf_op jit(solution)/shard_map/ppermute | solution.py:133
  20.8 13.8 %copy-start = (bf16[1,1,8,256,256]{4,3,2,1,0:T(8,128)(2,1)S(1)}, bf16[1,1,8,256,256]{4,3,2,1,0:T(8,128)(2,1)}, u32[]{:S(2)}) copy-start(bf16[1,1,8,256,256]{4,3,2,1,0:T(8,128)(2,1)} %param.8) | copy-start | bytes 3145732
  26.1 8.5 %collective-permute-start.5 = (bf16[272,512]{1,0:T(8,128)(2,1)S(1)}, bf16[272,512]{1,0:T(8,128)(2,1)S(1)}, u32[]{:S(2)}, u32[]{:S(2)}) collective-permute-start(bf16[272,512]{1,0:T(8,128)(2,1)S(1)} %collective-permute-done.4), channel_id=1, source_target_pairs={{4,0},{5,1},{6,2},{7,3},{20,16},{21,17},{22,18},{23,19}} | collective-permute-start | bytes 835592 | tf_op jit(solution)/shard_map/ppermute | solution.py:134
  37.9 2.1 %collective-permute-start.6 = (bf16[2,288,512]{2,1,0:T(8,128)(2,1)S(1)}, bf16[2,288,512]{2,1,0:T(8,128)(2,1)S(1)}, u32[]{:S(2)}, u32[]{:S(2)}) collective-permute-start(bf16[2,288,512]{2,1,0:T(8,128)(2,1)S(1)} %get-tuple-element.8), channel_id=1, source_target_pairs={{0,1},{1,0},{2,3},{3,2},{4,5},{5,4},{6,7},{7,6},{8,9},{9,8},{10,11... | collective-permute-start | bytes 1769480 | tf_op jit(solution)/shard_map/ppermute | solution.py:188
  40.2 9.3 %collective-permute-start.7 = (bf16[288,512]{1,0:T(8,128)(2,1)S(1)}, bf16[288,512]{1,0:T(8,128)(2,1)S(1)}, u32[]{:S(2)}, u32[]{:S(2)}) collective-permute-start(bf16[288,512]{1,0:T(8,128)(2,1)S(1)} %fusion), channel_id=1, source_target_pairs={{0,2},{2,0},{1,3},{3,1},{4,6},{6,4},{5,7},{7,5},{8,10},{10,8},{9,1... | collective-permute-start | bytes 884744 | tf_op jit(solution)/shard_map/ppermute | solution.py:148

commit v7 on v6

--- a/solution.py
+++ b/solution.py
@@ -125,15 +125,23 @@
 
 def _line_gather(payload, axis):
     n = lax.axis_size(axis)
+    if n <= 2:
+        far_up = far_down = None
+    else:
+        far_up = lax.ppermute(payload, axis, [(0, n - 1)])
+        far_down = lax.ppermute(payload, axis, [(n - 1, 0)])
     ups, downs = [], []
     up, down = payload, payload
-    for step in range(n - 1):
+    for step in range(n - 1 if far_up is None else n - 2):
         up_pairs = [(i, i + 1) for i in range(step, n - 1)]
         down_pairs = [(i + 1, i) for i in range(n - 1 - step)]
         up = lax.ppermute(up, axis, up_pairs)
         down = lax.ppermute(down, axis, down_pairs)
         ups.append(up)
         downs.append(down)
+    if far_up is not None:
+        ups.append(far_up)
+        downs.append(far_down)
     return jnp.stack(ups[::-1] + [payload] + downs)
 
 

time: 52.9 us -> 53.5 us (1.011)
  starting transfers between devices: 12.3 us -> 14.2 us
  waiting for transfers between devices: 28.1 us -> 26.4 us
    ppermute x0 -> x2, starting transfers between devices: none -> 4.61 us  [the longest x1 3.32 us: _line_gather(): far_up = lax.ppermute(payload, axis, [(0, n - 1)])]
    ppermute x3 -> x2, waiting for transfers between devices: 3.16 us -> 0.01 us  [_line_gather(): up = lax.ppermute(up, axis, up_pairs)]
    ppermute x3 -> x2, starting transfers between devices: 3.85 us -> 2.57 us  [_line_gather(): down = lax.ppermute(down, axis, down_pairs)]
    ppermute x3 -> x2, waiting for transfers between devices: 15.7 us -> 16.7 us  [_line_gather(): down = lax.ppermute(down, axis, down_pairs)]
    ppermute x1, starting transfers between devices: 2.02 us -> 1.32 us  [_ring_reduce_scatter(): arrived = lax.ppermute(carry.astype(jnp.bfloat16), axis, ring)]
    ppermute x3 -> x2, starting transfers between devices: 6.32 us -> 5.65 us  [_line_gather(): up = lax.ppermute(up, axis, up_pairs)]
  transfers between devices with their start and end apart: 8 -> 8, of which waited for: 6 -> 4; matrix products, arithmetic and copies ran while one was open for 6% -> 6% of each run, Pallas kernels for 0% -> 0%
where the time goes in v7:
time: 53.5 us; the launch traced here: 53.2 us
  waiting for transfers between devices  26.4 us (49%)
  starting transfers between devices  14.2 us (27%)
  Pallas kernels  5.75 us (11%)
  other arithmetic  3.09 us (6%)
  local copies, waits for them, and re-layouts  2.83 us (5%)
  between operations  0.89 us (2%)
    ppermute x2, waiting for transfers between devices, _line_gather(): down = lax.ppermute(down, axis, down_pairs)  16.7 us
    ppermute x1, waiting for transfers between devices, _ring_reduce_scatter(): arrived = lax.ppermute(carry.astype(jnp.bfloat16), axis, ring)  7.8 us
    ppermute x2, starting transfers between devices, _line_gather(): up = lax.ppermute(up, axis, up_pairs)  5.65 us
    pallas_call x1, Pallas kernels, _near_far(): pl.pallas_call(_near_far_kernel, grid_spec=grid_spec, out_shape=[out, out...  3.73 us
    ppermute x1, starting transfers between devices, _line_gather(): far_up = lax.ppermute(payload, axis, [(0, n - 1)])  3.32 us
    ppermute x2, starting transfers between devices, _line_gather(): down = lax.ppermute(down, axis, down_pairs)  2.57 us
    pallas_call x1, Pallas kernels, _epilogue(): pl.pallas_call(_epilogue_kernel, out_shape=jax.ShapeDtypeStruct((width, t...  2.02 us
    ppermute x1, waiting for transfers between devices, on_device(): arrived = lax.ppermute(theirs, 'sub', [(0, 1), (1, 0)])  1.97 us
  transfers between devices with their start and end apart: 8, of which 4 were waited for; matrix products, arithmetic and copies ran while one was open for 6% of the time, Pallas kernels for 0%

profile of v7, /device:TPU:0, one launch (start us, length us, event | category | flops | bytes accessed | tf_op | source)
XLA Modules:
  0.0 53.2 jit_solution(11389877319152786675)
XLA Ops:
  0.0 0.0 copy-start.1
  0.0 0.8 %slice_bitcast_fusion.1 = (bf16[16,256]{1,0:T(8,128)(2,1)S(1)}, bf16[16,256]{1,0:T(8,128)(2,1)S(1)}) fusion(bf16[1,32,256]{2,1,0:T(8,128)(2,1)} %basis_ref.1), kind=kLoop, calls=%fused_computation.14 | loop fusion | bytes 32768 | tf_op jit(solution)/shard_map/slice | solution.py:171
  0.8 1.0 %maximum_maximum_fusion = bf16[272,512]{1,0:T(8,128)(2,1)S(1)} fusion(bf16[16,256]{1,0:T(8,128)(2,1)S(1)} %get-tuple-element.10, bf16[16,256]{1,0:T(8,128)(2,1)S(1)} %get-tuple-element.9, bf16[256,512]{1,0:T(8,128)(2,1)} %param.6), kind=kLoop, calls=%fused_computation.4 | loop fusion | flops 835584 | bytes 557056 | tf_op jit(solution)/shard_map/concatenate | solution.py:172
  1.7 5.0 %collective-permute-start.1 = (bf16[272,512]{1,0:T(8,128)(2,1)S(1)}, bf16[272,512]{1,0:T(8,128)(2,1)S(1)}, u32[]{:S(2)}, u32[]{:S(2)}) collective-permute-start(bf16[272,512]{1,0:T(8,128)(2,1)S(1)} %maximum_maximum_fusion), channel_id=1, source_target_pairs={{0,4},{4,8},{8,12},{1,5},{5,9},{9,13},{2,6},{6,10},{10,14},{3,7},{... | collective-permute-start | bytes 835592 | tf_op jit(solution)/shard_map/ppermute | solution.py:138
  6.7 3.3 %collective-permute-start = (bf16[272,512]{1,0:T(8,128)(2,1)S(1)}, bf16[272,512]{1,0:T(8,128)(2,1)S(1)}, u32[]{:S(2)}, u32[]{:S(2)}) collective-permute-start(bf16[272,512]{1,0:T(8,128)(2,1)S(1)} %maximum_maximum_fusion), channel_id=1, source_target_pairs={{0,12},{1,13},{2,14},{3,15},{16,28},{17,29},{18,30},{19,31}} | collective-permute-start | bytes 835592 | tf_op jit(solution)/shard_map/ppermute | solution.py:131
  10.0 1.3 %collective-permute-start.3 = (bf16[272,512]{1,0:T(8,128)(2,1)S(1)}, bf16[272,512]{1,0:T(8,128)(2,1)S(1)}, u32[]{:S(2)}, u32[]{:S(2)}) collective-permute-start(bf16[272,512]{1,0:T(8,128)(2,1)S(1)} %maximum_maximum_fusion), channel_id=1, source_target_pairs={{4,0},{8,4},{12,8},{5,1},{9,5},{13,9},{6,2},{10,6},{14,10},{7,3},{... | collective-permute-start | bytes 835592 | tf_op jit(solution)/shard_map/ppermute | solution.py:139
  11.3 1.3 %collective-permute-start.5 = (bf16[272,512]{1,0:T(8,128)(2,1)S(1)}, bf16[272,512]{1,0:T(8,128)(2,1)S(1)}, u32[]{:S(2)}, u32[]{:S(2)}) collective-permute-start(bf16[272,512]{1,0:T(8,128)(2,1)S(1)} %maximum_maximum_fusion), channel_id=1, source_target_pairs={{12,0},{13,1},{14,2},{15,3},{28,16},{29,17},{30,18},{31,19}} | collective-permute-start | bytes 835592 | tf_op jit(solution)/shard_map/ppermute | solution.py:132
  13.3 0.8 %add_bitcast_fusion = s32[8]{0:T(128)S(1)} fusion(s32[8,2]{0,1:T(2,128)} %bitcast.41), kind=kLoop, calls=%fused_computation.21 | loop fusion | flops 16 | bytes 96 | tf_op jit(solution)/shard_map/eq | solution.py:180
  14.1 0.1 fusion.2
  14.2 0.1 convert_element_type.37
  14.2 0.1 copy.14
  14.4 0.9 %reshape_squeeze.11 = bf16[4,32,4,32]{3,2,1,0:T(4,128)(2,1)S(1)} reshape(bf16[1,1,128,128]{3,2,1,0:T(8,128)(2,1)} %param.11) | data formatting | bytes 65536 | tf_op jit(solution)/shard_map/reshape;squeeze | solution.py:188
  15.2 0.1 copy_multiply_fusion
  15.3 0.0 collective-permute-done.1
  15.3 0.7 %collective-permute-start.2 = (bf16[272,512]{1,0:T(8,128)(2,1)S(1)}, bf16[272,512]{1,0:T(8,128)(2,1)S(1)}, u32[]{:S(2)}, u32[]{:S(2)}) collective-permute-start(bf16[272,512]{1,0:T(8,128)(2,1)S(1)} %collective-permute-done.1), channel_id=1, source_target_pairs={{4,8},{8,12},{5,9},{9,13},{6,10},{10,14},{7,11},{11,15},{20,24},{2... | collective-permute-start | bytes 835592 | tf_op jit(solution)/shard_map/ppermute | solution.py:138
  16.0 0.1 pad_add_fusion.place_ref
  16.1 0.8 %copy.13 = s32[1,1,8,2]{3,2,1,0:T(8,128)S(1)} copy(s32[1,1,8,2]{2,3,1,0:T(2,128)} %param.9) | data formatting | bytes 128 | tf_op args[3]
  16.9 0.1 reshape_squeeze.9.pairs_ref
  16.9 0.0 copy-start
  16.9 9.7 %collective-permute-done.3 = bf16[272,512]{1,0:T(8,128)(2,1)S(1)} collective-permute-done((bf16[272,512]{1,0:T(8,128)(2,1)S(1)}, bf16[272,512]{1,0:T(8,128)(2,1)S(1)}, u32[]{:S(2)}, u32[]{:S(2)}) %collective-permute-start.3) | collective-permute-done | bytes 278560 | tf_op jit(solution)/shard_map/ppermute | solution.py:139
  26.6 1.3 %collective-permute-start.4 = (bf16[272,512]{1,0:T(8,128)(2,1)S(1)}, bf16[272,512]{1,0:T(8,128)(2,1)S(1)}, u32[]{:S(2)}, u32[]{:S(2)}) collective-permute-start(bf16[272,512]{1,0:T(8,128)(2,1)S(1)} %collective-permute-done.3), channel_id=1, source_target_pairs={{4,0},{8,4},{5,1},{9,5},{6,2},{10,6},{7,3},{11,7},{20,16},{24,20},... | collective-permute-start | bytes 835592 | tf_op jit(solution)/shard_map/ppermute | solution.py:139
  27.9 0.0 collective-permute-done
  28.0 0.0 collective-permute-done.2
  28.0 0.0 copy-done.1
  28.1 7.0 %collective-permute-done.4 = bf16[272,512]{1,0:T(8,128)(2,1)S(1)} collective-permute-done((bf16[272,512]{1,0:T(8,128)(2,1)S(1)}, bf16[272,512]{1,0:T(8,128)(2,1)S(1)}, u32[]{:S(2)}, u32[]{:S(2)}) %collective-permute-start.4) | collective-permute-done | bytes 278560 | tf_op jit(solution)/shard_map/ppermute | solution.py:139
  35.1 0.0 collective-permute-done.5
  35.1 0.0 copy-done
  35.1 3.7 %shard_map.64 = (bf16[2,288,512]{2,1,0:T(8,128)(2,1)S(1)}, bf16[2,288,512]{2,1,0:T(8,128)(2,1)S(1)}) custom-call(s32[16]{0:T(128)S(1)} %reshape_squeeze.9.pairs_ref, s32[1]{0:T(128)} %bitcast.37.count_ref, s32[2]{0:T(128)S(1)} %pad_add_fusion.place_ref, bf16[8,256,256]{2,1,0:T(8,128)(2,1)S(1)} %bitcast.39, ...), custom_call_target="tpu_custom_call" | custom-call | tf_op jit(solution)/shard_map/pallas_call | solution.py:98
  38.9 0.1 collective-permute-start.6
  39.0 2.0 %collective-permute-done.6 = bf16[2,288,512]{2,1,0:T(8,128)(2,1)S(1)} collective-permute-done((bf16[2,288,512]{2,1,0:T(8,128)(2,1)S(1)}, bf16[2,288,512]{2,1,0:T(8,128)(2,1)S(1)}, u32[]{:S(2)}, u32[]{:S(2)}) %collective-permute-start.6) | collective-permute-done | bytes 589856 | tf_op jit(solution)/shard_map/ppermute | solution.py:196
  41.0 0.2 convert_add_fusion
  41.2 1.3 %collective-permute-start.7 = (bf16[288,512]{1,0:T(8,128)(2,1)S(1)}, bf16[288,512]{1,0:T(8,128)(2,1)S(1)}, u32[]{:S(2)}, u32[]{:S(2)}) collective-permute-start(bf16[288,512]{1,0:T(8,128)(2,1)S(1)} %fusion), channel_id=1, source_target_pairs={{0,2},{2,0},{1,3},{3,1},{4,6},{6,4},{5,7},{7,5},{8,10},{10,8},{9,1... | collective-permute-start | bytes 884744 | tf_op jit(solution)/shard_map/ppermute | solution.py:156
  42.5 7.8 %collective-permute-done.7 = bf16[288,512]{1,0:T(8,128)(2,1)S(1)} collective-permute-done((bf16[288,512]{1,0:T(8,128)(2,1)S(1)}, bf16[288,512]{1,0:T(8,128)(2,1)S(1)}, u32[]{:S(2)}, u32[]{:S(2)}) %collective-permute-start.7) | collective-permute-done | bytes 294944 | tf_op jit(solution)/shard_map/ppermute | solution.py:156
  50.3 0.9 %bitcast_add_fusion.total_ref = f32[288,512]{1,0:T(8,128)} fusion(f32[2,288,512]{2,1,0:T(8,128)S(1)} %convert_add_fusion, s32[]{:T(128)S(6)} %select_n.21, bf16[288,512]{1,0:T(8,128)(2,1)S(1)} %collective-permute-done.7), kind=kLoop, calls=%fused_computation.1 | loop fusion | flops 294912 | bytes 1474564 | tf_op jit(solution)/shard_map/add | solution.py:158
  51.2 2.0 %shard_map.65 = bf16[256,512]{1,0:T(8,128)(2,1)} custom-call(f32[288,512]{1,0:T(8,128)} %bitcast_add_fusion.total_ref, bf16[1,32,256]{2,1,0:T(8,128)(2,1)} %basis_ref.1), custom_call_target="tpu_custom_call" | custom-call | tf_op jit(solution)/shard_map/pallas_call | solution.py:120
  (10 shorter events, 0.2 us)
Async XLA Ops:
  0.0 28.0 %copy-start.1 = (bf16[256,512]{1,0:T(8,128)(2,1)S(1)}, bf16[256,512]{1,0:T(8,128)(2,1)}, u32[]{:S(2)}) copy-start(bf16[256,512]{1,0:T(8,128)(2,1)} %param.6) | copy-start | bytes 786436
  1.7 13.6 %collective-permute-start.1 = (bf16[272,512]{1,0:T(8,128)(2,1)S(1)}, bf16[272,512]{1,0:T(8,128)(2,1)S(1)}, u32[]{:S(2)}, u32[]{:S(2)}) collective-permute-start(bf16[272,512]{1,0:T(8,128)(2,1)S(1)} %maximum_maximum_fusion), channel_id=1, source_target_pairs={{0,4},{4,8},{8,12},{1,5},{5,9},{9,13},{2,6},{6,10},{10,14},{3,7},{... | collective-permute-start | bytes 835592 | tf_op jit(solution)/shard_map/ppermute | solution.py:138
  6.7 21.2 %collective-permute-start = (bf16[272,512]{1,0:T(8,128)(2,1)S(1)}, bf16[272,512]{1,0:T(8,128)(2,1)S(1)}, u32[]{:S(2)}, u32[]{:S(2)}) collective-permute-start(bf16[272,512]{1,0:T(8,128)(2,1)S(1)} %maximum_maximum_fusion), channel_id=1, source_target_pairs={{0,12},{1,13},{2,14},{3,15},{16,28},{17,29},{18,30},{19,31}} | collective-permute-start | bytes 835592 | tf_op jit(solution)/shard_map/ppermute | solution.py:131
  10.0 16.6 %collective-permute-start.3 = (bf16[272,512]{1,0:T(8,128)(2,1)S(1)}, bf16[272,512]{1,0:T(8,128)(2,1)S(1)}, u32[]{:S(2)}, u32[]{:S(2)}) collective-permute-start(bf16[272,512]{1,0:T(8,128)(2,1)S(1)} %maximum_maximum_fusion), channel_id=1, source_target_pairs={{4,0},{8,4},{12,8},{5,1},{9,5},{13,9},{6,2},{10,6},{14,10},{7,3},{... | collective-permute-start | bytes 835592 | tf_op jit(solution)/shard_map/ppermute | solution.py:139
  11.3 23.8 %collective-permute-start.5 = (bf16[272,512]{1,0:T(8,128)(2,1)S(1)}, bf16[272,512]{1,0:T(8,128)(2,1)S(1)}, u32[]{:S(2)}, u32[]{:S(2)}) collective-permute-start(bf16[272,512]{1,0:T(8,128)(2,1)S(1)} %maximum_maximum_fusion), channel_id=1, source_target_pairs={{12,0},{13,1},{14,2},{15,3},{28,16},{29,17},{30,18},{31,19}} | collective-permute-start | bytes 835592 | tf_op jit(solution)/shard_map/ppermute | solution.py:132
  15.3 12.6 %collective-permute-start.2 = (bf16[272,512]{1,0:T(8,128)(2,1)S(1)}, bf16[272,512]{1,0:T(8,128)(2,1)S(1)}, u32[]{:S(2)}, u32[]{:S(2)}) collective-permute-start(bf16[272,512]{1,0:T(8,128)(2,1)S(1)} %collective-permute-done.1), channel_id=1, source_target_pairs={{4,8},{8,12},{5,9},{9,13},{6,10},{10,14},{7,11},{11,15},{20,24},{2... | collective-permute-start | bytes 835592 | tf_op jit(solution)/shard_map/ppermute | solution.py:138
  16.9 18.2 %copy-start = (bf16[1,1,8,256,256]{4,3,2,1,0:T(8,128)(2,1)S(1)}, bf16[1,1,8,256,256]{4,3,2,1,0:T(8,128)(2,1)}, u32[]{:S(2)}) copy-start(bf16[1,1,8,256,256]{4,3,2,1,0:T(8,128)(2,1)} %param.8) | copy-start | bytes 3145732
  26.6 8.4 %collective-permute-start.4 = (bf16[272,512]{1,0:T(8,128)(2,1)S(1)}, bf16[272,512]{1,0:T(8,128)(2,1)S(1)}, u32[]{:S(2)}, u32[]{:S(2)}) collective-permute-start(bf16[272,512]{1,0:T(8,128)(2,1)S(1)} %collective-permute-done.3), channel_id=1, source_target_pairs={{4,0},{8,4},{5,1},{9,5},{6,2},{10,6},{7,3},{11,7},{20,16},{24,20},... | collective-permute-start | bytes 835592 | tf_op jit(solution)/shard_map/ppermute | solution.py:139
  38.9 2.1 %collective-permute-start.6 = (bf16[2,288,512]{2,1,0:T(8,128)(2,1)S(1)}, bf16[2,288,512]{2,1,0:T(8,128)(2,1)S(1)}, u32[]{:S(2)}, u32[]{:S(2)}) collective-permute-start(bf16[2,288,512]{2,1,0:T(8,128)(2,1)S(1)} %get-tuple-element.8), channel_id=1, source_target_pairs={{0,1},{1,0},{2,3},{3,2},{4,5},{5,4},{6,7},{7,6},{8,9},{9,8},{10,11... | collective-permute-start | bytes 1769480 | tf_op jit(solution)/shard_map/ppermute | solution.py:196
  41.2 9.1 %collective-permute-start.7 = (bf16[288,512]{1,0:T(8,128)(2,1)S(1)}, bf16[288,512]{1,0:T(8,128)(2,1)S(1)}, u32[]{:S(2)}, u32[]{:S(2)}) collective-permute-start(bf16[288,512]{1,0:T(8,128)(2,1)S(1)} %fusion), channel_id=1, source_target_pairs={{0,2},{2,0},{1,3},{3,1},{4,6},{6,4},{5,7},{7,5},{8,10},{10,8},{9,1... | collective-permute-start | bytes 884744 | tf_op jit(solution)/shard_map/ppermute | solution.py:156

commit v8 on v7

--- a/solution.py
+++ b/solution.py
@@ -7,7 +7,16 @@
 
 
 def _near_far_kernel(
-    pairs_ref, count_ref, place_ref, tiles_ref, stack_ref, masked_ref, mine_ref, theirs_ref, acc_ref
+    pairs_ref,
+    count_ref,
+    place_ref,
+    tiles_ref,
+    stack_ref,
+    packed_ref,
+    masked_ref,
+    mine_ref,
+    theirs_ref,
+    acc_ref,
 ):
     slot = pl.program_id(0)
     slot_total = pl.num_programs(0)
@@ -38,9 +47,9 @@
     def _():
         coeffs = jnp.zeros((inner_count * rank_size, rhs_count), jnp.float32)
         for source in range(tgt_count):
-            block = stack_ref[source - own_tgt + tgt_count - 1]
-            dens = block[:width, :]
-            packed = block[width:, :]
+            offset = source - own_tgt + tgt_count - 1
+            dens = stack_ref[offset, :width, :]
+            packed = packed_ref[offset]
             top = jnp.dot(packed[:, :width], dens, preferred_element_type=jnp.float32)
             bottom = jnp.dot(packed[:, width:], dens, preferred_element_type=jnp.float32)
             projected = jnp.concatenate([top, bottom], axis=0).astype(jnp.bfloat16)
@@ -63,9 +72,10 @@
             write(theirs_ref, mine_ref)
 
 
-def _near_far(pairs_flat, count, place, tiles, stack, masked_t, inner_count, rank_size):
+def _near_far(pairs_flat, count, place, tiles, stack, masked_t, inner_count, rank_size, chunk, cols):
     slot_count, width, _ = tiles.shape
-    stack_count, rows, rhs_count = stack.shape
+    stack_count, rows, full_cols = stack.shape
+    half_rank = rank_size // 2
     half_count = inner_count // 2
     out_rows = width + rank_size
 
@@ -78,23 +88,27 @@
         grid=(slot_count,),
         in_specs=[
             pl.BlockSpec((None, width, width), tile_index),
-            pl.BlockSpec(stack.shape, whole),
+            pl.BlockSpec((stack_count, width, cols), lambda k, p, c, q: (0, 0, chunk)),
+            pl.BlockSpec(
+                (stack_count, half_rank, full_cols), lambda k, p, c, q: (0, width // half_rank, 0)
+            ),
             pl.BlockSpec(masked_t.shape, whole),
         ],
         out_specs=[
-            pl.BlockSpec((half_count, out_rows, rhs_count), whole),
-            pl.BlockSpec((half_count, out_rows, rhs_count), whole),
+            pl.BlockSpec((half_count, out_rows, cols), whole),
+            pl.BlockSpec((half_count, out_rows, cols), whole),
         ],
-        scratch_shapes=[pltpu.VMEM((inner_count, width, rhs_count), jnp.float32)],
-    )
-    out = jax.ShapeDtypeStruct((half_count, out_rows, rhs_count), jnp.bfloat16)
-    block_bytes = 2 * (
-        width * width * tiles.dtype.itemsize
-        + stack.size * stack.dtype.itemsize
-        + masked_t.size * masked_t.dtype.itemsize
-        + 2 * half_count * out_rows * rhs_count * 2
-    )
-    vmem_bytes = block_bytes + inner_count * width * rhs_count * 4 + (4 << 20)
+        scratch_shapes=[pltpu.VMEM((inner_count, width, cols), jnp.float32)],
+    )
+    out = jax.ShapeDtypeStruct((half_count, out_rows, cols), jnp.bfloat16)
+    block_bytes = 2 * 2 * (
+        width * width
+        + stack_count * width * cols
+        + stack_count * half_rank * full_cols
+        + masked_t.size
+        + 2 * half_count * out_rows * cols
+    )
+    vmem_bytes = block_bytes + inner_count * width * cols * 4 + (4 << 20)
     return pl.pallas_call(
         _near_far_kernel,
         grid_spec=grid_spec,
@@ -102,25 +116,52 @@
         compiler_params=pltpu.CompilerParams(
             dimension_semantics=("arbitrary",), vmem_limit_bytes=int(vmem_bytes)
         ),
-    )(pairs_flat, count, place, tiles, stack, masked_t)
-
-
-def _epilogue_kernel(total_ref, basis_ref, out_ref):
+    )(pairs_flat, count, place, tiles, stack, stack, masked_t)
+
+
+def _epilogue_kernel(me_ref, basis_ref, *refs):
+    piece_refs, out_ref = refs[:-1], refs[-1]
     width = out_ref.shape[0]
-    near = total_ref[:width, :]
-    coeffs = total_ref[width:, :].astype(jnp.bfloat16)
+    total = piece_refs[0][...].astype(jnp.float32)
+    for piece_ref in piece_refs[1:]:
+        total += piece_ref[...].astype(jnp.float32)
+    coeffs = total[width:, :].astype(jnp.bfloat16)
     far = lax.dot_general(
         basis_ref[0], coeffs, (((0,), (0,)), ((), ())), preferred_element_type=jnp.float32
     )
-    out_ref[...] = (near + far).astype(out_ref.dtype)
-
-
-def _epilogue(total, basis):
+    out_ref[...] = (total[:width, :] + far).astype(out_ref.dtype)
+
+
+def _epilogue(me, pieces, basis, chunk, rhs_count, previous):
     width = basis.shape[2]
+    cols = pieces[0].shape[-1]
+    in_specs = [pl.BlockSpec(basis.shape, lambda i, m: (0, 0, 0))]
+    for piece in pieces:
+        if piece.ndim == 3:
+            in_specs.append(pl.BlockSpec((None,) + piece.shape[1:], lambda i, m: (m[0], 0, 0)))
+        else:
+            in_specs.append(pl.BlockSpec(piece.shape, lambda i, m: (0, 0)))
+    args = [me, basis, *pieces]
+    aliases = {}
+    if previous is not None:
+        in_specs.append(pl.BlockSpec(memory_space=pl.ANY))
+        args.append(previous)
+        aliases = {len(args) - 1: 0}
+    grid_spec = pltpu.PrefetchScalarGridSpec(
+        num_scalar_prefetch=1,
+        grid=(1,),
+        in_specs=in_specs,
+        out_specs=pl.BlockSpec((width, cols), lambda i, m: (0, chunk)),
+    )
+    kernel = _epilogue_kernel
+    if previous is not None:
+        kernel = lambda m, b, *r: _epilogue_kernel(m, b, *r[:-2], r[-1])
     return pl.pallas_call(
-        _epilogue_kernel,
-        out_shape=jax.ShapeDtypeStruct((width, total.shape[1]), jnp.bfloat16),
-    )(total, basis)
+        kernel,
+        grid_spec=grid_spec,
+        out_shape=jax.ShapeDtypeStruct((width, rhs_count), jnp.bfloat16),
+        input_output_aliases=aliases,
+    )(*args)
 
 
 def _line_gather(payload, axis):
@@ -189,14 +230,29 @@
     masked_t = masked.transpose(2, 0, 1, 3).reshape(tgt_count, inner_count * rank_size, rank_size)
 
     place = jnp.stack([lax.axis_index("tgt"), lax.axis_index("sub")]).astype(jnp.int32)
-    mine, theirs = _near_far(
-        pair_list.reshape(-1), live_count.reshape(1), place, near_blocks[0, 0], stack, masked_t,
-        inner_count, rank_size,
-    )
-    arrived = lax.ppermute(theirs, "sub", [(0, 1), (1, 0)])
-    stage = mine.astype(jnp.float32) + arrived.astype(jnp.float32)
-    total = _ring_reduce_scatter(stage, "inner")
-    return _epilogue(total, cluster_basis)
+    chunk_count = 2
+    cols = rhs_count // chunk_count
+    result = None
+    for chunk in range(chunk_count):
+        mine, theirs = _near_far(
+            pair_list.reshape(-1), live_count.reshape(1), place, near_blocks[0, 0], stack,
+            masked_t, inner_count, rank_size, chunk, cols,
+        )
+        arrived = lax.ppermute(theirs, "sub", [(0, 1), (1, 0)])
+        if lax.axis_size("inner") == 2:
+            me = lax.axis_index("inner")
+            send = (
+                lax.dynamic_index_in_dim(mine, 1 - me, 0, False).astype(jnp.float32)
+                + lax.dynamic_index_in_dim(arrived, 1 - me, 0, False).astype(jnp.float32)
+            ).astype(jnp.bfloat16)
+            back = lax.ppermute(send, "inner", [(0, 1), (1, 0)])
+            pieces = (mine, arrived, back)
+        else:
+            stage = mine.astype(jnp.float32) + arrived.astype(jnp.float32)
+            pieces = (_ring_reduce_scatter(stage, "inner"),)
+        me_index = lax.axis_index("inner").astype(jnp.int32).reshape(1)
+        result = _epilogue(me_index, pieces, cluster_basis, chunk, rhs_count, result)
+    return result
 
 
 def solution(mesh):

time: 53.5 us -> 54.2 us (1.013)
  waiting for transfers between devices: 26.4 us -> 20.2 us
  Pallas kernels: 5.75 us -> 9.23 us
  starting transfers between devices: 14.2 us -> 17.2 us
  local copies, waits for them, and re-layouts: 2.83 us -> 4.12 us
  other arithmetic: 3.09 us -> 2.1 us
    ppermute x1 -> x2, waiting for transfers between devices: 7.8 us -> 3.52 us  [on_device(): back = lax.ppermute(send, 'inner', [(0, 1), (1, 0)])]
    ppermute x1 -> x2, starting transfers between devices: 1.32 us -> 3.73 us  [on_device(): back = lax.ppermute(send, 'inner', [(0, 1), (1, 0)])]
    ppermute x1 -> x2, waiting for transfers between devices: 1.97 us -> 0.01 us  [on_device(): arrived = lax.ppermute(theirs, 'sub', [(0, 1), (1, 0)])]
    pallas_call x1 -> x2, Pallas kernels: 2.02 us -> 3.87 us  [_epilogue(): pl.pallas_call(kernel, grid_spec=grid_spec, out_shape=jax.ShapeDtypeStruc...]
    pallas_call x1 -> x2, Pallas kernels: 3.73 us -> 5.35 us  [_near_far(): pl.pallas_call(_near_far_kernel, grid_spec=grid_spec, out_shape=[out, out...]
    unnamed x10 -> x22, local copies, waits for them, and re-layouts: 0.86 us -> 2.19 us
    add x2 -> x0, other arithmetic: 1.07 us -> none  [the longest x1 0.89 us: _ring_reduce_scatter(): carry = arrived.astype(jnp.float32) + own]
    ppermute x1 -> x2, starting transfers between devices: 0.07 us -> 0.63 us  [on_device(): arrived = lax.ppermute(theirs, 'sub', [(0, 1), (1, 0)])]
  transfers between devices with their start and end apart: 8 -> 10, of which waited for: 4 -> 4; matrix products, arithmetic and copies ran while one was open for 6% -> 6% of each run, Pallas kernels for 0% -> 9%
where the time goes in v8:
time: 54.2 us; the launch traced here: 53.7 us
  waiting for transfers between devices  20.2 us (37%)
  starting transfers between devices  17.2 us (32%)
  Pallas kernels  9.23 us (17%)
  local copies, waits for them, and re-layouts  4.12 us (8%)
  other arithmetic  2.1 us (4%)
  between operations  0.89 us (2%)
    ppermute x2, waiting for transfers between devices, _line_gather(): down = lax.ppermute(down, axis, down_pairs)  16.7 us
    ppermute x2, starting transfers between devices, _line_gather(): up = lax.ppermute(up, axis, up_pairs)  5.65 us
    pallas_call x2, Pallas kernels, _near_far(): pl.pallas_call(_near_far_kernel, grid_spec=grid_spec, out_shape=[out, out...  5.35 us
    pallas_call x2, Pallas kernels, _epilogue(): pl.pallas_call(kernel, grid_spec=grid_spec, out_shape=jax.ShapeDtypeStruc...  3.87 us
    ppermute x2, starting transfers between devices, on_device(): back = lax.ppermute(send, 'inner', [(0, 1), (1, 0)])  3.73 us
    ppermute x2, waiting for transfers between devices, on_device(): back = lax.ppermute(send, 'inner', [(0, 1), (1, 0)])  3.52 us
    ppermute x1, starting transfers between devices, _line_gather(): far_up = lax.ppermute(payload, axis, [(0, n - 1)])  3.32 us
    ppermute x2, starting transfers between devices, _line_gather(): down = lax.ppermute(down, axis, down_pairs)  2.57 us
  transfers between devices with their start and end apart: 10, of which 4 were waited for; matrix products, arithmetic and copies ran while one was open for 6% of the time, Pallas kernels for 9%

profile of v8, /device:TPU:0, one launch (start us, length us, event | category | flops | bytes accessed | tf_op | source)
XLA Modules:
  0.0 53.7 jit_solution(13487049460268444155)
XLA Ops:
  0.0 0.0 copy-start.3
  0.0 0.8 %slice_bitcast_fusion.1 = (bf16[16,256]{1,0:T(8,128)(2,1)S(1)}, bf16[16,256]{1,0:T(8,128)(2,1)S(1)}) fusion(bf16[1,32,256]{2,1,0:T(8,128)(2,1)} %b.1), kind=kLoop, calls=%fused_computation.14 | loop fusion | bytes 32768 | tf_op jit(solution)/shard_map/slice | solution.py:212
  0.8 1.0 %maximum_maximum_fusion = bf16[272,512]{1,0:T(8,128)(2,1)S(1)} fusion(bf16[16,256]{1,0:T(8,128)(2,1)S(1)} %get-tuple-element.14, bf16[16,256]{1,0:T(8,128)(2,1)S(1)} %get-tuple-element.13, bf16[256,512]{1,0:T(8,128)(2,1)} %param.6), kind=kLoop, calls=%fused_computation.2 | loop fusion | flops 835584 | bytes 557056 | tf_op jit(solution)/shard_map/concatenate | solution.py:213
  1.7 5.0 %collective-permute-start.1 = (bf16[272,512]{1,0:T(8,128)(2,1)S(1)}, bf16[272,512]{1,0:T(8,128)(2,1)S(1)}, u32[]{:S(2)}, u32[]{:S(2)}) collective-permute-start(bf16[272,512]{1,0:T(8,128)(2,1)S(1)} %maximum_maximum_fusion), channel_id=1, source_target_pairs={{0,4},{4,8},{8,12},{1,5},{5,9},{9,13},{2,6},{6,10},{10,14},{3,7},{... | collective-permute-start | bytes 835592 | tf_op jit(solution)/shard_map/ppermute | solution.py:179
  6.7 3.3 %collective-permute-start = (bf16[272,512]{1,0:T(8,128)(2,1)S(1)}, bf16[272,512]{1,0:T(8,128)(2,1)S(1)}, u32[]{:S(2)}, u32[]{:S(2)}) collective-permute-start(bf16[272,512]{1,0:T(8,128)(2,1)S(1)} %maximum_maximum_fusion), channel_id=1, source_target_pairs={{0,12},{1,13},{2,14},{3,15},{16,28},{17,29},{18,30},{19,31}} | collective-permute-start | bytes 835592 | tf_op jit(solution)/shard_map/ppermute | solution.py:172
  10.0 1.3 %collective-permute-start.3 = (bf16[272,512]{1,0:T(8,128)(2,1)S(1)}, bf16[272,512]{1,0:T(8,128)(2,1)S(1)}, u32[]{:S(2)}, u32[]{:S(2)}) collective-permute-start(bf16[272,512]{1,0:T(8,128)(2,1)S(1)} %maximum_maximum_fusion), channel_id=1, source_target_pairs={{4,0},{8,4},{12,8},{5,1},{9,5},{13,9},{6,2},{10,6},{14,10},{7,3},{... | collective-permute-start | bytes 835592 | tf_op jit(solution)/shard_map/ppermute | solution.py:180
  11.3 1.3 %collective-permute-start.5 = (bf16[272,512]{1,0:T(8,128)(2,1)S(1)}, bf16[272,512]{1,0:T(8,128)(2,1)S(1)}, u32[]{:S(2)}, u32[]{:S(2)}) collective-permute-start(bf16[272,512]{1,0:T(8,128)(2,1)S(1)} %maximum_maximum_fusion), channel_id=1, source_target_pairs={{12,0},{13,1},{14,2},{15,3},{28,16},{29,17},{30,18},{31,19}} | collective-permute-start | bytes 835592 | tf_op jit(solution)/shard_map/ppermute | solution.py:173
  13.3 0.8 %add_bitcast_fusion = s32[8]{0:T(128)S(1)} fusion(s32[8,2]{0,1:T(2,128)} %bitcast.45), kind=kLoop, calls=%fused_computation.21 | loop fusion | flops 16 | bytes 96 | tf_op jit(solution)/shard_map/eq | solution.py:221
  14.1 0.1 fusion.3
  14.2 0.1 convert_element_type.50
  14.2 0.1 copy.15
  14.4 0.9 %reshape_squeeze.13 = bf16[4,32,4,32]{3,2,1,0:T(4,128)(2,1)S(1)} reshape(bf16[1,1,128,128]{3,2,1,0:T(8,128)(2,1)} %param.11) | data formatting | bytes 65536 | tf_op jit(solution)/shard_map/reshape;squeeze | solution.py:229
  15.2 0.1 copy_multiply_fusion
  15.3 0.0 collective-permute-done.1
  15.3 0.7 %collective-permute-start.2 = (bf16[272,512]{1,0:T(8,128)(2,1)S(1)}, bf16[272,512]{1,0:T(8,128)(2,1)S(1)}, u32[]{:S(2)}, u32[]{:S(2)}) collective-permute-start(bf16[272,512]{1,0:T(8,128)(2,1)S(1)} %collective-permute-done.1), channel_id=1, source_target_pairs={{4,8},{8,12},{5,9},{9,13},{6,10},{10,14},{7,11},{11,15},{20,24},{2... | collective-permute-start | bytes 835592 | tf_op jit(solution)/shard_map/ppermute | solution.py:179
  16.0 0.1 pad_add_fusion.place_ref
  16.1 0.8 %copy.14 = s32[1,1,8,2]{3,2,1,0:T(8,128)S(1)} copy(s32[1,1,8,2]{2,3,1,0:T(2,128)} %param.9) | data formatting | bytes 128 | tf_op args[3]
  16.9 0.1 reshape_squeeze.11.pairs_ref
  16.9 0.0 copy-start
  16.9 9.7 %collective-permute-done.3 = bf16[272,512]{1,0:T(8,128)(2,1)S(1)} collective-permute-done((bf16[272,512]{1,0:T(8,128)(2,1)S(1)}, bf16[272,512]{1,0:T(8,128)(2,1)S(1)}, u32[]{:S(2)}, u32[]{:S(2)}) %collective-permute-start.3) | collective-permute-done | bytes 278560 | tf_op jit(solution)/shard_map/ppermute | solution.py:180
  26.6 1.3 %collective-permute-start.4 = (bf16[272,512]{1,0:T(8,128)(2,1)S(1)}, bf16[272,512]{1,0:T(8,128)(2,1)S(1)}, u32[]{:S(2)}, u32[]{:S(2)}) collective-permute-start(bf16[272,512]{1,0:T(8,128)(2,1)S(1)} %collective-permute-done.3), channel_id=1, source_target_pairs={{4,0},{8,4},{5,1},{9,5},{6,2},{10,6},{7,3},{11,7},{20,16},{24,20},... | collective-permute-start | bytes 835592 | tf_op jit(solution)/shard_map/ppermute | solution.py:180
  27.9 0.0 collective-permute-done
  28.0 0.0 collective-permute-done.2
  28.0 0.0 copy-done.3
  28.1 7.0 %collective-permute-done.4 = bf16[272,512]{1,0:T(8,128)(2,1)S(1)} collective-permute-done((bf16[272,512]{1,0:T(8,128)(2,1)S(1)}, bf16[272,512]{1,0:T(8,128)(2,1)S(1)}, u32[]{:S(2)}, u32[]{:S(2)}) %collective-permute-start.4) | collective-permute-done | bytes 278560 | tf_op jit(solution)/shard_map/ppermute | solution.py:180
  35.1 0.0 collective-permute-done.5
  35.1 0.0 copy-done
  35.1 2.7 %shard_map.65 = (bf16[2,288,256]{2,1,0:T(8,128)(2,1)S(1)}, bf16[2,288,256]{2,1,0:T(8,128)(2,1)S(1)}) custom-call(s32[16]{0:T(128)S(1)} %reshape_squeeze.11.pairs_ref, s32[1]{0:T(128)} %bitcast.39.count_ref, s32[2]{0:T(128)S(1)} %pad_add_fusion.place_ref, bf16[8,256,256]{2,1,0:T(8,128)(2,1)S(1)} %bitcast.41, ...), custom_call_target="tpu_custom_call" | custom-call | tf_op jit(solution)/shard_map/pallas_call | solution.py:112
  37.8 0.0 copy-start.1
  37.8 0.1 collective-permute-start.8
  37.9 2.7 %shard_map.64 = (bf16[2,288,256]{2,1,0:T(8,128)(2,1)S(1)}, bf16[2,288,256]{2,1,0:T(8,128)(2,1)S(1)}) custom-call(s32[16]{0:T(128)S(1)} %reshape_squeeze.11.pairs_ref, s32[1]{0:T(128)} %bitcast.38.count_ref, s32[2]{0:T(128)S(1)} %pad_add_fusion.place_ref, bf16[8,256,256]{2,1,0:T(8,128)(2,1)S(1)} %bitcast.42, ...), custom_call_target="tpu_custom_call" | custom-call | tf_op jit(solution)/shard_map/pallas_call | solution.py:112
  40.6 0.0 copy-start.2
  40.6 0.6 %collective-permute-start.6 = (bf16[2,288,256]{2,1,0:T(8,128)(2,1)S(1)}, bf16[2,288,256]{2,1,0:T(8,128)(2,1)S(1)}, u32[]{:S(2)}, u32[]{:S(2)}) collective-permute-start(bf16[2,288,256]{2,1,0:T(8,128)(2,1)S(1)} %get-tuple-element.10), channel_id=1, source_target_pairs={{0,1},{1,0},{2,3},{3,2},{4,5},{5,4},{6,7},{7,6},{8,9},{9,8},{10,11... | collective-permute-start | bytes 884744 | tf_op jit(solution)/shard_map/ppermute | solution.py:241
  41.2 0.0 collective-permute-done.8.refs_1_
  41.2 0.0 copy-start.4
  41.2 0.0 copy-done.1
  41.2 2.3 %collective-permute-start.9 = (bf16[288,256]{1,0:T(8,128)(2,1)S(1)}, bf16[288,256]{1,0:T(8,128)(2,1)S(1)}, u32[]{:S(2)}, u32[]{:S(2)}) collective-permute-start(bf16[288,256]{1,0:T(8,128)(2,1)S(1)} %fusion.1), channel_id=1, source_target_pairs={{0,2},{2,0},{1,3},{3,1},{4,6},{6,4},{5,7},{7,5},{8,10},{10,8},{9,1... | collective-permute-start | bytes 442376 | tf_op jit(solution)/shard_map/ppermute | solution.py:248
  43.5 0.0 collective-permute-done.6.r_1_
  43.5 0.0 copy-start.5
  43.5 1.5 %collective-permute-start.7 = (bf16[288,256]{1,0:T(8,128)(2,1)S(1)}, bf16[288,256]{1,0:T(8,128)(2,1)S(1)}, u32[]{:S(2)}, u32[]{:S(2)}) collective-permute-start(bf16[288,256]{1,0:T(8,128)(2,1)S(1)} %fusion), channel_id=1, source_target_pairs={{0,2},{2,0},{1,3},{3,1},{4,6},{6,4},{5,7},{7,5},{8,10},{10,8},{9,1... | collective-permute-start | bytes 442376 | tf_op jit(solution)/shard_map/ppermute | solution.py:248
  45.0 3.2 %collective-permute-done.9.refs_2_ = bf16[288,256]{1,0:T(8,128)(2,1)S(1)} collective-permute-done((bf16[288,256]{1,0:T(8,128)(2,1)S(1)}, bf16[288,256]{1,0:T(8,128)(2,1)S(1)}, u32[]{:S(2)}, u32[]{:S(2)}) %collective-permute-start.9) | collective-permute-done | bytes 147488 | tf_op jit(solution)/shard_map/ppermute | solution.py:248
  48.2 0.0 copy-start.6
  48.2 0.0 copy-done.4
  48.2 0.6 %copy-done.6 = bf16[288,256]{1,0:T(8,128)(2,1)} copy-done((bf16[288,256]{1,0:T(8,128)(2,1)}, bf16[288,256]{1,0:T(8,128)(2,1)S(1)}, u32[]{:S(2)}) %copy-start.6) | copy-done | bytes 147480
  48.8 1.9 %shard_map.66.r_3_ = bf16[256,512]{1,0:T(8,128)(2,1)} custom-call(s32[1]{0:T(128)} %bitcast.me_ref.m, bf16[1,32,256]{2,1,0:T(8,128)(2,1)} %b.1, bf16[2,288,256]{2,1,0:T(8,128)(2,1)} %copy-done.1, bf16[2,288,256]{2,1,0:T(8,128)(2,1)} %copy-done.4, bf16[288,256]{1,0:T(8,128)(2,1)} %copy-done.6), custom_call_target="tpu_custom_call" | custom-call | tf_op jit(solution)/shard_map/pallas_call | solution.py:159
  50.8 0.3 collective-permute-done.7.r_2_
  51.1 0.0 copy-done.2
  51.1 0.0 copy-done.5
  51.1 0.0 copy-start.7
  51.1 0.7 %copy-done.7 = bf16[288,256]{1,0:T(8,128)(2,1)} copy-done((bf16[288,256]{1,0:T(8,128)(2,1)}, bf16[288,256]{1,0:T(8,128)(2,1)S(1)}, u32[]{:S(2)}) %copy-start.7) | copy-done | bytes 147480
  51.8 1.9 %shard_map.67 = bf16[256,512]{1,0:T(8,128)(2,1)} custom-call(s32[1]{0:T(128)} %bitcast.me_ref.m, bf16[1,32,256]{2,1,0:T(8,128)(2,1)} %b.1, bf16[2,288,256]{2,1,0:T(8,128)(2,1)} %copy-done.2, bf16[2,288,256]{2,1,0:T(8,128)(2,1)} %copy-done.5, bf16[288,256]{1,0:T(8,128)(2,1)} %copy-done.7, bf16[256,512]{1,0:T(8,128)(2,1)} %shard_map.66.r_3_), custom_call_target="tpu_custom_call", output_to_operand_aliasing={{}: (5, {})} | custom-call | tf_op jit(solution)/shard_map/pallas_call | solution.py:159
  (11 shorter events, 0.2 us)
Async XLA Ops:
  0.0 28.0 %copy-start.3 = (bf16[256,512]{1,0:T(8,128)(2,1)S(1)}, bf16[256,512]{1,0:T(8,128)(2,1)}, u32[]{:S(2)}) copy-start(bf16[256,512]{1,0:T(8,128)(2,1)} %param.6) | copy-start | bytes 786436
  1.7 13.6 %collective-permute-start.1 = (bf16[272,512]{1,0:T(8,128)(2,1)S(1)}, bf16[272,512]{1,0:T(8,128)(2,1)S(1)}, u32[]{:S(2)}, u32[]{:S(2)}) collective-permute-start(bf16[272,512]{1,0:T(8,128)(2,1)S(1)} %maximum_maximum_fusion), channel_id=1, source_target_pairs={{0,4},{4,8},{8,12},{1,5},{5,9},{9,13},{2,6},{6,10},{10,14},{3,7},{... | collective-permute-start | bytes 835592 | tf_op jit(solution)/shard_map/ppermute | solution.py:179
  6.7 21.2 %collective-permute-start = (bf16[272,512]{1,0:T(8,128)(2,1)S(1)}, bf16[272,512]{1,0:T(8,128)(2,1)S(1)}, u32[]{:S(2)}, u32[]{:S(2)}) collective-permute-start(bf16[272,512]{1,0:T(8,128)(2,1)S(1)} %maximum_maximum_fusion), channel_id=1, source_target_pairs={{0,12},{1,13},{2,14},{3,15},{16,28},{17,29},{18,30},{19,31}} | collective-permute-start | bytes 835592 | tf_op jit(solution)/shard_map/ppermute | solution.py:172
  10.0 16.6 %collective-permute-start.3 = (bf16[272,512]{1,0:T(8,128)(2,1)S(1)}, bf16[272,512]{1,0:T(8,128)(2,1)S(1)}, u32[]{:S(2)}, u32[]{:S(2)}) collective-permute-start(bf16[272,512]{1,0:T(8,128)(2,1)S(1)} %maximum_maximum_fusion), channel_id=1, source_target_pairs={{4,0},{8,4},{12,8},{5,1},{9,5},{13,9},{6,2},{10,6},{14,10},{7,3},{... | collective-permute-start | bytes 835592 | tf_op jit(solution)/shard_map/ppermute | solution.py:180
  11.3 23.8 %collective-permute-start.5 = (bf16[272,512]{1,0:T(8,128)(2,1)S(1)}, bf16[272,512]{1,0:T(8,128)(2,1)S(1)}, u32[]{:S(2)}, u32[]{:S(2)}) collective-permute-start(bf16[272,512]{1,0:T(8,128)(2,1)S(1)} %maximum_maximum_fusion), channel_id=1, source_target_pairs={{12,0},{13,1},{14,2},{15,3},{28,16},{29,17},{30,18},{31,19}} | collective-permute-start | bytes 835592 | tf_op jit(solution)/shard_map/ppermute | solution.py:173
  15.3 12.6 %collective-permute-start.2 = (bf16[272,512]{1,0:T(8,128)(2,1)S(1)}, bf16[272,512]{1,0:T(8,128)(2,1)S(1)}, u32[]{:S(2)}, u32[]{:S(2)}) collective-permute-start(bf16[272,512]{1,0:T(8,128)(2,1)S(1)} %collective-permute-done.1), channel_id=1, source_target_pairs={{4,8},{8,12},{5,9},{9,13},{6,10},{10,14},{7,11},{11,15},{20,24},{2... | collective-permute-start | bytes 835592 | tf_op jit(solution)/shard_map/ppermute | solution.py:179
  16.9 18.2 %copy-start = (bf16[1,1,8,256,256]{4,3,2,1,0:T(8,128)(2,1)S(1)}, bf16[1,1,8,256,256]{4,3,2,1,0:T(8,128)(2,1)}, u32[]{:S(2)}) copy-start(bf16[1,1,8,256,256]{4,3,2,1,0:T(8,128)(2,1)} %param.8) | copy-start | bytes 3145732
  26.6 8.4 %collective-permute-start.4 = (bf16[272,512]{1,0:T(8,128)(2,1)S(1)}, bf16[272,512]{1,0:T(8,128)(2,1)S(1)}, u32[]{:S(2)}, u32[]{:S(2)}) collective-permute-start(bf16[272,512]{1,0:T(8,128)(2,1)S(1)} %collective-permute-done.3), channel_id=1, source_target_pairs={{4,0},{8,4},{5,1},{9,5},{6,2},{10,6},{7,3},{11,7},{20,16},{24,20},... | collective-permute-start | bytes 835592 | tf_op jit(solution)/shard_map/ppermute | solution.py:180
  37.8 3.3 %copy-start.1 = (bf16[2,288,256]{2,1,0:T(8,128)(2,1)}, bf16[2,288,256]{2,1,0:T(8,128)(2,1)S(1)}, u32[]{:S(2)}) copy-start(bf16[2,288,256]{2,1,0:T(8,128)(2,1)S(1)} %get-tuple-element.11.refs_0_) | copy-start | bytes 884740
  37.8 3.3 %collective-permute-start.8 = (bf16[2,288,256]{2,1,0:T(8,128)(2,1)S(1)}, bf16[2,288,256]{2,1,0:T(8,128)(2,1)S(1)}, u32[]{:S(2)}, u32[]{:S(2)}) collective-permute-start(bf16[2,288,256]{2,1,0:T(8,128)(2,1)S(1)} %get-tuple-element.12), channel_id=1, source_target_pairs={{0,1},{1,0},{2,3},{3,2},{4,5},{5,4},{6,7},{7,6},{8,9},{9,8},{10,11... | collective-permute-start | bytes 884744 | tf_op jit(solution)/shard_map/ppermute | solution.py:241
  40.6 10.5 %copy-start.2 = (bf16[2,288,256]{2,1,0:T(8,128)(2,1)}, bf16[2,288,256]{2,1,0:T(8,128)(2,1)S(1)}, u32[]{:S(2)}) copy-start(bf16[2,288,256]{2,1,0:T(8,128)(2,1)S(1)} %get-tuple-element.9.r_0_) | copy-start | bytes 884740
  40.6 2.9 %collective-permute-start.6 = (bf16[2,288,256]{2,1,0:T(8,128)(2,1)S(1)}, bf16[2,288,256]{2,1,0:T(8,128)(2,1)S(1)}, u32[]{:S(2)}, u32[]{:S(2)}) collective-permute-start(bf16[2,288,256]{2,1,0:T(8,128)(2,1)S(1)} %get-tuple-element.10), channel_id=1, source_target_pairs={{0,1},{1,0},{2,3},{3,2},{4,5},{5,4},{6,7},{7,6},{8,9},{9,8},{10,11... | collective-permute-start | bytes 884744 | tf_op jit(solution)/shard_map/ppermute | solution.py:241
  41.2 7.0 %copy-start.4 = (bf16[2,288,256]{2,1,0:T(8,128)(2,1)}, bf16[2,288,256]{2,1,0:T(8,128)(2,1)S(1)}, u32[]{:S(2)}) copy-start(bf16[2,288,256]{2,1,0:T(8,128)(2,1)S(1)} %collective-permute-done.8.refs_1_) | copy-start | bytes 884740
  41.2 7.0 %collective-permute-start.9 = (bf16[288,256]{1,0:T(8,128)(2,1)S(1)}, bf16[288,256]{1,0:T(8,128)(2,1)S(1)}, u32[]{:S(2)}, u32[]{:S(2)}) collective-permute-start(bf16[288,256]{1,0:T(8,128)(2,1)S(1)} %fusion.1), channel_id=1, source_target_pairs={{0,2},{2,0},{1,3},{3,1},{4,6},{6,4},{5,7},{7,5},{8,10},{10,8},{9,1... | collective-permute-start | bytes 442376 | tf_op jit(solution)/shard_map/ppermute | solution.py:248
  43.5 7.6 %copy-start.5 = (bf16[2,288,256]{2,1,0:T(8,128)(2,1)}, bf16[2,288,256]{2,1,0:T(8,128)(2,1)S(1)}, u32[]{:S(2)}) copy-start(bf16[2,288,256]{2,1,0:T(8,128)(2,1)S(1)} %collective-permute-done.6.r_1_) | copy-start | bytes 884740
  43.5 7.6 %collective-permute-start.7 = (bf16[288,256]{1,0:T(8,128)(2,1)S(1)}, bf16[288,256]{1,0:T(8,128)(2,1)S(1)}, u32[]{:S(2)}, u32[]{:S(2)}) collective-permute-start(bf16[288,256]{1,0:T(8,128)(2,1)S(1)} %fusion), channel_id=1, source_target_pairs={{0,2},{2,0},{1,3},{3,1},{4,6},{6,4},{5,7},{7,5},{8,10},{10,8},{9,1... | collective-permute-start | bytes 442376 | tf_op jit(solution)/shard_map/ppermute | solution.py:248
  48.2 0.7 %copy-start.6 = (bf16[288,256]{1,0:T(8,128)(2,1)}, bf16[288,256]{1,0:T(8,128)(2,1)S(1)}, u32[]{:S(2)}) copy-start(bf16[288,256]{1,0:T(8,128)(2,1)S(1)} %collective-permute-done.9.refs_2_) | copy-start | bytes 442372
  51.1 0.7 %copy-start.7 = (bf16[288,256]{1,0:T(8,128)(2,1)}, bf16[288,256]{1,0:T(8,128)(2,1)S(1)}, u32[]{:S(2)}) copy-start(bf16[288,256]{1,0:T(8,128)(2,1)S(1)} %collective-permute-done.7.r_2_) | copy-start | bytes 442372

commit v9 on v7

--- a/solution.py
+++ b/solution.py
@@ -9,58 +9,53 @@
 def _near_far_kernel(
     pairs_ref, count_ref, place_ref, tiles_ref, stack_ref, masked_ref, mine_ref, theirs_ref, acc_ref
 ):
-    slot = pl.program_id(0)
-    slot_total = pl.num_programs(0)
     inner_count, width, rhs_count = acc_ref.shape
+    slot_count = tiles_ref.shape[0]
     tgt_count = masked_ref.shape[0]
     rank_size = masked_ref.shape[2]
-    half_rank = rank_size // 2
     sub_count = 2
     own_tgt = place_ref[0]
     own_sub = place_ref[1]
-
-    @pl.when(slot == 0)
-    def _():
-        acc_ref[...] = jnp.zeros_like(acc_ref)
-
-    @pl.when(slot < count_ref[0])
-    def _():
+    acc_ref[...] = jnp.zeros_like(acc_ref)
+
+    def add_slot(slot, carry):
         target = jnp.clip(pairs_ref[2 * slot], 0, inner_count - 1)
         source = jnp.clip(pairs_ref[2 * slot + 1], 0, tgt_count - 1)
         term = jnp.dot(
-            tiles_ref[...],
+            tiles_ref[slot],
             stack_ref[source - own_tgt + tgt_count - 1, :width, :],
             preferred_element_type=jnp.float32,
         )
         acc_ref[target] += term
-
-    @pl.when(slot == slot_total - 1)
+        return carry
+
+    lax.fori_loop(0, jnp.clip(count_ref[0], 0, slot_count), add_slot, 0)
+
+    coeffs = jnp.zeros((inner_count * rank_size, rhs_count), jnp.float32)
+    for source in range(tgt_count):
+        block = stack_ref[source - own_tgt + tgt_count - 1]
+        dens = block[:width, :]
+        packed = block[width:, :]
+        top = jnp.dot(packed[:, :width], dens, preferred_element_type=jnp.float32)
+        bottom = jnp.dot(packed[:, width:], dens, preferred_element_type=jnp.float32)
+        projected = jnp.concatenate([top, bottom], axis=0).astype(jnp.bfloat16)
+        coeffs += jnp.dot(masked_ref[source], projected, preferred_element_type=jnp.float32)
+    coeffs = coeffs.astype(jnp.bfloat16)
+
+    def write(first_ref, second_ref):
+        for target in range(inner_count):
+            dest = first_ref if target % sub_count == 0 else second_ref
+            row = target // sub_count
+            dest[row, :width, :] = acc_ref[target].astype(dest.dtype)
+            dest[row, width:, :] = coeffs[target * rank_size : (target + 1) * rank_size]
+
+    @pl.when(own_sub == 0)
     def _():
-        coeffs = jnp.zeros((inner_count * rank_size, rhs_count), jnp.float32)
-        for source in range(tgt_count):
-            block = stack_ref[source - own_tgt + tgt_count - 1]
-            dens = block[:width, :]
-            packed = block[width:, :]
-            top = jnp.dot(packed[:, :width], dens, preferred_element_type=jnp.float32)
-            bottom = jnp.dot(packed[:, width:], dens, preferred_element_type=jnp.float32)
-            projected = jnp.concatenate([top, bottom], axis=0).astype(jnp.bfloat16)
-            coeffs += jnp.dot(masked_ref[source], projected, preferred_element_type=jnp.float32)
-        coeffs = coeffs.astype(jnp.bfloat16)
-
-        def write(first_ref, second_ref):
-            for target in range(inner_count):
-                dest = first_ref if target % sub_count == 0 else second_ref
-                row = target // sub_count
-                dest[row, :width, :] = acc_ref[target].astype(dest.dtype)
-                dest[row, width:, :] = coeffs[target * rank_size : (target + 1) * rank_size]
-
-        @pl.when(own_sub == 0)
-        def _():
-            write(mine_ref, theirs_ref)
-
-        @pl.when(own_sub != 0)
-        def _():
-            write(theirs_ref, mine_ref)
+        write(mine_ref, theirs_ref)
+
+    @pl.when(own_sub != 0)
+    def _():
+        write(theirs_ref, mine_ref)
 
 
 def _near_far(pairs_flat, count, place, tiles, stack, masked_t, inner_count, rank_size):
@@ -68,16 +63,12 @@
     stack_count, rows, rhs_count = stack.shape
     half_count = inner_count // 2
     out_rows = width + rank_size
-
-    def tile_index(k, pairs, cnt, place):
-        return (jnp.maximum(jnp.minimum(k, cnt[0] - 1), 0), 0, 0)
-
     whole = lambda k, p, c, q: (0, 0, 0)
     grid_spec = pltpu.PrefetchScalarGridSpec(
         num_scalar_prefetch=3,
-        grid=(slot_count,),
+        grid=(1,),
         in_specs=[
-            pl.BlockSpec((None, width, width), tile_index),
+            pl.BlockSpec(tiles.shape, whole),
             pl.BlockSpec(stack.shape, whole),
             pl.BlockSpec(masked_t.shape, whole),
         ],
@@ -89,7 +80,7 @@
     )
     out = jax.ShapeDtypeStruct((half_count, out_rows, rhs_count), jnp.bfloat16)
     block_bytes = 2 * (
-        width * width * tiles.dtype.itemsize
+        tiles.size * tiles.dtype.itemsize
         + stack.size * stack.dtype.itemsize
         + masked_t.size * masked_t.dtype.itemsize
         + 2 * half_count * out_rows * rhs_count * 2

time: 53.5 us -> 53 us (level)
  no operation moved by 1% of the time
where the time goes in v9:
time: 53 us; the launch traced here: 52.8 us
  waiting for transfers between devices  26 us (49%)
  starting transfers between devices  14.6 us (28%)
  Pallas kernels  5.31 us (10%)
  other arithmetic  3.09 us (6%)
  local copies, waits for them, and re-layouts  2.83 us (5%)
  between operations  0.89 us (2%)
    ppermute x2, waiting for transfers between devices, _line_gather(): down = lax.ppermute(down, axis, down_pairs)  16.7 us
    ppermute x1, waiting for transfers between devices, _ring_reduce_scatter(): arrived = lax.ppermute(carry.astype(jnp.bfloat16), axis, ring)  7.38 us
    ppermute x2, starting transfers between devices, _line_gather(): up = lax.ppermute(up, axis, up_pairs)  5.65 us
    ppermute x1, starting transfers between devices, _line_gather(): far_up = lax.ppermute(payload, axis, [(0, n - 1)])  3.32 us
    pallas_call x1, Pallas kernels, _near_far(): pl.pallas_call(_near_far_kernel, grid_spec=grid_spec, out_shape=[out, out...  3.29 us
    ppermute x2, starting transfers between devices, _line_gather(): down = lax.ppermute(down, axis, down_pairs)  2.57 us
    pallas_call x1, Pallas kernels, _epilogue(): pl.pallas_call(_epilogue_kernel, out_shape=jax.ShapeDtypeStruct((width, t...  2.02 us
    ppermute x1, waiting for transfers between devices, on_device(): arrived = lax.ppermute(theirs, 'sub', [(0, 1), (1, 0)])  1.97 us
  transfers between devices with their start and end apart: 8, of which 4 were waited for; matrix products, arithmetic and copies ran while one was open for 6% of the time, Pallas kernels for 0%

profile of v9, /device:TPU:0, one launch (start us, length us, event | category | flops | bytes accessed | tf_op | source)
XLA Modules:
  0.0 52.8 jit_solution(294254062336446782)
XLA Ops:
  0.0 0.0 copy-start.1
  0.0 0.8 %slice_bitcast_fusion.1 = (bf16[16,256]{1,0:T(8,128)(2,1)S(1)}, bf16[16,256]{1,0:T(8,128)(2,1)S(1)}) fusion(bf16[1,32,256]{2,1,0:T(8,128)(2,1)} %basis_ref.1), kind=kLoop, calls=%fused_computation.14 | loop fusion | bytes 32768 | tf_op jit(solution)/shard_map/slice | solution.py:162
  0.8 1.0 %maximum_maximum_fusion = bf16[272,512]{1,0:T(8,128)(2,1)S(1)} fusion(bf16[16,256]{1,0:T(8,128)(2,1)S(1)} %get-tuple-element.10, bf16[16,256]{1,0:T(8,128)(2,1)S(1)} %get-tuple-element.9, bf16[256,512]{1,0:T(8,128)(2,1)} %param.6), kind=kLoop, calls=%fused_computation.4 | loop fusion | flops 835584 | bytes 557056 | tf_op jit(solution)/shard_map/concatenate | solution.py:163
  1.7 5.0 %collective-permute-start.1 = (bf16[272,512]{1,0:T(8,128)(2,1)S(1)}, bf16[272,512]{1,0:T(8,128)(2,1)S(1)}, u32[]{:S(2)}, u32[]{:S(2)}) collective-permute-start(bf16[272,512]{1,0:T(8,128)(2,1)S(1)} %maximum_maximum_fusion), channel_id=1, source_target_pairs={{0,4},{4,8},{8,12},{1,5},{5,9},{9,13},{2,6},{6,10},{10,14},{3,7},{... | collective-permute-start | bytes 835592 | tf_op jit(solution)/shard_map/ppermute | solution.py:129
  6.7 3.3 %collective-permute-start = (bf16[272,512]{1,0:T(8,128)(2,1)S(1)}, bf16[272,512]{1,0:T(8,128)(2,1)S(1)}, u32[]{:S(2)}, u32[]{:S(2)}) collective-permute-start(bf16[272,512]{1,0:T(8,128)(2,1)S(1)} %maximum_maximum_fusion), channel_id=1, source_target_pairs={{0,12},{1,13},{2,14},{3,15},{16,28},{17,29},{18,30},{19,31}} | collective-permute-start | bytes 835592 | tf_op jit(solution)/shard_map/ppermute | solution.py:122
  10.0 1.3 %collective-permute-start.3 = (bf16[272,512]{1,0:T(8,128)(2,1)S(1)}, bf16[272,512]{1,0:T(8,128)(2,1)S(1)}, u32[]{:S(2)}, u32[]{:S(2)}) collective-permute-start(bf16[272,512]{1,0:T(8,128)(2,1)S(1)} %maximum_maximum_fusion), channel_id=1, source_target_pairs={{4,0},{8,4},{12,8},{5,1},{9,5},{13,9},{6,2},{10,6},{14,10},{7,3},{... | collective-permute-start | bytes 835592 | tf_op jit(solution)/shard_map/ppermute | solution.py:130
  11.3 1.3 %collective-permute-start.5 = (bf16[272,512]{1,0:T(8,128)(2,1)S(1)}, bf16[272,512]{1,0:T(8,128)(2,1)S(1)}, u32[]{:S(2)}, u32[]{:S(2)}) collective-permute-start(bf16[272,512]{1,0:T(8,128)(2,1)S(1)} %maximum_maximum_fusion), channel_id=1, source_target_pairs={{12,0},{13,1},{14,2},{15,3},{28,16},{29,17},{30,18},{31,19}} | collective-permute-start | bytes 835592 | tf_op jit(solution)/shard_map/ppermute | solution.py:123
  13.3 0.8 %add_bitcast_fusion = s32[8]{0:T(128)S(1)} fusion(s32[8,2]{0,1:T(2,128)} %bitcast.41), kind=kLoop, calls=%fused_computation.21 | loop fusion | flops 16 | bytes 96 | tf_op jit(solution)/shard_map/eq | solution.py:171
  14.1 0.1 fusion.2
  14.2 0.1 convert_element_type.37
  14.2 0.1 copy.14
  14.4 0.9 %reshape_squeeze.11 = bf16[4,32,4,32]{3,2,1,0:T(4,128)(2,1)S(1)} reshape(bf16[1,1,128,128]{3,2,1,0:T(8,128)(2,1)} %param.11) | data formatting | bytes 65536 | tf_op jit(solution)/shard_map/reshape;squeeze | solution.py:179
  15.2 0.1 copy_multiply_fusion
  15.3 0.0 collective-permute-done.1
  15.3 0.7 %collective-permute-start.2 = (bf16[272,512]{1,0:T(8,128)(2,1)S(1)}, bf16[272,512]{1,0:T(8,128)(2,1)S(1)}, u32[]{:S(2)}, u32[]{:S(2)}) collective-permute-start(bf16[272,512]{1,0:T(8,128)(2,1)S(1)} %collective-permute-done.1), channel_id=1, source_target_pairs={{4,8},{8,12},{5,9},{9,13},{6,10},{10,14},{7,11},{11,15},{20,24},{2... | collective-permute-start | bytes 835592 | tf_op jit(solution)/shard_map/ppermute | solution.py:129
  16.0 0.1 pad_add_fusion.place_ref
  16.1 0.8 %copy.13 = s32[1,1,8,2]{3,2,1,0:T(8,128)S(1)} copy(s32[1,1,8,2]{2,3,1,0:T(2,128)} %param.9) | data formatting | bytes 128 | tf_op args[3]
  16.9 0.1 reshape_squeeze.9.pairs_ref
  16.9 0.0 copy-start
  16.9 9.7 %collective-permute-done.3 = bf16[272,512]{1,0:T(8,128)(2,1)S(1)} collective-permute-done((bf16[272,512]{1,0:T(8,128)(2,1)S(1)}, bf16[272,512]{1,0:T(8,128)(2,1)S(1)}, u32[]{:S(2)}, u32[]{:S(2)}) %collective-permute-start.3) | collective-permute-done | bytes 278560 | tf_op jit(solution)/shard_map/ppermute | solution.py:130
  26.6 1.3 %collective-permute-start.4 = (bf16[272,512]{1,0:T(8,128)(2,1)S(1)}, bf16[272,512]{1,0:T(8,128)(2,1)S(1)}, u32[]{:S(2)}, u32[]{:S(2)}) collective-permute-start(bf16[272,512]{1,0:T(8,128)(2,1)S(1)} %collective-permute-done.3), channel_id=1, source_target_pairs={{4,0},{8,4},{5,1},{9,5},{6,2},{10,6},{7,3},{11,7},{20,16},{24,20},... | collective-permute-start | bytes 835592 | tf_op jit(solution)/shard_map/ppermute | solution.py:130
  27.9 0.0 collective-permute-done
  28.0 0.0 collective-permute-done.2
  28.0 0.0 copy-done.1
  28.1 7.0 %collective-permute-done.4 = bf16[272,512]{1,0:T(8,128)(2,1)S(1)} collective-permute-done((bf16[272,512]{1,0:T(8,128)(2,1)S(1)}, bf16[272,512]{1,0:T(8,128)(2,1)S(1)}, u32[]{:S(2)}, u32[]{:S(2)}) %collective-permute-start.4) | collective-permute-done | bytes 278560 | tf_op jit(solution)/shard_map/ppermute | solution.py:130
  35.1 0.0 collective-permute-done.5
  35.1 0.0 copy-done
  35.1 3.3 %shard_map.64 = (bf16[2,288,512]{2,1,0:T(8,128)(2,1)S(1)}, bf16[2,288,512]{2,1,0:T(8,128)(2,1)S(1)}) custom-call(s32[16]{0:T(128)S(1)} %reshape_squeeze.9.pairs_ref, s32[1]{0:T(128)} %bitcast.37.count_ref, s32[2]{0:T(128)S(1)} %pad_add_fusion.place_ref, bf16[8,256,256]{2,1,0:T(8,128)(2,1)S(1)} %bitcast.39, ...), custom_call_target="tpu_custom_call" | custom-call | tf_op jit(solution)/shard_map/pallas_call | solution.py:89
  38.4 0.1 collective-permute-start.6
  38.5 2.0 %collective-permute-done.6 = bf16[2,288,512]{2,1,0:T(8,128)(2,1)S(1)} collective-permute-done((bf16[2,288,512]{2,1,0:T(8,128)(2,1)S(1)}, bf16[2,288,512]{2,1,0:T(8,128)(2,1)S(1)}, u32[]{:S(2)}, u32[]{:S(2)}) %collective-permute-start.6) | collective-permute-done | bytes 589856 | tf_op jit(solution)/shard_map/ppermute | solution.py:187
  40.5 0.2 convert_add_fusion
  40.8 1.7 %collective-permute-start.7 = (bf16[288,512]{1,0:T(8,128)(2,1)S(1)}, bf16[288,512]{1,0:T(8,128)(2,1)S(1)}, u32[]{:S(2)}, u32[]{:S(2)}) collective-permute-start(bf16[288,512]{1,0:T(8,128)(2,1)S(1)} %fusion), channel_id=1, source_target_pairs={{0,2},{2,0},{1,3},{3,1},{4,6},{6,4},{5,7},{7,5},{8,10},{10,8},{9,1... | collective-permute-start | bytes 884744 | tf_op jit(solution)/shard_map/ppermute | solution.py:147
  42.5 7.4 %collective-permute-done.7 = bf16[288,512]{1,0:T(8,128)(2,1)S(1)} collective-permute-done((bf16[288,512]{1,0:T(8,128)(2,1)S(1)}, bf16[288,512]{1,0:T(8,128)(2,1)S(1)}, u32[]{:S(2)}, u32[]{:S(2)}) %collective-permute-start.7) | collective-permute-done | bytes 294944 | tf_op jit(solution)/shard_map/ppermute | solution.py:147
  49.9 0.9 %bitcast_add_fusion.total_ref = f32[288,512]{1,0:T(8,128)} fusion(f32[2,288,512]{2,1,0:T(8,128)S(1)} %convert_add_fusion, s32[]{:T(128)S(6)} %select_n.21, bf16[288,512]{1,0:T(8,128)(2,1)S(1)} %collective-permute-done.7), kind=kLoop, calls=%fused_computation.1 | loop fusion | flops 294912 | bytes 1474564 | tf_op jit(solution)/shard_map/add | solution.py:149
  50.8 2.0 %shard_map.65 = bf16[256,512]{1,0:T(8,128)(2,1)} custom-call(f32[288,512]{1,0:T(8,128)} %bitcast_add_fusion.total_ref, bf16[1,32,256]{2,1,0:T(8,128)(2,1)} %basis_ref.1), custom_call_target="tpu_custom_call" | custom-call | tf_op jit(solution)/shard_map/pallas_call | solution.py:111
  (10 shorter events, 0.2 us)
Async XLA Ops:
  0.0 28.0 %copy-start.1 = (bf16[256,512]{1,0:T(8,128)(2,1)S(1)}, bf16[256,512]{1,0:T(8,128)(2,1)}, u32[]{:S(2)}) copy-start(bf16[256,512]{1,0:T(8,128)(2,1)} %param.6) | copy-start | bytes 786436
  1.7 13.6 %collective-permute-start.1 = (bf16[272,512]{1,0:T(8,128)(2,1)S(1)}, bf16[272,512]{1,0:T(8,128)(2,1)S(1)}, u32[]{:S(2)}, u32[]{:S(2)}) collective-permute-start(bf16[272,512]{1,0:T(8,128)(2,1)S(1)} %maximum_maximum_fusion), channel_id=1, source_target_pairs={{0,4},{4,8},{8,12},{1,5},{5,9},{9,13},{2,6},{6,10},{10,14},{3,7},{... | collective-permute-start | bytes 835592 | tf_op jit(solution)/shard_map/ppermute | solution.py:129
  6.7 21.2 %collective-permute-start = (bf16[272,512]{1,0:T(8,128)(2,1)S(1)}, bf16[272,512]{1,0:T(8,128)(2,1)S(1)}, u32[]{:S(2)}, u32[]{:S(2)}) collective-permute-start(bf16[272,512]{1,0:T(8,128)(2,1)S(1)} %maximum_maximum_fusion), channel_id=1, source_target_pairs={{0,12},{1,13},{2,14},{3,15},{16,28},{17,29},{18,30},{19,31}} | collective-permute-start | bytes 835592 | tf_op jit(solution)/shard_map/ppermute | solution.py:122
  10.0 16.6 %collective-permute-start.3 = (bf16[272,512]{1,0:T(8,128)(2,1)S(1)}, bf16[272,512]{1,0:T(8,128)(2,1)S(1)}, u32[]{:S(2)}, u32[]{:S(2)}) collective-permute-start(bf16[272,512]{1,0:T(8,128)(2,1)S(1)} %maximum_maximum_fusion), channel_id=1, source_target_pairs={{4,0},{8,4},{12,8},{5,1},{9,5},{13,9},{6,2},{10,6},{14,10},{7,3},{... | collective-permute-start | bytes 835592 | tf_op jit(solution)/shard_map/ppermute | solution.py:130
  11.3 23.8 %collective-permute-start.5 = (bf16[272,512]{1,0:T(8,128)(2,1)S(1)}, bf16[272,512]{1,0:T(8,128)(2,1)S(1)}, u32[]{:S(2)}, u32[]{:S(2)}) collective-permute-start(bf16[272,512]{1,0:T(8,128)(2,1)S(1)} %maximum_maximum_fusion), channel_id=1, source_target_pairs={{12,0},{13,1},{14,2},{15,3},{28,16},{29,17},{30,18},{31,19}} | collective-permute-start | bytes 835592 | tf_op jit(solution)/shard_map/ppermute | solution.py:123
  15.3 12.6 %collective-permute-start.2 = (bf16[272,512]{1,0:T(8,128)(2,1)S(1)}, bf16[272,512]{1,0:T(8,128)(2,1)S(1)}, u32[]{:S(2)}, u32[]{:S(2)}) collective-permute-start(bf16[272,512]{1,0:T(8,128)(2,1)S(1)} %collective-permute-done.1), channel_id=1, source_target_pairs={{4,8},{8,12},{5,9},{9,13},{6,10},{10,14},{7,11},{11,15},{20,24},{2... | collective-permute-start | bytes 835592 | tf_op jit(solution)/shard_map/ppermute | solution.py:129
  16.9 18.2 %copy-start = (bf16[1,1,8,256,256]{4,3,2,1,0:T(8,128)(2,1)S(1)}, bf16[1,1,8,256,256]{4,3,2,1,0:T(8,128)(2,1)}, u32[]{:S(2)}) copy-start(bf16[1,1,8,256,256]{4,3,2,1,0:T(8,128)(2,1)} %param.8) | copy-start | bytes 3145732
  26.6 8.4 %collective-permute-start.4 = (bf16[272,512]{1,0:T(8,128)(2,1)S(1)}, bf16[272,512]{1,0:T(8,128)(2,1)S(1)}, u32[]{:S(2)}, u32[]{:S(2)}) collective-permute-start(bf16[272,512]{1,0:T(8,128)(2,1)S(1)} %collective-permute-done.3), channel_id=1, source_target_pairs={{4,0},{8,4},{5,1},{9,5},{6,2},{10,6},{7,3},{11,7},{20,16},{24,20},... | collective-permute-start | bytes 835592 | tf_op jit(solution)/shard_map/ppermute | solution.py:130
  38.4 2.1 %collective-permute-start.6 = (bf16[2,288,512]{2,1,0:T(8,128)(2,1)S(1)}, bf16[2,288,512]{2,1,0:T(8,128)(2,1)S(1)}, u32[]{:S(2)}, u32[]{:S(2)}) collective-permute-start(bf16[2,288,512]{2,1,0:T(8,128)(2,1)S(1)} %get-tuple-element.8), channel_id=1, source_target_pairs={{0,1},{1,0},{2,3},{3,2},{4,5},{5,4},{6,7},{7,6},{8,9},{9,8},{10,11... | collective-permute-start | bytes 1769480 | tf_op jit(solution)/shard_map/ppermute | solution.py:187
  40.8 9.1 %collective-permute-start.7 = (bf16[288,512]{1,0:T(8,128)(2,1)S(1)}, bf16[288,512]{1,0:T(8,128)(2,1)S(1)}, u32[]{:S(2)}, u32[]{:S(2)}) collective-permute-start(bf16[288,512]{1,0:T(8,128)(2,1)S(1)} %fusion), channel_id=1, source_target_pairs={{0,2},{2,0},{1,3},{3,1},{4,6},{6,4},{5,7},{7,5},{8,10},{10,8},{9,1... | collective-permute-start | bytes 884744 | tf_op jit(solution)/shard_map/ppermute | solution.py:147

commit v10 on v9

--- a/solution.py
+++ b/solution.py
@@ -96,22 +96,37 @@
     )(pairs_flat, count, place, tiles, stack, masked_t)
 
 
-def _epilogue_kernel(total_ref, basis_ref, out_ref):
+def _epilogue_kernel(me_ref, basis_t_ref, *refs):
+    piece_refs, out_ref = refs[:-1], refs[-1]
     width = out_ref.shape[0]
-    near = total_ref[:width, :]
-    coeffs = total_ref[width:, :].astype(jnp.bfloat16)
-    far = lax.dot_general(
-        basis_ref[0], coeffs, (((0,), (0,)), ((), ())), preferred_element_type=jnp.float32
-    )
-    out_ref[...] = (near + far).astype(out_ref.dtype)
-
-
-def _epilogue(total, basis):
-    width = basis.shape[2]
+    total = piece_refs[0][...].astype(jnp.float32)
+    for piece_ref in piece_refs[1:]:
+        total += piece_ref[...].astype(jnp.float32)
+    coeffs = total[width:, :].astype(jnp.bfloat16)
+    far = jnp.dot(basis_t_ref[...], coeffs, preferred_element_type=jnp.float32)
+    out_ref[...] = (total[:width, :] + far).astype(out_ref.dtype)
+
+
+def _epilogue(me, pieces, basis_t):
+    width = basis_t.shape[0]
+    cols = pieces[0].shape[-1]
+    in_specs = [pl.BlockSpec(basis_t.shape, lambda i, m: (0, 0))]
+    for piece in pieces:
+        if piece.ndim == 3:
+            in_specs.append(pl.BlockSpec((None,) + piece.shape[1:], lambda i, m: (m[0], 0, 0)))
+        else:
+            in_specs.append(pl.BlockSpec(piece.shape, lambda i, m: (0, 0)))
+    grid_spec = pltpu.PrefetchScalarGridSpec(
+        num_scalar_prefetch=1,
+        grid=(1,),
+        in_specs=in_specs,
+        out_specs=pl.BlockSpec((width, cols), lambda i, m: (0, 0)),
+    )
     return pl.pallas_call(
         _epilogue_kernel,
-        out_shape=jax.ShapeDtypeStruct((width, total.shape[1]), jnp.bfloat16),
-    )(total, basis)
+        grid_spec=grid_spec,
+        out_shape=jax.ShapeDtypeStruct((width, cols), jnp.bfloat16),
+    )(me, basis_t, *pieces)
 
 
 def _line_gather(payload, axis):
@@ -185,9 +200,19 @@
         inner_count, rank_size,
     )
     arrived = lax.ppermute(theirs, "sub", [(0, 1), (1, 0)])
-    stage = mine.astype(jnp.float32) + arrived.astype(jnp.float32)
-    total = _ring_reduce_scatter(stage, "inner")
-    return _epilogue(total, cluster_basis)
+    basis_t = cluster_basis[0].T
+    me = lax.axis_index("inner")
+    if lax.axis_size("inner") == 2:
+        send = (
+            lax.dynamic_index_in_dim(mine, 1 - me, 0, False).astype(jnp.float32)
+            + lax.dynamic_index_in_dim(arrived, 1 - me, 0, False).astype(jnp.float32)
+        ).astype(jnp.bfloat16)
+        back = lax.ppermute(send, "inner", [(0, 1), (1, 0)])
+        pieces = (mine, arrived, back)
+    else:
+        stage = mine.astype(jnp.float32) + arrived.astype(jnp.float32)
+        pieces = (_ring_reduce_scatter(stage, "inner"),)
+    return _epilogue(me.astype(jnp.int32).reshape(1), pieces, basis_t)
 
 
 def solution(mesh):

time: 53 us -> 53 us (level)
  local copies, waits for them, and re-layouts: 2.83 us -> 4.22 us
  other arithmetic: 3.09 us -> 2.1 us
  starting transfers between devices: 14.6 us -> 15.4 us
  waiting for transfers between devices: 26 us -> 25.3 us
  Pallas kernels: 5.31 us -> 4.65 us
    unnamed x10 -> x19, local copies, waits for them, and re-layouts: 0.86 us -> 2.3 us
    add x2 -> x0, other arithmetic: 1.07 us -> none  [the longest x1 0.89 us: _ring_reduce_scatter(): carry = arrived.astype(jnp.float32) + own]
    ppermute x1, waiting for transfers between devices: 7.38 us -> 6.59 us  [on_device(): back = lax.ppermute(send, 'inner', [(0, 1), (1, 0)])]
    ppermute x1, starting transfers between devices: 1.73 us -> 2.51 us  [on_device(): back = lax.ppermute(send, 'inner', [(0, 1), (1, 0)])]
    pallas_call x1, Pallas kernels: 3.29 us -> 2.56 us  [_near_far(): pl.pallas_call(_near_far_kernel, grid_spec=grid_spec, out_shape=[out, out...]
  transfers between devices with their start and end apart: 8 -> 8, of which waited for: 4 -> 4; matrix products, arithmetic and copies ran while one was open for 6% -> 7% of each run, Pallas kernels for 0% -> 0%
where the time goes in v10:
time: 53 us; the launch traced here: 52.5 us
  waiting for transfers between devices  25.3 us (48%)
  starting transfers between devices  15.4 us (29%)
  Pallas kernels  4.65 us (9%)
  local copies, waits for them, and re-layouts  4.22 us (8%)
  other arithmetic  2.1 us (4%)
  between operations  0.87 us (2%)
    ppermute x2, waiting for transfers between devices, _line_gather(): down = lax.ppermute(down, axis, down_pairs)  16.7 us
    ppermute x1, waiting for transfers between devices, on_device(): back = lax.ppermute(send, 'inner', [(0, 1), (1, 0)])  6.59 us
    ppermute x2, starting transfers between devices, _line_gather(): up = lax.ppermute(up, axis, up_pairs)  5.65 us
    ppermute x1, starting transfers between devices, _line_gather(): far_up = lax.ppermute(payload, axis, [(0, n - 1)])  3.32 us
    ppermute x2, starting transfers between devices, _line_gather(): down = lax.ppermute(down, axis, down_pairs)  2.57 us
    pallas_call x1, Pallas kernels, _near_far(): pl.pallas_call(_near_far_kernel, grid_spec=grid_spec, out_shape=[out, out...  2.56 us
    ppermute x1, starting transfers between devices, on_device(): back = lax.ppermute(send, 'inner', [(0, 1), (1, 0)])  2.51 us
    unnamed x19, local copies, waits for them, and re-layouts  2.3 us
  transfers between devices with their start and end apart: 8, of which 4 were waited for; matrix products, arithmetic and copies ran while one was open for 7% of the time, Pallas kernels for 0%

profile of v10, /device:TPU:0, one launch (start us, length us, event | category | flops | bytes accessed | tf_op | source)
XLA Modules:
  0.0 52.5 jit_solution(18171231345828699545)
XLA Ops:
  0.0 0.0 copy-start.3
  0.0 0.8 %slice_bitcast_fusion.1 = (bf16[16,256]{1,0:T(8,128)(2,1)S(1)}, bf16[16,256]{1,0:T(8,128)(2,1)S(1)}) fusion(bf16[1,32,256]{2,1,0:T(8,128)(2,1)} %param.7), kind=kLoop, calls=%fused_computation.12 | loop fusion | bytes 32768 | tf_op jit(solution)/shard_map/slice | solution.py:177
  0.8 1.0 %maximum_maximum_fusion = bf16[272,512]{1,0:T(8,128)(2,1)S(1)} fusion(bf16[16,256]{1,0:T(8,128)(2,1)S(1)} %get-tuple-element.10, bf16[16,256]{1,0:T(8,128)(2,1)S(1)} %get-tuple-element.9, bf16[256,512]{1,0:T(8,128)(2,1)} %param.6), kind=kLoop, calls=%fused_computation.2 | loop fusion | flops 835584 | bytes 557056 | tf_op jit(solution)/shard_map/concatenate | solution.py:178
  1.7 5.0 %collective-permute-start.1 = (bf16[272,512]{1,0:T(8,128)(2,1)S(1)}, bf16[272,512]{1,0:T(8,128)(2,1)S(1)}, u32[]{:S(2)}, u32[]{:S(2)}) collective-permute-start(bf16[272,512]{1,0:T(8,128)(2,1)S(1)} %maximum_maximum_fusion), channel_id=1, source_target_pairs={{0,4},{4,8},{8,12},{1,5},{5,9},{9,13},{2,6},{6,10},{10,14},{3,7},{... | collective-permute-start | bytes 835592 | tf_op jit(solution)/shard_map/ppermute | solution.py:144
  6.7 3.3 %collective-permute-start = (bf16[272,512]{1,0:T(8,128)(2,1)S(1)}, bf16[272,512]{1,0:T(8,128)(2,1)S(1)}, u32[]{:S(2)}, u32[]{:S(2)}) collective-permute-start(bf16[272,512]{1,0:T(8,128)(2,1)S(1)} %maximum_maximum_fusion), channel_id=1, source_target_pairs={{0,12},{1,13},{2,14},{3,15},{16,28},{17,29},{18,30},{19,31}} | collective-permute-start | bytes 835592 | tf_op jit(solution)/shard_map/ppermute | solution.py:137
  10.0 1.3 %collective-permute-start.3 = (bf16[272,512]{1,0:T(8,128)(2,1)S(1)}, bf16[272,512]{1,0:T(8,128)(2,1)S(1)}, u32[]{:S(2)}, u32[]{:S(2)}) collective-permute-start(bf16[272,512]{1,0:T(8,128)(2,1)S(1)} %maximum_maximum_fusion), channel_id=1, source_target_pairs={{4,0},{8,4},{12,8},{5,1},{9,5},{13,9},{6,2},{10,6},{14,10},{7,3},{... | collective-permute-start | bytes 835592 | tf_op jit(solution)/shard_map/ppermute | solution.py:145
  11.3 1.3 %collective-permute-start.5 = (bf16[272,512]{1,0:T(8,128)(2,1)S(1)}, bf16[272,512]{1,0:T(8,128)(2,1)S(1)}, u32[]{:S(2)}, u32[]{:S(2)}) collective-permute-start(bf16[272,512]{1,0:T(8,128)(2,1)S(1)} %maximum_maximum_fusion), channel_id=1, source_target_pairs={{12,0},{13,1},{14,2},{15,3},{28,16},{29,17},{30,18},{31,19}} | collective-permute-start | bytes 835592 | tf_op jit(solution)/shard_map/ppermute | solution.py:138
  13.3 0.8 %add_bitcast_fusion = s32[8]{0:T(128)S(1)} fusion(s32[8,2]{0,1:T(2,128)} %bitcast.44), kind=kLoop, calls=%fused_computation.19 | loop fusion | flops 16 | bytes 96 | tf_op jit(solution)/shard_map/eq | solution.py:186
  14.1 0.1 fusion.2
  14.2 0.1 convert_element_type.36
  14.2 0.1 copy.17
  14.4 0.9 %reshape_squeeze.11 = bf16[4,32,4,32]{3,2,1,0:T(4,128)(2,1)S(1)} reshape(bf16[1,1,128,128]{3,2,1,0:T(8,128)(2,1)} %param.11) | data formatting | bytes 65536 | tf_op jit(solution)/shard_map/reshape;squeeze | solution.py:194
  15.2 0.1 copy_multiply_fusion
  15.3 0.0 collective-permute-done.1
  15.3 0.7 %collective-permute-start.2 = (bf16[272,512]{1,0:T(8,128)(2,1)S(1)}, bf16[272,512]{1,0:T(8,128)(2,1)S(1)}, u32[]{:S(2)}, u32[]{:S(2)}) collective-permute-start(bf16[272,512]{1,0:T(8,128)(2,1)S(1)} %collective-permute-done.1), channel_id=1, source_target_pairs={{4,8},{8,12},{5,9},{9,13},{6,10},{10,14},{7,11},{11,15},{20,24},{2... | collective-permute-start | bytes 835592 | tf_op jit(solution)/shard_map/ppermute | solution.py:144
  16.0 0.1 pad_add_fusion.place_ref
  16.1 0.8 %copy.16 = s32[1,1,8,2]{3,2,1,0:T(8,128)S(1)} copy(s32[1,1,8,2]{2,3,1,0:T(2,128)} %param.9) | data formatting | bytes 128 | tf_op args[3]
  16.9 0.1 reshape_squeeze.9.pairs_ref
  16.9 0.0 copy-start.1
  16.9 9.7 %collective-permute-done.3 = bf16[272,512]{1,0:T(8,128)(2,1)S(1)} collective-permute-done((bf16[272,512]{1,0:T(8,128)(2,1)S(1)}, bf16[272,512]{1,0:T(8,128)(2,1)S(1)}, u32[]{:S(2)}, u32[]{:S(2)}) %collective-permute-start.3) | collective-permute-done | bytes 278560 | tf_op jit(solution)/shard_map/ppermute | solution.py:145
  26.6 1.3 %collective-permute-start.4 = (bf16[272,512]{1,0:T(8,128)(2,1)S(1)}, bf16[272,512]{1,0:T(8,128)(2,1)S(1)}, u32[]{:S(2)}, u32[]{:S(2)}) collective-permute-start(bf16[272,512]{1,0:T(8,128)(2,1)S(1)} %collective-permute-done.3), channel_id=1, source_target_pairs={{4,0},{8,4},{5,1},{9,5},{6,2},{10,6},{7,3},{11,7},{20,16},{24,20},... | collective-permute-start | bytes 835592 | tf_op jit(solution)/shard_map/ppermute | solution.py:145
  27.9 0.0 collective-permute-done
  28.0 0.0 collective-permute-done.2
  28.0 0.0 copy-done.3
  28.1 7.0 %collective-permute-done.4 = bf16[272,512]{1,0:T(8,128)(2,1)S(1)} collective-permute-done((bf16[272,512]{1,0:T(8,128)(2,1)S(1)}, bf16[272,512]{1,0:T(8,128)(2,1)S(1)}, u32[]{:S(2)}, u32[]{:S(2)}) %collective-permute-start.4) | collective-permute-done | bytes 278560 | tf_op jit(solution)/shard_map/ppermute | solution.py:145
  35.1 0.0 collective-permute-done.5
  35.1 0.0 copy-done.1
  35.1 0.0 copy-start.5
  35.2 2.6 %shard_map.64 = (bf16[2,288,512]{2,1,0:T(8,128)(2,1)S(1)}, bf16[2,288,512]{2,1,0:T(8,128)(2,1)S(1)}) custom-call(s32[16]{0:T(128)S(1)} %reshape_squeeze.9.pairs_ref, s32[1]{0:T(128)} %bitcast.39.count_ref, s32[2]{0:T(128)S(1)} %pad_add_fusion.place_ref, bf16[8,256,256]{2,1,0:T(8,128)(2,1)S(1)} %bitcast.41, ...), custom_call_target="tpu_custom_call" | custom-call | tf_op jit(solution)/shard_map/pallas_call | solution.py:89
  37.7 0.0 copy-start
  37.7 0.1 collective-permute-start.6
  37.8 2.0 %collective-permute-done.6.refs_1_ = bf16[2,288,512]{2,1,0:T(8,128)(2,1)S(1)} collective-permute-done((bf16[2,288,512]{2,1,0:T(8,128)(2,1)S(1)}, bf16[2,288,512]{2,1,0:T(8,128)(2,1)S(1)}, u32[]{:S(2)}, u32[]{:S(2)}) %collective-permute-start.6) | collective-permute-done | bytes 589856 | tf_op jit(solution)/shard_map/ppermute | solution.py:202
  39.8 0.0 copy-start.2
  39.8 0.1 fusion
  39.9 2.5 %collective-permute-start.7 = (bf16[288,512]{1,0:T(8,128)(2,1)S(1)}, bf16[288,512]{1,0:T(8,128)(2,1)S(1)}, u32[]{:S(2)}, u32[]{:S(2)}) collective-permute-start(bf16[288,512]{1,0:T(8,128)(2,1)S(1)} %fusion), channel_id=1, source_target_pairs={{0,2},{2,0},{1,3},{3,1},{4,6},{6,4},{5,7},{7,5},{8,10},{10,8},{9,1... | collective-permute-start | bytes 884744 | tf_op jit(solution)/shard_map/ppermute | solution.py:210
  42.4 0.0 copy-done.5
  42.4 0.7 %copy.15 = bf16[1,32,256]{1,2,0:T(8,128)(2,1)} copy(bf16[1,32,256]{2,1,0:T(8,128)(2,1)S(1)} %copy-done.5) | data formatting | bytes 32768 | tf_op args[1]
  43.1 6.6 %collective-permute-done.7.refs_2_ = bf16[288,512]{1,0:T(8,128)(2,1)S(1)} collective-permute-done((bf16[288,512]{1,0:T(8,128)(2,1)S(1)}, bf16[288,512]{1,0:T(8,128)(2,1)S(1)}, u32[]{:S(2)}, u32[]{:S(2)}) %collective-permute-start.7) | collective-permute-done | bytes 294944 | tf_op jit(solution)/shard_map/ppermute | solution.py:210
  49.7 0.0 copy-start.4
  49.7 0.0 copy-done
  49.7 0.0 copy-done.2
  49.7 0.7 %copy-done.4 = bf16[288,512]{1,0:T(8,128)(2,1)} copy-done((bf16[288,512]{1,0:T(8,128)(2,1)}, bf16[288,512]{1,0:T(8,128)(2,1)S(1)}, u32[]{:S(2)}) %copy-start.4) | copy-done | bytes 294936
  50.4 2.1 %shard_map.65 = bf16[256,512]{1,0:T(8,128)(2,1)} custom-call(s32[1]{0:T(128)} %bitcast.me_ref, bf16[256,32]{1,0:T(8,128)(2,1)} %bitcast.43, bf16[2,288,512]{2,1,0:T(8,128)(2,1)} %copy-done, bf16[2,288,512]{2,1,0:T(8,128)(2,1)} %copy-done.2, bf16[288,512]{1,0:T(8,128)(2,1)} %copy-done.4), custom_call_target="tpu_custom_call" | custom-call | tf_op jit(solution)/shard_map/pallas_call | solution.py:125
  (9 shorter events, 0.2 us)
Async XLA Ops:
  0.0 28.0 %copy-start.3 = (bf16[256,512]{1,0:T(8,128)(2,1)S(1)}, bf16[256,512]{1,0:T(8,128)(2,1)}, u32[]{:S(2)}) copy-start(bf16[256,512]{1,0:T(8,128)(2,1)} %param.6) | copy-start | bytes 786436
  1.7 13.6 %collective-permute-start.1 = (bf16[272,512]{1,0:T(8,128)(2,1)S(1)}, bf16[272,512]{1,0:T(8,128)(2,1)S(1)}, u32[]{:S(2)}, u32[]{:S(2)}) collective-permute-start(bf16[272,512]{1,0:T(8,128)(2,1)S(1)} %maximum_maximum_fusion), channel_id=1, source_target_pairs={{0,4},{4,8},{8,12},{1,5},{5,9},{9,13},{2,6},{6,10},{10,14},{3,7},{... | collective-permute-start | bytes 835592 | tf_op jit(solution)/shard_map/ppermute | solution.py:144
  6.7 21.2 %collective-permute-start = (bf16[272,512]{1,0:T(8,128)(2,1)S(1)}, bf16[272,512]{1,0:T(8,128)(2,1)S(1)}, u32[]{:S(2)}, u32[]{:S(2)}) collective-permute-start(bf16[272,512]{1,0:T(8,128)(2,1)S(1)} %maximum_maximum_fusion), channel_id=1, source_target_pairs={{0,12},{1,13},{2,14},{3,15},{16,28},{17,29},{18,30},{19,31}} | collective-permute-start | bytes 835592 | tf_op jit(solution)/shard_map/ppermute | solution.py:137
  10.0 16.6 %collective-permute-start.3 = (bf16[272,512]{1,0:T(8,128)(2,1)S(1)}, bf16[272,512]{1,0:T(8,128)(2,1)S(1)}, u32[]{:S(2)}, u32[]{:S(2)}) collective-permute-start(bf16[272,512]{1,0:T(8,128)(2,1)S(1)} %maximum_maximum_fusion), channel_id=1, source_target_pairs={{4,0},{8,4},{12,8},{5,1},{9,5},{13,9},{6,2},{10,6},{14,10},{7,3},{... | collective-permute-start | bytes 835592 | tf_op jit(solution)/shard_map/ppermute | solution.py:145
  11.3 23.8 %collective-permute-start.5 = (bf16[272,512]{1,0:T(8,128)(2,1)S(1)}, bf16[272,512]{1,0:T(8,128)(2,1)S(1)}, u32[]{:S(2)}, u32[]{:S(2)}) collective-permute-start(bf16[272,512]{1,0:T(8,128)(2,1)S(1)} %maximum_maximum_fusion), channel_id=1, source_target_pairs={{12,0},{13,1},{14,2},{15,3},{28,16},{29,17},{30,18},{31,19}} | collective-permute-start | bytes 835592 | tf_op jit(solution)/shard_map/ppermute | solution.py:138
  15.3 12.6 %collective-permute-start.2 = (bf16[272,512]{1,0:T(8,128)(2,1)S(1)}, bf16[272,512]{1,0:T(8,128)(2,1)S(1)}, u32[]{:S(2)}, u32[]{:S(2)}) collective-permute-start(bf16[272,512]{1,0:T(8,128)(2,1)S(1)} %collective-permute-done.1), channel_id=1, source_target_pairs={{4,8},{8,12},{5,9},{9,13},{6,10},{10,14},{7,11},{11,15},{20,24},{2... | collective-permute-start | bytes 835592 | tf_op jit(solution)/shard_map/ppermute | solution.py:144
  16.9 18.2 %copy-start.1 = (bf16[1,1,8,256,256]{4,3,2,1,0:T(8,128)(2,1)S(1)}, bf16[1,1,8,256,256]{4,3,2,1,0:T(8,128)(2,1)}, u32[]{:S(2)}) copy-start(bf16[1,1,8,256,256]{4,3,2,1,0:T(8,128)(2,1)} %param.8) | copy-start | bytes 3145732
  26.6 8.4 %collective-permute-start.4 = (bf16[272,512]{1,0:T(8,128)(2,1)S(1)}, bf16[272,512]{1,0:T(8,128)(2,1)S(1)}, u32[]{:S(2)}, u32[]{:S(2)}) collective-permute-start(bf16[272,512]{1,0:T(8,128)(2,1)S(1)} %collective-permute-done.3), channel_id=1, source_target_pairs={{4,0},{8,4},{5,1},{9,5},{6,2},{10,6},{7,3},{11,7},{20,16},{24,20},... | collective-permute-start | bytes 835592 | tf_op jit(solution)/shard_map/ppermute | solution.py:145
  35.1 7.3 %copy-start.5 = (bf16[1,32,256]{2,1,0:T(8,128)(2,1)S(1)}, bf16[1,32,256]{2,1,0:T(8,128)(2,1)}, u32[]{:S(2)}) copy-start(bf16[1,32,256]{2,1,0:T(8,128)(2,1)} %param.7) | copy-start | bytes 49156
  37.7 12.0 %copy-start = (bf16[2,288,512]{2,1,0:T(8,128)(2,1)}, bf16[2,288,512]{2,1,0:T(8,128)(2,1)S(1)}, u32[]{:S(2)}) copy-start(bf16[2,288,512]{2,1,0:T(8,128)(2,1)S(1)} %get-tuple-element.7.refs_0_) | copy-start | bytes 1769476
  37.7 2.1 %collective-permute-start.6 = (bf16[2,288,512]{2,1,0:T(8,128)(2,1)S(1)}, bf16[2,288,512]{2,1,0:T(8,128)(2,1)S(1)}, u32[]{:S(2)}, u32[]{:S(2)}) collective-permute-start(bf16[2,288,512]{2,1,0:T(8,128)(2,1)S(1)} %get-tuple-element.8), channel_id=1, source_target_pairs={{0,1},{1,0},{2,3},{3,2},{4,5},{5,4},{6,7},{7,6},{8,9},{9,8},{10,11... | collective-permute-start | bytes 1769480 | tf_op jit(solution)/shard_map/ppermute | solution.py:202
  39.8 9.9 %copy-start.2 = (bf16[2,288,512]{2,1,0:T(8,128)(2,1)}, bf16[2,288,512]{2,1,0:T(8,128)(2,1)S(1)}, u32[]{:S(2)}) copy-start(bf16[2,288,512]{2,1,0:T(8,128)(2,1)S(1)} %collective-permute-done.6.refs_1_) | copy-start | bytes 1769476
  39.9 9.8 %collective-permute-start.7 = (bf16[288,512]{1,0:T(8,128)(2,1)S(1)}, bf16[288,512]{1,0:T(8,128)(2,1)S(1)}, u32[]{:S(2)}, u32[]{:S(2)}) collective-permute-start(bf16[288,512]{1,0:T(8,128)(2,1)S(1)} %fusion), channel_id=1, source_target_pairs={{0,2},{2,0},{1,3},{3,1},{4,6},{6,4},{5,7},{7,5},{8,10},{10,8},{9,1... | collective-permute-start | bytes 884744 | tf_op jit(solution)/shard_map/ppermute | solution.py:210
  49.7 0.7 %copy-start.4 = (bf16[288,512]{1,0:T(8,128)(2,1)}, bf16[288,512]{1,0:T(8,128)(2,1)S(1)}, u32[]{:S(2)}) copy-start(bf16[288,512]{1,0:T(8,128)(2,1)S(1)} %collective-permute-done.7.refs_2_) | copy-start | bytes 884740

commit v11 on v10

--- a/solution.py
+++ b/solution.py
@@ -212,7 +212,15 @@
     else:
         stage = mine.astype(jnp.float32) + arrived.astype(jnp.float32)
         pieces = (_ring_reduce_scatter(stage, "inner"),)
-    return _epilogue(me.astype(jnp.int32).reshape(1), pieces, basis_t)
+    width = basis_t.shape[0]
+    total = None
+    for piece in pieces:
+        if piece.ndim == 3:
+            piece = lax.dynamic_index_in_dim(piece, me, 0, False)
+        piece = piece.astype(jnp.float32)
+        total = piece if total is None else total + piece
+    far = jnp.dot(basis_t, total[width:].astype(jnp.bfloat16), preferred_element_type=jnp.float32)
+    return (total[:width] + far).astype(jnp.bfloat16)
 
 
 def solution(mesh):

time: 53 us -> 50.9 us (0.960)
  Pallas kernels: 4.65 us -> 2.82 us
  local copies, waits for them, and re-layouts: 4.22 us -> 2.79 us
  starting transfers between devices: 15.4 us -> 14.2 us
  waiting for transfers between devices: 25.3 us -> 26.5 us
  matrix products: 0 us -> 0.97 us
    pallas_call x1 -> x0, Pallas kernels: 2.09 us -> none  [_epilogue(): pl.pallas_call(_epilogue_kernel, grid_spec=grid_spec, out_shape=jax.Shape...]
    unnamed x19 -> x12, local copies, waits for them, and re-layouts: 2.3 us -> 0.87 us
    ppermute x1, waiting for transfers between devices: 6.59 us -> 7.82 us  [on_device(): back = lax.ppermute(send, 'inner', [(0, 1), (1, 0)])]
    ppermute x1, starting transfers between devices: 2.51 us -> 1.29 us  [on_device(): back = lax.ppermute(send, 'inner', [(0, 1), (1, 0)])]
    dot_general x0 -> x1, matrix products: none -> 0.97 us  [on_device(): jnp.dot(basis_t, total[width:].astype(jnp.bfloat16), preferred_element_ty...]
  transfers between devices with their start and end apart: 8 -> 8, of which waited for: 4 -> 4; matrix products, arithmetic and copies ran while one was open for 7% -> 6% of each run, Pallas kernels for 0% -> 0%
where the time goes in v11:
time: 50.9 us; the launch traced here: 50.4 us
  waiting for transfers between devices  26.5 us (52%)
  starting transfers between devices  14.2 us (28%)
  Pallas kernels  2.82 us (6%)
  local copies, waits for them, and re-layouts  2.79 us (5%)
  other arithmetic  2.21 us (4%)
  matrix products  0.97 us (2%)
  between operations  0.88 us (2%)
    ppermute x2, waiting for transfers between devices, _line_gather(): down = lax.ppermute(down, axis, down_pairs)  16.7 us
    ppermute x1, waiting for transfers between devices, on_device(): back = lax.ppermute(send, 'inner', [(0, 1), (1, 0)])  7.82 us
    ppermute x2, starting transfers between devices, _line_gather(): up = lax.ppermute(up, axis, up_pairs)  5.65 us
    ppermute x1, starting transfers between devices, _line_gather(): far_up = lax.ppermute(payload, axis, [(0, n - 1)])  3.32 us
    pallas_call x1, Pallas kernels, _near_far(): pl.pallas_call(_near_far_kernel, grid_spec=grid_spec, out_shape=[out, out...  2.82 us
    ppermute x2, starting transfers between devices, _line_gather(): down = lax.ppermute(down, axis, down_pairs)  2.57 us
    ppermute x1, waiting for transfers between devices, on_device(): arrived = lax.ppermute(theirs, 'sub', [(0, 1), (1, 0)])  1.99 us
    ppermute x1, starting transfers between devices, on_device(): back = lax.ppermute(send, 'inner', [(0, 1), (1, 0)])  1.29 us
  transfers between devices with their start and end apart: 8, of which 4 were waited for; matrix products, arithmetic and copies ran while one was open for 6% of the time, Pallas kernels for 0%

profile of v11, /device:TPU:0, one launch (start us, length us, event | category | flops | bytes accessed | tf_op | source)
XLA Modules:
  0.0 50.4 jit_solution(12476223422027635394)
XLA Ops:
  0.0 0.0 copy-start.1
  0.0 0.8 %slice_bitcast_fusion.1 = (bf16[16,256]{1,0:T(8,128)(2,1)S(1)}, bf16[16,256]{1,0:T(8,128)(2,1)S(1)}) fusion(bf16[1,32,256]{2,1,0:T(8,128)(2,1)} %param.7), kind=kLoop, calls=%fused_computation.18 | loop fusion | bytes 32768 | tf_op jit(solution)/shard_map/slice | solution.py:177
  0.8 1.0 %maximum_maximum_fusion = bf16[272,512]{1,0:T(8,128)(2,1)S(1)} fusion(bf16[16,256]{1,0:T(8,128)(2,1)S(1)} %get-tuple-element.10, bf16[16,256]{1,0:T(8,128)(2,1)S(1)} %get-tuple-element.9, bf16[256,512]{1,0:T(8,128)(2,1)} %param.6), kind=kLoop, calls=%fused_computation.6 | loop fusion | flops 835584 | bytes 557056 | tf_op jit(solution)/shard_map/concatenate | solution.py:178
  1.7 5.0 %collective-permute-start.1 = (bf16[272,512]{1,0:T(8,128)(2,1)S(1)}, bf16[272,512]{1,0:T(8,128)(2,1)S(1)}, u32[]{:S(2)}, u32[]{:S(2)}) collective-permute-start(bf16[272,512]{1,0:T(8,128)(2,1)S(1)} %maximum_maximum_fusion), channel_id=1, source_target_pairs={{0,4},{4,8},{8,12},{1,5},{5,9},{9,13},{2,6},{6,10},{10,14},{3,7},{... | collective-permute-start | bytes 835592 | tf_op jit(solution)/shard_map/ppermute | solution.py:144
  6.7 3.3 %collective-permute-start = (bf16[272,512]{1,0:T(8,128)(2,1)S(1)}, bf16[272,512]{1,0:T(8,128)(2,1)S(1)}, u32[]{:S(2)}, u32[]{:S(2)}) collective-permute-start(bf16[272,512]{1,0:T(8,128)(2,1)S(1)} %maximum_maximum_fusion), channel_id=1, source_target_pairs={{0,12},{1,13},{2,14},{3,15},{16,28},{17,29},{18,30},{19,31}} | collective-permute-start | bytes 835592 | tf_op jit(solution)/shard_map/ppermute | solution.py:137
  10.0 1.3 %collective-permute-start.3 = (bf16[272,512]{1,0:T(8,128)(2,1)S(1)}, bf16[272,512]{1,0:T(8,128)(2,1)S(1)}, u32[]{:S(2)}, u32[]{:S(2)}) collective-permute-start(bf16[272,512]{1,0:T(8,128)(2,1)S(1)} %maximum_maximum_fusion), channel_id=1, source_target_pairs={{4,0},{8,4},{12,8},{5,1},{9,5},{13,9},{6,2},{10,6},{14,10},{7,3},{... | collective-permute-start | bytes 835592 | tf_op jit(solution)/shard_map/ppermute | solution.py:145
  11.3 1.3 %collective-permute-start.5 = (bf16[272,512]{1,0:T(8,128)(2,1)S(1)}, bf16[272,512]{1,0:T(8,128)(2,1)S(1)}, u32[]{:S(2)}, u32[]{:S(2)}) collective-permute-start(bf16[272,512]{1,0:T(8,128)(2,1)S(1)} %maximum_maximum_fusion), channel_id=1, source_target_pairs={{12,0},{13,1},{14,2},{15,3},{28,16},{29,17},{30,18},{31,19}} | collective-permute-start | bytes 835592 | tf_op jit(solution)/shard_map/ppermute | solution.py:138
  13.3 0.8 %add_bitcast_fusion = s32[8]{0:T(128)S(1)} fusion(s32[8,2]{0,1:T(2,128)} %bitcast.48), kind=kLoop, calls=%fused_computation.25 | loop fusion | flops 16 | bytes 96 | tf_op jit(solution)/shard_map/eq | solution.py:186
  14.1 0.1 fusion.4
  14.2 0.1 convert_element_type.51
  14.2 0.1 copy.16
  14.4 0.9 %reshape_squeeze.11 = bf16[4,32,4,32]{3,2,1,0:T(4,128)(2,1)S(1)} reshape(bf16[1,1,128,128]{3,2,1,0:T(8,128)(2,1)} %param.11) | data formatting | bytes 65536 | tf_op jit(solution)/shard_map/reshape;squeeze | solution.py:194
  15.2 0.1 copy_multiply_fusion
  15.3 0.0 collective-permute-done.1
  15.3 0.7 %collective-permute-start.2 = (bf16[272,512]{1,0:T(8,128)(2,1)S(1)}, bf16[272,512]{1,0:T(8,128)(2,1)S(1)}, u32[]{:S(2)}, u32[]{:S(2)}) collective-permute-start(bf16[272,512]{1,0:T(8,128)(2,1)S(1)} %collective-permute-done.1), channel_id=1, source_target_pairs={{4,8},{8,12},{5,9},{9,13},{6,10},{10,14},{7,11},{11,15},{20,24},{2... | collective-permute-start | bytes 835592 | tf_op jit(solution)/shard_map/ppermute | solution.py:144
  16.0 0.1 pad_add_fusion.place_ref
  16.1 0.8 %copy.15 = s32[1,1,8,2]{3,2,1,0:T(8,128)S(1)} copy(s32[1,1,8,2]{2,3,1,0:T(2,128)} %param.9) | data formatting | bytes 128 | tf_op args[3]
  16.9 0.1 reshape_squeeze.9.pairs_ref
  16.9 0.0 copy-start
  16.9 9.7 %collective-permute-done.3 = bf16[272,512]{1,0:T(8,128)(2,1)S(1)} collective-permute-done((bf16[272,512]{1,0:T(8,128)(2,1)S(1)}, bf16[272,512]{1,0:T(8,128)(2,1)S(1)}, u32[]{:S(2)}, u32[]{:S(2)}) %collective-permute-start.3) | collective-permute-done | bytes 278560 | tf_op jit(solution)/shard_map/ppermute | solution.py:145
  26.6 1.3 %collective-permute-start.4 = (bf16[272,512]{1,0:T(8,128)(2,1)S(1)}, bf16[272,512]{1,0:T(8,128)(2,1)S(1)}, u32[]{:S(2)}, u32[]{:S(2)}) collective-permute-start(bf16[272,512]{1,0:T(8,128)(2,1)S(1)} %collective-permute-done.3), channel_id=1, source_target_pairs={{4,0},{8,4},{5,1},{9,5},{6,2},{10,6},{7,3},{11,7},{20,16},{24,20},... | collective-permute-start | bytes 835592 | tf_op jit(solution)/shard_map/ppermute | solution.py:145
  27.9 0.0 collective-permute-done
  28.0 0.0 collective-permute-done.2
  28.0 0.0 copy-done.1
  28.1 7.0 %collective-permute-done.4 = bf16[272,512]{1,0:T(8,128)(2,1)S(1)} collective-permute-done((bf16[272,512]{1,0:T(8,128)(2,1)S(1)}, bf16[272,512]{1,0:T(8,128)(2,1)S(1)}, u32[]{:S(2)}, u32[]{:S(2)}) %collective-permute-start.4) | collective-permute-done | bytes 278560 | tf_op jit(solution)/shard_map/ppermute | solution.py:145
  35.1 0.0 collective-permute-done.5
  35.1 0.0 copy-done
  35.1 2.8 %shard_map.64 = (bf16[2,288,512]{2,1,0:T(8,128)(2,1)S(1)}, bf16[2,288,512]{2,1,0:T(8,128)(2,1)S(1)}) custom-call(s32[16]{0:T(128)S(1)} %reshape_squeeze.9.pairs_ref, s32[1]{0:T(128)} %bitcast.44.count_ref, s32[2]{0:T(128)S(1)} %pad_add_fusion.place_ref, bf16[8,256,256]{2,1,0:T(8,128)(2,1)S(1)} %bitcast.46, ...), custom_call_target="tpu_custom_call" | custom-call | tf_op jit(solution)/shard_map/pallas_call | solution.py:89
  38.0 0.0 copy-start.2
  38.0 0.1 collective-permute-start.6
  38.1 2.0 %collective-permute-done.6 = bf16[2,288,512]{2,1,0:T(8,128)(2,1)S(1)} collective-permute-done((bf16[2,288,512]{2,1,0:T(8,128)(2,1)S(1)}, bf16[2,288,512]{2,1,0:T(8,128)(2,1)S(1)}, u32[]{:S(2)}, u32[]{:S(2)}) %collective-permute-start.6) | collective-permute-done | bytes 589856 | tf_op jit(solution)/shard_map/ppermute | solution.py:202
  40.1 0.1 fusion.1
  40.1 1.3 %collective-permute-start.7 = (bf16[288,512]{1,0:T(8,128)(2,1)S(1)}, bf16[288,512]{1,0:T(8,128)(2,1)S(1)}, u32[]{:S(2)}, u32[]{:S(2)}) collective-permute-start(bf16[288,512]{1,0:T(8,128)(2,1)S(1)} %fusion.1), channel_id=1, source_target_pairs={{0,2},{2,0},{1,3},{3,1},{4,6},{6,4},{5,7},{7,5},{8,10},{10,8},{9,1... | collective-permute-start | bytes 884744 | tf_op jit(solution)/shard_map/ppermute | solution.py:210
  41.4 7.8 %collective-permute-done.7 = bf16[288,512]{1,0:T(8,128)(2,1)S(1)} collective-permute-done((bf16[288,512]{1,0:T(8,128)(2,1)S(1)}, bf16[288,512]{1,0:T(8,128)(2,1)S(1)}, u32[]{:S(2)}, u32[]{:S(2)}) %collective-permute-start.7) | collective-permute-done | bytes 294944 | tf_op jit(solution)/shard_map/ppermute | solution.py:210
  49.3 0.1 bitcast_add_fusion
  49.4 0.0 copy-done.2
  49.4 1.0 %fusion = bf16[256,512]{1,0:T(8,128)(2,1)} fusion(f32[288,512]{1,0:T(8,128)S(1)} %bitcast_add_fusion, bf16[1,32,256]{2,1,0:T(8,128)(2,1)S(1)} %copy-done.2), kind=kOutput, calls=%fused_computation.4 | convolution fusion | flops 8667136 | bytes 868352 | tf_op jit(solution)/shard_map/dot_general | solution.py:222
  (9 shorter events, 0.2 us)
Async XLA Ops:
  0.0 28.0 %copy-start.1 = (bf16[256,512]{1,0:T(8,128)(2,1)S(1)}, bf16[256,512]{1,0:T(8,128)(2,1)}, u32[]{:S(2)}) copy-start(bf16[256,512]{1,0:T(8,128)(2,1)} %param.6) | copy-start | bytes 786436
  1.7 13.6 %collective-permute-start.1 = (bf16[272,512]{1,0:T(8,128)(2,1)S(1)}, bf16[272,512]{1,0:T(8,128)(2,1)S(1)}, u32[]{:S(2)}, u32[]{:S(2)}) collective-permute-start(bf16[272,512]{1,0:T(8,128)(2,1)S(1)} %maximum_maximum_fusion), channel_id=1, source_target_pairs={{0,4},{4,8},{8,12},{1,5},{5,9},{9,13},{2,6},{6,10},{10,14},{3,7},{... | collective-permute-start | bytes 835592 | tf_op jit(solution)/shard_map/ppermute | solution.py:144
  6.7 21.2 %collective-permute-start = (bf16[272,512]{1,0:T(8,128)(2,1)S(1)}, bf16[272,512]{1,0:T(8,128)(2,1)S(1)}, u32[]{:S(2)}, u32[]{:S(2)}) collective-permute-start(bf16[272,512]{1,0:T(8,128)(2,1)S(1)} %maximum_maximum_fusion), channel_id=1, source_target_pairs={{0,12},{1,13},{2,14},{3,15},{16,28},{17,29},{18,30},{19,31}} | collective-permute-start | bytes 835592 | tf_op jit(solution)/shard_map/ppermute | solution.py:137
  10.0 16.6 %collective-permute-start.3 = (bf16[272,512]{1,0:T(8,128)(2,1)S(1)}, bf16[272,512]{1,0:T(8,128)(2,1)S(1)}, u32[]{:S(2)}, u32[]{:S(2)}) collective-permute-start(bf16[272,512]{1,0:T(8,128)(2,1)S(1)} %maximum_maximum_fusion), channel_id=1, source_target_pairs={{4,0},{8,4},{12,8},{5,1},{9,5},{13,9},{6,2},{10,6},{14,10},{7,3},{... | collective-permute-start | bytes 835592 | tf_op jit(solution)/shard_map/ppermute | solution.py:145
  11.3 23.8 %collective-permute-start.5 = (bf16[272,512]{1,0:T(8,128)(2,1)S(1)}, bf16[272,512]{1,0:T(8,128)(2,1)S(1)}, u32[]{:S(2)}, u32[]{:S(2)}) collective-permute-start(bf16[272,512]{1,0:T(8,128)(2,1)S(1)} %maximum_maximum_fusion), channel_id=1, source_target_pairs={{12,0},{13,1},{14,2},{15,3},{28,16},{29,17},{30,18},{31,19}} | collective-permute-start | bytes 835592 | tf_op jit(solution)/shard_map/ppermute | solution.py:138
  15.3 12.6 %collective-permute-start.2 = (bf16[272,512]{1,0:T(8,128)(2,1)S(1)}, bf16[272,512]{1,0:T(8,128)(2,1)S(1)}, u32[]{:S(2)}, u32[]{:S(2)}) collective-permute-start(bf16[272,512]{1,0:T(8,128)(2,1)S(1)} %collective-permute-done.1), channel_id=1, source_target_pairs={{4,8},{8,12},{5,9},{9,13},{6,10},{10,14},{7,11},{11,15},{20,24},{2... | collective-permute-start | bytes 835592 | tf_op jit(solution)/shard_map/ppermute | solution.py:144
  16.9 18.2 %copy-start = (bf16[1,1,8,256,256]{4,3,2,1,0:T(8,128)(2,1)S(1)}, bf16[1,1,8,256,256]{4,3,2,1,0:T(8,128)(2,1)}, u32[]{:S(2)}) copy-start(bf16[1,1,8,256,256]{4,3,2,1,0:T(8,128)(2,1)} %param.8) | copy-start | bytes 3145732
  26.6 8.4 %collective-permute-start.4 = (bf16[272,512]{1,0:T(8,128)(2,1)S(1)}, bf16[272,512]{1,0:T(8,128)(2,1)S(1)}, u32[]{:S(2)}, u32[]{:S(2)}) collective-permute-start(bf16[272,512]{1,0:T(8,128)(2,1)S(1)} %collective-permute-done.3), channel_id=1, source_target_pairs={{4,0},{8,4},{5,1},{9,5},{6,2},{10,6},{7,3},{11,7},{20,16},{24,20},... | collective-permute-start | bytes 835592 | tf_op jit(solution)/shard_map/ppermute | solution.py:145
  38.0 11.4 %copy-start.2 = (bf16[1,32,256]{2,1,0:T(8,128)(2,1)S(1)}, bf16[1,32,256]{2,1,0:T(8,128)(2,1)}, u32[]{:S(2)}) copy-start(bf16[1,32,256]{2,1,0:T(8,128)(2,1)} %param.7) | copy-start | bytes 49156
  38.0 2.1 %collective-permute-start.6 = (bf16[2,288,512]{2,1,0:T(8,128)(2,1)S(1)}, bf16[2,288,512]{2,1,0:T(8,128)(2,1)S(1)}, u32[]{:S(2)}, u32[]{:S(2)}) collective-permute-start(bf16[2,288,512]{2,1,0:T(8,128)(2,1)S(1)} %get-tuple-element.8), channel_id=1, source_target_pairs={{0,1},{1,0},{2,3},{3,2},{4,5},{5,4},{6,7},{7,6},{8,9},{9,8},{10,11... | collective-permute-start | bytes 1769480 | tf_op jit(solution)/shard_map/ppermute | solution.py:202
  40.1 9.1 %collective-permute-start.7 = (bf16[288,512]{1,0:T(8,128)(2,1)S(1)}, bf16[288,512]{1,0:T(8,128)(2,1)S(1)}, u32[]{:S(2)}, u32[]{:S(2)}) collective-permute-start(bf16[288,512]{1,0:T(8,128)(2,1)S(1)} %fusion.1), channel_id=1, source_target_pairs={{0,2},{2,0},{1,3},{3,1},{4,6},{6,4},{5,7},{7,5},{8,10},{10,8},{9,1... | collective-permute-start | bytes 884744 | tf_op jit(solution)/shard_map/ppermute | solution.py:210

commit v12 on v11

--- a/solution.py
+++ b/solution.py
@@ -63,36 +63,24 @@
     stack_count, rows, rhs_count = stack.shape
     half_count = inner_count // 2
     out_rows = width + rank_size
-    whole = lambda k, p, c, q: (0, 0, 0)
-    grid_spec = pltpu.PrefetchScalarGridSpec(
-        num_scalar_prefetch=3,
-        grid=(1,),
-        in_specs=[
-            pl.BlockSpec(tiles.shape, whole),
-            pl.BlockSpec(stack.shape, whole),
-            pl.BlockSpec(masked_t.shape, whole),
-        ],
-        out_specs=[
-            pl.BlockSpec((half_count, out_rows, rhs_count), whole),
-            pl.BlockSpec((half_count, out_rows, rhs_count), whole),
-        ],
-        scratch_shapes=[pltpu.VMEM((inner_count, width, rhs_count), jnp.float32)],
-    )
+    smem = pl.BlockSpec(memory_space=pltpu.MemorySpace.SMEM)
+    vmem = pl.BlockSpec(memory_space=pltpu.MemorySpace.VMEM)
     out = jax.ShapeDtypeStruct((half_count, out_rows, rhs_count), jnp.bfloat16)
-    block_bytes = 2 * (
+    vmem_bytes = (
         tiles.size * tiles.dtype.itemsize
         + stack.size * stack.dtype.itemsize
         + masked_t.size * masked_t.dtype.itemsize
         + 2 * half_count * out_rows * rhs_count * 2
-    )
-    vmem_bytes = block_bytes + inner_count * width * rhs_count * 4 + (4 << 20)
+        + inner_count * width * rhs_count * 4
+        + (4 << 20)
+    )
     return pl.pallas_call(
         _near_far_kernel,
-        grid_spec=grid_spec,
+        in_specs=[smem, smem, smem, vmem, vmem, vmem],
+        out_specs=[vmem, vmem],
         out_shape=[out, out],
-        compiler_params=pltpu.CompilerParams(
-            dimension_semantics=("arbitrary",), vmem_limit_bytes=int(vmem_bytes)
-        ),
+        scratch_shapes=[pltpu.VMEM((inner_count, width, rhs_count), jnp.float32)],
+        compiler_params=pltpu.CompilerParams(vmem_limit_bytes=int(vmem_bytes)),
     )(pairs_flat, count, place, tiles, stack, masked_t)
 
 
@@ -174,7 +162,7 @@
     assert lax.axis_size("sub") == 2 and 2 * width == rhs_count and rank_size % 2 == 0
     basis = cluster_basis[0]
     half_rank = rank_size // 2
-    packed = jnp.concatenate([basis[:half_rank], basis[half_rank:]], axis=1)
+    packed = basis.reshape(half_rank, 2 * width)
     payload = jnp.concatenate([density, packed], axis=0)
     stack = _line_gather(payload, "tgt")
 
@@ -193,6 +181,8 @@
     )
     masked = coupling[0, 0].reshape(inner_count, rank_size, tgt_count, rank_size) * keep_mask
     masked_t = masked.transpose(2, 0, 1, 3).reshape(tgt_count, inner_count * rank_size, rank_size)
+    rank_order = jnp.concatenate([jnp.arange(0, rank_size, 2), jnp.arange(1, rank_size, 2)])
+    masked_t = masked_t[:, :, rank_order]
 
     place = jnp.stack([lax.axis_index("tgt"), lax.axis_index("sub")]).astype(jnp.int32)
     mine, theirs = _near_far(

time: 50.9 us -> 51.1 us (level)
  local copies, waits for them, and re-layouts: 2.79 us -> 4.8 us
  waiting for transfers between devices: 26.5 us -> 25.1 us
  other arithmetic: 2.21 us -> 1.35 us
    ppermute x2, waiting for transfers between devices: 16.7 us -> 15.5 us  [_line_gather(): down = lax.ppermute(down, axis, down_pairs)]
    unnamed x12, local copies, waits for them, and re-layouts: 0.87 us -> 1.85 us
    concatenate x1, other arithmetic: 0.97 us -> 0.01 us  [on_device(): jnp.concatenate([jnp.arange(0, rank_size, 2), jnp.arange(1, rank_size, 2)])]
    slice x1 -> x0, local copies, waits for them, and re-layouts: 0.76 us -> none  [on_device(): packed = jnp.concatenate([basis[:half_rank], basis[half_rank:]], axis=1)]
    gather x0 -> x2, local copies, waits for them, and re-layouts: none -> 0.74 us  [on_device(): masked_t = masked_t[:, :, rank_order]]
    another operation x0 -> x1, local copies, waits for them, and re-layouts: none -> 0.73 us  [on_device(): packed = basis.reshape(half_rank, 2 * width)]
    another operation x1 -> x2, local copies, waits for them, and re-layouts: 0.87 us -> 1.05 us  [on_device(): coupling[0, 0].reshape(inner_count, rank_size, tgt_count, rank_size)]
  transfers between devices with their start and end apart: 8 -> 8, of which waited for: 4 -> 4; matrix products, arithmetic and copies ran while one was open for 6% -> 8% of each run, Pallas kernels for 0% -> 0%
where the time goes in v12:
time: 51.1 us; the launch traced here: 50.3 us
  waiting for transfers between devices  25.1 us (49%)
  starting transfers between devices  14.4 us (28%)
  local copies, waits for them, and re-layouts  4.8 us (9%)
  Pallas kernels  2.81 us (5%)
  other arithmetic  1.35 us (3%)
  matrix products  0.97 us (2%)
  between operations  0.9 us (2%)
    ppermute x2, waiting for transfers between devices, _line_gather(): down = lax.ppermute(down, axis, down_pairs)  15.5 us
    ppermute x1, waiting for transfers between devices, on_device(): back = lax.ppermute(send, 'inner', [(0, 1), (1, 0)])  7.59 us
    ppermute x2, starting transfers between devices, _line_gather(): up = lax.ppermute(up, axis, up_pairs)  5.65 us
    ppermute x1, starting transfers between devices, _line_gather(): far_up = lax.ppermute(payload, axis, [(0, n - 1)])  3.32 us
    pallas_call x1, Pallas kernels, _near_far(): pl.pallas_call(_near_far_kernel, in_specs=[smem, smem, smem, vmem, vmem,...  2.81 us
    ppermute x2, starting transfers between devices, _line_gather(): down = lax.ppermute(down, axis, down_pairs)  2.57 us
    ppermute x1, waiting for transfers between devices, on_device(): arrived = lax.ppermute(theirs, 'sub', [(0, 1), (1, 0)])  1.99 us
    unnamed x12, local copies, waits for them, and re-layouts  1.85 us
  transfers between devices with their start and end apart: 8, of which 4 were waited for; matrix products, arithmetic and copies ran while one was open for 8% of the time, Pallas kernels for 0%

profile of v12, /device:TPU:0, one launch (start us, length us, event | category | flops | bytes accessed | tf_op | source)
XLA Modules:
  0.0 50.3 jit_solution(1047989689013300538)
XLA Ops:
  0.0 1.0 %constant_dynamic-update-slice_fusion.1 = bf16[272,512]{1,0:T(8,128)(2,1)S(1)} fusion(bf16[256,512]{1,0:T(8,128)(2,1)} %param.6), kind=kLoop, calls=%fused_computation.17 | loop fusion | bytes 524288
  1.0 0.7 %reshape_squeeze.14 = bf16[16,512]{1,0:T(8,128)(2,1)S(1)} reshape(bf16[1,32,256]{2,1,0:T(8,128)(2,1)} %param.7) | data formatting | bytes 32768 | tf_op jit(solution)/shard_map/reshape;squeeze | solution.py:165
  1.7 5.0 %collective-permute-start.1 = (bf16[272,512]{1,0:T(8,128)(2,1)S(1)}, bf16[272,512]{1,0:T(8,128)(2,1)S(1)}, u32[]{:S(2)}, u32[]{:S(2)}) collective-permute-start(bf16[272,512]{1,0:T(8,128)(2,1)S(1)} %constant_dynamic-update-slice_fusion), channel_id=1, source_target_pairs={{0,4},{4,8},{8,12},{1,5},{5,9},{9,13},{2,6},{6,10},{10,14},{3,7},{... | collective-permute-start | bytes 835592 | tf_op jit(solution)/shard_map/ppermute | solution.py:132
  6.7 3.3 %collective-permute-start = (bf16[272,512]{1,0:T(8,128)(2,1)S(1)}, bf16[272,512]{1,0:T(8,128)(2,1)S(1)}, u32[]{:S(2)}, u32[]{:S(2)}) collective-permute-start(bf16[272,512]{1,0:T(8,128)(2,1)S(1)} %constant_dynamic-update-slice_fusion), channel_id=1, source_target_pairs={{0,12},{1,13},{2,14},{3,15},{16,28},{17,29},{18,30},{19,31}} | collective-permute-start | bytes 835592 | tf_op jit(solution)/shard_map/ppermute | solution.py:125
  10.0 1.3 %collective-permute-start.3 = (bf16[272,512]{1,0:T(8,128)(2,1)S(1)}, bf16[272,512]{1,0:T(8,128)(2,1)S(1)}, u32[]{:S(2)}, u32[]{:S(2)}) collective-permute-start(bf16[272,512]{1,0:T(8,128)(2,1)S(1)} %constant_dynamic-update-slice_fusion), channel_id=1, source_target_pairs={{4,0},{8,4},{12,8},{5,1},{9,5},{13,9},{6,2},{10,6},{14,10},{7,3},{... | collective-permute-start | bytes 835592 | tf_op jit(solution)/shard_map/ppermute | solution.py:133
  11.3 1.3 %collective-permute-start.5 = (bf16[272,512]{1,0:T(8,128)(2,1)S(1)}, bf16[272,512]{1,0:T(8,128)(2,1)S(1)}, u32[]{:S(2)}, u32[]{:S(2)}) collective-permute-start(bf16[272,512]{1,0:T(8,128)(2,1)S(1)} %constant_dynamic-update-slice_fusion), channel_id=1, source_target_pairs={{12,0},{13,1},{14,2},{15,3},{28,16},{29,17},{30,18},{31,19}} | collective-permute-start | bytes 835592 | tf_op jit(solution)/shard_map/ppermute | solution.py:126
  13.3 0.8 %add_bitcast_fusion.1 = s32[8]{0:T(128)S(1)} fusion(s32[8,2]{0,1:T(2,128)} %bitcast.52), kind=kLoop, calls=%fused_computation.31 | loop fusion | flops 16 | bytes 96 | tf_op jit(solution)/shard_map/eq | solution.py:174
  14.0 0.1 fusion.4
  14.1 0.1 convert_element_type.51
  14.2 0.1 copy.15
  14.3 0.9 %reshape_squeeze.15 = bf16[4,32,4,32]{3,2,1,0:T(4,128)(2,1)S(1)} reshape(bf16[1,1,128,128]{3,2,1,0:T(8,128)(2,1)} %param.11) | data formatting | bytes 65536 | tf_op jit(solution)/shard_map/reshape;squeeze | solution.py:182
  15.2 0.2 copy.16
  15.4 0.1 multiply_bitcast_fusion
  15.6 0.1 fusion.5
  15.6 0.0 collective-permute-done.1
  15.6 0.7 %collective-permute-start.2 = (bf16[272,512]{1,0:T(8,128)(2,1)S(1)}, bf16[272,512]{1,0:T(8,128)(2,1)S(1)}, u32[]{:S(2)}, u32[]{:S(2)}) collective-permute-start(bf16[272,512]{1,0:T(8,128)(2,1)S(1)} %collective-permute-done.1), channel_id=1, source_target_pairs={{4,8},{8,12},{5,9},{9,13},{6,10},{10,14},{7,11},{11,15},{20,24},{2... | collective-permute-start | bytes 835592 | tf_op jit(solution)/shard_map/ppermute | solution.py:132
  16.3 0.1 pad_add_fusion.place_ref
  16.4 0.8 %copy.14 = s32[1,1,8,2]{3,2,1,0:T(8,128)S(1)} copy(s32[1,1,8,2]{2,3,1,0:T(2,128)} %param.9) | data formatting | bytes 128 | tf_op args[3]
  17.2 0.1 reshape.82
  17.3 0.6 %gather_fusion = bf16[32,4,128]{2,1,0:T(4,128)(2,1)S(1)} fusion(bf16[4,128,32]{1,0,2:T(4,128)(2,1)S(1)} %reshape.82, s32[1024]{0:T(1024)S(1)} %pad_clamp_fusion), kind=kCustom, calls=%fused_computation | custom fusion | bytes 65664 | tf_op jit(solution)/shard_map/gather | solution.py:185
  17.9 0.1 copy.17
  18.0 0.1 reshape_squeeze.12.pairs_ref
  18.1 0.0 copy-start
  18.1 8.5 %collective-permute-done.3 = bf16[272,512]{1,0:T(8,128)(2,1)S(1)} collective-permute-done((bf16[272,512]{1,0:T(8,128)(2,1)S(1)}, bf16[272,512]{1,0:T(8,128)(2,1)S(1)}, u32[]{:S(2)}, u32[]{:S(2)}) %collective-permute-start.3) | collective-permute-done | bytes 278560 | tf_op jit(solution)/shard_map/ppermute | solution.py:133
  26.6 1.3 %collective-permute-start.4 = (bf16[272,512]{1,0:T(8,128)(2,1)S(1)}, bf16[272,512]{1,0:T(8,128)(2,1)S(1)}, u32[]{:S(2)}, u32[]{:S(2)}) collective-permute-start(bf16[272,512]{1,0:T(8,128)(2,1)S(1)} %collective-permute-done.3), channel_id=1, source_target_pairs={{4,0},{8,4},{5,1},{9,5},{6,2},{10,6},{7,3},{11,7},{20,16},{24,20},... | collective-permute-start | bytes 835592 | tf_op jit(solution)/shard_map/ppermute | solution.py:133
  27.9 0.0 collective-permute-done
  28.0 0.0 collective-permute-done.2
  28.1 7.0 %collective-permute-done.4 = bf16[272,512]{1,0:T(8,128)(2,1)S(1)} collective-permute-done((bf16[272,512]{1,0:T(8,128)(2,1)S(1)}, bf16[272,512]{1,0:T(8,128)(2,1)S(1)}, u32[]{:S(2)}, u32[]{:S(2)}) %collective-permute-start.4) | collective-permute-done | bytes 278560 | tf_op jit(solution)/shard_map/ppermute | solution.py:133
  35.1 0.0 collective-permute-done.5
  35.1 0.0 copy-done
  35.1 2.8 %shard_map.64 = (bf16[2,288,512]{2,1,0:T(8,128)(2,1)S(1)}, bf16[2,288,512]{2,1,0:T(8,128)(2,1)S(1)}) custom-call(s32[16]{0:T(128)S(1)} %reshape_squeeze.12.pairs_ref, s32[1]{0:T(128)} %bitcast.48.count_ref, s32[2]{0:T(128)S(1)} %pad_add_fusion.place_ref, bf16[8,256,256]{2,1,0:T(8,128)(2,1)S(1)} %bitcast.50, ...), custom_call_target="tpu_custom_call" | custom-call | tf_op jit(solution)/shard_map/pallas_call | solution.py:77
  38.0 0.0 copy-start.1
  38.0 0.1 collective-permute-start.6
  38.0 2.0 %collective-permute-done.6 = bf16[2,288,512]{2,1,0:T(8,128)(2,1)S(1)} collective-permute-done((bf16[2,288,512]{2,1,0:T(8,128)(2,1)S(1)}, bf16[2,288,512]{2,1,0:T(8,128)(2,1)S(1)}, u32[]{:S(2)}, u32[]{:S(2)}) %collective-permute-start.6) | collective-permute-done | bytes 589856 | tf_op jit(solution)/shard_map/ppermute | solution.py:192
  40.0 0.1 fusion.1
  40.1 1.5 %collective-permute-start.7 = (bf16[288,512]{1,0:T(8,128)(2,1)S(1)}, bf16[288,512]{1,0:T(8,128)(2,1)S(1)}, u32[]{:S(2)}, u32[]{:S(2)}) collective-permute-start(bf16[288,512]{1,0:T(8,128)(2,1)S(1)} %fusion.1), channel_id=1, source_target_pairs={{0,2},{2,0},{1,3},{3,1},{4,6},{6,4},{5,7},{7,5},{8,10},{10,8},{9,1... | collective-permute-start | bytes 884744 | tf_op jit(solution)/shard_map/ppermute | solution.py:200
  41.6 7.6 %collective-permute-done.7 = bf16[288,512]{1,0:T(8,128)(2,1)S(1)} collective-permute-done((bf16[288,512]{1,0:T(8,128)(2,1)S(1)}, bf16[288,512]{1,0:T(8,128)(2,1)S(1)}, u32[]{:S(2)}, u32[]{:S(2)}) %collective-permute-start.7) | collective-permute-done | bytes 294944 | tf_op jit(solution)/shard_map/ppermute | solution.py:200
  49.2 0.1 bitcast_add_fusion
  49.3 0.0 copy-done.1
  49.4 1.0 %fusion = bf16[256,512]{1,0:T(8,128)(2,1)} fusion(f32[288,512]{1,0:T(8,128)S(1)} %bitcast_add_fusion, bf16[1,32,256]{2,1,0:T(8,128)(2,1)S(1)} %copy-done.1), kind=kOutput, calls=%fused_computation.5 | convolution fusion | flops 8667136 | bytes 868352 | tf_op jit(solution)/shard_map/dot_general | solution.py:212
  (12 shorter events, 0.2 us)
Async XLA Ops:
  1.7 13.9 %collective-permute-start.1 = (bf16[272,512]{1,0:T(8,128)(2,1)S(1)}, bf16[272,512]{1,0:T(8,128)(2,1)S(1)}, u32[]{:S(2)}, u32[]{:S(2)}) collective-permute-start(bf16[272,512]{1,0:T(8,128)(2,1)S(1)} %constant_dynamic-update-slice_fusion), channel_id=1, source_target_pairs={{0,4},{4,8},{8,12},{1,5},{5,9},{9,13},{2,6},{6,10},{10,14},{3,7},{... | collective-permute-start | bytes 835592 | tf_op jit(solution)/shard_map/ppermute | solution.py:132
  6.7 21.2 %collective-permute-start = (bf16[272,512]{1,0:T(8,128)(2,1)S(1)}, bf16[272,512]{1,0:T(8,128)(2,1)S(1)}, u32[]{:S(2)}, u32[]{:S(2)}) collective-permute-start(bf16[272,512]{1,0:T(8,128)(2,1)S(1)} %constant_dynamic-update-slice_fusion), channel_id=1, source_target_pairs={{0,12},{1,13},{2,14},{3,15},{16,28},{17,29},{18,30},{19,31}} | collective-permute-start | bytes 835592 | tf_op jit(solution)/shard_map/ppermute | solution.py:125
  10.0 16.6 %collective-permute-start.3 = (bf16[272,512]{1,0:T(8,128)(2,1)S(1)}, bf16[272,512]{1,0:T(8,128)(2,1)S(1)}, u32[]{:S(2)}, u32[]{:S(2)}) collective-permute-start(bf16[272,512]{1,0:T(8,128)(2,1)S(1)} %constant_dynamic-update-slice_fusion), channel_id=1, source_target_pairs={{4,0},{8,4},{12,8},{5,1},{9,5},{13,9},{6,2},{10,6},{14,10},{7,3},{... | collective-permute-start | bytes 835592 | tf_op jit(solution)/shard_map/ppermute | solution.py:133
  11.3 23.8 %collective-permute-start.5 = (bf16[272,512]{1,0:T(8,128)(2,1)S(1)}, bf16[272,512]{1,0:T(8,128)(2,1)S(1)}, u32[]{:S(2)}, u32[]{:S(2)}) collective-permute-start(bf16[272,512]{1,0:T(8,128)(2,1)S(1)} %constant_dynamic-update-slice_fusion), channel_id=1, source_target_pairs={{12,0},{13,1},{14,2},{15,3},{28,16},{29,17},{30,18},{31,19}} | collective-permute-start | bytes 835592 | tf_op jit(solution)/shard_map/ppermute | solution.py:126
  15.6 12.3 %collective-permute-start.2 = (bf16[272,512]{1,0:T(8,128)(2,1)S(1)}, bf16[272,512]{1,0:T(8,128)(2,1)S(1)}, u32[]{:S(2)}, u32[]{:S(2)}) collective-permute-start(bf16[272,512]{1,0:T(8,128)(2,1)S(1)} %collective-permute-done.1), channel_id=1, source_target_pairs={{4,8},{8,12},{5,9},{9,13},{6,10},{10,14},{7,11},{11,15},{20,24},{2... | collective-permute-start | bytes 835592 | tf_op jit(solution)/shard_map/ppermute | solution.py:132
  18.1 17.0 %copy-start = (bf16[1,1,8,256,256]{4,3,2,1,0:T(8,128)(2,1)S(1)}, bf16[1,1,8,256,256]{4,3,2,1,0:T(8,128)(2,1)}, u32[]{:S(2)}) copy-start(bf16[1,1,8,256,256]{4,3,2,1,0:T(8,128)(2,1)} %param.8) | copy-start | bytes 3145732
  26.6 8.4 %collective-permute-start.4 = (bf16[272,512]{1,0:T(8,128)(2,1)S(1)}, bf16[272,512]{1,0:T(8,128)(2,1)S(1)}, u32[]{:S(2)}, u32[]{:S(2)}) collective-permute-start(bf16[272,512]{1,0:T(8,128)(2,1)S(1)} %collective-permute-done.3), channel_id=1, source_target_pairs={{4,0},{8,4},{5,1},{9,5},{6,2},{10,6},{7,3},{11,7},{20,16},{24,20},... | collective-permute-start | bytes 835592 | tf_op jit(solution)/shard_map/ppermute | solution.py:133
  38.0 11.4 %copy-start.1 = (bf16[1,32,256]{2,1,0:T(8,128)(2,1)S(1)}, bf16[1,32,256]{2,1,0:T(8,128)(2,1)}, u32[]{:S(2)}) copy-start(bf16[1,32,256]{2,1,0:T(8,128)(2,1)} %param.7) | copy-start | bytes 49156
  38.0 2.1 %collective-permute-start.6 = (bf16[2,288,512]{2,1,0:T(8,128)(2,1)S(1)}, bf16[2,288,512]{2,1,0:T(8,128)(2,1)S(1)}, u32[]{:S(2)}, u32[]{:S(2)}) collective-permute-start(bf16[2,288,512]{2,1,0:T(8,128)(2,1)S(1)} %get-tuple-element.8), channel_id=1, source_target_pairs={{0,1},{1,0},{2,3},{3,2},{4,5},{5,4},{6,7},{7,6},{8,9},{9,8},{10,11... | collective-permute-start | bytes 1769480 | tf_op jit(solution)/shard_map/ppermute | solution.py:192
  40.1 9.1 %collective-permute-start.7 = (bf16[288,512]{1,0:T(8,128)(2,1)S(1)}, bf16[288,512]{1,0:T(8,128)(2,1)S(1)}, u32[]{:S(2)}, u32[]{:S(2)}) collective-permute-start(bf16[288,512]{1,0:T(8,128)(2,1)S(1)} %fusion.1), channel_id=1, source_target_pairs={{0,2},{2,0},{1,3},{3,1},{4,6},{6,4},{5,7},{7,5},{8,10},{10,8},{9,1... | collective-permute-start | bytes 884744 | tf_op jit(solution)/shard_map/ppermute | solution.py:200

commit v13 on v11

--- a/solution.py
+++ b/solution.py
@@ -199,17 +199,21 @@
         pair_list.reshape(-1), live_count.reshape(1), place, near_blocks[0, 0], stack, masked_t,
         inner_count, rank_size,
     )
-    arrived = lax.ppermute(theirs, "sub", [(0, 1), (1, 0)])
     basis_t = cluster_basis[0].T
     me = lax.axis_index("inner")
+    swap = [(0, 1), (1, 0)]
     if lax.axis_size("inner") == 2:
+        onward = lax.ppermute(lax.dynamic_index_in_dim(theirs, 1 - me, 0, False), "sub", swap)
         send = (
             lax.dynamic_index_in_dim(mine, 1 - me, 0, False).astype(jnp.float32)
-            + lax.dynamic_index_in_dim(arrived, 1 - me, 0, False).astype(jnp.float32)
+            + onward.astype(jnp.float32)
         ).astype(jnp.bfloat16)
-        back = lax.ppermute(send, "inner", [(0, 1), (1, 0)])
-        pieces = (mine, arrived, back)
+        back = lax.ppermute(send, "inner", swap)
+        keep_src = lax.optimization_barrier((lax.dynamic_index_in_dim(theirs, me, 0, False), send))[0]
+        kept = lax.ppermute(keep_src, "sub", swap)
+        pieces = (mine, kept, back)
     else:
+        arrived = lax.ppermute(theirs, "sub", swap)
         stage = mine.astype(jnp.float32) + arrived.astype(jnp.float32)
         pieces = (_ring_reduce_scatter(stage, "inner"),)
     width = basis_t.shape[0]

time: 50.9 us -> 51.2 us (level)
  starting transfers between devices: 14.2 us -> 15.2 us
  waiting for transfers between devices: 26.5 us -> 25.8 us
    ppermute x2 -> x3, starting transfers between devices: 1.36 us -> 2.41 us  [the longest x1 2.14 us: on_device(): back = lax.ppermute(send, 'inner', swap)]
    ppermute x2 -> x3, waiting for transfers between devices: 9.81 us -> 9.11 us  [the longest x1 7.54 us: on_device(): back = lax.ppermute(send, 'inner', swap)]
  transfers between devices with their start and end apart: 8 -> 9, of which waited for: 4 -> 4; matrix products, arithmetic and copies ran while one was open for 6% -> 6% of each run, Pallas kernels for 0% -> 0%
where the time goes in v13:
time: 51.2 us; the launch traced here: 50.8 us
  waiting for transfers between devices  25.8 us (50%)
  starting transfers between devices  15.2 us (30%)
  local copies, waits for them, and re-layouts  2.84 us (6%)
  Pallas kernels  2.82 us (6%)
  other arithmetic  2.22 us (4%)
  matrix products  0.97 us (2%)
  between operations  0.88 us (2%)
    ppermute x2, waiting for transfers between devices, _line_gather(): down = lax.ppermute(down, axis, down_pairs)  16.7 us
    ppermute x1, waiting for transfers between devices, on_device(): back = lax.ppermute(send, 'inner', swap)  7.54 us
    ppermute x2, starting transfers between devices, _line_gather(): up = lax.ppermute(up, axis, up_pairs)  5.65 us
    ppermute x1, starting transfers between devices, _line_gather(): far_up = lax.ppermute(payload, axis, [(0, n - 1)])  3.32 us
    pallas_call x1, Pallas kernels, _near_far(): pl.pallas_call(_near_far_kernel, grid_spec=grid_spec, out_shape=[out, out...  2.82 us
    ppermute x2, starting transfers between devices, _line_gather(): down = lax.ppermute(down, axis, down_pairs)  2.57 us
    ppermute x1, starting transfers between devices, on_device(): back = lax.ppermute(send, 'inner', swap)  2.14 us
    ppermute x1, waiting for transfers between devices, on_device(): lax.ppermute(lax.dynamic_index_in_dim(theirs, 1 - me, 0, False), 'sub', s...  1.57 us
  transfers between devices with their start and end apart: 9, of which 4 were waited for; matrix products, arithmetic and copies ran while one was open for 6% of the time, Pallas kernels for 0%

profile of v13, /device:TPU:0, one launch (start us, length us, event | category | flops | bytes accessed | tf_op | source)
XLA Modules:
  0.0 50.8 jit_solution(10285872583372499640)
XLA Ops:
  0.0 0.0 copy-start.1
  0.0 0.8 %slice_bitcast_fusion.1 = (bf16[16,256]{1,0:T(8,128)(2,1)S(1)}, bf16[16,256]{1,0:T(8,128)(2,1)S(1)}) fusion(bf16[1,32,256]{2,1,0:T(8,128)(2,1)} %param.7), kind=kLoop, calls=%fused_computation.21 | loop fusion | bytes 32768 | tf_op jit(solution)/shard_map/slice | solution.py:177
  0.8 1.0 %maximum_maximum_fusion = bf16[272,512]{1,0:T(8,128)(2,1)S(1)} fusion(bf16[16,256]{1,0:T(8,128)(2,1)S(1)} %get-tuple-element.14, bf16[16,256]{1,0:T(8,128)(2,1)S(1)} %get-tuple-element.13, bf16[256,512]{1,0:T(8,128)(2,1)} %param.6), kind=kLoop, calls=%fused_computation.9 | loop fusion | flops 835584 | bytes 557056 | tf_op jit(solution)/shard_map/concatenate | solution.py:178
  1.7 5.0 %collective-permute-start.1 = (bf16[272,512]{1,0:T(8,128)(2,1)S(1)}, bf16[272,512]{1,0:T(8,128)(2,1)S(1)}, u32[]{:S(2)}, u32[]{:S(2)}) collective-permute-start(bf16[272,512]{1,0:T(8,128)(2,1)S(1)} %maximum_maximum_fusion), channel_id=1, source_target_pairs={{0,4},{4,8},{8,12},{1,5},{5,9},{9,13},{2,6},{6,10},{10,14},{3,7},{... | collective-permute-start | bytes 835592 | tf_op jit(solution)/shard_map/ppermute | solution.py:144
  6.7 3.3 %collective-permute-start = (bf16[272,512]{1,0:T(8,128)(2,1)S(1)}, bf16[272,512]{1,0:T(8,128)(2,1)S(1)}, u32[]{:S(2)}, u32[]{:S(2)}) collective-permute-start(bf16[272,512]{1,0:T(8,128)(2,1)S(1)} %maximum_maximum_fusion), channel_id=1, source_target_pairs={{0,12},{1,13},{2,14},{3,15},{16,28},{17,29},{18,30},{19,31}} | collective-permute-start | bytes 835592 | tf_op jit(solution)/shard_map/ppermute | solution.py:137
  10.0 1.3 %collective-permute-start.3 = (bf16[272,512]{1,0:T(8,128)(2,1)S(1)}, bf16[272,512]{1,0:T(8,128)(2,1)S(1)}, u32[]{:S(2)}, u32[]{:S(2)}) collective-permute-start(bf16[272,512]{1,0:T(8,128)(2,1)S(1)} %maximum_maximum_fusion), channel_id=1, source_target_pairs={{4,0},{8,4},{12,8},{5,1},{9,5},{13,9},{6,2},{10,6},{14,10},{7,3},{... | collective-permute-start | bytes 835592 | tf_op jit(solution)/shard_map/ppermute | solution.py:145
  11.3 1.3 %collective-permute-start.5 = (bf16[272,512]{1,0:T(8,128)(2,1)S(1)}, bf16[272,512]{1,0:T(8,128)(2,1)S(1)}, u32[]{:S(2)}, u32[]{:S(2)}) collective-permute-start(bf16[272,512]{1,0:T(8,128)(2,1)S(1)} %maximum_maximum_fusion), channel_id=1, source_target_pairs={{12,0},{13,1},{14,2},{15,3},{28,16},{29,17},{30,18},{31,19}} | collective-permute-start | bytes 835592 | tf_op jit(solution)/shard_map/ppermute | solution.py:138
  13.3 0.8 %add_bitcast_fusion = s32[8]{0:T(128)S(1)} fusion(s32[8,2]{0,1:T(2,128)} %bitcast.54), kind=kLoop, calls=%fused_computation.28 | loop fusion | flops 16 | bytes 96 | tf_op jit(solution)/shard_map/eq | solution.py:186
  14.1 0.1 fusion.5
  14.2 0.1 convert_element_type.50
  14.2 0.1 copy.16
  14.4 0.9 %reshape_squeeze.11 = bf16[4,32,4,32]{3,2,1,0:T(4,128)(2,1)S(1)} reshape(bf16[1,1,128,128]{3,2,1,0:T(8,128)(2,1)} %param.11) | data formatting | bytes 65536 | tf_op jit(solution)/shard_map/reshape;squeeze | solution.py:194
  15.2 0.1 copy_multiply_fusion
  15.3 0.0 collective-permute-done.1
  15.3 0.7 %collective-permute-start.2 = (bf16[272,512]{1,0:T(8,128)(2,1)S(1)}, bf16[272,512]{1,0:T(8,128)(2,1)S(1)}, u32[]{:S(2)}, u32[]{:S(2)}) collective-permute-start(bf16[272,512]{1,0:T(8,128)(2,1)S(1)} %collective-permute-done.1), channel_id=1, source_target_pairs={{4,8},{8,12},{5,9},{9,13},{6,10},{10,14},{7,11},{11,15},{20,24},{2... | collective-permute-start | bytes 835592 | tf_op jit(solution)/shard_map/ppermute | solution.py:144
  16.0 0.1 pad_add_fusion.place_ref
  16.1 0.8 %copy.15 = s32[1,1,8,2]{3,2,1,0:T(8,128)S(1)} copy(s32[1,1,8,2]{2,3,1,0:T(2,128)} %param.9) | data formatting | bytes 128 | tf_op args[3]
  16.9 0.1 reshape_squeeze.9.pairs_ref
  16.9 0.0 copy-start
  16.9 9.7 %collective-permute-done.3 = bf16[272,512]{1,0:T(8,128)(2,1)S(1)} collective-permute-done((bf16[272,512]{1,0:T(8,128)(2,1)S(1)}, bf16[272,512]{1,0:T(8,128)(2,1)S(1)}, u32[]{:S(2)}, u32[]{:S(2)}) %collective-permute-start.3) | collective-permute-done | bytes 278560 | tf_op jit(solution)/shard_map/ppermute | solution.py:145
  26.6 1.3 %collective-permute-start.4 = (bf16[272,512]{1,0:T(8,128)(2,1)S(1)}, bf16[272,512]{1,0:T(8,128)(2,1)S(1)}, u32[]{:S(2)}, u32[]{:S(2)}) collective-permute-start(bf16[272,512]{1,0:T(8,128)(2,1)S(1)} %collective-permute-done.3), channel_id=1, source_target_pairs={{4,0},{8,4},{5,1},{9,5},{6,2},{10,6},{7,3},{11,7},{20,16},{24,20},... | collective-permute-start | bytes 835592 | tf_op jit(solution)/shard_map/ppermute | solution.py:145
  27.9 0.0 collective-permute-done
  28.0 0.0 collective-permute-done.2
  28.0 0.0 copy-done.1
  28.1 7.0 %collective-permute-done.4 = bf16[272,512]{1,0:T(8,128)(2,1)S(1)} collective-permute-done((bf16[272,512]{1,0:T(8,128)(2,1)S(1)}, bf16[272,512]{1,0:T(8,128)(2,1)S(1)}, u32[]{:S(2)}, u32[]{:S(2)}) %collective-permute-start.4) | collective-permute-done | bytes 278560 | tf_op jit(solution)/shard_map/ppermute | solution.py:145
  35.1 0.0 collective-permute-done.5
  35.1 0.0 copy-done
  35.1 2.8 %shard_map.64 = (bf16[2,288,512]{2,1,0:T(8,128)(2,1)S(1)}, bf16[2,288,512]{2,1,0:T(8,128)(2,1)S(1)}) custom-call(s32[16]{0:T(128)S(1)} %reshape_squeeze.9.pairs_ref, s32[1]{0:T(128)} %bitcast.50.count_ref, s32[2]{0:T(128)S(1)} %pad_add_fusion.place_ref, bf16[8,256,256]{2,1,0:T(8,128)(2,1)S(1)} %bitcast.52, ...), custom_call_target="tpu_custom_call" | custom-call | tf_op jit(solution)/shard_map/pallas_call | solution.py:89
  38.0 0.0 copy-start.2
  38.0 0.1 collective-permute-start.6
  38.1 1.6 %collective-permute-done.6 = bf16[288,512]{1,0:T(8,128)(2,1)S(1)} collective-permute-done((bf16[288,512]{1,0:T(8,128)(2,1)S(1)}, bf16[288,512]{1,0:T(8,128)(2,1)S(1)}, u32[]{:S(2)}, u32[]{:S(2)}) %collective-permute-start.6) | collective-permute-done | bytes 294944 | tf_op jit(solution)/shard_map/ppermute | solution.py:206
  39.7 0.1 fusion
  39.8 0.2 collective-permute-start.7
  40.0 2.1 %collective-permute-start.8 = (bf16[288,512]{1,0:T(8,128)(2,1)S(1)}, bf16[288,512]{1,0:T(8,128)(2,1)S(1)}, u32[]{:S(2)}, u32[]{:S(2)}) collective-permute-start(bf16[288,512]{1,0:T(8,128)(2,1)S(1)} %fusion), channel_id=1, source_target_pairs={{0,2},{2,0},{1,3},{3,1},{4,6},{6,4},{5,7},{7,5},{8,10},{10,8},{9,1... | collective-permute-start | bytes 884744 | tf_op jit(solution)/shard_map/ppermute | solution.py:211
  42.1 0.0 collective-permute-done.7
  42.1 7.5 %collective-permute-done.8 = bf16[288,512]{1,0:T(8,128)(2,1)S(1)} collective-permute-done((bf16[288,512]{1,0:T(8,128)(2,1)S(1)}, bf16[288,512]{1,0:T(8,128)(2,1)S(1)}, u32[]{:S(2)}, u32[]{:S(2)}) %collective-permute-start.8) | collective-permute-done | bytes 294944 | tf_op jit(solution)/shard_map/ppermute | solution.py:211
  49.7 0.1 fusion.1
  49.8 0.0 copy-done.2
  49.8 1.0 %fusion.2 = bf16[256,512]{1,0:T(8,128)(2,1)} fusion(f32[288,512]{1,0:T(8,128)S(1)} %fusion.1, bf16[1,32,256]{2,1,0:T(8,128)(2,1)S(1)} %copy-done.2), kind=kOutput, calls=%fused_computation.6 | convolution fusion | flops 8667136 | bytes 868352 | tf_op jit(solution)/shard_map/dot_general | solution.py:226
  (10 shorter events, 0.2 us)
Async XLA Ops:
  0.0 28.0 %copy-start.1 = (bf16[256,512]{1,0:T(8,128)(2,1)S(1)}, bf16[256,512]{1,0:T(8,128)(2,1)}, u32[]{:S(2)}) copy-start(bf16[256,512]{1,0:T(8,128)(2,1)} %param.6) | copy-start | bytes 786436
  1.7 13.6 %collective-permute-start.1 = (bf16[272,512]{1,0:T(8,128)(2,1)S(1)}, bf16[272,512]{1,0:T(8,128)(2,1)S(1)}, u32[]{:S(2)}, u32[]{:S(2)}) collective-permute-start(bf16[272,512]{1,0:T(8,128)(2,1)S(1)} %maximum_maximum_fusion), channel_id=1, source_target_pairs={{0,4},{4,8},{8,12},{1,5},{5,9},{9,13},{2,6},{6,10},{10,14},{3,7},{... | collective-permute-start | bytes 835592 | tf_op jit(solution)/shard_map/ppermute | solution.py:144
  6.7 21.2 %collective-permute-start = (bf16[272,512]{1,0:T(8,128)(2,1)S(1)}, bf16[272,512]{1,0:T(8,128)(2,1)S(1)}, u32[]{:S(2)}, u32[]{:S(2)}) collective-permute-start(bf16[272,512]{1,0:T(8,128)(2,1)S(1)} %maximum_maximum_fusion), channel_id=1, source_target_pairs={{0,12},{1,13},{2,14},{3,15},{16,28},{17,29},{18,30},{19,31}} | collective-permute-start | bytes 835592 | tf_op jit(solution)/shard_map/ppermute | solution.py:137
  10.0 16.6 %collective-permute-start.3 = (bf16[272,512]{1,0:T(8,128)(2,1)S(1)}, bf16[272,512]{1,0:T(8,128)(2,1)S(1)}, u32[]{:S(2)}, u32[]{:S(2)}) collective-permute-start(bf16[272,512]{1,0:T(8,128)(2,1)S(1)} %maximum_maximum_fusion), channel_id=1, source_target_pairs={{4,0},{8,4},{12,8},{5,1},{9,5},{13,9},{6,2},{10,6},{14,10},{7,3},{... | collective-permute-start | bytes 835592 | tf_op jit(solution)/shard_map/ppermute | solution.py:145
  11.3 23.8 %collective-permute-start.5 = (bf16[272,512]{1,0:T(8,128)(2,1)S(1)}, bf16[272,512]{1,0:T(8,128)(2,1)S(1)}, u32[]{:S(2)}, u32[]{:S(2)}) collective-permute-start(bf16[272,512]{1,0:T(8,128)(2,1)S(1)} %maximum_maximum_fusion), channel_id=1, source_target_pairs={{12,0},{13,1},{14,2},{15,3},{28,16},{29,17},{30,18},{31,19}} | collective-permute-start | bytes 835592 | tf_op jit(solution)/shard_map/ppermute | solution.py:138
  15.3 12.6 %collective-permute-start.2 = (bf16[272,512]{1,0:T(8,128)(2,1)S(1)}, bf16[272,512]{1,0:T(8,128)(2,1)S(1)}, u32[]{:S(2)}, u32[]{:S(2)}) collective-permute-start(bf16[272,512]{1,0:T(8,128)(2,1)S(1)} %collective-permute-done.1), channel_id=1, source_target_pairs={{4,8},{8,12},{5,9},{9,13},{6,10},{10,14},{7,11},{11,15},{20,24},{2... | collective-permute-start | bytes 835592 | tf_op jit(solution)/shard_map/ppermute | solution.py:144
  16.9 18.2 %copy-start = (bf16[1,1,8,256,256]{4,3,2,1,0:T(8,128)(2,1)S(1)}, bf16[1,1,8,256,256]{4,3,2,1,0:T(8,128)(2,1)}, u32[]{:S(2)}) copy-start(bf16[1,1,8,256,256]{4,3,2,1,0:T(8,128)(2,1)} %param.8) | copy-start | bytes 3145732
  26.6 8.4 %collective-permute-start.4 = (bf16[272,512]{1,0:T(8,128)(2,1)S(1)}, bf16[272,512]{1,0:T(8,128)(2,1)S(1)}, u32[]{:S(2)}, u32[]{:S(2)}) collective-permute-start(bf16[272,512]{1,0:T(8,128)(2,1)S(1)} %collective-permute-done.3), channel_id=1, source_target_pairs={{4,0},{8,4},{5,1},{9,5},{6,2},{10,6},{7,3},{11,7},{20,16},{24,20},... | collective-permute-start | bytes 835592 | tf_op jit(solution)/shard_map/ppermute | solution.py:145
  38.0 11.8 %copy-start.2 = (bf16[1,32,256]{2,1,0:T(8,128)(2,1)S(1)}, bf16[1,32,256]{2,1,0:T(8,128)(2,1)}, u32[]{:S(2)}) copy-start(bf16[1,32,256]{2,1,0:T(8,128)(2,1)} %param.7) | copy-start | bytes 49156
  38.0 1.6 %collective-permute-start.6 = (bf16[288,512]{1,0:T(8,128)(2,1)S(1)}, bf16[288,512]{1,0:T(8,128)(2,1)S(1)}, u32[]{:S(2)}, u32[]{:S(2)}) collective-permute-start(bf16[288,512]{1,0:T(8,128)(2,1)S(1)} %get-tuple-element.12), channel_id=1, source_target_pairs={{0,1},{1,0},{2,3},{3,2},{4,5},{5,4},{6,7},{7,6},{8,9},{9,8},{10,11... | collective-permute-start | bytes 884744 | tf_op jit(solution)/shard_map/ppermute | solution.py:206
  39.8 2.3 %collective-permute-start.7 = (bf16[288,512]{1,0:T(8,128)(2,1)S(1)}, bf16[288,512]{1,0:T(8,128)(2,1)S(1)}, u32[]{:S(2)}, u32[]{:S(2)}) collective-permute-start(bf16[288,512]{1,0:T(8,128)(2,1)S(1)} %get-tuple-element.10), channel_id=1, source_target_pairs={{0,1},{1,0},{2,3},{3,2},{4,5},{5,4},{6,7},{7,6},{8,9},{9,8},{10,11... | collective-permute-start | bytes 884744 | tf_op jit(solution)/shard_map/ppermute | solution.py:213
  40.0 9.7 %collective-permute-start.8 = (bf16[288,512]{1,0:T(8,128)(2,1)S(1)}, bf16[288,512]{1,0:T(8,128)(2,1)S(1)}, u32[]{:S(2)}, u32[]{:S(2)}) collective-permute-start(bf16[288,512]{1,0:T(8,128)(2,1)S(1)} %fusion), channel_id=1, source_target_pairs={{0,2},{2,0},{1,3},{3,1},{4,6},{6,4},{5,7},{7,5},{8,10},{10,8},{9,1... | collective-permute-start | bytes 884744 | tf_op jit(solution)/shard_map/ppermute | solution.py:211

commit v14 on v10

--- a/solution.py
+++ b/solution.py
@@ -7,7 +7,16 @@
 
 
 def _near_far_kernel(
-    pairs_ref, count_ref, place_ref, tiles_ref, stack_ref, masked_ref, mine_ref, theirs_ref, acc_ref
+    pairs_ref,
+    count_ref,
+    place_ref,
+    tiles_ref,
+    stack_ref,
+    basis_ref,
+    masked_ref,
+    mine_ref,
+    theirs_ref,
+    acc_ref,
 ):
     inner_count, width, rhs_count = acc_ref.shape
     slot_count = tiles_ref.shape[0]
@@ -33,12 +42,10 @@
 
     coeffs = jnp.zeros((inner_count * rank_size, rhs_count), jnp.float32)
     for source in range(tgt_count):
-        block = stack_ref[source - own_tgt + tgt_count - 1]
-        dens = block[:width, :]
-        packed = block[width:, :]
-        top = jnp.dot(packed[:, :width], dens, preferred_element_type=jnp.float32)
-        bottom = jnp.dot(packed[:, width:], dens, preferred_element_type=jnp.float32)
-        projected = jnp.concatenate([top, bottom], axis=0).astype(jnp.bfloat16)
+        offset = source - own_tgt + tgt_count - 1
+        projected = jnp.dot(
+            basis_ref[offset], stack_ref[offset, :width, :], preferred_element_type=jnp.float32
+        ).astype(jnp.bfloat16)
         coeffs += jnp.dot(masked_ref[source], projected, preferred_element_type=jnp.float32)
     coeffs = coeffs.astype(jnp.bfloat16)
 
@@ -58,7 +65,7 @@
         write(theirs_ref, mine_ref)
 
 
-def _near_far(pairs_flat, count, place, tiles, stack, masked_t, inner_count, rank_size):
+def _near_far(pairs_flat, count, place, tiles, stack, basis_src, masked_t, inner_count, rank_size):
     slot_count, width, _ = tiles.shape
     stack_count, rows, rhs_count = stack.shape
     half_count = inner_count // 2
@@ -69,7 +76,10 @@
         grid=(1,),
         in_specs=[
             pl.BlockSpec(tiles.shape, whole),
-            pl.BlockSpec(stack.shape, whole),
+            pl.BlockSpec((stack_count, width, rhs_count), whole),
+            pl.BlockSpec(
+                (stack_count, rank_size, width), lambda k, p, c, q: (0, width // rank_size, 0)
+            ),
             pl.BlockSpec(masked_t.shape, whole),
         ],
         out_specs=[
@@ -79,11 +89,12 @@
         scratch_shapes=[pltpu.VMEM((inner_count, width, rhs_count), jnp.float32)],
     )
     out = jax.ShapeDtypeStruct((half_count, out_rows, rhs_count), jnp.bfloat16)
-    block_bytes = 2 * (
-        tiles.size * tiles.dtype.itemsize
-        + stack.size * stack.dtype.itemsize
-        + masked_t.size * masked_t.dtype.itemsize
-        + 2 * half_count * out_rows * rhs_count * 2
+    block_bytes = 2 * 2 * (
+        tiles.size
+        + stack_count * width * rhs_count
+        + stack_count * rank_size * width
+        + masked_t.size
+        + 2 * half_count * out_rows * rhs_count
     )
     vmem_bytes = block_bytes + inner_count * width * rhs_count * 4 + (4 << 20)
     return pl.pallas_call(
@@ -93,7 +104,7 @@
         compiler_params=pltpu.CompilerParams(
             dimension_semantics=("arbitrary",), vmem_limit_bytes=int(vmem_bytes)
         ),
-    )(pairs_flat, count, place, tiles, stack, masked_t)
+    )(pairs_flat, count, place, tiles, stack, basis_src, masked_t)
 
 
 def _epilogue_kernel(me_ref, basis_t_ref, *refs):
@@ -129,8 +140,10 @@
     )(me, basis_t, *pieces)
 
 
-def _line_gather(payload, axis):
+def _line_gather(payload, axis, ties=()):
     n = lax.axis_size(axis)
+    if ties:
+        payload = lax.optimization_barrier((payload,) + tuple(ties[0]))[0]
     if n <= 2:
         far_up = far_down = None
     else:
@@ -139,6 +152,8 @@
     ups, downs = [], []
     up, down = payload, payload
     for step in range(n - 1 if far_up is None else n - 2):
+        if 0 < step < len(ties):
+            up, down = lax.optimization_barrier((up, down) + tuple(ties[step]))[:2]
         up_pairs = [(i, i + 1) for i in range(step, n - 1)]
         down_pairs = [(i + 1, i) for i in range(n - 1 - step)]
         up = lax.ppermute(up, axis, up_pairs)
@@ -148,7 +163,8 @@
     if far_up is not None:
         ups.append(far_up)
         downs.append(far_down)
-    return jnp.stack(ups[::-1] + [payload] + downs)
+    last = tuple(x for x in (up, down, far_up, far_down) if x is not None)
+    return jnp.stack(ups[::-1] + [payload] + downs), last
 
 
 def _ring_reduce_scatter(blocks, axis):
@@ -173,10 +189,8 @@
     inner_count = lax.axis_size(("inner", "sub"))
     assert lax.axis_size("sub") == 2 and 2 * width == rhs_count and rank_size % 2 == 0
     basis = cluster_basis[0]
-    half_rank = rank_size // 2
-    packed = jnp.concatenate([basis[:half_rank], basis[half_rank:]], axis=1)
-    payload = jnp.concatenate([density, packed], axis=0)
-    stack = _line_gather(payload, "tgt")
+    chunk_count = 2
+    cols = rhs_count // chunk_count
 
     pair_list = near_pairs[0, 0]
     live_count = near_count[0, 0]
@@ -193,26 +207,51 @@
     )
     masked = coupling[0, 0].reshape(inner_count, rank_size, tgt_count, rank_size) * keep_mask
     masked_t = masked.transpose(2, 0, 1, 3).reshape(tgt_count, inner_count * rank_size, rank_size)
-
     place = jnp.stack([lax.axis_index("tgt"), lax.axis_index("sub")]).astype(jnp.int32)
-    mine, theirs = _near_far(
-        pair_list.reshape(-1), live_count.reshape(1), place, near_blocks[0, 0], stack, masked_t,
-        inner_count, rank_size,
-    )
-    arrived = lax.ppermute(theirs, "sub", [(0, 1), (1, 0)])
-    basis_t = cluster_basis[0].T
+    basis_t = basis.T
     me = lax.axis_index("inner")
-    if lax.axis_size("inner") == 2:
-        send = (
-            lax.dynamic_index_in_dim(mine, 1 - me, 0, False).astype(jnp.float32)
-            + lax.dynamic_index_in_dim(arrived, 1 - me, 0, False).astype(jnp.float32)
-        ).astype(jnp.bfloat16)
-        back = lax.ppermute(send, "inner", [(0, 1), (1, 0)])
-        pieces = (mine, arrived, back)
-    else:
-        stage = mine.astype(jnp.float32) + arrived.astype(jnp.float32)
-        pieces = (_ring_reduce_scatter(stage, "inner"),)
-    return _epilogue(me.astype(jnp.int32).reshape(1), pieces, basis_t)
+    swap = [(0, 1), (1, 0)]
+
+    outs = []
+    basis_src = None
+    previous = None
+    for chunk in range(chunk_count):
+        piece = density[:, chunk * cols : (chunk + 1) * cols]
+        if chunk == 0:
+            stack, last_round = _line_gather(jnp.concatenate([piece, basis], axis=0), "tgt")
+            basis_src = stack
+        else:
+            stack, last_round = _line_gather(piece, "tgt", (previous[0], previous[1]))
+            stack = lax.optimization_barrier((stack, previous[2]))[0]
+        mine, theirs = _near_far(
+            pair_list.reshape(-1), live_count.reshape(1), place, near_blocks[0, 0], stack,
+            basis_src, masked_t, inner_count, rank_size,
+        )
+        arrived = lax.ppermute(theirs, "sub", swap)
+        if lax.axis_size("inner") == 2:
+            send = (
+                lax.dynamic_index_in_dim(mine, 1 - me, 0, False).astype(jnp.float32)
+                + lax.dynamic_index_in_dim(arrived, 1 - me, 0, False).astype(jnp.float32)
+            ).astype(jnp.bfloat16)
+            back = lax.ppermute(send, "inner", swap)
+            pieces = (mine, arrived, back)
+            reduced, onward = back, send
+        else:
+            stage = mine.astype(jnp.float32) + arrived.astype(jnp.float32)
+            pieces = (_ring_reduce_scatter(stage, "inner"),)
+            reduced, onward = pieces[0], stage
+        previous = (tuple(last_round), (onward,), reduced)
+        total = None
+        for part in pieces:
+            if part.ndim == 3:
+                part = lax.dynamic_index_in_dim(part, me, 0, False)
+            part = part.astype(jnp.float32)
+            total = part if total is None else total + part
+        far = jnp.dot(
+            basis_t, total[width:].astype(jnp.bfloat16), preferred_element_type=jnp.float32
+        )
+        outs.append((total[:width] + far).astype(jnp.bfloat16))
+    return jnp.concatenate(outs, axis=1)
 
 
 def solution(mesh):

time: 53 us -> 64 us (1.21)
  starting transfers between devices: 15.4 us -> 26.7 us
  local copies, waits for them, and re-layouts: 4.22 us -> 3.21 us
    ppermute x2 -> x4, starting transfers between devices: 5.65 us -> 11.9 us  [_line_gather(): up = lax.ppermute(up, axis, up_pairs)]
    ppermute x2 -> x4, starting transfers between devices: 2.57 us -> 5.14 us  [_line_gather(): down = lax.ppermute(down, axis, down_pairs)]
    ppermute x2 -> x4, waiting for transfers between devices: 8.57 us -> 6.12 us  [the longest x2 5.51 us: on_device(): back = lax.ppermute(send, 'inner', swap)]
    pallas_call x1 -> x0, Pallas kernels: 2.09 us -> none  [_epilogue(): pl.pallas_call(_epilogue_kernel, grid_spec=grid_spec, out_shape=jax.Shape...]
    pallas_call x1 -> x2, Pallas kernels: 2.56 us -> 4.6 us  [_near_far(): pl.pallas_call(_near_far_kernel, grid_spec=grid_spec, out_shape=[out, out...]
    ppermute x1 -> x2, starting transfers between devices: 3.32 us -> 5.26 us  [_line_gather(): far_up = lax.ppermute(payload, axis, [(0, n - 1)])]
    ppermute x1 -> x2, waiting for transfers between devices: 0.01 us -> 1.71 us  [_line_gather(): far_up = lax.ppermute(payload, axis, [(0, n - 1)])]
    ppermute x1 -> x2, starting transfers between devices: 1.29 us -> 2.57 us  [_line_gather(): far_down = lax.ppermute(payload, axis, [(n - 1, 0)])]
  transfers between devices with their start and end apart: 8 -> 16, of which waited for: 4 -> 7; matrix products, arithmetic and copies ran while one was open for 7% -> 5% of each run, Pallas kernels for 0% -> 0%
where the time goes in v14:
time: 64 us; the launch traced here: 63.5 us
  starting transfers between devices  26.7 us (42%)
  waiting for transfers between devices  25.3 us (40%)
  Pallas kernels  4.6 us (7%)
  local copies, waits for them, and re-layouts  3.21 us (5%)
  other arithmetic  2.13 us (3%)
  between operations  1.06 us (2%)
    ppermute x4, waiting for transfers between devices, _line_gather(): down = lax.ppermute(down, axis, down_pairs)  16.9 us
    ppermute x4, starting transfers between devices, _line_gather(): up = lax.ppermute(up, axis, up_pairs)  11.9 us
    ppermute x2, waiting for transfers between devices, on_device(): back = lax.ppermute(send, 'inner', swap)  5.51 us
    ppermute x2, starting transfers between devices, _line_gather(): far_up = lax.ppermute(payload, axis, [(0, n - 1)])  5.26 us
    ppermute x4, starting transfers between devices, _line_gather(): down = lax.ppermute(down, axis, down_pairs)  5.14 us
    pallas_call x2, Pallas kernels, _near_far(): pl.pallas_call(_near_far_kernel, grid_spec=grid_spec, out_shape=[out, out...  4.6 us
    ppermute x2, starting transfers between devices, _line_gather(): far_down = lax.ppermute(payload, axis, [(n - 1, 0)])  2.57 us
    unnamed x22, local copies, waits for them, and re-layouts  1.8 us
  transfers between devices with their start and end apart: 16, of which 7 were waited for; matrix products, arithmetic and copies ran while one was open for 5% of the time, Pallas kernels for 0%

profile of v14, /device:TPU:0, one launch (start us, length us, event | category | flops | bytes accessed | tf_op | source)
XLA Modules:
  0.0 63.5 jit_solution(14081615388013728488)
XLA Ops:
  0.0 0.0 copy-start.1
  0.0 1.0 %fusion.8 = (bf16[256,256]{1,0:T(8,128)(2,1)S(1)}, bf16[256,256]{1,0:T(8,128)(2,1)S(1)}) fusion(bf16[256,512]{1,0:T(8,128)(2,1)} %param.6), kind=kLoop, calls=%fused_computation.40 | loop fusion | bytes 524288 | tf_op jit(solution)/shard_map/slice | solution.py:219
  1.0 0.0 copy-done.1
  1.0 0.0 copy-start.3
  1.0 5.0 %collective-permute-start.1 = (bf16[288,256]{1,0:T(8,128)(2,1)S(1)}, bf16[288,256]{1,0:T(8,128)(2,1)S(1)}, u32[]{:S(2)}, u32[]{:S(2)}) collective-permute-start(bf16[288,256]{1,0:T(8,128)(2,1)S(1)} %pad_maximum_fusion.1), channel_id=1, source_target_pairs={{0,4},{4,8},{8,12},{1,5},{5,9},{9,13},{2,6},{6,10},{10,14},{3,7},{... | collective-permute-start | bytes 442376 | tf_op jit(solution)/shard_map/ppermute | solution.py:159
  6.0 3.3 %collective-permute-start = (bf16[288,256]{1,0:T(8,128)(2,1)S(1)}, bf16[288,256]{1,0:T(8,128)(2,1)S(1)}, u32[]{:S(2)}, u32[]{:S(2)}) collective-permute-start(bf16[288,256]{1,0:T(8,128)(2,1)S(1)} %pad_maximum_fusion.1), channel_id=1, source_target_pairs={{0,12},{1,13},{2,14},{3,15},{16,28},{17,29},{18,30},{19,31}} | collective-permute-start | bytes 442376 | tf_op jit(solution)/shard_map/ppermute | solution.py:150
  9.3 1.3 %collective-permute-start.3 = (bf16[288,256]{1,0:T(8,128)(2,1)S(1)}, bf16[288,256]{1,0:T(8,128)(2,1)S(1)}, u32[]{:S(2)}, u32[]{:S(2)}) collective-permute-start(bf16[288,256]{1,0:T(8,128)(2,1)S(1)} %pad_maximum_fusion.1), channel_id=1, source_target_pairs={{4,0},{8,4},{12,8},{5,1},{9,5},{13,9},{6,2},{10,6},{14,10},{7,3},{... | collective-permute-start | bytes 442376 | tf_op jit(solution)/shard_map/ppermute | solution.py:160
  10.6 1.3 %collective-permute-start.5 = (bf16[288,256]{1,0:T(8,128)(2,1)S(1)}, bf16[288,256]{1,0:T(8,128)(2,1)S(1)}, u32[]{:S(2)}, u32[]{:S(2)}) collective-permute-start(bf16[288,256]{1,0:T(8,128)(2,1)S(1)} %pad_maximum_fusion.1), channel_id=1, source_target_pairs={{12,0},{13,1},{14,2},{15,3},{28,16},{29,17},{30,18},{31,19}} | collective-permute-start | bytes 442376 | tf_op jit(solution)/shard_map/ppermute | solution.py:151
  12.6 0.0 copy-start.4
  12.6 0.7 %copy-done.4 = s32[1,1,8,2]{2,3,1,0:T(2,128)S(1)} copy-done((s32[1,1,8,2]{2,3,1,0:T(2,128)S(1)}, s32[1,1,8,2]{2,3,1,0:T(2,128)}, u32[]{:S(2)}) %copy-start.4) | copy-done | bytes 88
  13.3 0.1 fusion.5
  13.4 0.1 convert_element_type.80
  13.5 0.1 copy.18
  13.6 0.0 copy-done.3
  13.6 0.1 reshape_squeeze.13
  13.7 0.1 copy_multiply_fusion
  13.8 0.0 copy-start
  13.8 0.1 copy.17
  13.9 0.1 reshape_squeeze.11.pairs_ref
  14.0 0.1 pad_add_fusion.place_ref
  14.1 0.0 collective-permute-done.1
  14.1 0.8 %collective-permute-start.2 = (bf16[288,256]{1,0:T(8,128)(2,1)S(1)}, bf16[288,256]{1,0:T(8,128)(2,1)S(1)}, u32[]{:S(2)}, u32[]{:S(2)}) collective-permute-start(bf16[288,256]{1,0:T(8,128)(2,1)S(1)} %collective-permute-done.1), channel_id=1, source_target_pairs={{4,8},{8,12},{5,9},{9,13},{6,10},{10,14},{7,11},{11,15},{20,24},{2... | collective-permute-start | bytes 442376 | tf_op jit(solution)/shard_map/ppermute | solution.py:159
  14.9 1.7 %collective-permute-done.3 = bf16[288,256]{1,0:T(8,128)(2,1)S(1)} collective-permute-done((bf16[288,256]{1,0:T(8,128)(2,1)S(1)}, bf16[288,256]{1,0:T(8,128)(2,1)S(1)}, u32[]{:S(2)}, u32[]{:S(2)}) %collective-permute-start.3) | collective-permute-done | bytes 147488 | tf_op jit(solution)/shard_map/ppermute | solution.py:160
  16.6 1.3 %collective-permute-start.4 = (bf16[288,256]{1,0:T(8,128)(2,1)S(1)}, bf16[288,256]{1,0:T(8,128)(2,1)S(1)}, u32[]{:S(2)}, u32[]{:S(2)}) collective-permute-start(bf16[288,256]{1,0:T(8,128)(2,1)S(1)} %collective-permute-done.3), channel_id=1, source_target_pairs={{4,0},{8,4},{5,1},{9,5},{6,2},{10,6},{7,3},{11,7},{20,16},{24,20},... | collective-permute-start | bytes 442376 | tf_op jit(solution)/shard_map/ppermute | solution.py:160
  17.8 0.0 collective-permute-done
  17.9 0.0 collective-permute-done.2
  18.0 5.6 %collective-permute-done.4 = bf16[288,256]{1,0:T(8,128)(2,1)S(1)} collective-permute-done((bf16[288,256]{1,0:T(8,128)(2,1)S(1)}, bf16[288,256]{1,0:T(8,128)(2,1)S(1)}, u32[]{:S(2)}, u32[]{:S(2)}) %collective-permute-start.4) | collective-permute-done | bytes 147488 | tf_op jit(solution)/shard_map/ppermute | solution.py:160
  23.6 0.0 collective-permute-done.5
  23.6 0.0 copy-done
  23.6 2.3 %shard_map.64 = (bf16[2,288,256]{2,1,0:T(8,128)(2,1)S(1)}, bf16[2,288,256]{2,1,0:T(8,128)(2,1)S(1)}) custom-call(s32[16]{0:T(128)S(1)} %reshape_squeeze.11.pairs_ref, s32[1]{0:T(128)} %bitcast.64.count_ref, s32[2]{0:T(128)S(1)} %pad_add_fusion.place_ref, bf16[8,256,256]{2,1,0:T(8,128)(2,1)S(1)} %bitcast.67, ...), custom_call_target="tpu_custom_call" | custom-call | tf_op jit(solution)/shard_map/pallas_call | solution.py:100
  26.0 0.1 collective-permute-start.6
  26.1 1.3 %collective-permute-start.10 = (bf16[256,256]{1,0:T(8,128)(2,1)S(1)}, bf16[256,256]{1,0:T(8,128)(2,1)S(1)}, u32[]{:S(2)}, u32[]{:S(2)}) collective-permute-start(bf16[256,256]{1,0:T(8,128)(2,1)S(1)} %get-tuple-element.15), channel_id=1, source_target_pairs={{4,0},{8,4},{12,8},{5,1},{9,5},{13,9},{6,2},{10,6},{14,10},{7,3},{... | collective-permute-start | bytes 393224 | tf_op jit(solution)/shard_map/ppermute | solution.py:160
  27.4 5.4 %collective-permute-start.9 = (bf16[256,256]{1,0:T(8,128)(2,1)S(1)}, bf16[256,256]{1,0:T(8,128)(2,1)S(1)}, u32[]{:S(2)}, u32[]{:S(2)}) collective-permute-start(bf16[256,256]{1,0:T(8,128)(2,1)S(1)} %get-tuple-element.15), channel_id=1, source_target_pairs={{0,4},{4,8},{8,12},{1,5},{5,9},{9,13},{2,6},{6,10},{10,14},{3,7},{... | collective-permute-start | bytes 393224 | tf_op jit(solution)/shard_map/ppermute | solution.py:159
  32.8 1.9 %collective-permute-start.8 = (bf16[256,256]{1,0:T(8,128)(2,1)S(1)}, bf16[256,256]{1,0:T(8,128)(2,1)}, u32[]{:S(2)}, u32[]{:S(2)}) collective-permute-start(bf16[256,256]{1,0:T(8,128)(2,1)S(1)} %get-tuple-element.15), channel_id=1, source_target_pairs={{0,12},{1,13},{2,14},{3,15},{16,28},{17,29},{18,30},{19,31}} | collective-permute-start | bytes 393224 | tf_op jit(solution)/shard_map/ppermute | solution.py:150
  34.7 1.3 %collective-permute-start.13 = (bf16[256,256]{1,0:T(8,128)(2,1)S(1)}, bf16[256,256]{1,0:T(8,128)(2,1)S(1)}, u32[]{:S(2)}, u32[]{:S(2)}) collective-permute-start(bf16[256,256]{1,0:T(8,128)(2,1)S(1)} %get-tuple-element.15), channel_id=1, source_target_pairs={{12,0},{13,1},{14,2},{15,3},{28,16},{29,17},{30,18},{31,19}} | collective-permute-start | bytes 393224 | tf_op jit(solution)/shard_map/ppermute | solution.py:151
  36.0 0.0 collective-permute-done.6
  36.1 0.0 collective-permute-done.10
  36.1 0.6 collective-permute-done.9
  36.7 0.7 %collective-permute-start.11 = (bf16[256,256]{1,0:T(8,128)(2,1)S(1)}, bf16[256,256]{1,0:T(8,128)(2,1)S(1)}, u32[]{:S(2)}, u32[]{:S(2)}) collective-permute-start(bf16[256,256]{1,0:T(8,128)(2,1)S(1)} %collective-permute-done.9), channel_id=1, source_target_pairs={{4,8},{8,12},{5,9},{9,13},{6,10},{10,14},{7,11},{11,15},{20,24},{2... | collective-permute-start | bytes 393224 | tf_op jit(solution)/shard_map/ppermute | solution.py:159
  37.3 1.7 %collective-permute-done.8 = bf16[256,256]{1,0:T(8,128)(2,1)} collective-permute-done((bf16[256,256]{1,0:T(8,128)(2,1)S(1)}, bf16[256,256]{1,0:T(8,128)(2,1)}, u32[]{:S(2)}, u32[]{:S(2)}) %collective-permute-start.8) | collective-permute-done | bytes 131104 | tf_op jit(solution)/shard_map/ppermute | solution.py:150
  39.0 0.9 %bitcast_dynamic-update-slice_fusion.13 = bf16[7,256,256]{2,1,0:T(8,128)(2,1)S(1)} fusion(bf16[256,256]{1,0:T(8,128)(2,1)} %collective-permute-done.8), kind=kLoop, calls=%fused_computation.27 | loop fusion | bytes 262144
  39.9 1.6 %collective-permute-start.7 = (bf16[288,256]{1,0:T(8,128)(2,1)S(1)}, bf16[288,256]{1,0:T(8,128)(2,1)S(1)}, u32[]{:S(2)}, u32[]{:S(2)}) collective-permute-start(bf16[288,256]{1,0:T(8,128)(2,1)S(1)} %fusion.2), channel_id=1, source_target_pairs={{0,2},{2,0},{1,3},{3,1},{4,6},{6,4},{5,7},{7,5},{8,10},{10,8},{9,1... | collective-permute-start | bytes 442376 | tf_op jit(solution)/shard_map/ppermute | solution.py:236
  41.5 1.3 %collective-permute-start.12 = (bf16[256,256]{1,0:T(8,128)(2,1)S(1)}, bf16[256,256]{1,0:T(8,128)(2,1)S(1)}, u32[]{:S(2)}, u32[]{:S(2)}) collective-permute-start(bf16[256,256]{1,0:T(8,128)(2,1)S(1)} %collective-permute-done.10), channel_id=1, source_target_pairs={{4,0},{8,4},{5,1},{9,5},{6,2},{10,6},{7,3},{11,7},{20,16},{24,20},... | collective-permute-start | bytes 393224 | tf_op jit(solution)/shard_map/ppermute | solution.py:160
  42.8 0.0 collective-permute-done.11
  42.9 9.6 %collective-permute-done.12 = bf16[256,256]{1,0:T(8,128)(2,1)S(1)} collective-permute-done((bf16[256,256]{1,0:T(8,128)(2,1)S(1)}, bf16[256,256]{1,0:T(8,128)(2,1)S(1)}, u32[]{:S(2)}, u32[]{:S(2)}) %collective-permute-start.12) | collective-permute-done | bytes 131104 | tf_op jit(solution)/shard_map/ppermute | solution.py:160
  52.4 0.0 collective-permute-done.13
  52.5 0.0 collective-permute-done.7
  52.5 0.0 copy-start.2
  52.5 2.3 %shard_map.65 = (bf16[2,288,256]{2,1,0:T(8,128)(2,1)S(1)}, bf16[2,288,256]{2,1,0:T(8,128)(2,1)S(1)}) custom-call(s32[16]{0:T(128)S(1)} %reshape_squeeze.11.pairs_ref, s32[1]{0:T(128)} %bitcast.65.count_ref, s32[2]{0:T(128)S(1)} %pad_add_fusion.place_ref, bf16[8,256,256]{2,1,0:T(8,128)(2,1)S(1)} %bitcast.68, ...), custom_call_target="tpu_custom_call" | custom-call | tf_op jit(solution)/shard_map/pallas_call | solution.py:100
  54.8 0.0 copy-done.2
  54.8 0.1 collective-permute-start.14
  54.9 1.0 %bitcast_add_fusion.1 = f32[288,256]{1,0:T(8,128)S(1)} fusion(bf16[288,256]{1,0:T(8,128)(2,1)} %copy-done.2, bf16[2,288,256]{2,1,0:T(8,128)(2,1)S(1)} %collective-permute-done.6, s32[]{:T(128)S(6)} %select_n.13, bf16[2,288,256]{2,1,0:T(8,128)(2,1)S(1)} %get-tuple-element.13), kind=kLoop, calls=%fused_computation.3 | loop fusion | flops 368640 | bytes 737284 | tf_op jit(solution)/shard_map/add | solution.py:249
  55.8 0.6 collective-permute-done.14
  56.5 0.2 collective-permute-start.15
  56.7 0.2 fusion.1
  56.9 5.5 %collective-permute-done.15 = bf16[288,256]{1,0:T(8,128)(2,1)S(1)} collective-permute-done((bf16[288,256]{1,0:T(8,128)(2,1)S(1)}, bf16[288,256]{1,0:T(8,128)(2,1)S(1)}, u32[]{:S(2)}, u32[]{:S(2)}) %collective-permute-start.15) | collective-permute-done | bytes 147488 | tf_op jit(solution)/shard_map/ppermute | solution.py:236
  62.4 0.1 bitcast_add_fusion
  62.5 0.2 fusion
  62.7 0.7 %pad_maximum_fusion = bf16[256,512]{1,0:T(8,128)(2,1)} fusion(bf16[256,256]{1,0:T(8,128)(2,1)S(1)} %fusion, bf16[256,256]{1,0:T(8,128)(2,1)S(1)} %fusion.1), kind=kLoop, calls=%fused_computation.10 | loop fusion | flops 524288 | bytes 524288 | tf_op jit(solution)/shard_map/concatenate | solution.py:254
  (19 shorter events, 0.3 us)
Async XLA Ops:
  0.0 1.0 %copy-start.1 = (bf16[1,32,256]{2,1,0:T(8,128)(2,1)S(1)}, bf16[1,32,256]{2,1,0:T(8,128)(2,1)}, u32[]{:S(2)}) copy-start(bf16[1,32,256]{2,1,0:T(8,128)(2,1)} %param.7) | copy-start | bytes 49156
  1.0 12.6 %copy-start.3 = (bf16[1,1,128,128]{3,2,1,0:T(8,128)(2,1)S(1)}, bf16[1,1,128,128]{3,2,1,0:T(8,128)(2,1)}, u32[]{:S(2)}) copy-start(bf16[1,1,128,128]{3,2,1,0:T(8,128)(2,1)} %param.11) | copy-start | bytes 98308
  1.0 13.0 %collective-permute-start.1 = (bf16[288,256]{1,0:T(8,128)(2,1)S(1)}, bf16[288,256]{1,0:T(8,128)(2,1)S(1)}, u32[]{:S(2)}, u32[]{:S(2)}) collective-permute-start(bf16[288,256]{1,0:T(8,128)(2,1)S(1)} %pad_maximum_fusion.1), channel_id=1, source_target_pairs={{0,4},{4,8},{8,12},{1,5},{5,9},{9,13},{2,6},{6,10},{10,14},{3,7},{... | collective-permute-start | bytes 442376 | tf_op jit(solution)/shard_map/ppermute | solution.py:159
  6.0 11.8 %collective-permute-start = (bf16[288,256]{1,0:T(8,128)(2,1)S(1)}, bf16[288,256]{1,0:T(8,128)(2,1)S(1)}, u32[]{:S(2)}, u32[]{:S(2)}) collective-permute-start(bf16[288,256]{1,0:T(8,128)(2,1)S(1)} %pad_maximum_fusion.1), channel_id=1, source_target_pairs={{0,12},{1,13},{2,14},{3,15},{16,28},{17,29},{18,30},{19,31}} | collective-permute-start | bytes 442376 | tf_op jit(solution)/shard_map/ppermute | solution.py:150
  9.3 7.2 %collective-permute-start.3 = (bf16[288,256]{1,0:T(8,128)(2,1)S(1)}, bf16[288,256]{1,0:T(8,128)(2,1)S(1)}, u32[]{:S(2)}, u32[]{:S(2)}) collective-permute-start(bf16[288,256]{1,0:T(8,128)(2,1)S(1)} %pad_maximum_fusion.1), channel_id=1, source_target_pairs={{4,0},{8,4},{12,8},{5,1},{9,5},{13,9},{6,2},{10,6},{14,10},{7,3},{... | collective-permute-start | bytes 442376 | tf_op jit(solution)/shard_map/ppermute | solution.py:160
  10.6 13.0 %collective-permute-start.5 = (bf16[288,256]{1,0:T(8,128)(2,1)S(1)}, bf16[288,256]{1,0:T(8,128)(2,1)S(1)}, u32[]{:S(2)}, u32[]{:S(2)}) collective-permute-start(bf16[288,256]{1,0:T(8,128)(2,1)S(1)} %pad_maximum_fusion.1), channel_id=1, source_target_pairs={{12,0},{13,1},{14,2},{15,3},{28,16},{29,17},{30,18},{31,19}} | collective-permute-start | bytes 442376 | tf_op jit(solution)/shard_map/ppermute | solution.py:151
  12.6 0.7 %copy-start.4 = (s32[1,1,8,2]{2,3,1,0:T(2,128)S(1)}, s32[1,1,8,2]{2,3,1,0:T(2,128)}, u32[]{:S(2)}) copy-start(s32[1,1,8,2]{2,3,1,0:T(2,128)} %param.9) | copy-start | bytes 196
  13.8 9.8 %copy-start = (bf16[1,1,8,256,256]{4,3,2,1,0:T(8,128)(2,1)S(1)}, bf16[1,1,8,256,256]{4,3,2,1,0:T(8,128)(2,1)}, u32[]{:S(2)}) copy-start(bf16[1,1,8,256,256]{4,3,2,1,0:T(8,128)(2,1)} %param.8) | copy-start | bytes 3145732
  14.1 3.8 %collective-permute-start.2 = (bf16[288,256]{1,0:T(8,128)(2,1)S(1)}, bf16[288,256]{1,0:T(8,128)(2,1)S(1)}, u32[]{:S(2)}, u32[]{:S(2)}) collective-permute-start(bf16[288,256]{1,0:T(8,128)(2,1)S(1)} %collective-permute-done.1), channel_id=1, source_target_pairs={{4,8},{8,12},{5,9},{9,13},{6,10},{10,14},{7,11},{11,15},{20,24},{2... | collective-permute-start | bytes 442376 | tf_op jit(solution)/shard_map/ppermute | solution.py:159
  16.6 7.0 %collective-permute-start.4 = (bf16[288,256]{1,0:T(8,128)(2,1)S(1)}, bf16[288,256]{1,0:T(8,128)(2,1)S(1)}, u32[]{:S(2)}, u32[]{:S(2)}) collective-permute-start(bf16[288,256]{1,0:T(8,128)(2,1)S(1)} %collective-permute-done.3), channel_id=1, source_target_pairs={{4,0},{8,4},{5,1},{9,5},{6,2},{10,6},{7,3},{11,7},{20,16},{24,20},... | collective-permute-start | bytes 442376 | tf_op jit(solution)/shard_map/ppermute | solution.py:160
  26.0 10.1 %collective-permute-start.6 = (bf16[2,288,256]{2,1,0:T(8,128)(2,1)S(1)}, bf16[2,288,256]{2,1,0:T(8,128)(2,1)S(1)}, u32[]{:S(2)}, u32[]{:S(2)}) collective-permute-start(bf16[2,288,256]{2,1,0:T(8,128)(2,1)S(1)} %get-tuple-element.14), channel_id=1, source_target_pairs={{0,1},{1,0},{2,3},{3,2},{4,5},{5,4},{6,7},{7,6},{8,9},{9,8},{10,11... | collective-permute-start | bytes 884744 | tf_op jit(solution)/shard_map/ppermute | solution.py:230
  26.1 10.0 %collective-permute-start.10 = (bf16[256,256]{1,0:T(8,128)(2,1)S(1)}, bf16[256,256]{1,0:T(8,128)(2,1)S(1)}, u32[]{:S(2)}, u32[]{:S(2)}) collective-permute-start(bf16[256,256]{1,0:T(8,128)(2,1)S(1)} %get-tuple-element.15), channel_id=1, source_target_pairs={{4,0},{8,4},{12,8},{5,1},{9,5},{13,9},{6,2},{10,6},{14,10},{7,3},{... | collective-permute-start | bytes 393224 | tf_op jit(solution)/shard_map/ppermute | solution.py:160
  27.4 9.3 %collective-permute-start.9 = (bf16[256,256]{1,0:T(8,128)(2,1)S(1)}, bf16[256,256]{1,0:T(8,128)(2,1)S(1)}, u32[]{:S(2)}, u32[]{:S(2)}) collective-permute-start(bf16[256,256]{1,0:T(8,128)(2,1)S(1)} %get-tuple-element.15), channel_id=1, source_target_pairs={{0,4},{4,8},{8,12},{1,5},{5,9},{9,13},{2,6},{6,10},{10,14},{3,7},{... | collective-permute-start | bytes 393224 | tf_op jit(solution)/shard_map/ppermute | solution.py:159
  32.8 6.2 %collective-permute-start.8 = (bf16[256,256]{1,0:T(8,128)(2,1)S(1)}, bf16[256,256]{1,0:T(8,128)(2,1)}, u32[]{:S(2)}, u32[]{:S(2)}) collective-permute-start(bf16[256,256]{1,0:T(8,128)(2,1)S(1)} %get-tuple-element.15), channel_id=1, source_target_pairs={{0,12},{1,13},{2,14},{3,15},{16,28},{17,29},{18,30},{19,31}} | collective-permute-start | bytes 393224 | tf_op jit(solution)/shard_map/ppermute | solution.py:150
  34.7 17.7 %collective-permute-start.13 = (bf16[256,256]{1,0:T(8,128)(2,1)S(1)}, bf16[256,256]{1,0:T(8,128)(2,1)S(1)}, u32[]{:S(2)}, u32[]{:S(2)}) collective-permute-start(bf16[256,256]{1,0:T(8,128)(2,1)S(1)} %get-tuple-element.15), channel_id=1, source_target_pairs={{12,0},{13,1},{14,2},{15,3},{28,16},{29,17},{30,18},{31,19}} | collective-permute-start | bytes 393224 | tf_op jit(solution)/shard_map/ppermute | solution.py:151
  36.7 6.1 %collective-permute-start.11 = (bf16[256,256]{1,0:T(8,128)(2,1)S(1)}, bf16[256,256]{1,0:T(8,128)(2,1)S(1)}, u32[]{:S(2)}, u32[]{:S(2)}) collective-permute-start(bf16[256,256]{1,0:T(8,128)(2,1)S(1)} %collective-permute-done.9), channel_id=1, source_target_pairs={{4,8},{8,12},{5,9},{9,13},{6,10},{10,14},{7,11},{11,15},{20,24},{2... | collective-permute-start | bytes 393224 | tf_op jit(solution)/shard_map/ppermute | solution.py:159
  39.9 12.5 %collective-permute-start.7 = (bf16[288,256]{1,0:T(8,128)(2,1)S(1)}, bf16[288,256]{1,0:T(8,128)(2,1)S(1)}, u32[]{:S(2)}, u32[]{:S(2)}) collective-permute-start(bf16[288,256]{1,0:T(8,128)(2,1)S(1)} %fusion.2), channel_id=1, source_target_pairs={{0,2},{2,0},{1,3},{3,1},{4,6},{6,4},{5,7},{7,5},{8,10},{10,8},{9,1... | collective-permute-start | bytes 442376 | tf_op jit(solution)/shard_map/ppermute | solution.py:236
  41.5 10.9 %collective-permute-start.12 = (bf16[256,256]{1,0:T(8,128)(2,1)S(1)}, bf16[256,256]{1,0:T(8,128)(2,1)S(1)}, u32[]{:S(2)}, u32[]{:S(2)}) collective-permute-start(bf16[256,256]{1,0:T(8,128)(2,1)S(1)} %collective-permute-done.10), channel_id=1, source_target_pairs={{4,0},{8,4},{5,1},{9,5},{6,2},{10,6},{7,3},{11,7},{20,16},{24,20},... | collective-permute-start | bytes 393224 | tf_op jit(solution)/shard_map/ppermute | solution.py:160
  52.5 2.3 %copy-start.2 = (bf16[288,256]{1,0:T(8,128)(2,1)}, bf16[288,256]{1,0:T(8,128)(2,1)S(1)}, u32[]{:S(2)}) copy-start(bf16[288,256]{1,0:T(8,128)(2,1)S(1)} %collective-permute-done.7) | copy-start | bytes 442372
  54.8 1.6 %collective-permute-start.14 = (bf16[2,288,256]{2,1,0:T(8,128)(2,1)S(1)}, bf16[2,288,256]{2,1,0:T(8,128)(2,1)S(1)}, u32[]{:S(2)}, u32[]{:S(2)}) collective-permute-start(bf16[2,288,256]{2,1,0:T(8,128)(2,1)S(1)} %get-tuple-element.20), channel_id=1, source_target_pairs={{0,1},{1,0},{2,3},{3,2},{4,5},{5,4},{6,7},{7,6},{8,9},{9,8},{10,11... | collective-permute-start | bytes 884744 | tf_op jit(solution)/shard_map/ppermute | solution.py:230
  56.5 6.0 %collective-permute-start.15 = (bf16[288,256]{1,0:T(8,128)(2,1)S(1)}, bf16[288,256]{1,0:T(8,128)(2,1)S(1)}, u32[]{:S(2)}, u32[]{:S(2)}) collective-permute-start(bf16[288,256]{1,0:T(8,128)(2,1)S(1)} %fusion.3), channel_id=1, source_target_pairs={{0,2},{2,0},{1,3},{3,1},{4,6},{6,4},{5,7},{7,5},{8,10},{10,8},{9,1... | collective-permute-start | bytes 442376 | tf_op jit(solution)/shard_map/ppermute | solution.py:236

commit v15 on v11

--- a/solution.py
+++ b/solution.py
@@ -7,7 +7,16 @@
 
 
 def _near_far_kernel(
-    pairs_ref, count_ref, place_ref, tiles_ref, stack_ref, masked_ref, mine_ref, theirs_ref, acc_ref
+    pairs_ref,
+    count_ref,
+    place_ref,
+    tiles_ref,
+    stack_ref,
+    packed_ref,
+    masked_ref,
+    mine_ref,
+    theirs_ref,
+    acc_ref,
 ):
     inner_count, width, rhs_count = acc_ref.shape
     slot_count = tiles_ref.shape[0]
@@ -33,9 +42,9 @@
 
     coeffs = jnp.zeros((inner_count * rank_size, rhs_count), jnp.float32)
     for source in range(tgt_count):
-        block = stack_ref[source - own_tgt + tgt_count - 1]
-        dens = block[:width, :]
-        packed = block[width:, :]
+        offset = source - own_tgt + tgt_count - 1
+        dens = stack_ref[offset]
+        packed = packed_ref[offset]
         top = jnp.dot(packed[:, :width], dens, preferred_element_type=jnp.float32)
         bottom = jnp.dot(packed[:, width:], dens, preferred_element_type=jnp.float32)
         projected = jnp.concatenate([top, bottom], axis=0).astype(jnp.bfloat16)
@@ -58,7 +67,7 @@
         write(theirs_ref, mine_ref)
 
 
-def _near_far(pairs_flat, count, place, tiles, stack, masked_t, inner_count, rank_size):
+def _near_far(pairs_flat, count, place, tiles, stack, packed, masked_t, inner_count, rank_size):
     slot_count, width, _ = tiles.shape
     stack_count, rows, rhs_count = stack.shape
     half_count = inner_count // 2
@@ -70,6 +79,7 @@
         in_specs=[
             pl.BlockSpec(tiles.shape, whole),
             pl.BlockSpec(stack.shape, whole),
+            pl.BlockSpec(packed.shape, whole),
             pl.BlockSpec(masked_t.shape, whole),
         ],
         out_specs=[
@@ -82,6 +92,7 @@
     block_bytes = 2 * (
         tiles.size * tiles.dtype.itemsize
         + stack.size * stack.dtype.itemsize
+        + packed.size * packed.dtype.itemsize
         + masked_t.size * masked_t.dtype.itemsize
         + 2 * half_count * out_rows * rhs_count * 2
     )
@@ -93,7 +104,7 @@
         compiler_params=pltpu.CompilerParams(
             dimension_semantics=("arbitrary",), vmem_limit_bytes=int(vmem_bytes)
         ),
-    )(pairs_flat, count, place, tiles, stack, masked_t)
+    )(pairs_flat, count, place, tiles, stack, packed, masked_t)
 
 
 def _epilogue_kernel(me_ref, basis_t_ref, *refs):
@@ -148,7 +159,8 @@
     if far_up is not None:
         ups.append(far_up)
         downs.append(far_down)
-    return jnp.stack(ups[::-1] + [payload] + downs)
+    order = ups[::-1] + [payload] + downs
+    return tuple(jnp.stack(parts) for parts in zip(*order))
 
 
 def _ring_reduce_scatter(blocks, axis):
@@ -175,8 +187,7 @@
     basis = cluster_basis[0]
     half_rank = rank_size // 2
     packed = jnp.concatenate([basis[:half_rank], basis[half_rank:]], axis=1)
-    payload = jnp.concatenate([density, packed], axis=0)
-    stack = _line_gather(payload, "tgt")
+    stack, packed_stack = _line_gather((density, packed), "tgt")
 
     pair_list = near_pairs[0, 0]
     live_count = near_count[0, 0]
@@ -196,7 +207,8 @@
 
     place = jnp.stack([lax.axis_index("tgt"), lax.axis_index("sub")]).astype(jnp.int32)
     mine, theirs = _near_far(
-        pair_list.reshape(-1), live_count.reshape(1), place, near_blocks[0, 0], stack, masked_t,
+        pair_list.reshape(-1), live_count.reshape(1), place, near_blocks[0, 0], stack, packed_stack,
+        masked_t,
         inner_count, rank_size,
     )
     arrived = lax.ppermute(theirs, "sub", [(0, 1), (1, 0)])

time: 50.9 us -> 65.1 us (1.28)
  starting transfers between devices: 14.2 us -> 26 us
  waiting for transfers between devices: 26.5 us -> 30 us
  other arithmetic: 2.21 us -> 1.23 us
    ppermute x1 -> x2, starting transfers between devices: 3.32 us -> 11.6 us  [_line_gather(): far_up = lax.ppermute(payload, axis, [(0, n - 1)])]
    ppermute x1 -> x2, waiting for transfers between devices: 0.01 us -> 5.53 us  [_line_gather(): far_down = lax.ppermute(payload, axis, [(n - 1, 0)])]
    ppermute x2 -> x4, starting transfers between devices: 2.57 us -> 5.3 us  [_line_gather(): down = lax.ppermute(down, axis, down_pairs)]
    ppermute x2 -> x4, starting transfers between devices: 5.65 us -> 3.94 us  [_line_gather(): up = lax.ppermute(up, axis, up_pairs)]
    ppermute x2 -> x4, waiting for transfers between devices: 16.7 us -> 15.2 us  [_line_gather(): down = lax.ppermute(down, axis, down_pairs)]
    ppermute x1 -> x2, starting transfers between devices: 1.29 us -> 2.56 us  [_line_gather(): far_down = lax.ppermute(payload, axis, [(n - 1, 0)])]
    ppermute x1, starting transfers between devices: 1.29 us -> 2.51 us  [on_device(): back = lax.ppermute(send, 'inner', [(0, 1), (1, 0)])]
    concatenate x1, other arithmetic: 0.97 us -> 0.01 us  [on_device(): packed = jnp.concatenate([basis[:half_rank], basis[half_rank:]], axis=1)]
  transfers between devices with their start and end apart: 8 -> 14, of which waited for: 4 -> 6; matrix products, arithmetic and copies ran while one was open for 6% -> 6% of each run, Pallas kernels for 0% -> 0%
where the time goes in v15:
time: 65.1 us; the launch traced here: 64.6 us
  waiting for transfers between devices  30 us (46%)
  starting transfers between devices  26 us (40%)
  local copies, waits for them, and re-layouts  2.79 us (4%)
  Pallas kernels  2.56 us (4%)
  other arithmetic  1.23 us (2%)
  between operations  0.99 us (2%)
  matrix products  0.97 us (1%)
    ppermute x4, waiting for transfers between devices, _line_gather(): down = lax.ppermute(down, axis, down_pairs)  15.2 us
    ppermute x2, starting transfers between devices, _line_gather(): far_up = lax.ppermute(payload, axis, [(0, n - 1)])  11.6 us
    ppermute x1, waiting for transfers between devices, on_device(): back = lax.ppermute(send, 'inner', [(0, 1), (1, 0)])  7.31 us
    ppermute x2, waiting for transfers between devices, _line_gather(): far_down = lax.ppermute(payload, axis, [(n - 1, 0)])  5.53 us
    ppermute x4, starting transfers between devices, _line_gather(): down = lax.ppermute(down, axis, down_pairs)  5.3 us
    ppermute x4, starting transfers between devices, _line_gather(): up = lax.ppermute(up, axis, up_pairs)  3.94 us
    ppermute x2, starting transfers between devices, _line_gather(): far_down = lax.ppermute(payload, axis, [(n - 1, 0)])  2.56 us
    pallas_call x1, Pallas kernels, _near_far(): pl.pallas_call(_near_far_kernel, grid_spec=grid_spec, out_shape=[out, out...  2.56 us
  transfers between devices with their start and end apart: 14, of which 6 were waited for; matrix products, arithmetic and copies ran while one was open for 6% of the time, Pallas kernels for 0%

profile of v15, /device:TPU:0, one launch (start us, length us, event | category | flops | bytes accessed | tf_op | source)
XLA Modules:
  0.0 64.6 jit_solution(15586528881233257248)
XLA Ops:
  0.0 0.0 copy-start.1
  0.0 7.1 %collective-permute-start = (bf16[256,512]{1,0:T(8,128)(2,1)}, bf16[256,512]{1,0:T(8,128)(2,1)S(1)}, u32[]{:S(2)}, u32[]{:S(2)}) collective-permute-start(bf16[256,512]{1,0:T(8,128)(2,1)} %param.6), channel_id=1, source_target_pairs={{0,12},{1,13},{2,14},{3,15},{16,28},{17,29},{18,30},{19,31}} | collective-permute-start | bytes 786440 | tf_op jit(solution)/shard_map/ppermute | solution.py:148
  7.1 1.3 %collective-permute-start.1 = (bf16[256,512]{1,0:T(8,128)(2,1)}, bf16[256,512]{1,0:T(8,128)(2,1)S(1)}, u32[]{:S(2)}, u32[]{:S(2)}) collective-permute-start(bf16[256,512]{1,0:T(8,128)(2,1)} %param.6), channel_id=1, source_target_pairs={{0,4},{4,8},{8,12},{1,5},{5,9},{9,13},{2,6},{6,10},{10,14},{3,7},{... | collective-permute-start | bytes 786440 | tf_op jit(solution)/shard_map/ppermute | solution.py:155
  8.4 1.3 %collective-permute-start.3 = (bf16[256,512]{1,0:T(8,128)(2,1)}, bf16[256,512]{1,0:T(8,128)(2,1)S(1)}, u32[]{:S(2)}, u32[]{:S(2)}) collective-permute-start(bf16[256,512]{1,0:T(8,128)(2,1)} %param.6), channel_id=1, source_target_pairs={{4,0},{8,4},{12,8},{5,1},{9,5},{13,9},{6,2},{10,6},{14,10},{7,3},{... | collective-permute-start | bytes 786440 | tf_op jit(solution)/shard_map/ppermute | solution.py:156
  9.7 0.7 %slice_bitcast_fusion.1 = (bf16[16,256]{1,0:T(8,128)(2,1)S(1)}, bf16[16,256]{1,0:T(8,128)(2,1)S(1)}) fusion(bf16[1,32,256]{2,1,0:T(8,128)(2,1)} %param.7), kind=kLoop, calls=%fused_computation.25 | loop fusion | bytes 32768 | tf_op jit(solution)/shard_map/slice | solution.py:189
  10.5 4.5 %collective-permute-start.6 = (bf16[16,512]{1,0:T(8,128)(2,1)S(1)}, bf16[16,512]{1,0:T(8,128)(2,1)S(1)}, u32[]{:S(2)}, u32[]{:S(2)}) collective-permute-start(bf16[16,512]{1,0:T(8,128)(2,1)S(1)} %pad_maximum_fusion), channel_id=1, source_target_pairs={{0,12},{1,13},{2,14},{3,15},{16,28},{17,29},{18,30},{19,31}} | collective-permute-start | bytes 49160 | tf_op jit(solution)/shard_map/ppermute | solution.py:148
  15.0 1.3 %collective-permute-start.7 = (bf16[16,512]{1,0:T(8,128)(2,1)S(1)}, bf16[16,512]{1,0:T(8,128)(2,1)S(1)}, u32[]{:S(2)}, u32[]{:S(2)}) collective-permute-start(bf16[16,512]{1,0:T(8,128)(2,1)S(1)} %pad_maximum_fusion), channel_id=1, source_target_pairs={{0,4},{4,8},{8,12},{1,5},{5,9},{9,13},{2,6},{6,10},{10,14},{3,7},{... | collective-permute-start | bytes 49160 | tf_op jit(solution)/shard_map/ppermute | solution.py:155
  17.0 0.9 %reshape_squeeze.11 = bf16[4,32,4,32]{3,2,1,0:T(4,128)(2,1)S(1)} reshape(bf16[1,1,128,128]{3,2,1,0:T(8,128)(2,1)} %param.11) | data formatting | bytes 65536 | tf_op jit(solution)/shard_map/reshape;squeeze | solution.py:205
  17.8 0.8 %add_bitcast_fusion = s32[8]{0:T(128)S(1)} fusion(s32[8,2]{0,1:T(2,128)} %bitcast.62), kind=kLoop, calls=%fused_computation.32 | loop fusion | flops 16 | bytes 96 | tf_op jit(solution)/shard_map/eq | solution.py:197
  18.6 0.1 fusion.4
  18.7 0.1 convert_element_type.51
  18.8 0.1 copy.16
  18.9 0.1 copy_multiply_fusion
  19.0 0.1 pad_add_fusion.place_ref
  19.1 0.8 %copy.15 = s32[1,1,8,2]{3,2,1,0:T(8,128)S(1)} copy(s32[1,1,8,2]{2,3,1,0:T(2,128)} %param.9) | data formatting | bytes 128 | tf_op args[3]
  19.8 0.1 reshape_squeeze.9.pairs_ref
  19.9 0.0 collective-permute-done.6
  19.9 1.3 %collective-permute-start.9 = (bf16[16,512]{1,0:T(8,128)(2,1)S(1)}, bf16[16,512]{1,0:T(8,128)(2,1)S(1)}, u32[]{:S(2)}, u32[]{:S(2)}) collective-permute-start(bf16[16,512]{1,0:T(8,128)(2,1)S(1)} %pad_maximum_fusion), channel_id=1, source_target_pairs={{4,0},{8,4},{12,8},{5,1},{9,5},{13,9},{6,2},{10,6},{14,10},{7,3},{... | collective-permute-start | bytes 49160 | tf_op jit(solution)/shard_map/ppermute | solution.py:156
  21.2 0.0 collective-permute-done.7
  21.2 0.7 %collective-permute-start.8 = (bf16[16,512]{1,0:T(8,128)(2,1)S(1)}, bf16[16,512]{1,0:T(8,128)(2,1)S(1)}, u32[]{:S(2)}, u32[]{:S(2)}) collective-permute-start(bf16[16,512]{1,0:T(8,128)(2,1)S(1)} %collective-permute-done.7), channel_id=1, source_target_pairs={{4,8},{8,12},{5,9},{9,13},{6,10},{10,14},{7,11},{11,15},{20,24},{2... | collective-permute-start | bytes 49160 | tf_op jit(solution)/shard_map/ppermute | solution.py:155
  21.9 3.6 %collective-permute-done.9 = bf16[16,512]{1,0:T(8,128)(2,1)S(1)} collective-permute-done((bf16[16,512]{1,0:T(8,128)(2,1)S(1)}, bf16[16,512]{1,0:T(8,128)(2,1)S(1)}, u32[]{:S(2)}, u32[]{:S(2)}) %collective-permute-start.9) | collective-permute-done | bytes 16416 | tf_op jit(solution)/shard_map/ppermute | solution.py:156
  25.5 1.3 %collective-permute-start.5 = (bf16[256,512]{1,0:T(8,128)(2,1)}, bf16[256,512]{1,0:T(8,128)(2,1)S(1)}, u32[]{:S(2)}, u32[]{:S(2)}) collective-permute-start(bf16[256,512]{1,0:T(8,128)(2,1)} %param.6), channel_id=1, source_target_pairs={{12,0},{13,1},{14,2},{15,3},{28,16},{29,17},{30,18},{31,19}} | collective-permute-start | bytes 786440 | tf_op jit(solution)/shard_map/ppermute | solution.py:149
  26.8 0.0 collective-permute-done.8
  26.8 1.3 %collective-permute-start.10 = (bf16[16,512]{1,0:T(8,128)(2,1)S(1)}, bf16[16,512]{1,0:T(8,128)(2,1)S(1)}, u32[]{:S(2)}, u32[]{:S(2)}) collective-permute-start(bf16[16,512]{1,0:T(8,128)(2,1)S(1)} %collective-permute-done.9), channel_id=1, source_target_pairs={{4,0},{8,4},{5,1},{9,5},{6,2},{10,6},{7,3},{11,7},{20,16},{24,20},... | collective-permute-start | bytes 49160 | tf_op jit(solution)/shard_map/ppermute | solution.py:156
  28.2 4.7 %collective-permute-done.10 = bf16[16,512]{1,0:T(8,128)(2,1)S(1)} collective-permute-done((bf16[16,512]{1,0:T(8,128)(2,1)S(1)}, bf16[16,512]{1,0:T(8,128)(2,1)S(1)}, u32[]{:S(2)}, u32[]{:S(2)}) %collective-permute-start.10) | collective-permute-done | bytes 16416 | tf_op jit(solution)/shard_map/ppermute | solution.py:156
  32.9 1.3 %collective-permute-start.11 = (bf16[16,512]{1,0:T(8,128)(2,1)S(1)}, bf16[16,512]{1,0:T(8,128)(2,1)S(1)}, u32[]{:S(2)}, u32[]{:S(2)}) collective-permute-start(bf16[16,512]{1,0:T(8,128)(2,1)S(1)} %pad_maximum_fusion), channel_id=1, source_target_pairs={{12,0},{13,1},{14,2},{15,3},{28,16},{29,17},{30,18},{31,19}} | collective-permute-start | bytes 49160 | tf_op jit(solution)/shard_map/ppermute | solution.py:149
  34.2 0.0 collective-permute-done.1
  34.2 0.7 %collective-permute-start.2 = (bf16[256,512]{1,0:T(8,128)(2,1)S(1)}, bf16[256,512]{1,0:T(8,128)(2,1)S(1)}, u32[]{:S(2)}, u32[]{:S(2)}) collective-permute-start(bf16[256,512]{1,0:T(8,128)(2,1)S(1)} %collective-permute-done.1), channel_id=1, source_target_pairs={{4,8},{8,12},{5,9},{9,13},{6,10},{10,14},{7,11},{11,15},{20,24},{2... | collective-permute-start | bytes 786440 | tf_op jit(solution)/shard_map/ppermute | solution.py:155
  34.9 5.5 %collective-permute-done.11 = bf16[16,512]{1,0:T(8,128)(2,1)S(1)} collective-permute-done((bf16[16,512]{1,0:T(8,128)(2,1)S(1)}, bf16[16,512]{1,0:T(8,128)(2,1)S(1)}, u32[]{:S(2)}, u32[]{:S(2)}) %collective-permute-start.11) | collective-permute-done | bytes 16416 | tf_op jit(solution)/shard_map/ppermute | solution.py:149
  40.5 0.0 copy-start
  40.5 0.0 collective-permute-done.3
  40.5 1.4 %collective-permute-start.4 = (bf16[256,512]{1,0:T(8,128)(2,1)S(1)}, bf16[256,512]{1,0:T(8,128)(2,1)S(1)}, u32[]{:S(2)}, u32[]{:S(2)}) collective-permute-start(bf16[256,512]{1,0:T(8,128)(2,1)S(1)} %collective-permute-done.3), channel_id=1, source_target_pairs={{4,0},{8,4},{5,1},{9,5},{6,2},{10,6},{7,3},{11,7},{20,16},{24,20},... | collective-permute-start | bytes 786440 | tf_op jit(solution)/shard_map/ppermute | solution.py:156
  41.9 0.0 collective-permute-done
  41.9 0.0 collective-permute-done.2
  42.0 0.0 copy-done.1
  42.1 6.8 %collective-permute-done.4 = bf16[256,512]{1,0:T(8,128)(2,1)S(1)} collective-permute-done((bf16[256,512]{1,0:T(8,128)(2,1)S(1)}, bf16[256,512]{1,0:T(8,128)(2,1)S(1)}, u32[]{:S(2)}, u32[]{:S(2)}) %collective-permute-start.4) | collective-permute-done | bytes 262176 | tf_op jit(solution)/shard_map/ppermute | solution.py:156
  48.9 0.0 collective-permute-done.5
  48.9 0.0 copy-done
  48.9 2.6 %shard_map.64 = (bf16[2,288,512]{2,1,0:T(8,128)(2,1)S(1)}, bf16[2,288,512]{2,1,0:T(8,128)(2,1)S(1)}) custom-call(s32[16]{0:T(128)S(1)} %reshape_squeeze.9.pairs_ref, s32[1]{0:T(128)} %bitcast.58.count_ref, s32[2]{0:T(128)S(1)} %pad_add_fusion.place_ref, bf16[8,256,256]{2,1,0:T(8,128)(2,1)S(1)} %bitcast.60, ...), custom_call_target="tpu_custom_call" | custom-call | tf_op jit(solution)/shard_map/pallas_call | solution.py:100
  51.5 0.0 copy-start.2
  51.5 0.1 collective-permute-start.12
  51.6 2.0 %collective-permute-done.12 = bf16[2,288,512]{2,1,0:T(8,128)(2,1)S(1)} collective-permute-done((bf16[2,288,512]{2,1,0:T(8,128)(2,1)S(1)}, bf16[2,288,512]{2,1,0:T(8,128)(2,1)S(1)}, u32[]{:S(2)}, u32[]{:S(2)}) %collective-permute-start.12) | collective-permute-done | bytes 589856 | tf_op jit(solution)/shard_map/ppermute | solution.py:214
  53.6 0.1 fusion.1
  53.7 2.5 %collective-permute-start.13 = (bf16[288,512]{1,0:T(8,128)(2,1)S(1)}, bf16[288,512]{1,0:T(8,128)(2,1)S(1)}, u32[]{:S(2)}, u32[]{:S(2)}) collective-permute-start(bf16[288,512]{1,0:T(8,128)(2,1)S(1)} %fusion.1), channel_id=1, source_target_pairs={{0,2},{2,0},{1,3},{3,1},{4,6},{6,4},{5,7},{7,5},{8,10},{10,8},{9,1... | collective-permute-start | bytes 884744 | tf_op jit(solution)/shard_map/ppermute | solution.py:222
  56.2 7.3 %collective-permute-done.13 = bf16[288,512]{1,0:T(8,128)(2,1)S(1)} collective-permute-done((bf16[288,512]{1,0:T(8,128)(2,1)S(1)}, bf16[288,512]{1,0:T(8,128)(2,1)S(1)}, u32[]{:S(2)}, u32[]{:S(2)}) %collective-permute-start.13) | collective-permute-done | bytes 294944 | tf_op jit(solution)/shard_map/ppermute | solution.py:222
  63.5 0.1 bitcast_add_fusion
  63.6 0.0 copy-done.2
  63.6 1.0 %fusion = bf16[256,512]{1,0:T(8,128)(2,1)} fusion(f32[288,512]{1,0:T(8,128)S(1)} %bitcast_add_fusion, bf16[1,32,256]{2,1,0:T(8,128)(2,1)S(1)} %copy-done.2), kind=kOutput, calls=%fused_computation.4 | convolution fusion | flops 8667136 | bytes 868352 | tf_op jit(solution)/shard_map/dot_general | solution.py:234
  (17 shorter events, 0.2 us)
Async XLA Ops:
  0.0 42.0 %copy-start.1 = (bf16[256,512]{1,0:T(8,128)(2,1)S(1)}, bf16[256,512]{1,0:T(8,128)(2,1)}, u32[]{:S(2)}) copy-start(bf16[256,512]{1,0:T(8,128)(2,1)} %param.6) | copy-start | bytes 786436
  0.0 41.9 %collective-permute-start = (bf16[256,512]{1,0:T(8,128)(2,1)}, bf16[256,512]{1,0:T(8,128)(2,1)S(1)}, u32[]{:S(2)}, u32[]{:S(2)}) collective-permute-start(bf16[256,512]{1,0:T(8,128)(2,1)} %param.6), channel_id=1, source_target_pairs={{0,12},{1,13},{2,14},{3,15},{16,28},{17,29},{18,30},{19,31}} | collective-permute-start | bytes 786440 | tf_op jit(solution)/shard_map/ppermute | solution.py:148
  7.1 27.1 %collective-permute-start.1 = (bf16[256,512]{1,0:T(8,128)(2,1)}, bf16[256,512]{1,0:T(8,128)(2,1)S(1)}, u32[]{:S(2)}, u32[]{:S(2)}) collective-permute-start(bf16[256,512]{1,0:T(8,128)(2,1)} %param.6), channel_id=1, source_target_pairs={{0,4},{4,8},{8,12},{1,5},{5,9},{9,13},{2,6},{6,10},{10,14},{3,7},{... | collective-permute-start | bytes 786440 | tf_op jit(solution)/shard_map/ppermute | solution.py:155
  8.4 32.0 %collective-permute-start.3 = (bf16[256,512]{1,0:T(8,128)(2,1)}, bf16[256,512]{1,0:T(8,128)(2,1)S(1)}, u32[]{:S(2)}, u32[]{:S(2)}) collective-permute-start(bf16[256,512]{1,0:T(8,128)(2,1)} %param.6), channel_id=1, source_target_pairs={{4,0},{8,4},{12,8},{5,1},{9,5},{13,9},{6,2},{10,6},{14,10},{7,3},{... | collective-permute-start | bytes 786440 | tf_op jit(solution)/shard_map/ppermute | solution.py:156
  10.5 9.4 %collective-permute-start.6 = (bf16[16,512]{1,0:T(8,128)(2,1)S(1)}, bf16[16,512]{1,0:T(8,128)(2,1)S(1)}, u32[]{:S(2)}, u32[]{:S(2)}) collective-permute-start(bf16[16,512]{1,0:T(8,128)(2,1)S(1)} %pad_maximum_fusion), channel_id=1, source_target_pairs={{0,12},{1,13},{2,14},{3,15},{16,28},{17,29},{18,30},{19,31}} | collective-permute-start | bytes 49160 | tf_op jit(solution)/shard_map/ppermute | solution.py:148
  15.0 6.2 %collective-permute-start.7 = (bf16[16,512]{1,0:T(8,128)(2,1)S(1)}, bf16[16,512]{1,0:T(8,128)(2,1)S(1)}, u32[]{:S(2)}, u32[]{:S(2)}) collective-permute-start(bf16[16,512]{1,0:T(8,128)(2,1)S(1)} %pad_maximum_fusion), channel_id=1, source_target_pairs={{0,4},{4,8},{8,12},{1,5},{5,9},{9,13},{2,6},{6,10},{10,14},{3,7},{... | collective-permute-start | bytes 49160 | tf_op jit(solution)/shard_map/ppermute | solution.py:155
  19.9 5.6 %collective-permute-start.9 = (bf16[16,512]{1,0:T(8,128)(2,1)S(1)}, bf16[16,512]{1,0:T(8,128)(2,1)S(1)}, u32[]{:S(2)}, u32[]{:S(2)}) collective-permute-start(bf16[16,512]{1,0:T(8,128)(2,1)S(1)} %pad_maximum_fusion), channel_id=1, source_target_pairs={{4,0},{8,4},{12,8},{5,1},{9,5},{13,9},{6,2},{10,6},{14,10},{7,3},{... | collective-permute-start | bytes 49160 | tf_op jit(solution)/shard_map/ppermute | solution.py:156
  21.2 5.6 %collective-permute-start.8 = (bf16[16,512]{1,0:T(8,128)(2,1)S(1)}, bf16[16,512]{1,0:T(8,128)(2,1)S(1)}, u32[]{:S(2)}, u32[]{:S(2)}) collective-permute-start(bf16[16,512]{1,0:T(8,128)(2,1)S(1)} %collective-permute-done.7), channel_id=1, source_target_pairs={{4,8},{8,12},{5,9},{9,13},{6,10},{10,14},{7,11},{11,15},{20,24},{2... | collective-permute-start | bytes 49160 | tf_op jit(solution)/shard_map/ppermute | solution.py:155
  25.5 23.3 %collective-permute-start.5 = (bf16[256,512]{1,0:T(8,128)(2,1)}, bf16[256,512]{1,0:T(8,128)(2,1)S(1)}, u32[]{:S(2)}, u32[]{:S(2)}) collective-permute-start(bf16[256,512]{1,0:T(8,128)(2,1)} %param.6), channel_id=1, source_target_pairs={{12,0},{13,1},{14,2},{15,3},{28,16},{29,17},{30,18},{31,19}} | collective-permute-start | bytes 786440 | tf_op jit(solution)/shard_map/ppermute | solution.py:149
  26.8 6.1 %collective-permute-start.10 = (bf16[16,512]{1,0:T(8,128)(2,1)S(1)}, bf16[16,512]{1,0:T(8,128)(2,1)S(1)}, u32[]{:S(2)}, u32[]{:S(2)}) collective-permute-start(bf16[16,512]{1,0:T(8,128)(2,1)S(1)} %collective-permute-done.9), channel_id=1, source_target_pairs={{4,0},{8,4},{5,1},{9,5},{6,2},{10,6},{7,3},{11,7},{20,16},{24,20},... | collective-permute-start | bytes 49160 | tf_op jit(solution)/shard_map/ppermute | solution.py:156
  32.9 7.5 %collective-permute-start.11 = (bf16[16,512]{1,0:T(8,128)(2,1)S(1)}, bf16[16,512]{1,0:T(8,128)(2,1)S(1)}, u32[]{:S(2)}, u32[]{:S(2)}) collective-permute-start(bf16[16,512]{1,0:T(8,128)(2,1)S(1)} %pad_maximum_fusion), channel_id=1, source_target_pairs={{12,0},{13,1},{14,2},{15,3},{28,16},{29,17},{30,18},{31,19}} | collective-permute-start | bytes 49160 | tf_op jit(solution)/shard_map/ppermute | solution.py:149
  34.2 7.7 %collective-permute-start.2 = (bf16[256,512]{1,0:T(8,128)(2,1)S(1)}, bf16[256,512]{1,0:T(8,128)(2,1)S(1)}, u32[]{:S(2)}, u32[]{:S(2)}) collective-permute-start(bf16[256,512]{1,0:T(8,128)(2,1)S(1)} %collective-permute-done.1), channel_id=1, source_target_pairs={{4,8},{8,12},{5,9},{9,13},{6,10},{10,14},{7,11},{11,15},{20,24},{2... | collective-permute-start | bytes 786440 | tf_op jit(solution)/shard_map/ppermute | solution.py:155
  40.5 8.5 %copy-start = (bf16[1,1,8,256,256]{4,3,2,1,0:T(8,128)(2,1)S(1)}, bf16[1,1,8,256,256]{4,3,2,1,0:T(8,128)(2,1)}, u32[]{:S(2)}) copy-start(bf16[1,1,8,256,256]{4,3,2,1,0:T(8,128)(2,1)} %param.8) | copy-start | bytes 3145732
  40.5 8.4 %collective-permute-start.4 = (bf16[256,512]{1,0:T(8,128)(2,1)S(1)}, bf16[256,512]{1,0:T(8,128)(2,1)S(1)}, u32[]{:S(2)}, u32[]{:S(2)}) collective-permute-start(bf16[256,512]{1,0:T(8,128)(2,1)S(1)} %collective-permute-done.3), channel_id=1, source_target_pairs={{4,0},{8,4},{5,1},{9,5},{6,2},{10,6},{7,3},{11,7},{20,16},{24,20},... | collective-permute-start | bytes 786440 | tf_op jit(solution)/shard_map/ppermute | solution.py:156
  51.5 12.1 %copy-start.2 = (bf16[1,32,256]{2,1,0:T(8,128)(2,1)S(1)}, bf16[1,32,256]{2,1,0:T(8,128)(2,1)}, u32[]{:S(2)}) copy-start(bf16[1,32,256]{2,1,0:T(8,128)(2,1)} %param.7) | copy-start | bytes 49156
  51.5 2.1 %collective-permute-start.12 = (bf16[2,288,512]{2,1,0:T(8,128)(2,1)S(1)}, bf16[2,288,512]{2,1,0:T(8,128)(2,1)S(1)}, u32[]{:S(2)}, u32[]{:S(2)}) collective-permute-start(bf16[2,288,512]{2,1,0:T(8,128)(2,1)S(1)} %get-tuple-element.8), channel_id=1, source_target_pairs={{0,1},{1,0},{2,3},{3,2},{4,5},{5,4},{6,7},{7,6},{8,9},{9,8},{10,11... | collective-permute-start | bytes 1769480 | tf_op jit(solution)/shard_map/ppermute | solution.py:214
  53.7 9.8 %collective-permute-start.13 = (bf16[288,512]{1,0:T(8,128)(2,1)S(1)}, bf16[288,512]{1,0:T(8,128)(2,1)S(1)}, u32[]{:S(2)}, u32[]{:S(2)}) collective-permute-start(bf16[288,512]{1,0:T(8,128)(2,1)S(1)} %fusion.1), channel_id=1, source_target_pairs={{0,2},{2,0},{1,3},{3,1},{4,6},{6,4},{5,7},{7,5},{8,10},{10,8},{9,1... | collective-permute-start | bytes 884744 | tf_op jit(solution)/shard_map/ppermute | solution.py:222

commit v16 on v11

--- a/solution.py
+++ b/solution.py
@@ -131,23 +131,22 @@
 
 def _line_gather(payload, axis):
     n = lax.axis_size(axis)
-    if n <= 2:
-        far_up = far_down = None
-    else:
-        far_up = lax.ppermute(payload, axis, [(0, n - 1)])
-        far_down = lax.ppermute(payload, axis, [(n - 1, 0)])
-    ups, downs = [], []
-    up, down = payload, payload
-    for step in range(n - 1 if far_up is None else n - 2):
+    if n == 1:
+        return payload[None]
+    first_up = lax.ppermute(payload, axis, [(i, (i + 1) % n) for i in range(n)])
+    first_down = lax.ppermute(payload, axis, [(i, (i - 1) % n) for i in range(n)])
+    ups, downs = [first_up], [first_down]
+    up, down = first_up, first_down
+    for step in range(1, n - 2):
         up_pairs = [(i, i + 1) for i in range(step, n - 1)]
         down_pairs = [(i + 1, i) for i in range(n - 1 - step)]
         up = lax.ppermute(up, axis, up_pairs)
         down = lax.ppermute(down, axis, down_pairs)
         ups.append(up)
         downs.append(down)
-    if far_up is not None:
-        ups.append(far_up)
-        downs.append(far_down)
+    if n > 2:
+        ups.append(first_down)
+        downs.append(first_up)
     return jnp.stack(ups[::-1] + [payload] + downs)
 
 

time: 50.9 us -> 47.2 us (0.927)
  starting transfers between devices: 14.2 us -> 8.16 us
  waiting for transfers between devices: 26.5 us -> 28.9 us
    ppermute x2, waiting for transfers between devices: 0.01 us -> 10.1 us  [the longest x1 10.1 us: _line_gather(): first_up = lax.ppermute(payload, axis, [(i, (i + 1) % n) for i in range(n)])]
    ppermute x2 -> x1, waiting for transfers between devices: 16.7 us -> 8.53 us  [_line_gather(): down = lax.ppermute(down, axis, down_pairs)]
    ppermute x2 -> x1, starting transfers between devices: 5.65 us -> 0.67 us  [_line_gather(): up = lax.ppermute(up, axis, up_pairs)]
    ppermute x2 -> x1, starting transfers between devices: 2.57 us -> 1.42 us  [_line_gather(): down = lax.ppermute(down, axis, down_pairs)]
    ppermute x2, starting transfers between devices: 4.61 us -> 5.13 us  [the longest x1 5.13 us: _line_gather(): lax.ppermute(payload, axis, [(i, (i - 1) % n) for i in range(n)])]
  transfers between devices with their start and end apart: 8 -> 6, of which waited for: 4 -> 4; matrix products, arithmetic and copies ran while one was open for 6% -> 6% of each run, Pallas kernels for 0% -> 0%
where the time goes in v16:
time: 47.2 us; the launch traced here: 47.1 us
  waiting for transfers between devices  28.9 us (61%)
  starting transfers between devices  8.16 us (17%)
  Pallas kernels  3.28 us (7%)
  local copies, waits for them, and re-layouts  2.79 us (6%)
  other arithmetic  2.21 us (5%)
  matrix products  0.97 us (2%)
  between operations  0.83 us (2%)
    ppermute x1, waiting for transfers between devices, _line_gather(): first_up = lax.ppermute(payload, axis, [(i, (i + 1) % n) for i in range(n)])  10.1 us
    ppermute x1, waiting for transfers between devices, _line_gather(): down = lax.ppermute(down, axis, down_pairs)  8.53 us
    ppermute x1, waiting for transfers between devices, on_device(): back = lax.ppermute(send, 'inner', [(0, 1), (1, 0)])  8.25 us
    ppermute x1, starting transfers between devices, _line_gather(): lax.ppermute(payload, axis, [(i, (i - 1) % n) for i in range(n)])  5.13 us
    pallas_call x1, Pallas kernels, _near_far(): pl.pallas_call(_near_far_kernel, grid_spec=grid_spec, out_shape=[out, out...  3.28 us
    ppermute x1, waiting for transfers between devices, on_device(): arrived = lax.ppermute(theirs, 'sub', [(0, 1), (1, 0)])  1.99 us
    ppermute x1, starting transfers between devices, _line_gather(): down = lax.ppermute(down, axis, down_pairs)  1.42 us
    dot_general x1, matrix products, on_device(): jnp.dot(basis_t, total[width:].astype(jnp.bfloat16), preferred_element_ty...  0.97 us
  transfers between devices with their start and end apart: 6, of which 4 were waited for; matrix products, arithmetic and copies ran while one was open for 6% of the time, Pallas kernels for 0%

profile of v16, /device:TPU:0, one launch (start us, length us, event | category | flops | bytes accessed | tf_op | source)
XLA Modules:
  0.0 47.1 jit_solution(7137447945563689565)
XLA Ops:
  0.0 0.0 copy-start.1
  0.0 0.8 %slice_bitcast_fusion.1 = (bf16[16,256]{1,0:T(8,128)(2,1)S(1)}, bf16[16,256]{1,0:T(8,128)(2,1)S(1)}) fusion(bf16[1,32,256]{2,1,0:T(8,128)(2,1)} %param.7), kind=kLoop, calls=%fused_computation.18 | loop fusion | bytes 32768 | tf_op jit(solution)/shard_map/slice | solution.py:176
  0.8 1.0 %maximum_maximum_fusion = bf16[272,512]{1,0:T(8,128)(2,1)S(1)} fusion(bf16[16,256]{1,0:T(8,128)(2,1)S(1)} %get-tuple-element.10, bf16[16,256]{1,0:T(8,128)(2,1)S(1)} %get-tuple-element.9, bf16[256,512]{1,0:T(8,128)(2,1)} %param.6), kind=kLoop, calls=%fused_computation.6 | loop fusion | flops 835584 | bytes 557056 | tf_op jit(solution)/shard_map/concatenate | solution.py:177
  1.7 5.1 %collective-permute-start = (bf16[272,512]{1,0:T(8,128)(2,1)S(1)}, bf16[272,512]{1,0:T(8,128)(2,1)S(1)}, u32[]{:S(2)}, u32[]{:S(2)}) collective-permute-start(bf16[272,512]{1,0:T(8,128)(2,1)S(1)} %maximum_maximum_fusion), channel_id=1, source_target_pairs={{0,12},{4,0},{8,4},{12,8},{1,13},{5,1},{9,5},{13,9},{2,14},{6,2},{... | collective-permute-start | bytes 835592 | tf_op jit(solution)/shard_map/ppermute | solution.py:137
  6.9 0.0 collective-permute-start.1
  7.5 0.8 %add_bitcast_fusion = s32[8]{0:T(128)S(1)} fusion(s32[8,2]{0,1:T(2,128)} %bitcast.46), kind=kLoop, calls=%fused_computation.25 | loop fusion | flops 16 | bytes 96 | tf_op jit(solution)/shard_map/eq | solution.py:185
  8.3 0.1 fusion.4
  8.4 0.1 convert_element_type.51
  8.5 0.1 copy.16
  8.6 0.9 %reshape_squeeze.11 = bf16[4,32,4,32]{3,2,1,0:T(4,128)(2,1)S(1)} reshape(bf16[1,1,128,128]{3,2,1,0:T(8,128)(2,1)} %param.11) | data formatting | bytes 65536 | tf_op jit(solution)/shard_map/reshape;squeeze | solution.py:193
  9.5 0.1 copy_multiply_fusion
  9.6 10.1 %collective-permute-done.1 = bf16[272,512]{1,0:T(8,128)(2,1)S(1)} collective-permute-done((bf16[272,512]{1,0:T(8,128)(2,1)S(1)}, bf16[272,512]{1,0:T(8,128)(2,1)S(1)}, u32[]{:S(2)}, u32[]{:S(2)}) %collective-permute-start.1) | collective-permute-done | bytes 278560 | tf_op jit(solution)/shard_map/ppermute | solution.py:136
  19.7 0.7 %collective-permute-start.2 = (bf16[272,512]{1,0:T(8,128)(2,1)S(1)}, bf16[272,512]{1,0:T(8,128)(2,1)S(1)}, u32[]{:S(2)}, u32[]{:S(2)}) collective-permute-start(bf16[272,512]{1,0:T(8,128)(2,1)S(1)} %collective-permute-done.1), channel_id=1, source_target_pairs={{4,8},{8,12},{5,9},{9,13},{6,10},{10,14},{7,11},{11,15},{20,24},{2... | collective-permute-start | bytes 835592 | tf_op jit(solution)/shard_map/ppermute | solution.py:143
  20.3 0.1 pad_add_fusion.place_ref
  20.4 0.8 %copy.15 = s32[1,1,8,2]{3,2,1,0:T(8,128)S(1)} copy(s32[1,1,8,2]{2,3,1,0:T(2,128)} %param.9) | data formatting | bytes 128 | tf_op args[3]
  21.2 0.1 reshape_squeeze.9.pairs_ref
  21.2 0.0 copy-start
  21.2 0.0 collective-permute-done
  21.2 1.4 %collective-permute-start.3 = (bf16[272,512]{1,0:T(8,128)(2,1)S(1)}, bf16[272,512]{1,0:T(8,128)(2,1)S(1)}, u32[]{:S(2)}, u32[]{:S(2)}) collective-permute-start(bf16[272,512]{1,0:T(8,128)(2,1)S(1)} %collective-permute-done), channel_id=1, source_target_pairs={{4,0},{8,4},{5,1},{9,5},{6,2},{10,6},{7,3},{11,7},{20,16},{24,20},... | collective-permute-start | bytes 835592 | tf_op jit(solution)/shard_map/ppermute | solution.py:144
  22.7 0.0 collective-permute-done.2
  22.8 0.0 copy-done.1
  22.8 8.5 %collective-permute-done.3 = bf16[272,512]{1,0:T(8,128)(2,1)S(1)} collective-permute-done((bf16[272,512]{1,0:T(8,128)(2,1)S(1)}, bf16[272,512]{1,0:T(8,128)(2,1)S(1)}, u32[]{:S(2)}, u32[]{:S(2)}) %collective-permute-start.3) | collective-permute-done | bytes 278560 | tf_op jit(solution)/shard_map/ppermute | solution.py:144
  31.4 0.0 copy-done
  31.4 3.3 %shard_map.64 = (bf16[2,288,512]{2,1,0:T(8,128)(2,1)S(1)}, bf16[2,288,512]{2,1,0:T(8,128)(2,1)S(1)}) custom-call(s32[16]{0:T(128)S(1)} %reshape_squeeze.9.pairs_ref, s32[1]{0:T(128)} %bitcast.42.count_ref, s32[2]{0:T(128)S(1)} %pad_add_fusion.place_ref, bf16[8,256,256]{2,1,0:T(8,128)(2,1)S(1)} %bitcast.44, ...), custom_call_target="tpu_custom_call" | custom-call | tf_op jit(solution)/shard_map/pallas_call | solution.py:89
  34.7 0.0 copy-start.2
  34.7 0.1 collective-permute-start.4
  34.8 2.0 %collective-permute-done.4 = bf16[2,288,512]{2,1,0:T(8,128)(2,1)S(1)} collective-permute-done((bf16[2,288,512]{2,1,0:T(8,128)(2,1)S(1)}, bf16[2,288,512]{2,1,0:T(8,128)(2,1)S(1)}, u32[]{:S(2)}, u32[]{:S(2)}) %collective-permute-start.4) | collective-permute-done | bytes 589856 | tf_op jit(solution)/shard_map/ppermute | solution.py:201
  36.8 0.1 fusion.1
  36.9 0.9 %collective-permute-start.5 = (bf16[288,512]{1,0:T(8,128)(2,1)S(1)}, bf16[288,512]{1,0:T(8,128)(2,1)S(1)}, u32[]{:S(2)}, u32[]{:S(2)}) collective-permute-start(bf16[288,512]{1,0:T(8,128)(2,1)S(1)} %fusion.1), channel_id=1, source_target_pairs={{0,2},{2,0},{1,3},{3,1},{4,6},{6,4},{5,7},{7,5},{8,10},{10,8},{9,1... | collective-permute-start | bytes 884744 | tf_op jit(solution)/shard_map/ppermute | solution.py:209
  37.8 8.3 %collective-permute-done.5 = bf16[288,512]{1,0:T(8,128)(2,1)S(1)} collective-permute-done((bf16[288,512]{1,0:T(8,128)(2,1)S(1)}, bf16[288,512]{1,0:T(8,128)(2,1)S(1)}, u32[]{:S(2)}, u32[]{:S(2)}) %collective-permute-start.5) | collective-permute-done | bytes 294944 | tf_op jit(solution)/shard_map/ppermute | solution.py:209
  46.0 0.1 bitcast_add_fusion
  46.1 0.0 copy-done.2
  46.1 1.0 %fusion = bf16[256,512]{1,0:T(8,128)(2,1)} fusion(f32[288,512]{1,0:T(8,128)S(1)} %bitcast_add_fusion, bf16[1,32,256]{2,1,0:T(8,128)(2,1)S(1)} %copy-done.2), kind=kOutput, calls=%fused_computation.4 | convolution fusion | flops 8667136 | bytes 868352 | tf_op jit(solution)/shard_map/dot_general | solution.py:221
  (9 shorter events, 0.2 us)
Async XLA Ops:
  0.0 22.8 %copy-start.1 = (bf16[256,512]{1,0:T(8,128)(2,1)S(1)}, bf16[256,512]{1,0:T(8,128)(2,1)}, u32[]{:S(2)}) copy-start(bf16[256,512]{1,0:T(8,128)(2,1)} %param.6) | copy-start | bytes 786436
  1.7 19.5 %collective-permute-start = (bf16[272,512]{1,0:T(8,128)(2,1)S(1)}, bf16[272,512]{1,0:T(8,128)(2,1)S(1)}, u32[]{:S(2)}, u32[]{:S(2)}) collective-permute-start(bf16[272,512]{1,0:T(8,128)(2,1)S(1)} %maximum_maximum_fusion), channel_id=1, source_target_pairs={{0,12},{4,0},{8,4},{12,8},{1,13},{5,1},{9,5},{13,9},{2,14},{6,2},{... | collective-permute-start | bytes 835592 | tf_op jit(solution)/shard_map/ppermute | solution.py:137
  6.9 12.8 %collective-permute-start.1 = (bf16[272,512]{1,0:T(8,128)(2,1)S(1)}, bf16[272,512]{1,0:T(8,128)(2,1)S(1)}, u32[]{:S(2)}, u32[]{:S(2)}) collective-permute-start(bf16[272,512]{1,0:T(8,128)(2,1)S(1)} %maximum_maximum_fusion), channel_id=1, source_target_pairs={{0,4},{4,8},{8,12},{12,0},{1,5},{5,9},{9,13},{13,1},{2,6},{6,10},{... | collective-permute-start | bytes 835592 | tf_op jit(solution)/shard_map/ppermute | solution.py:136
  19.7 3.1 %collective-permute-start.2 = (bf16[272,512]{1,0:T(8,128)(2,1)S(1)}, bf16[272,512]{1,0:T(8,128)(2,1)S(1)}, u32[]{:S(2)}, u32[]{:S(2)}) collective-permute-start(bf16[272,512]{1,0:T(8,128)(2,1)S(1)} %collective-permute-done.1), channel_id=1, source_target_pairs={{4,8},{8,12},{5,9},{9,13},{6,10},{10,14},{7,11},{11,15},{20,24},{2... | collective-permute-start | bytes 835592 | tf_op jit(solution)/shard_map/ppermute | solution.py:143
  21.2 10.2 %copy-start = (bf16[1,1,8,256,256]{4,3,2,1,0:T(8,128)(2,1)S(1)}, bf16[1,1,8,256,256]{4,3,2,1,0:T(8,128)(2,1)}, u32[]{:S(2)}) copy-start(bf16[1,1,8,256,256]{4,3,2,1,0:T(8,128)(2,1)} %param.8) | copy-start | bytes 3145732
  21.2 10.1 %collective-permute-start.3 = (bf16[272,512]{1,0:T(8,128)(2,1)S(1)}, bf16[272,512]{1,0:T(8,128)(2,1)S(1)}, u32[]{:S(2)}, u32[]{:S(2)}) collective-permute-start(bf16[272,512]{1,0:T(8,128)(2,1)S(1)} %collective-permute-done), channel_id=1, source_target_pairs={{4,0},{8,4},{5,1},{9,5},{6,2},{10,6},{7,3},{11,7},{20,16},{24,20},... | collective-permute-start | bytes 835592 | tf_op jit(solution)/shard_map/ppermute | solution.py:144
  34.7 11.4 %copy-start.2 = (bf16[1,32,256]{2,1,0:T(8,128)(2,1)S(1)}, bf16[1,32,256]{2,1,0:T(8,128)(2,1)}, u32[]{:S(2)}) copy-start(bf16[1,32,256]{2,1,0:T(8,128)(2,1)} %param.7) | copy-start | bytes 49156
  34.7 2.1 %collective-permute-start.4 = (bf16[2,288,512]{2,1,0:T(8,128)(2,1)S(1)}, bf16[2,288,512]{2,1,0:T(8,128)(2,1)S(1)}, u32[]{:S(2)}, u32[]{:S(2)}) collective-permute-start(bf16[2,288,512]{2,1,0:T(8,128)(2,1)S(1)} %get-tuple-element.8), channel_id=1, source_target_pairs={{0,1},{1,0},{2,3},{3,2},{4,5},{5,4},{6,7},{7,6},{8,9},{9,8},{10,11... | collective-permute-start | bytes 1769480 | tf_op jit(solution)/shard_map/ppermute | solution.py:201
  36.9 9.1 %collective-permute-start.5 = (bf16[288,512]{1,0:T(8,128)(2,1)S(1)}, bf16[288,512]{1,0:T(8,128)(2,1)S(1)}, u32[]{:S(2)}, u32[]{:S(2)}) collective-permute-start(bf16[288,512]{1,0:T(8,128)(2,1)S(1)} %fusion.1), channel_id=1, source_target_pairs={{0,2},{2,0},{1,3},{3,1},{4,6},{6,4},{5,7},{7,5},{8,10},{10,8},{9,1... | collective-permute-start | bytes 884744 | tf_op jit(solution)/shard_map/ppermute | solution.py:209

commit v17 on v16

--- a/solution.py
+++ b/solution.py
@@ -198,17 +198,21 @@
         pair_list.reshape(-1), live_count.reshape(1), place, near_blocks[0, 0], stack, masked_t,
         inner_count, rank_size,
     )
-    arrived = lax.ppermute(theirs, "sub", [(0, 1), (1, 0)])
     basis_t = cluster_basis[0].T
     me = lax.axis_index("inner")
+    swap = [(0, 1), (1, 0)]
     if lax.axis_size("inner") == 2:
+        onward = lax.ppermute(lax.dynamic_index_in_dim(theirs, 1 - me, 0, False), "sub", swap)
         send = (
             lax.dynamic_index_in_dim(mine, 1 - me, 0, False).astype(jnp.float32)
-            + lax.dynamic_index_in_dim(arrived, 1 - me, 0, False).astype(jnp.float32)
+            + onward.astype(jnp.float32)
         ).astype(jnp.bfloat16)
-        back = lax.ppermute(send, "inner", [(0, 1), (1, 0)])
-        pieces = (mine, arrived, back)
+        back = lax.ppermute(send, "inner", swap)
+        keep_src = lax.optimization_barrier((lax.dynamic_index_in_dim(theirs, me, 0, False), send))[0]
+        kept = lax.ppermute(keep_src, "sub", swap)
+        pieces = (mine, kept, back)
     else:
+        arrived = lax.ppermute(theirs, "sub", swap)
         stage = mine.astype(jnp.float32) + arrived.astype(jnp.float32)
         pieces = (_ring_reduce_scatter(stage, "inner"),)
     width = basis_t.shape[0]

time: 47.2 us -> 47.4 us (level)
  starting transfers between devices: 8.16 us -> 9.46 us
  waiting for transfers between devices: 28.9 us -> 27.7 us
    ppermute x2 -> x3, starting transfers between devices: 0.93 us -> 2.23 us  [the longest x1 1.96 us: on_device(): back = lax.ppermute(send, 'inner', swap)]
    ppermute x2 -> x3, waiting for transfers between devices: 10.2 us -> 9.11 us  [the longest x1 7.54 us: on_device(): back = lax.ppermute(send, 'inner', swap)]
  transfers between devices with their start and end apart: 6 -> 7, of which waited for: 4 -> 4; matrix products, arithmetic and copies ran while one was open for 6% -> 6% of each run, Pallas kernels for 0% -> 0%
where the time goes in v17:
time: 47.4 us; the launch traced here: 46.9 us
  waiting for transfers between devices  27.7 us (58%)
  starting transfers between devices  9.46 us (20%)
  local copies, waits for them, and re-layouts  2.84 us (6%)
  Pallas kernels  2.81 us (6%)
  other arithmetic  2.22 us (5%)
  matrix products  0.97 us (2%)
  between operations  0.83 us (2%)
    ppermute x1, waiting for transfers between devices, _line_gather(): first_up = lax.ppermute(payload, axis, [(i, (i + 1) % n) for i in range(n)])  10.1 us
    ppermute x1, waiting for transfers between devices, _line_gather(): down = lax.ppermute(down, axis, down_pairs)  8.53 us
    ppermute x1, waiting for transfers between devices, on_device(): back = lax.ppermute(send, 'inner', swap)  7.54 us
    ppermute x1, starting transfers between devices, _line_gather(): lax.ppermute(payload, axis, [(i, (i - 1) % n) for i in range(n)])  5.13 us
    pallas_call x1, Pallas kernels, _near_far(): pl.pallas_call(_near_far_kernel, grid_spec=grid_spec, out_shape=[out, out...  2.81 us
    ppermute x1, starting transfers between devices, on_device(): back = lax.ppermute(send, 'inner', swap)  1.96 us
    ppermute x1, waiting for transfers between devices, on_device(): lax.ppermute(lax.dynamic_index_in_dim(theirs, 1 - me, 0, False), 'sub', s...  1.57 us
    ppermute x1, starting transfers between devices, _line_gather(): down = lax.ppermute(down, axis, down_pairs)  1.42 us
  transfers between devices with their start and end apart: 7, of which 4 were waited for; matrix products, arithmetic and copies ran while one was open for 6% of the time, Pallas kernels for 0%

profile of v17, /device:TPU:0, one launch (start us, length us, event | category | flops | bytes accessed | tf_op | source)
XLA Modules:
  0.0 46.9 jit_solution(11021854201900002947)
XLA Ops:
  0.0 0.0 copy-start.1
  0.0 0.8 %slice_bitcast_fusion.1 = (bf16[16,256]{1,0:T(8,128)(2,1)S(1)}, bf16[16,256]{1,0:T(8,128)(2,1)S(1)}) fusion(bf16[1,32,256]{2,1,0:T(8,128)(2,1)} %param.7), kind=kLoop, calls=%fused_computation.21 | loop fusion | bytes 32768 | tf_op jit(solution)/shard_map/slice | solution.py:176
  0.8 1.0 %maximum_maximum_fusion = bf16[272,512]{1,0:T(8,128)(2,1)S(1)} fusion(bf16[16,256]{1,0:T(8,128)(2,1)S(1)} %get-tuple-element.14, bf16[16,256]{1,0:T(8,128)(2,1)S(1)} %get-tuple-element.13, bf16[256,512]{1,0:T(8,128)(2,1)} %param.6), kind=kLoop, calls=%fused_computation.9 | loop fusion | flops 835584 | bytes 557056 | tf_op jit(solution)/shard_map/concatenate | solution.py:177
  1.7 5.1 %collective-permute-start = (bf16[272,512]{1,0:T(8,128)(2,1)S(1)}, bf16[272,512]{1,0:T(8,128)(2,1)S(1)}, u32[]{:S(2)}, u32[]{:S(2)}) collective-permute-start(bf16[272,512]{1,0:T(8,128)(2,1)S(1)} %maximum_maximum_fusion), channel_id=1, source_target_pairs={{0,12},{4,0},{8,4},{12,8},{1,13},{5,1},{9,5},{13,9},{2,14},{6,2},{... | collective-permute-start | bytes 835592 | tf_op jit(solution)/shard_map/ppermute | solution.py:137
  6.9 0.0 collective-permute-start.1
  7.5 0.8 %add_bitcast_fusion = s32[8]{0:T(128)S(1)} fusion(s32[8,2]{0,1:T(2,128)} %bitcast.52), kind=kLoop, calls=%fused_computation.28 | loop fusion | flops 16 | bytes 96 | tf_op jit(solution)/shard_map/eq | solution.py:185
  8.3 0.1 fusion.5
  8.4 0.1 convert_element_type.50
  8.5 0.1 copy.16
  8.6 0.9 %reshape_squeeze.11 = bf16[4,32,4,32]{3,2,1,0:T(4,128)(2,1)S(1)} reshape(bf16[1,1,128,128]{3,2,1,0:T(8,128)(2,1)} %param.11) | data formatting | bytes 65536 | tf_op jit(solution)/shard_map/reshape;squeeze | solution.py:193
  9.5 0.1 copy_multiply_fusion
  9.6 10.1 %collective-permute-done.1 = bf16[272,512]{1,0:T(8,128)(2,1)S(1)} collective-permute-done((bf16[272,512]{1,0:T(8,128)(2,1)S(1)}, bf16[272,512]{1,0:T(8,128)(2,1)S(1)}, u32[]{:S(2)}, u32[]{:S(2)}) %collective-permute-start.1) | collective-permute-done | bytes 278560 | tf_op jit(solution)/shard_map/ppermute | solution.py:136
  19.7 0.7 %collective-permute-start.2 = (bf16[272,512]{1,0:T(8,128)(2,1)S(1)}, bf16[272,512]{1,0:T(8,128)(2,1)S(1)}, u32[]{:S(2)}, u32[]{:S(2)}) collective-permute-start(bf16[272,512]{1,0:T(8,128)(2,1)S(1)} %collective-permute-done.1), channel_id=1, source_target_pairs={{4,8},{8,12},{5,9},{9,13},{6,10},{10,14},{7,11},{11,15},{20,24},{2... | collective-permute-start | bytes 835592 | tf_op jit(solution)/shard_map/ppermute | solution.py:143
  20.3 0.1 pad_add_fusion.place_ref
  20.4 0.8 %copy.15 = s32[1,1,8,2]{3,2,1,0:T(8,128)S(1)} copy(s32[1,1,8,2]{2,3,1,0:T(2,128)} %param.9) | data formatting | bytes 128 | tf_op args[3]
  21.2 0.1 reshape_squeeze.9.pairs_ref
  21.2 0.0 copy-start
  21.2 0.0 collective-permute-done
  21.2 1.4 %collective-permute-start.3 = (bf16[272,512]{1,0:T(8,128)(2,1)S(1)}, bf16[272,512]{1,0:T(8,128)(2,1)S(1)}, u32[]{:S(2)}, u32[]{:S(2)}) collective-permute-start(bf16[272,512]{1,0:T(8,128)(2,1)S(1)} %collective-permute-done), channel_id=1, source_target_pairs={{4,0},{8,4},{5,1},{9,5},{6,2},{10,6},{7,3},{11,7},{20,16},{24,20},... | collective-permute-start | bytes 835592 | tf_op jit(solution)/shard_map/ppermute | solution.py:144
  22.7 0.0 collective-permute-done.2
  22.8 0.0 copy-done.1
  22.8 8.5 %collective-permute-done.3 = bf16[272,512]{1,0:T(8,128)(2,1)S(1)} collective-permute-done((bf16[272,512]{1,0:T(8,128)(2,1)S(1)}, bf16[272,512]{1,0:T(8,128)(2,1)S(1)}, u32[]{:S(2)}, u32[]{:S(2)}) %collective-permute-start.3) | collective-permute-done | bytes 278560 | tf_op jit(solution)/shard_map/ppermute | solution.py:144
  31.4 0.0 copy-done
  31.4 2.8 %shard_map.64 = (bf16[2,288,512]{2,1,0:T(8,128)(2,1)S(1)}, bf16[2,288,512]{2,1,0:T(8,128)(2,1)S(1)}) custom-call(s32[16]{0:T(128)S(1)} %reshape_squeeze.9.pairs_ref, s32[1]{0:T(128)} %bitcast.48.count_ref, s32[2]{0:T(128)S(1)} %pad_add_fusion.place_ref, bf16[8,256,256]{2,1,0:T(8,128)(2,1)S(1)} %bitcast.50, ...), custom_call_target="tpu_custom_call" | custom-call | tf_op jit(solution)/shard_map/pallas_call | solution.py:89
  34.3 0.0 copy-start.2
  34.3 0.1 collective-permute-start.4
  34.4 1.6 %collective-permute-done.4 = bf16[288,512]{1,0:T(8,128)(2,1)S(1)} collective-permute-done((bf16[288,512]{1,0:T(8,128)(2,1)S(1)}, bf16[288,512]{1,0:T(8,128)(2,1)S(1)}, u32[]{:S(2)}, u32[]{:S(2)}) %collective-permute-start.4) | collective-permute-done | bytes 294944 | tf_op jit(solution)/shard_map/ppermute | solution.py:205
  36.0 0.1 fusion
  36.1 0.2 collective-permute-start.5
  36.3 2.0 %collective-permute-start.6 = (bf16[288,512]{1,0:T(8,128)(2,1)S(1)}, bf16[288,512]{1,0:T(8,128)(2,1)S(1)}, u32[]{:S(2)}, u32[]{:S(2)}) collective-permute-start(bf16[288,512]{1,0:T(8,128)(2,1)S(1)} %fusion), channel_id=1, source_target_pairs={{0,2},{2,0},{1,3},{3,1},{4,6},{6,4},{5,7},{7,5},{8,10},{10,8},{9,1... | collective-permute-start | bytes 884744 | tf_op jit(solution)/shard_map/ppermute | solution.py:210
  38.2 0.0 collective-permute-done.5
  38.2 7.5 %collective-permute-done.6 = bf16[288,512]{1,0:T(8,128)(2,1)S(1)} collective-permute-done((bf16[288,512]{1,0:T(8,128)(2,1)S(1)}, bf16[288,512]{1,0:T(8,128)(2,1)S(1)}, u32[]{:S(2)}, u32[]{:S(2)}) %collective-permute-start.6) | collective-permute-done | bytes 294944 | tf_op jit(solution)/shard_map/ppermute | solution.py:210
  45.8 0.1 fusion.1
  45.9 0.0 copy-done.2
  45.9 1.0 %fusion.2 = bf16[256,512]{1,0:T(8,128)(2,1)} fusion(f32[288,512]{1,0:T(8,128)S(1)} %fusion.1, bf16[1,32,256]{2,1,0:T(8,128)(2,1)S(1)} %copy-done.2), kind=kOutput, calls=%fused_computation.6 | convolution fusion | flops 8667136 | bytes 868352 | tf_op jit(solution)/shard_map/dot_general | solution.py:225
  (10 shorter events, 0.2 us)
Async XLA Ops:
  0.0 22.8 %copy-start.1 = (bf16[256,512]{1,0:T(8,128)(2,1)S(1)}, bf16[256,512]{1,0:T(8,128)(2,1)}, u32[]{:S(2)}) copy-start(bf16[256,512]{1,0:T(8,128)(2,1)} %param.6) | copy-start | bytes 786436
  1.7 19.5 %collective-permute-start = (bf16[272,512]{1,0:T(8,128)(2,1)S(1)}, bf16[272,512]{1,0:T(8,128)(2,1)S(1)}, u32[]{:S(2)}, u32[]{:S(2)}) collective-permute-start(bf16[272,512]{1,0:T(8,128)(2,1)S(1)} %maximum_maximum_fusion), channel_id=1, source_target_pairs={{0,12},{4,0},{8,4},{12,8},{1,13},{5,1},{9,5},{13,9},{2,14},{6,2},{... | collective-permute-start | bytes 835592 | tf_op jit(solution)/shard_map/ppermute | solution.py:137
  6.9 12.8 %collective-permute-start.1 = (bf16[272,512]{1,0:T(8,128)(2,1)S(1)}, bf16[272,512]{1,0:T(8,128)(2,1)S(1)}, u32[]{:S(2)}, u32[]{:S(2)}) collective-permute-start(bf16[272,512]{1,0:T(8,128)(2,1)S(1)} %maximum_maximum_fusion), channel_id=1, source_target_pairs={{0,4},{4,8},{8,12},{12,0},{1,5},{5,9},{9,13},{13,1},{2,6},{6,10},{... | collective-permute-start | bytes 835592 | tf_op jit(solution)/shard_map/ppermute | solution.py:136
  19.7 3.1 %collective-permute-start.2 = (bf16[272,512]{1,0:T(8,128)(2,1)S(1)}, bf16[272,512]{1,0:T(8,128)(2,1)S(1)}, u32[]{:S(2)}, u32[]{:S(2)}) collective-permute-start(bf16[272,512]{1,0:T(8,128)(2,1)S(1)} %collective-permute-done.1), channel_id=1, source_target_pairs={{4,8},{8,12},{5,9},{9,13},{6,10},{10,14},{7,11},{11,15},{20,24},{2... | collective-permute-start | bytes 835592 | tf_op jit(solution)/shard_map/ppermute | solution.py:143
  21.2 10.2 %copy-start = (bf16[1,1,8,256,256]{4,3,2,1,0:T(8,128)(2,1)S(1)}, bf16[1,1,8,256,256]{4,3,2,1,0:T(8,128)(2,1)}, u32[]{:S(2)}) copy-start(bf16[1,1,8,256,256]{4,3,2,1,0:T(8,128)(2,1)} %param.8) | copy-start | bytes 3145732
  21.2 10.1 %collective-permute-start.3 = (bf16[272,512]{1,0:T(8,128)(2,1)S(1)}, bf16[272,512]{1,0:T(8,128)(2,1)S(1)}, u32[]{:S(2)}, u32[]{:S(2)}) collective-permute-start(bf16[272,512]{1,0:T(8,128)(2,1)S(1)} %collective-permute-done), channel_id=1, source_target_pairs={{4,0},{8,4},{5,1},{9,5},{6,2},{10,6},{7,3},{11,7},{20,16},{24,20},... | collective-permute-start | bytes 835592 | tf_op jit(solution)/shard_map/ppermute | solution.py:144
  34.3 11.6 %copy-start.2 = (bf16[1,32,256]{2,1,0:T(8,128)(2,1)S(1)}, bf16[1,32,256]{2,1,0:T(8,128)(2,1)}, u32[]{:S(2)}) copy-start(bf16[1,32,256]{2,1,0:T(8,128)(2,1)} %param.7) | copy-start | bytes 49156
  34.3 1.6 %collective-permute-start.4 = (bf16[288,512]{1,0:T(8,128)(2,1)S(1)}, bf16[288,512]{1,0:T(8,128)(2,1)S(1)}, u32[]{:S(2)}, u32[]{:S(2)}) collective-permute-start(bf16[288,512]{1,0:T(8,128)(2,1)S(1)} %get-tuple-element.12), channel_id=1, source_target_pairs={{0,1},{1,0},{2,3},{3,2},{4,5},{5,4},{6,7},{7,6},{8,9},{9,8},{10,11... | collective-permute-start | bytes 884744 | tf_op jit(solution)/shard_map/ppermute | solution.py:205
  36.1 2.2 %collective-permute-start.5 = (bf16[288,512]{1,0:T(8,128)(2,1)S(1)}, bf16[288,512]{1,0:T(8,128)(2,1)S(1)}, u32[]{:S(2)}, u32[]{:S(2)}) collective-permute-start(bf16[288,512]{1,0:T(8,128)(2,1)S(1)} %get-tuple-element.10), channel_id=1, source_target_pairs={{0,1},{1,0},{2,3},{3,2},{4,5},{5,4},{6,7},{7,6},{8,9},{9,8},{10,11... | collective-permute-start | bytes 884744 | tf_op jit(solution)/shard_map/ppermute | solution.py:212
  36.3 9.5 %collective-permute-start.6 = (bf16[288,512]{1,0:T(8,128)(2,1)S(1)}, bf16[288,512]{1,0:T(8,128)(2,1)S(1)}, u32[]{:S(2)}, u32[]{:S(2)}) collective-permute-start(bf16[288,512]{1,0:T(8,128)(2,1)S(1)} %fusion), channel_id=1, source_target_pairs={{0,2},{2,0},{1,3},{3,1},{4,6},{6,4},{5,7},{7,5},{8,10},{10,8},{9,1... | collective-permute-start | bytes 884744 | tf_op jit(solution)/shard_map/ppermute | solution.py:210

commit v18 on v17

--- a/solution.py
+++ b/solution.py
@@ -6,94 +6,130 @@
 from jax.sharding import PartitionSpec as P
 
 
-def _near_far_kernel(
-    pairs_ref, count_ref, place_ref, tiles_ref, stack_ref, masked_ref, mine_ref, theirs_ref, acc_ref
-):
-    inner_count, width, rhs_count = acc_ref.shape
+def _early(offset, tgt_count):
+    return (offset == 0) | (jnp.abs(offset) == 1) | (jnp.abs(offset) == tgt_count - 1)
+
+
+def _partial_kernel(late, pairs_ref, count_ref, place_ref, tiles_ref, stack_ref, masked_ref, *refs):
+    inner_count, width, rhs_count = tiles_ref.shape[1], tiles_ref.shape[1], stack_ref.shape[2]
     slot_count = tiles_ref.shape[0]
     tgt_count = masked_ref.shape[0]
     rank_size = masked_ref.shape[2]
     sub_count = 2
     own_tgt = place_ref[0]
     own_sub = place_ref[1]
-    acc_ref[...] = jnp.zeros_like(acc_ref)
+    if late:
+        acc_in, coeff_in, mine_ref, theirs_ref, acc_ref, coeff_ref = refs
+        inner_count = acc_in.shape[0]
+        acc_ref[...] = acc_in[...]
+        coeff_ref[...] = coeff_in[...]
+    else:
+        acc_ref, coeff_ref = refs
+        inner_count = acc_ref.shape[0]
+        acc_ref[...] = jnp.zeros_like(acc_ref)
+        coeff_ref[...] = jnp.zeros_like(coeff_ref)
 
     def add_slot(slot, carry):
         target = jnp.clip(pairs_ref[2 * slot], 0, inner_count - 1)
         source = jnp.clip(pairs_ref[2 * slot + 1], 0, tgt_count - 1)
-        term = jnp.dot(
-            tiles_ref[slot],
-            stack_ref[source - own_tgt + tgt_count - 1, :width, :],
-            preferred_element_type=jnp.float32,
-        )
-        acc_ref[target] += term
+        offset = source - own_tgt
+        wanted = jnp.logical_not(_early(offset, tgt_count)) if late else _early(offset, tgt_count)
+
+        @pl.when(wanted)
+        def _():
+            term = jnp.dot(
+                tiles_ref[slot],
+                stack_ref[offset + tgt_count - 1, :width, :],
+                preferred_element_type=jnp.float32,
+            )
+            acc_ref[target] += term
+
         return carry
 
     lax.fori_loop(0, jnp.clip(count_ref[0], 0, slot_count), add_slot, 0)
 
-    coeffs = jnp.zeros((inner_count * rank_size, rhs_count), jnp.float32)
     for source in range(tgt_count):
-        block = stack_ref[source - own_tgt + tgt_count - 1]
-        dens = block[:width, :]
-        packed = block[width:, :]
-        top = jnp.dot(packed[:, :width], dens, preferred_element_type=jnp.float32)
-        bottom = jnp.dot(packed[:, width:], dens, preferred_element_type=jnp.float32)
-        projected = jnp.concatenate([top, bottom], axis=0).astype(jnp.bfloat16)
-        coeffs += jnp.dot(masked_ref[source], projected, preferred_element_type=jnp.float32)
-    coeffs = coeffs.astype(jnp.bfloat16)
-
-    def write(first_ref, second_ref):
-        for target in range(inner_count):
-            dest = first_ref if target % sub_count == 0 else second_ref
-            row = target // sub_count
-            dest[row, :width, :] = acc_ref[target].astype(dest.dtype)
-            dest[row, width:, :] = coeffs[target * rank_size : (target + 1) * rank_size]
-
-    @pl.when(own_sub == 0)
-    def _():
-        write(mine_ref, theirs_ref)
-
-    @pl.when(own_sub != 0)
-    def _():
-        write(theirs_ref, mine_ref)
-
-
-def _near_far(pairs_flat, count, place, tiles, stack, masked_t, inner_count, rank_size):
+        offset = source - own_tgt
+        wanted = jnp.logical_not(_early(offset, tgt_count)) if late else _early(offset, tgt_count)
+
+        @pl.when(wanted)
+        def _():
+            block = stack_ref[offset + tgt_count - 1]
+            dens = block[:width, :]
+            packed = block[width:, :]
+            top = jnp.dot(packed[:, :width], dens, preferred_element_type=jnp.float32)
+            bottom = jnp.dot(packed[:, width:], dens, preferred_element_type=jnp.float32)
+            projected = jnp.concatenate([top, bottom], axis=0).astype(jnp.bfloat16)
+            coeff_ref[...] += jnp.dot(
+                masked_ref[source], projected, preferred_element_type=jnp.float32
+            )
+
+    if late:
+        coeffs = coeff_ref[...].astype(jnp.bfloat16)
+
+        def write(first_ref, second_ref):
+            for target in range(inner_count):
+                dest = first_ref if target % sub_count == 0 else second_ref
+                row = target // sub_count
+                dest[row, :width, :] = acc_ref[target].astype(dest.dtype)
+                dest[row, width:, :] = coeffs[target * rank_size : (target + 1) * rank_size]
+
+        @pl.when(own_sub == 0)
+        def _():
+            write(mine_ref, theirs_ref)
+
+        @pl.when(own_sub != 0)
+        def _():
+            write(theirs_ref, mine_ref)
+
+
+def _near_far(pairs_flat, count, place, tiles, early_stack, stack, masked_t, inner_count, rank_size):
     slot_count, width, _ = tiles.shape
-    stack_count, rows, rhs_count = stack.shape
+    stack_count, rows, rhs_count = early_stack.shape
     half_count = inner_count // 2
     out_rows = width + rank_size
     whole = lambda k, p, c, q: (0, 0, 0)
-    grid_spec = pltpu.PrefetchScalarGridSpec(
-        num_scalar_prefetch=3,
-        grid=(1,),
-        in_specs=[
-            pl.BlockSpec(tiles.shape, whole),
-            pl.BlockSpec(stack.shape, whole),
-            pl.BlockSpec(masked_t.shape, whole),
+    acc_shape = (inner_count, width, rhs_count)
+    coeff_shape = (inner_count * rank_size, rhs_count)
+    base_specs = [
+        pl.BlockSpec(tiles.shape, whole),
+        pl.BlockSpec(early_stack.shape, whole),
+        pl.BlockSpec(masked_t.shape, whole),
+    ]
+    acc_spec = pl.BlockSpec(acc_shape, whole)
+    coeff_spec = pl.BlockSpec(coeff_shape, lambda k, p, c, q: (0, 0))
+    vmem_bytes = (
+        2 * (tiles.size * 2 + early_stack.size * 2 + masked_t.size * 2 + 2 * half_count * out_rows * rhs_count * 2)
+        + 6 * (inner_count * width * rhs_count * 4 + inner_count * rank_size * rhs_count * 4)
+        + (4 << 20)
+    )
+    params = pltpu.CompilerParams(dimension_semantics=("arbitrary",), vmem_limit_bytes=int(vmem_bytes))
+    acc, coeff = pl.pallas_call(
+        lambda *r: _partial_kernel(False, *r),
+        grid_spec=pltpu.PrefetchScalarGridSpec(
+            num_scalar_prefetch=3, grid=(1,), in_specs=base_specs, out_specs=[acc_spec, coeff_spec]
+        ),
+        out_shape=[
+            jax.ShapeDtypeStruct(acc_shape, jnp.float32),
+            jax.ShapeDtypeStruct(coeff_shape, jnp.float32),
         ],
-        out_specs=[
-            pl.BlockSpec((half_count, out_rows, rhs_count), whole),
-            pl.BlockSpec((half_count, out_rows, rhs_count), whole),
-        ],
-        scratch_shapes=[pltpu.VMEM((inner_count, width, rhs_count), jnp.float32)],
-    )
+        compiler_params=params,
+    )(pairs_flat, count, place, tiles, early_stack, masked_t)
+    stack = jnp.stack(lax.optimization_barrier((tuple(stack), acc, coeff))[0])
     out = jax.ShapeDtypeStruct((half_count, out_rows, rhs_count), jnp.bfloat16)
-    block_bytes = 2 * (
-        tiles.size * tiles.dtype.itemsize
-        + stack.size * stack.dtype.itemsize
-        + masked_t.size * masked_t.dtype.itemsize
-        + 2 * half_count * out_rows * rhs_count * 2
-    )
-    vmem_bytes = block_bytes + inner_count * width * rhs_count * 4 + (4 << 20)
+    half_spec = pl.BlockSpec((half_count, out_rows, rhs_count), whole)
     return pl.pallas_call(
-        _near_far_kernel,
-        grid_spec=grid_spec,
+        lambda *r: _partial_kernel(True, *r),
+        grid_spec=pltpu.PrefetchScalarGridSpec(
+            num_scalar_prefetch=3,
+            grid=(1,),
+            in_specs=base_specs + [acc_spec, coeff_spec],
+            out_specs=[half_spec, half_spec],
+            scratch_shapes=[pltpu.VMEM(acc_shape, jnp.float32), pltpu.VMEM(coeff_shape, jnp.float32)],
+        ),
         out_shape=[out, out],
-        compiler_params=pltpu.CompilerParams(
-            dimension_semantics=("arbitrary",), vmem_limit_bytes=int(vmem_bytes)
-        ),
-    )(pairs_flat, count, place, tiles, stack, masked_t)
+        compiler_params=params,
+    )(pairs_flat, count, place, tiles, stack, masked_t, acc, coeff)
 
 
 def _epilogue_kernel(me_ref, basis_t_ref, *refs):
@@ -132,7 +168,7 @@
 def _line_gather(payload, axis):
     n = lax.axis_size(axis)
     if n == 1:
-        return payload[None]
+        return payload[None], [payload]
     first_up = lax.ppermute(payload, axis, [(i, (i + 1) % n) for i in range(n)])
     first_down = lax.ppermute(payload, axis, [(i, (i - 1) % n) for i in range(n)])
     ups, downs = [first_up], [first_down]
@@ -147,7 +183,11 @@
     if n > 2:
         ups.append(first_down)
         downs.append(first_up)
-    return jnp.stack(ups[::-1] + [payload] + downs)
+    early_ups = [first_up] * (len(ups) - 1) + [first_down]
+    early_downs = [first_down] * (len(downs) - 1) + [first_up]
+    if n <= 2:
+        early_ups, early_downs = [first_up], [first_down]
+    return jnp.stack(early_ups[::-1] + [payload] + early_downs), (ups[::-1] + [payload] + downs)
 
 
 def _ring_reduce_scatter(blocks, axis):
@@ -175,7 +215,7 @@
     half_rank = rank_size // 2
     packed = jnp.concatenate([basis[:half_rank], basis[half_rank:]], axis=1)
     payload = jnp.concatenate([density, packed], axis=0)
-    stack = _line_gather(payload, "tgt")
+    early_stack, stack = _line_gather(payload, "tgt")
 
     pair_list = near_pairs[0, 0]
     live_count = near_count[0, 0]
@@ -195,7 +235,7 @@
 
     place = jnp.stack([lax.axis_index("tgt"), lax.axis_index("sub")]).astype(jnp.int32)
     mine, theirs = _near_far(
-        pair_list.reshape(-1), live_count.reshape(1), place, near_blocks[0, 0], stack, masked_t,
+        pair_list.reshape(-1), live_count.reshape(1), place, near_blocks[0, 0], early_stack, stack, masked_t,
         inner_count, rank_size,
     )
     basis_t = cluster_basis[0].T

time: 47.4 us -> 45 us (0.949)
  waiting for transfers between devices: 27.7 us -> 24.2 us
  Pallas kernels: 2.81 us -> 4.98 us
  starting transfers between devices: 9.46 us -> 8.58 us
    ppermute x1, waiting for transfers between devices: 10.1 us -> 5.72 us  [_line_gather(): first_up = lax.ppermute(payload, axis, [(i, (i + 1) % n) for i in range(n)])]
    ppermute x1, waiting for transfers between devices: 0.01 us -> 3.44 us  [_line_gather(): lax.ppermute(payload, axis, [(i, (i - 1) % n) for i in range(n)])]
    ppermute x1, waiting for transfers between devices: 8.53 us -> 5.39 us  [_line_gather(): down = lax.ppermute(down, axis, down_pairs)]
    pallas_call x1 -> x2, Pallas kernels: 2.81 us -> 4.98 us  [the longest x1 3.19 us: _near_far(): pl.pallas_call(lambda *r: _partial_kernel(False, *r), grid_spec=pltpu.Pre...]
    ppermute x1, starting transfers between devices: 1.96 us -> 1.21 us  [on_device(): back = lax.ppermute(send, 'inner', swap)]
    unnamed x12 -> x18, local copies, waits for them, and re-layouts: 0.87 us -> 0.99 us
  transfers between devices with their start and end apart: 7 -> 7, of which waited for: 4 -> 6; matrix products, arithmetic and copies ran while one was open for 6% -> 7% of each run, Pallas kernels for 0% -> 7%
where the time goes in v18:
time: 45 us; the launch traced here: 44.8 us
  waiting for transfers between devices  24.2 us (54%)
  starting transfers between devices  8.58 us (19%)
  Pallas kernels  4.98 us (11%)
  local copies, waits for them, and re-layouts  2.98 us (7%)
  other arithmetic  2.22 us (5%)
  matrix products  0.97 us (2%)
  between operations  0.89 us (2%)
    ppermute x1, waiting for transfers between devices, on_device(): back = lax.ppermute(send, 'inner', swap)  7.84 us
    ppermute x1, waiting for transfers between devices, _line_gather(): first_up = lax.ppermute(payload, axis, [(i, (i + 1) % n) for i in range(n)])  5.72 us
    ppermute x1, waiting for transfers between devices, _line_gather(): down = lax.ppermute(down, axis, down_pairs)  5.39 us
    ppermute x1, starting transfers between devices, _line_gather(): lax.ppermute(payload, axis, [(i, (i - 1) % n) for i in range(n)])  5.13 us
    ppermute x1, waiting for transfers between devices, _line_gather(): lax.ppermute(payload, axis, [(i, (i - 1) % n) for i in range(n)])  3.44 us
    pallas_call x1, Pallas kernels, _near_far(): pl.pallas_call(lambda *r: _partial_kernel(False, *r), grid_spec=pltpu.Pre...  3.19 us
    pallas_call x1, Pallas kernels, _near_far(): pl.pallas_call(lambda *r: _partial_kernel(True, *r), grid_spec=pltpu.Pref...  1.79 us
    ppermute x1, waiting for transfers between devices, on_device(): lax.ppermute(lax.dynamic_index_in_dim(theirs, 1 - me, 0, False), 'sub', s...  1.57 us
  transfers between devices with their start and end apart: 7, of which 6 were waited for; matrix products, arithmetic and copies ran while one was open for 7% of the time, Pallas kernels for 7%

profile of v18, /device:TPU:0, one launch (start us, length us, event | category | flops | bytes accessed | tf_op | source)
XLA Modules:
  0.0 44.8 jit_solution(10692038704008354999)
XLA Ops:
  0.0 0.0 copy-start.1
  0.0 0.8 %slice_bitcast_fusion.1 = (bf16[16,256]{1,0:T(8,128)(2,1)S(1)}, bf16[16,256]{1,0:T(8,128)(2,1)S(1)}) fusion(bf16[1,32,256]{2,1,0:T(8,128)(2,1)} %param.7), kind=kLoop, calls=%fused_computation.28 | loop fusion | bytes 32768 | tf_op jit(solution)/shard_map/slice | solution.py:216
  0.8 1.0 %maximum_maximum_fusion = bf16[272,512]{1,0:T(8,128)(2,1)S(1)} fusion(bf16[16,256]{1,0:T(8,128)(2,1)S(1)} %get-tuple-element.32, bf16[16,256]{1,0:T(8,128)(2,1)S(1)} %get-tuple-element.31, bf16[256,512]{1,0:T(8,128)(2,1)} %param.6), kind=kLoop, calls=%fused_computation.9 | loop fusion | flops 835584 | bytes 557056 | tf_op jit(solution)/shard_map/concatenate | solution.py:217
  1.7 5.1 %collective-permute-start = (bf16[272,512]{1,0:T(8,128)(2,1)S(1)}, bf16[272,512]{1,0:T(8,128)(2,1)S(1)}, u32[]{:S(2)}, u32[]{:S(2)}) collective-permute-start(bf16[272,512]{1,0:T(8,128)(2,1)S(1)} %maximum_maximum_fusion), channel_id=1, source_target_pairs={{0,12},{4,0},{8,4},{12,8},{1,13},{5,1},{9,5},{13,9},{2,14},{6,2},{... | collective-permute-start | bytes 835592 | tf_op jit(solution)/shard_map/ppermute | solution.py:173
  6.9 0.0 collective-permute-start.1
  7.5 0.8 %add_bitcast_fusion = s32[8]{0:T(128)S(1)} fusion(s32[8,2]{0,1:T(2,128)} %bitcast.67), kind=kLoop, calls=%fused_computation.35 | loop fusion | flops 16 | bytes 96 | tf_op jit(solution)/shard_map/eq | solution.py:225
  8.3 0.1 fusion.5
  8.4 0.1 convert_element_type.50
  8.5 0.1 copy.16
  8.6 0.9 %reshape_squeeze.11 = bf16[4,32,4,32]{3,2,1,0:T(4,128)(2,1)S(1)} reshape(bf16[1,1,128,128]{3,2,1,0:T(8,128)(2,1)} %param.11) | data formatting | bytes 65536 | tf_op jit(solution)/shard_map/reshape;squeeze | solution.py:233
  9.5 0.1 copy_multiply_fusion
  9.6 0.1 pad_add_fusion.r_2_
  9.6 0.8 %copy.15 = s32[1,1,8,2]{3,2,1,0:T(8,128)S(1)} copy(s32[1,1,8,2]{2,3,1,0:T(2,128)} %param.9) | data formatting | bytes 128 | tf_op args[3]
  10.4 0.1 reshape_squeeze.9.r_0_
  10.5 0.0 copy-start
  10.5 3.4 %collective-permute-done = bf16[272,512]{1,0:T(8,128)(2,1)S(1)} collective-permute-done((bf16[272,512]{1,0:T(8,128)(2,1)S(1)}, bf16[272,512]{1,0:T(8,128)(2,1)S(1)}, u32[]{:S(2)}, u32[]{:S(2)}) %collective-permute-start) | collective-permute-done | bytes 278560 | tf_op jit(solution)/shard_map/ppermute | solution.py:173
  13.9 5.7 %collective-permute-done.1 = bf16[272,512]{1,0:T(8,128)(2,1)S(1)} collective-permute-done((bf16[272,512]{1,0:T(8,128)(2,1)S(1)}, bf16[272,512]{1,0:T(8,128)(2,1)S(1)}, u32[]{:S(2)}, u32[]{:S(2)}) %collective-permute-start.1) | collective-permute-done | bytes 278560 | tf_op jit(solution)/shard_map/ppermute | solution.py:172
  19.7 0.0 copy-done.1
  19.7 0.7 %collective-permute-start.2 = (bf16[272,512]{1,0:T(8,128)(2,1)S(1)}, bf16[272,512]{1,0:T(8,128)(2,1)S(1)}, u32[]{:S(2)}, u32[]{:S(2)}) collective-permute-start(bf16[272,512]{1,0:T(8,128)(2,1)S(1)} %collective-permute-done.1), channel_id=1, source_target_pairs={{4,8},{8,12},{5,9},{9,13},{6,10},{10,14},{7,11},{11,15},{20,24},{2... | collective-permute-start | bytes 835592 | tf_op jit(solution)/shard_map/ppermute | solution.py:179
  20.4 1.3 %collective-permute-start.3 = (bf16[272,512]{1,0:T(8,128)(2,1)S(1)}, bf16[272,512]{1,0:T(8,128)(2,1)S(1)}, u32[]{:S(2)}, u32[]{:S(2)}) collective-permute-start(bf16[272,512]{1,0:T(8,128)(2,1)S(1)} %collective-permute-done), channel_id=1, source_target_pairs={{4,0},{8,4},{5,1},{9,5},{6,2},{10,6},{7,3},{11,7},{20,16},{24,20},... | collective-permute-start | bytes 835592 | tf_op jit(solution)/shard_map/ppermute | solution.py:180
  21.8 0.0 copy-done
  21.8 3.2 %shard_map.64 = (f32[4,256,512]{2,1,0:T(8,128)S(1)}, f32[128,512]{1,0:T(8,128)S(1)}) custom-call(s32[16]{0:T(128)S(1)} %reshape_squeeze.9.r_0_, s32[1]{0:T(128)} %bitcast.60.r_1_, s32[2]{0:T(128)S(1)} %pad_add_fusion.r_2_, bf16[8,256,256]{2,1,0:T(8,128)(2,1)S(1)} %bitcast.63, bf16[7,272,512]{2,1,0:T(8,128)(2,1)S(1)} %bitcast_dynamic-update-slice_fusion.10.r_4_, ...), custom_call_target="tpu_custom_call" | custom-call | tf_op jit(solution)/shard_map/pallas_call | solution.py:107
  25.0 0.0 collective-permute-done.2
  25.0 5.4 %collective-permute-done.3 = bf16[272,512]{1,0:T(8,128)(2,1)S(1)} collective-permute-done((bf16[272,512]{1,0:T(8,128)(2,1)S(1)}, bf16[272,512]{1,0:T(8,128)(2,1)S(1)}, u32[]{:S(2)}, u32[]{:S(2)}) %collective-permute-start.3) | collective-permute-done | bytes 278560 | tf_op jit(solution)/shard_map/ppermute | solution.py:180
  30.6 1.8 %shard_map.65 = (bf16[2,288,512]{2,1,0:T(8,128)(2,1)S(1)}, bf16[2,288,512]{2,1,0:T(8,128)(2,1)S(1)}) custom-call(s32[16]{0:T(128)S(1)} %reshape_squeeze.9.r_0_, s32[1]{0:T(128)} %bitcast.61.r_1_, s32[2]{0:T(128)S(1)} %pad_add_fusion.r_2_, bf16[8,256,256]{2,1,0:T(8,128)(2,1)S(1)} %bitcast.64, bf16[7,272,512]{2,1,0:T(8,128)(2,1)S(1)} %bitcast_dynamic-update-slice_fusion.r_4_, ...), custom_call_target="tpu_custom_call" | custom-call | tf_op jit(solution)/shard_map/pallas_call | solution.py:121
  32.4 0.0 copy-start.2
  32.5 0.1 collective-permute-start.4
  32.6 1.6 %collective-permute-done.4 = bf16[288,512]{1,0:T(8,128)(2,1)S(1)} collective-permute-done((bf16[288,512]{1,0:T(8,128)(2,1)S(1)}, bf16[288,512]{1,0:T(8,128)(2,1)S(1)}, u32[]{:S(2)}, u32[]{:S(2)}) %collective-permute-start.4) | collective-permute-done | bytes 294944 | tf_op jit(solution)/shard_map/ppermute | solution.py:245
  34.1 0.1 fusion
  34.2 0.2 collective-permute-start.5
  34.4 1.2 %collective-permute-start.6 = (bf16[288,512]{1,0:T(8,128)(2,1)S(1)}, bf16[288,512]{1,0:T(8,128)(2,1)S(1)}, u32[]{:S(2)}, u32[]{:S(2)}) collective-permute-start(bf16[288,512]{1,0:T(8,128)(2,1)S(1)} %fusion), channel_id=1, source_target_pairs={{0,2},{2,0},{1,3},{3,1},{4,6},{6,4},{5,7},{7,5},{8,10},{10,8},{9,1... | collective-permute-start | bytes 884744 | tf_op jit(solution)/shard_map/ppermute | solution.py:250
  35.6 0.2 collective-permute-done.5
  35.9 7.8 %collective-permute-done.6 = bf16[288,512]{1,0:T(8,128)(2,1)S(1)} collective-permute-done((bf16[288,512]{1,0:T(8,128)(2,1)S(1)}, bf16[288,512]{1,0:T(8,128)(2,1)S(1)}, u32[]{:S(2)}, u32[]{:S(2)}) %collective-permute-start.6) | collective-permute-done | bytes 294944 | tf_op jit(solution)/shard_map/ppermute | solution.py:250
  43.7 0.1 fusion.1
  43.8 0.0 copy-done.2
  43.8 1.0 %fusion.2 = bf16[256,512]{1,0:T(8,128)(2,1)} fusion(f32[288,512]{1,0:T(8,128)S(1)} %fusion.1, bf16[1,32,256]{2,1,0:T(8,128)(2,1)S(1)} %copy-done.2), kind=kOutput, calls=%fused_computation.6 | convolution fusion | flops 8667136 | bytes 868352 | tf_op jit(solution)/shard_map/dot_general | solution.py:265
  (17 shorter events, 0.3 us)
Async XLA Ops:
  0.0 19.7 %copy-start.1 = (bf16[256,512]{1,0:T(8,128)(2,1)S(1)}, bf16[256,512]{1,0:T(8,128)(2,1)}, u32[]{:S(2)}) copy-start(bf16[256,512]{1,0:T(8,128)(2,1)} %param.6) | copy-start | bytes 786436
  1.7 12.2 %collective-permute-start = (bf16[272,512]{1,0:T(8,128)(2,1)S(1)}, bf16[272,512]{1,0:T(8,128)(2,1)S(1)}, u32[]{:S(2)}, u32[]{:S(2)}) collective-permute-start(bf16[272,512]{1,0:T(8,128)(2,1)S(1)} %maximum_maximum_fusion), channel_id=1, source_target_pairs={{0,12},{4,0},{8,4},{12,8},{1,13},{5,1},{9,5},{13,9},{2,14},{6,2},{... | collective-permute-start | bytes 835592 | tf_op jit(solution)/shard_map/ppermute | solution.py:173
  6.9 12.8 %collective-permute-start.1 = (bf16[272,512]{1,0:T(8,128)(2,1)S(1)}, bf16[272,512]{1,0:T(8,128)(2,1)S(1)}, u32[]{:S(2)}, u32[]{:S(2)}) collective-permute-start(bf16[272,512]{1,0:T(8,128)(2,1)S(1)} %maximum_maximum_fusion), channel_id=1, source_target_pairs={{0,4},{4,8},{8,12},{12,0},{1,5},{5,9},{9,13},{13,1},{2,6},{6,10},{... | collective-permute-start | bytes 835592 | tf_op jit(solution)/shard_map/ppermute | solution.py:172
  10.5 11.3 %copy-start = (bf16[1,1,8,256,256]{4,3,2,1,0:T(8,128)(2,1)S(1)}, bf16[1,1,8,256,256]{4,3,2,1,0:T(8,128)(2,1)}, u32[]{:S(2)}) copy-start(bf16[1,1,8,256,256]{4,3,2,1,0:T(8,128)(2,1)} %param.8) | copy-start | bytes 3145732
  19.7 5.3 %collective-permute-start.2 = (bf16[272,512]{1,0:T(8,128)(2,1)S(1)}, bf16[272,512]{1,0:T(8,128)(2,1)S(1)}, u32[]{:S(2)}, u32[]{:S(2)}) collective-permute-start(bf16[272,512]{1,0:T(8,128)(2,1)S(1)} %collective-permute-done.1), channel_id=1, source_target_pairs={{4,8},{8,12},{5,9},{9,13},{6,10},{10,14},{7,11},{11,15},{20,24},{2... | collective-permute-start | bytes 835592 | tf_op jit(solution)/shard_map/ppermute | solution.py:179
  20.4 10.0 %collective-permute-start.3 = (bf16[272,512]{1,0:T(8,128)(2,1)S(1)}, bf16[272,512]{1,0:T(8,128)(2,1)S(1)}, u32[]{:S(2)}, u32[]{:S(2)}) collective-permute-start(bf16[272,512]{1,0:T(8,128)(2,1)S(1)} %collective-permute-done), channel_id=1, source_target_pairs={{4,0},{8,4},{5,1},{9,5},{6,2},{10,6},{7,3},{11,7},{20,16},{24,20},... | collective-permute-start | bytes 835592 | tf_op jit(solution)/shard_map/ppermute | solution.py:180
  32.4 11.4 %copy-start.2 = (bf16[1,32,256]{2,1,0:T(8,128)(2,1)S(1)}, bf16[1,32,256]{2,1,0:T(8,128)(2,1)}, u32[]{:S(2)}) copy-start(bf16[1,32,256]{2,1,0:T(8,128)(2,1)} %param.7) | copy-start | bytes 49156
  32.5 1.6 %collective-permute-start.4 = (bf16[288,512]{1,0:T(8,128)(2,1)S(1)}, bf16[288,512]{1,0:T(8,128)(2,1)S(1)}, u32[]{:S(2)}, u32[]{:S(2)}) collective-permute-start(bf16[288,512]{1,0:T(8,128)(2,1)S(1)} %get-tuple-element.30), channel_id=1, source_target_pairs={{0,1},{1,0},{2,3},{3,2},{4,5},{5,4},{6,7},{7,6},{8,9},{9,8},{10,11... | collective-permute-start | bytes 884744 | tf_op jit(solution)/shard_map/ppermute | solution.py:245
  34.2 1.6 %collective-permute-start.5 = (bf16[288,512]{1,0:T(8,128)(2,1)S(1)}, bf16[288,512]{1,0:T(8,128)(2,1)S(1)}, u32[]{:S(2)}, u32[]{:S(2)}) collective-permute-start(bf16[288,512]{1,0:T(8,128)(2,1)S(1)} %get-tuple-element.28), channel_id=1, source_target_pairs={{0,1},{1,0},{2,3},{3,2},{4,5},{5,4},{6,7},{7,6},{8,9},{9,8},{10,11... | collective-permute-start | bytes 884744 | tf_op jit(solution)/shard_map/ppermute | solution.py:252
  34.4 9.3 %collective-permute-start.6 = (bf16[288,512]{1,0:T(8,128)(2,1)S(1)}, bf16[288,512]{1,0:T(8,128)(2,1)S(1)}, u32[]{:S(2)}, u32[]{:S(2)}) collective-permute-start(bf16[288,512]{1,0:T(8,128)(2,1)S(1)} %fusion), channel_id=1, source_target_pairs={{0,2},{2,0},{1,3},{3,1},{4,6},{6,4},{5,7},{7,5},{8,10},{10,8},{9,1... | collective-permute-start | bytes 884744 | tf_op jit(solution)/shard_map/ppermute | solution.py:250

commit v19 on v18

--- a/solution.py
+++ b/solution.py
@@ -18,6 +18,14 @@
     sub_count = 2
     own_tgt = place_ref[0]
     own_sub = place_ref[1]
+    stack_count = stack_ref.shape[0]
+
+    def stack_index(offset):
+        if not late:
+            return offset + tgt_count - 1
+        place = jnp.where(offset < 0, tgt_count - 2 + offset, offset + tgt_count - 5)
+        return jnp.clip(place, 0, stack_count - 1)
+
     if late:
         acc_in, coeff_in, mine_ref, theirs_ref, acc_ref, coeff_ref = refs
         inner_count = acc_in.shape[0]
@@ -39,7 +47,7 @@
         def _():
             term = jnp.dot(
                 tiles_ref[slot],
-                stack_ref[offset + tgt_count - 1, :width, :],
+                stack_ref[stack_index(offset), :width, :],
                 preferred_element_type=jnp.float32,
             )
             acc_ref[target] += term
@@ -54,7 +62,7 @@
 
         @pl.when(wanted)
         def _():
-            block = stack_ref[offset + tgt_count - 1]
+            block = stack_ref[stack_index(offset)]
             dens = block[:width, :]
             packed = block[width:, :]
             top = jnp.dot(packed[:, :width], dens, preferred_element_type=jnp.float32)
@@ -116,6 +124,7 @@
         compiler_params=params,
     )(pairs_flat, count, place, tiles, early_stack, masked_t)
     stack = jnp.stack(lax.optimization_barrier((tuple(stack), acc, coeff))[0])
+    late_specs = [base_specs[0], pl.BlockSpec(stack.shape, whole), base_specs[2]]
     out = jax.ShapeDtypeStruct((half_count, out_rows, rhs_count), jnp.bfloat16)
     half_spec = pl.BlockSpec((half_count, out_rows, rhs_count), whole)
     return pl.pallas_call(
@@ -123,7 +132,7 @@
         grid_spec=pltpu.PrefetchScalarGridSpec(
             num_scalar_prefetch=3,
             grid=(1,),
-            in_specs=base_specs + [acc_spec, coeff_spec],
+            in_specs=late_specs + [acc_spec, coeff_spec],
             out_specs=[half_spec, half_spec],
             scratch_shapes=[pltpu.VMEM(acc_shape, jnp.float32), pltpu.VMEM(coeff_shape, jnp.float32)],
         ),
@@ -187,7 +196,8 @@
     early_downs = [first_down] * (len(downs) - 1) + [first_up]
     if n <= 2:
         early_ups, early_downs = [first_up], [first_down]
-    return jnp.stack(early_ups[::-1] + [payload] + early_downs), (ups[::-1] + [payload] + downs)
+    late = ups[1:-1][::-1] + downs[1:-1] if n > 3 else [payload]
+    return jnp.stack(early_ups[::-1] + [payload] + early_downs), late
 
 
 def _ring_reduce_scatter(blocks, axis):

time: 45 us -> 44.8 us (level)
  Pallas kernels: 4.98 us -> 3.97 us
    ppermute x1, waiting for transfers between devices: 5.39 us -> 6.1 us  [_line_gather(): down = lax.ppermute(down, axis, down_pairs)]
    pallas_call x1, Pallas kernels: 3.19 us -> 2.48 us  [_near_far(): pl.pallas_call(lambda *r: _partial_kernel(False, *r), grid_spec=pltpu.Pre...]
    unnamed x18 -> x12, local copies, waits for them, and re-layouts: 0.99 us -> 0.87 us
  transfers between devices with their start and end apart: 7 -> 7, of which waited for: 6 -> 5; matrix products, arithmetic and copies ran while one was open for 7% -> 7% of each run, Pallas kernels for 7% -> 6%
where the time goes in v19:
time: 44.8 us; the launch traced here: 44.4 us
  waiting for transfers between devices  24.5 us (55%)
  starting transfers between devices  8.94 us (20%)
  Pallas kernels  3.97 us (9%)
  local copies, waits for them, and re-layouts  2.84 us (6%)
  other arithmetic  2.27 us (5%)
  matrix products  0.97 us (2%)
  between operations  0.84 us (2%)
    ppermute x1, waiting for transfers between devices, on_device(): back = lax.ppermute(send, 'inner', swap)  7.71 us
    ppermute x1, waiting for transfers between devices, _line_gather(): down = lax.ppermute(down, axis, down_pairs)  6.1 us
    ppermute x1, waiting for transfers between devices, _line_gather(): first_up = lax.ppermute(payload, axis, [(i, (i + 1) % n) for i in range(n)])  5.72 us
    ppermute x1, starting transfers between devices, _line_gather(): lax.ppermute(payload, axis, [(i, (i - 1) % n) for i in range(n)])  5.13 us
    ppermute x1, waiting for transfers between devices, _line_gather(): lax.ppermute(payload, axis, [(i, (i - 1) % n) for i in range(n)])  3.44 us
    pallas_call x1, Pallas kernels, _near_far(): pl.pallas_call(lambda *r: _partial_kernel(False, *r), grid_spec=pltpu.Pre...  2.48 us
    ppermute x1, waiting for transfers between devices, on_device(): lax.ppermute(lax.dynamic_index_in_dim(theirs, 1 - me, 0, False), 'sub', s...  1.57 us
    ppermute x1, starting transfers between devices, on_device(): back = lax.ppermute(send, 'inner', swap)  1.57 us
  transfers between devices with their start and end apart: 7, of which 5 were waited for; matrix products, arithmetic and copies ran while one was open for 7% of the time, Pallas kernels for 6%

profile of v19, /device:TPU:0, one launch (start us, length us, event | category | flops | bytes accessed | tf_op | source)
XLA Modules:
  0.0 44.4 jit_solution(1695939039299688585)
XLA Ops:
  0.0 0.0 copy-start.1
  0.0 0.8 %slice_bitcast_fusion.1 = (bf16[16,256]{1,0:T(8,128)(2,1)S(1)}, bf16[16,256]{1,0:T(8,128)(2,1)S(1)}) fusion(bf16[1,32,256]{2,1,0:T(8,128)(2,1)} %param.7), kind=kLoop, calls=%fused_computation.22 | loop fusion | bytes 32768 | tf_op jit(solution)/shard_map/slice | solution.py:226
  0.8 1.0 %maximum_maximum_fusion = bf16[272,512]{1,0:T(8,128)(2,1)S(1)} fusion(bf16[16,256]{1,0:T(8,128)(2,1)S(1)} %get-tuple-element.22, bf16[16,256]{1,0:T(8,128)(2,1)S(1)} %get-tuple-element.21, bf16[256,512]{1,0:T(8,128)(2,1)} %param.6), kind=kLoop, calls=%fused_computation.10 | loop fusion | flops 835584 | bytes 557056 | tf_op jit(solution)/shard_map/concatenate | solution.py:227
  1.7 5.1 %collective-permute-start.2 = (bf16[272,512]{1,0:T(8,128)(2,1)S(1)}, bf16[272,512]{1,0:T(8,128)(2,1)S(1)}, u32[]{:S(2)}, u32[]{:S(2)}) collective-permute-start(bf16[272,512]{1,0:T(8,128)(2,1)S(1)} %maximum_maximum_fusion), channel_id=1, source_target_pairs={{0,12},{4,0},{8,4},{12,8},{1,13},{5,1},{9,5},{13,9},{2,14},{6,2},{... | collective-permute-start | bytes 835592 | tf_op jit(solution)/shard_map/ppermute | solution.py:182
  6.9 0.0 collective-permute-start
  7.5 0.8 %add_bitcast_fusion = s32[8]{0:T(128)S(1)} fusion(s32[8,2]{0,1:T(2,128)} %bitcast.57), kind=kLoop, calls=%fused_computation.29 | loop fusion | flops 16 | bytes 96 | tf_op jit(solution)/shard_map/eq | solution.py:235
  8.3 0.1 fusion.5
  8.4 0.1 convert_element_type.50
  8.5 0.1 copy.16
  8.6 0.9 %reshape_squeeze.11 = bf16[4,32,4,32]{3,2,1,0:T(4,128)(2,1)S(1)} reshape(bf16[1,1,128,128]{3,2,1,0:T(8,128)(2,1)} %param.11) | data formatting | bytes 65536 | tf_op jit(solution)/shard_map/reshape;squeeze | solution.py:243
  9.5 0.1 copy_multiply_fusion
  9.6 0.1 pad_add_fusion.r_2_
  9.6 0.8 %copy.15 = s32[1,1,8,2]{3,2,1,0:T(8,128)S(1)} copy(s32[1,1,8,2]{2,3,1,0:T(2,128)} %param.9) | data formatting | bytes 128 | tf_op args[3]
  10.4 0.1 reshape_squeeze.9.r_0_
  10.5 0.0 copy-start
  10.5 3.4 %collective-permute-done.2 = bf16[272,512]{1,0:T(8,128)(2,1)S(1)} collective-permute-done((bf16[272,512]{1,0:T(8,128)(2,1)S(1)}, bf16[272,512]{1,0:T(8,128)(2,1)S(1)}, u32[]{:S(2)}, u32[]{:S(2)}) %collective-permute-start.2) | collective-permute-done | bytes 278560 | tf_op jit(solution)/shard_map/ppermute | solution.py:182
  13.9 5.7 %collective-permute-done = bf16[272,512]{1,0:T(8,128)(2,1)S(1)} collective-permute-done((bf16[272,512]{1,0:T(8,128)(2,1)S(1)}, bf16[272,512]{1,0:T(8,128)(2,1)S(1)}, u32[]{:S(2)}, u32[]{:S(2)}) %collective-permute-start) | collective-permute-done | bytes 278560 | tf_op jit(solution)/shard_map/ppermute | solution.py:181
  19.7 0.0 copy-done.1
  19.7 0.7 %collective-permute-start.1 = (bf16[272,512]{1,0:T(8,128)(2,1)S(1)}, bf16[272,512]{1,0:T(8,128)(2,1)S(1)}, u32[]{:S(2)}, u32[]{:S(2)}) collective-permute-start(bf16[272,512]{1,0:T(8,128)(2,1)S(1)} %collective-permute-done), channel_id=1, source_target_pairs={{4,8},{8,12},{5,9},{9,13},{6,10},{10,14},{7,11},{11,15},{20,24},{2... | collective-permute-start | bytes 835592 | tf_op jit(solution)/shard_map/ppermute | solution.py:188
  20.4 1.3 %collective-permute-start.3 = (bf16[272,512]{1,0:T(8,128)(2,1)S(1)}, bf16[272,512]{1,0:T(8,128)(2,1)S(1)}, u32[]{:S(2)}, u32[]{:S(2)}) collective-permute-start(bf16[272,512]{1,0:T(8,128)(2,1)S(1)} %collective-permute-done.2), channel_id=1, source_target_pairs={{4,0},{8,4},{5,1},{9,5},{6,2},{10,6},{7,3},{11,7},{20,16},{24,20},... | collective-permute-start | bytes 835592 | tf_op jit(solution)/shard_map/ppermute | solution.py:189
  21.8 0.0 copy-done
  21.8 2.5 %shard_map.64 = (f32[4,256,512]{2,1,0:T(8,128)S(1)}, f32[128,512]{1,0:T(8,128)S(1)}) custom-call(s32[16]{0:T(128)S(1)} %reshape_squeeze.9.r_0_, s32[1]{0:T(128)} %bitcast.48.r_1_, s32[2]{0:T(128)S(1)} %pad_add_fusion.r_2_, bf16[8,256,256]{2,1,0:T(8,128)(2,1)S(1)} %bitcast.51, bf16[7,272,512]{2,1,0:T(8,128)(2,1)S(1)} %bitcast_dynamic-update-slice_fusion.3.r_4_, ...), custom_call_target="tpu_custom_call" | custom-call | tf_op jit(solution)/shard_map/pallas_call | solution.py:115
  24.3 0.0 collective-permute-done.1
  24.3 6.1 %collective-permute-done.3 = bf16[272,512]{1,0:T(8,128)(2,1)S(1)} collective-permute-done((bf16[272,512]{1,0:T(8,128)(2,1)S(1)}, bf16[272,512]{1,0:T(8,128)(2,1)S(1)}, u32[]{:S(2)}, u32[]{:S(2)}) %collective-permute-start.3) | collective-permute-done | bytes 278560 | tf_op jit(solution)/shard_map/ppermute | solution.py:189
  30.4 0.1 pad_maximum_fusion.r_4_
  30.5 1.5 %shard_map.65 = (bf16[2,288,512]{2,1,0:T(8,128)(2,1)S(1)}, bf16[2,288,512]{2,1,0:T(8,128)(2,1)S(1)}) custom-call(s32[16]{0:T(128)S(1)} %reshape_squeeze.9.r_0_, s32[1]{0:T(128)} %bitcast.49.r_1_, s32[2]{0:T(128)S(1)} %pad_add_fusion.r_2_, bf16[8,256,256]{2,1,0:T(8,128)(2,1)S(1)} %bitcast.52, bf16[2,272,512]{2,1,0:T(8,128)(2,1)S(1)} %pad_maximum_fusion.r_4_, ...), custom_call_target="tpu_custom_call" | custom-call | tf_op jit(solution)/shard_map/pallas_call | solution.py:130
  32.0 0.0 copy-start.2
  32.1 0.1 collective-permute-start.4
  32.1 1.6 %collective-permute-done.4 = bf16[288,512]{1,0:T(8,128)(2,1)S(1)} collective-permute-done((bf16[288,512]{1,0:T(8,128)(2,1)S(1)}, bf16[288,512]{1,0:T(8,128)(2,1)S(1)}, u32[]{:S(2)}, u32[]{:S(2)}) %collective-permute-start.4) | collective-permute-done | bytes 294944 | tf_op jit(solution)/shard_map/ppermute | solution.py:255
  33.7 0.1 fusion
  33.8 0.2 collective-permute-start.5
  34.0 1.6 %collective-permute-start.6 = (bf16[288,512]{1,0:T(8,128)(2,1)S(1)}, bf16[288,512]{1,0:T(8,128)(2,1)S(1)}, u32[]{:S(2)}, u32[]{:S(2)}) collective-permute-start(bf16[288,512]{1,0:T(8,128)(2,1)S(1)} %fusion), channel_id=1, source_target_pairs={{0,2},{2,0},{1,3},{3,1},{4,6},{6,4},{5,7},{7,5},{8,10},{10,8},{9,1... | collective-permute-start | bytes 884744 | tf_op jit(solution)/shard_map/ppermute | solution.py:260
  35.6 0.0 collective-permute-done.5
  35.6 7.7 %collective-permute-done.6 = bf16[288,512]{1,0:T(8,128)(2,1)S(1)} collective-permute-done((bf16[288,512]{1,0:T(8,128)(2,1)S(1)}, bf16[288,512]{1,0:T(8,128)(2,1)S(1)}, u32[]{:S(2)}, u32[]{:S(2)}) %collective-permute-start.6) | collective-permute-done | bytes 294944 | tf_op jit(solution)/shard_map/ppermute | solution.py:260
  43.3 0.1 fusion.1
  43.4 0.0 copy-done.2
  43.4 1.0 %fusion.2 = bf16[256,512]{1,0:T(8,128)(2,1)} fusion(f32[288,512]{1,0:T(8,128)S(1)} %fusion.1, bf16[1,32,256]{2,1,0:T(8,128)(2,1)S(1)} %copy-done.2), kind=kOutput, calls=%fused_computation.7 | convolution fusion | flops 8667136 | bytes 868352 | tf_op jit(solution)/shard_map/dot_general | solution.py:275
  (10 shorter events, 0.2 us)
Async XLA Ops:
  0.0 19.7 %copy-start.1 = (bf16[256,512]{1,0:T(8,128)(2,1)S(1)}, bf16[256,512]{1,0:T(8,128)(2,1)}, u32[]{:S(2)}) copy-start(bf16[256,512]{1,0:T(8,128)(2,1)} %param.6) | copy-start | bytes 786436
  1.7 12.2 %collective-permute-start.2 = (bf16[272,512]{1,0:T(8,128)(2,1)S(1)}, bf16[272,512]{1,0:T(8,128)(2,1)S(1)}, u32[]{:S(2)}, u32[]{:S(2)}) collective-permute-start(bf16[272,512]{1,0:T(8,128)(2,1)S(1)} %maximum_maximum_fusion), channel_id=1, source_target_pairs={{0,12},{4,0},{8,4},{12,8},{1,13},{5,1},{9,5},{13,9},{2,14},{6,2},{... | collective-permute-start | bytes 835592 | tf_op jit(solution)/shard_map/ppermute | solution.py:182
  6.9 12.8 %collective-permute-start = (bf16[272,512]{1,0:T(8,128)(2,1)S(1)}, bf16[272,512]{1,0:T(8,128)(2,1)S(1)}, u32[]{:S(2)}, u32[]{:S(2)}) collective-permute-start(bf16[272,512]{1,0:T(8,128)(2,1)S(1)} %maximum_maximum_fusion), channel_id=1, source_target_pairs={{0,4},{4,8},{8,12},{12,0},{1,5},{5,9},{9,13},{13,1},{2,6},{6,10},{... | collective-permute-start | bytes 835592 | tf_op jit(solution)/shard_map/ppermute | solution.py:181
  10.5 11.3 %copy-start = (bf16[1,1,8,256,256]{4,3,2,1,0:T(8,128)(2,1)S(1)}, bf16[1,1,8,256,256]{4,3,2,1,0:T(8,128)(2,1)}, u32[]{:S(2)}) copy-start(bf16[1,1,8,256,256]{4,3,2,1,0:T(8,128)(2,1)} %param.8) | copy-start | bytes 3145732
  19.7 4.6 %collective-permute-start.1 = (bf16[272,512]{1,0:T(8,128)(2,1)S(1)}, bf16[272,512]{1,0:T(8,128)(2,1)S(1)}, u32[]{:S(2)}, u32[]{:S(2)}) collective-permute-start(bf16[272,512]{1,0:T(8,128)(2,1)S(1)} %collective-permute-done), channel_id=1, source_target_pairs={{4,8},{8,12},{5,9},{9,13},{6,10},{10,14},{7,11},{11,15},{20,24},{2... | collective-permute-start | bytes 835592 | tf_op jit(solution)/shard_map/ppermute | solution.py:188
  20.4 10.0 %collective-permute-start.3 = (bf16[272,512]{1,0:T(8,128)(2,1)S(1)}, bf16[272,512]{1,0:T(8,128)(2,1)S(1)}, u32[]{:S(2)}, u32[]{:S(2)}) collective-permute-start(bf16[272,512]{1,0:T(8,128)(2,1)S(1)} %collective-permute-done.2), channel_id=1, source_target_pairs={{4,0},{8,4},{5,1},{9,5},{6,2},{10,6},{7,3},{11,7},{20,16},{24,20},... | collective-permute-start | bytes 835592 | tf_op jit(solution)/shard_map/ppermute | solution.py:189
  32.0 11.4 %copy-start.2 = (bf16[1,32,256]{2,1,0:T(8,128)(2,1)S(1)}, bf16[1,32,256]{2,1,0:T(8,128)(2,1)}, u32[]{:S(2)}) copy-start(bf16[1,32,256]{2,1,0:T(8,128)(2,1)} %param.7) | copy-start | bytes 49156
  32.1 1.6 %collective-permute-start.4 = (bf16[288,512]{1,0:T(8,128)(2,1)S(1)}, bf16[288,512]{1,0:T(8,128)(2,1)S(1)}, u32[]{:S(2)}, u32[]{:S(2)}) collective-permute-start(bf16[288,512]{1,0:T(8,128)(2,1)S(1)} %get-tuple-element.20), channel_id=1, source_target_pairs={{0,1},{1,0},{2,3},{3,2},{4,5},{5,4},{6,7},{7,6},{8,9},{9,8},{10,11... | collective-permute-start | bytes 884744 | tf_op jit(solution)/shard_map/ppermute | solution.py:255
  33.8 1.8 %collective-permute-start.5 = (bf16[288,512]{1,0:T(8,128)(2,1)S(1)}, bf16[288,512]{1,0:T(8,128)(2,1)S(1)}, u32[]{:S(2)}, u32[]{:S(2)}) collective-permute-start(bf16[288,512]{1,0:T(8,128)(2,1)S(1)} %get-tuple-element.18), channel_id=1, source_target_pairs={{0,1},{1,0},{2,3},{3,2},{4,5},{5,4},{6,7},{7,6},{8,9},{9,8},{10,11... | collective-permute-start | bytes 884744 | tf_op jit(solution)/shard_map/ppermute | solution.py:262
  34.0 9.3 %collective-permute-start.6 = (bf16[288,512]{1,0:T(8,128)(2,1)S(1)}, bf16[288,512]{1,0:T(8,128)(2,1)S(1)}, u32[]{:S(2)}, u32[]{:S(2)}) collective-permute-start(bf16[288,512]{1,0:T(8,128)(2,1)S(1)} %fusion), channel_id=1, source_target_pairs={{0,2},{2,0},{1,3},{3,1},{4,6},{6,4},{5,7},{7,5},{8,10},{10,8},{9,1... | collective-permute-start | bytes 884744 | tf_op jit(solution)/shard_map/ppermute | solution.py:260

commit v20 on v19

--- a/solution.py
+++ b/solution.py
@@ -27,10 +27,8 @@
         return jnp.clip(place, 0, stack_count - 1)
 
     if late:
-        acc_in, coeff_in, mine_ref, theirs_ref, acc_ref, coeff_ref = refs
-        inner_count = acc_in.shape[0]
-        acc_ref[...] = acc_in[...]
-        coeff_ref[...] = coeff_in[...]
+        acc_ref, coeff_ref, mine_ref, theirs_ref = refs
+        inner_count = acc_ref.shape[0]
     else:
         acc_ref, coeff_ref = refs
         inner_count = acc_ref.shape[0]
@@ -134,7 +132,6 @@
             grid=(1,),
             in_specs=late_specs + [acc_spec, coeff_spec],
             out_specs=[half_spec, half_spec],
-            scratch_shapes=[pltpu.VMEM(acc_shape, jnp.float32), pltpu.VMEM(coeff_shape, jnp.float32)],
         ),
         out_shape=[out, out],
         compiler_params=params,

time: 44.8 us -> 45 us (level)
  waiting for transfers between devices: 24.5 us -> 25.5 us
  starting transfers between devices: 8.94 us -> 8.41 us
    ppermute x1, starting transfers between devices: 1.57 us -> 1.04 us  [on_device(): back = lax.ppermute(send, 'inner', swap)]
  transfers between devices with their start and end apart: 7 -> 7, of which waited for: 5 -> 6; matrix products, arithmetic and copies ran while one was open for 7% -> 7% of each run, Pallas kernels for 6% -> 5%
where the time goes in v20:
time: 45 us; the launch traced here: 44.7 us
  waiting for transfers between devices  25.5 us (57%)
  starting transfers between devices  8.41 us (19%)
  Pallas kernels  3.84 us (9%)
  local copies, waits for them, and re-layouts  2.84 us (6%)
  other arithmetic  2.27 us (5%)
  matrix products  0.97 us (2%)
  between operations  0.84 us (2%)
    ppermute x1, waiting for transfers between devices, on_device(): back = lax.ppermute(send, 'inner', swap)  7.84 us
    ppermute x1, waiting for transfers between devices, _line_gather(): down = lax.ppermute(down, axis, down_pairs)  6.55 us
    ppermute x1, waiting for transfers between devices, _line_gather(): first_up = lax.ppermute(payload, axis, [(i, (i + 1) % n) for i in range(n)])  5.72 us
    ppermute x1, starting transfers between devices, _line_gather(): lax.ppermute(payload, axis, [(i, (i - 1) % n) for i in range(n)])  5.13 us
    ppermute x1, waiting for transfers between devices, _line_gather(): lax.ppermute(payload, axis, [(i, (i - 1) % n) for i in range(n)])  3.44 us
    pallas_call x1, Pallas kernels, _near_far(): pl.pallas_call(lambda *r: _partial_kernel(False, *r), grid_spec=pltpu.Pre...  2.03 us
    pallas_call x1, Pallas kernels, _near_far(): pl.pallas_call(lambda *r: _partial_kernel(True, *r), grid_spec=pltpu.Pref...  1.81 us
    ppermute x1, waiting for transfers between devices, on_device(): lax.ppermute(lax.dynamic_index_in_dim(theirs, 1 - me, 0, False), 'sub', s...  1.57 us
  transfers between devices with their start and end apart: 7, of which 6 were waited for; matrix products, arithmetic and copies ran while one was open for 7% of the time, Pallas kernels for 5%

profile of v20, /device:TPU:0, one launch (start us, length us, event | category | flops | bytes accessed | tf_op | source)
XLA Modules:
  0.0 44.7 jit_solution(14598039207203915912)
XLA Ops:
  0.0 0.0 copy-start.1
  0.0 0.8 %slice_bitcast_fusion.1 = (bf16[16,256]{1,0:T(8,128)(2,1)S(1)}, bf16[16,256]{1,0:T(8,128)(2,1)S(1)}) fusion(bf16[1,32,256]{2,1,0:T(8,128)(2,1)} %param.7), kind=kLoop, calls=%fused_computation.22 | loop fusion | bytes 32768 | tf_op jit(solution)/shard_map/slice | solution.py:223
  0.8 1.0 %maximum_maximum_fusion = bf16[272,512]{1,0:T(8,128)(2,1)S(1)} fusion(bf16[16,256]{1,0:T(8,128)(2,1)S(1)} %get-tuple-element.22, bf16[16,256]{1,0:T(8,128)(2,1)S(1)} %get-tuple-element.21, bf16[256,512]{1,0:T(8,128)(2,1)} %param.6), kind=kLoop, calls=%fused_computation.10 | loop fusion | flops 835584 | bytes 557056 | tf_op jit(solution)/shard_map/concatenate | solution.py:224
  1.7 5.1 %collective-permute-start.2 = (bf16[272,512]{1,0:T(8,128)(2,1)S(1)}, bf16[272,512]{1,0:T(8,128)(2,1)S(1)}, u32[]{:S(2)}, u32[]{:S(2)}) collective-permute-start(bf16[272,512]{1,0:T(8,128)(2,1)S(1)} %maximum_maximum_fusion), channel_id=1, source_target_pairs={{0,12},{4,0},{8,4},{12,8},{1,13},{5,1},{9,5},{13,9},{2,14},{6,2},{... | collective-permute-start | bytes 835592 | tf_op jit(solution)/shard_map/ppermute | solution.py:179
  6.9 0.0 collective-permute-start
  7.5 0.8 %add_bitcast_fusion = s32[8]{0:T(128)S(1)} fusion(s32[8,2]{0,1:T(2,128)} %bitcast.57), kind=kLoop, calls=%fused_computation.29 | loop fusion | flops 16 | bytes 96 | tf_op jit(solution)/shard_map/eq | solution.py:232
  8.3 0.1 fusion.5
  8.4 0.1 convert_element_type.50
  8.5 0.1 copy.16
  8.6 0.9 %reshape_squeeze.11 = bf16[4,32,4,32]{3,2,1,0:T(4,128)(2,1)S(1)} reshape(bf16[1,1,128,128]{3,2,1,0:T(8,128)(2,1)} %param.11) | data formatting | bytes 65536 | tf_op jit(solution)/shard_map/reshape;squeeze | solution.py:240
  9.5 0.1 copy_multiply_fusion
  9.6 0.1 pad_add_fusion.r_2_
  9.6 0.8 %copy.15 = s32[1,1,8,2]{3,2,1,0:T(8,128)S(1)} copy(s32[1,1,8,2]{2,3,1,0:T(2,128)} %param.9) | data formatting | bytes 128 | tf_op args[3]
  10.4 0.1 reshape_squeeze.9.r_0_
  10.5 0.0 copy-start
  10.5 3.4 %collective-permute-done.2 = bf16[272,512]{1,0:T(8,128)(2,1)S(1)} collective-permute-done((bf16[272,512]{1,0:T(8,128)(2,1)S(1)}, bf16[272,512]{1,0:T(8,128)(2,1)S(1)}, u32[]{:S(2)}, u32[]{:S(2)}) %collective-permute-start.2) | collective-permute-done | bytes 278560 | tf_op jit(solution)/shard_map/ppermute | solution.py:179
  13.9 5.7 %collective-permute-done = bf16[272,512]{1,0:T(8,128)(2,1)S(1)} collective-permute-done((bf16[272,512]{1,0:T(8,128)(2,1)S(1)}, bf16[272,512]{1,0:T(8,128)(2,1)S(1)}, u32[]{:S(2)}, u32[]{:S(2)}) %collective-permute-start) | collective-permute-done | bytes 278560 | tf_op jit(solution)/shard_map/ppermute | solution.py:178
  19.7 0.0 copy-done.1
  19.7 0.7 %collective-permute-start.1 = (bf16[272,512]{1,0:T(8,128)(2,1)S(1)}, bf16[272,512]{1,0:T(8,128)(2,1)S(1)}, u32[]{:S(2)}, u32[]{:S(2)}) collective-permute-start(bf16[272,512]{1,0:T(8,128)(2,1)S(1)} %collective-permute-done), channel_id=1, source_target_pairs={{4,8},{8,12},{5,9},{9,13},{6,10},{10,14},{7,11},{11,15},{20,24},{2... | collective-permute-start | bytes 835592 | tf_op jit(solution)/shard_map/ppermute | solution.py:185
  20.4 1.3 %collective-permute-start.3 = (bf16[272,512]{1,0:T(8,128)(2,1)S(1)}, bf16[272,512]{1,0:T(8,128)(2,1)S(1)}, u32[]{:S(2)}, u32[]{:S(2)}) collective-permute-start(bf16[272,512]{1,0:T(8,128)(2,1)S(1)} %collective-permute-done.2), channel_id=1, source_target_pairs={{4,0},{8,4},{5,1},{9,5},{6,2},{10,6},{7,3},{11,7},{20,16},{24,20},... | collective-permute-start | bytes 835592 | tf_op jit(solution)/shard_map/ppermute | solution.py:186
  21.8 0.0 copy-done
  21.8 2.0 %shard_map.64 = (f32[4,256,512]{2,1,0:T(8,128)S(1)}, f32[128,512]{1,0:T(8,128)S(1)}) custom-call(s32[16]{0:T(128)S(1)} %reshape_squeeze.9.r_0_, s32[1]{0:T(128)} %bitcast.48.r_1_, s32[2]{0:T(128)S(1)} %pad_add_fusion.r_2_, bf16[8,256,256]{2,1,0:T(8,128)(2,1)S(1)} %bitcast.51, bf16[7,272,512]{2,1,0:T(8,128)(2,1)S(1)} %bitcast_dynamic-update-slice_fusion.3.r_4_, ...), custom_call_target="tpu_custom_call" | custom-call | tf_op jit(solution)/shard_map/pallas_call | solution.py:113
  23.9 0.0 collective-permute-done.1
  23.9 6.5 %collective-permute-done.3 = bf16[272,512]{1,0:T(8,128)(2,1)S(1)} collective-permute-done((bf16[272,512]{1,0:T(8,128)(2,1)S(1)}, bf16[272,512]{1,0:T(8,128)(2,1)S(1)}, u32[]{:S(2)}, u32[]{:S(2)}) %collective-permute-start.3) | collective-permute-done | bytes 278560 | tf_op jit(solution)/shard_map/ppermute | solution.py:186
  30.4 0.1 pad_maximum_fusion.r_4_
  30.5 1.8 %shard_map.65 = (bf16[2,288,512]{2,1,0:T(8,128)(2,1)S(1)}, bf16[2,288,512]{2,1,0:T(8,128)(2,1)S(1)}) custom-call(s32[16]{0:T(128)S(1)} %reshape_squeeze.9.r_0_, s32[1]{0:T(128)} %bitcast.49.r_1_, s32[2]{0:T(128)S(1)} %pad_add_fusion.r_2_, bf16[8,256,256]{2,1,0:T(8,128)(2,1)S(1)} %bitcast.52, bf16[2,272,512]{2,1,0:T(8,128)(2,1)S(1)} %pad_maximum_fusion.r_4_, ...), custom_call_target="tpu_custom_call" | custom-call | tf_op jit(solution)/shard_map/pallas_call | solution.py:128
  32.3 0.0 copy-start.2
  32.4 0.1 collective-permute-start.4
  32.4 1.6 %collective-permute-done.4 = bf16[288,512]{1,0:T(8,128)(2,1)S(1)} collective-permute-done((bf16[288,512]{1,0:T(8,128)(2,1)S(1)}, bf16[288,512]{1,0:T(8,128)(2,1)S(1)}, u32[]{:S(2)}, u32[]{:S(2)}) %collective-permute-start.4) | collective-permute-done | bytes 294944 | tf_op jit(solution)/shard_map/ppermute | solution.py:252
  34.0 0.1 fusion
  34.1 0.2 collective-permute-start.5
  34.3 1.0 %collective-permute-start.6 = (bf16[288,512]{1,0:T(8,128)(2,1)S(1)}, bf16[288,512]{1,0:T(8,128)(2,1)S(1)}, u32[]{:S(2)}, u32[]{:S(2)}) collective-permute-start(bf16[288,512]{1,0:T(8,128)(2,1)S(1)} %fusion), channel_id=1, source_target_pairs={{0,2},{2,0},{1,3},{3,1},{4,6},{6,4},{5,7},{7,5},{8,10},{10,8},{9,1... | collective-permute-start | bytes 884744 | tf_op jit(solution)/shard_map/ppermute | solution.py:257
  35.3 0.4 collective-permute-done.5
  35.8 7.8 %collective-permute-done.6 = bf16[288,512]{1,0:T(8,128)(2,1)S(1)} collective-permute-done((bf16[288,512]{1,0:T(8,128)(2,1)S(1)}, bf16[288,512]{1,0:T(8,128)(2,1)S(1)}, u32[]{:S(2)}, u32[]{:S(2)}) %collective-permute-start.6) | collective-permute-done | bytes 294944 | tf_op jit(solution)/shard_map/ppermute | solution.py:257
  43.6 0.1 fusion.1
  43.7 0.0 copy-done.2
  43.7 1.0 %fusion.2 = bf16[256,512]{1,0:T(8,128)(2,1)} fusion(f32[288,512]{1,0:T(8,128)S(1)} %fusion.1, bf16[1,32,256]{2,1,0:T(8,128)(2,1)S(1)} %copy-done.2), kind=kOutput, calls=%fused_computation.7 | convolution fusion | flops 8667136 | bytes 868352 | tf_op jit(solution)/shard_map/dot_general | solution.py:272
  (10 shorter events, 0.2 us)
Async XLA Ops:
  0.0 19.7 %copy-start.1 = (bf16[256,512]{1,0:T(8,128)(2,1)S(1)}, bf16[256,512]{1,0:T(8,128)(2,1)}, u32[]{:S(2)}) copy-start(bf16[256,512]{1,0:T(8,128)(2,1)} %param.6) | copy-start | bytes 786436
  1.7 12.2 %collective-permute-start.2 = (bf16[272,512]{1,0:T(8,128)(2,1)S(1)}, bf16[272,512]{1,0:T(8,128)(2,1)S(1)}, u32[]{:S(2)}, u32[]{:S(2)}) collective-permute-start(bf16[272,512]{1,0:T(8,128)(2,1)S(1)} %maximum_maximum_fusion), channel_id=1, source_target_pairs={{0,12},{4,0},{8,4},{12,8},{1,13},{5,1},{9,5},{13,9},{2,14},{6,2},{... | collective-permute-start | bytes 835592 | tf_op jit(solution)/shard_map/ppermute | solution.py:179
  6.9 12.8 %collective-permute-start = (bf16[272,512]{1,0:T(8,128)(2,1)S(1)}, bf16[272,512]{1,0:T(8,128)(2,1)S(1)}, u32[]{:S(2)}, u32[]{:S(2)}) collective-permute-start(bf16[272,512]{1,0:T(8,128)(2,1)S(1)} %maximum_maximum_fusion), channel_id=1, source_target_pairs={{0,4},{4,8},{8,12},{12,0},{1,5},{5,9},{9,13},{13,1},{2,6},{6,10},{... | collective-permute-start | bytes 835592 | tf_op jit(solution)/shard_map/ppermute | solution.py:178
  10.5 11.3 %copy-start = (bf16[1,1,8,256,256]{4,3,2,1,0:T(8,128)(2,1)S(1)}, bf16[1,1,8,256,256]{4,3,2,1,0:T(8,128)(2,1)}, u32[]{:S(2)}) copy-start(bf16[1,1,8,256,256]{4,3,2,1,0:T(8,128)(2,1)} %param.8) | copy-start | bytes 3145732
  19.7 4.1 %collective-permute-start.1 = (bf16[272,512]{1,0:T(8,128)(2,1)S(1)}, bf16[272,512]{1,0:T(8,128)(2,1)S(1)}, u32[]{:S(2)}, u32[]{:S(2)}) collective-permute-start(bf16[272,512]{1,0:T(8,128)(2,1)S(1)} %collective-permute-done), channel_id=1, source_target_pairs={{4,8},{8,12},{5,9},{9,13},{6,10},{10,14},{7,11},{11,15},{20,24},{2... | collective-permute-start | bytes 835592 | tf_op jit(solution)/shard_map/ppermute | solution.py:185
  20.4 10.0 %collective-permute-start.3 = (bf16[272,512]{1,0:T(8,128)(2,1)S(1)}, bf16[272,512]{1,0:T(8,128)(2,1)S(1)}, u32[]{:S(2)}, u32[]{:S(2)}) collective-permute-start(bf16[272,512]{1,0:T(8,128)(2,1)S(1)} %collective-permute-done.2), channel_id=1, source_target_pairs={{4,0},{8,4},{5,1},{9,5},{6,2},{10,6},{7,3},{11,7},{20,16},{24,20},... | collective-permute-start | bytes 835592 | tf_op jit(solution)/shard_map/ppermute | solution.py:186
  32.3 11.4 %copy-start.2 = (bf16[1,32,256]{2,1,0:T(8,128)(2,1)S(1)}, bf16[1,32,256]{2,1,0:T(8,128)(2,1)}, u32[]{:S(2)}) copy-start(bf16[1,32,256]{2,1,0:T(8,128)(2,1)} %param.7) | copy-start | bytes 49156
  32.4 1.6 %collective-permute-start.4 = (bf16[288,512]{1,0:T(8,128)(2,1)S(1)}, bf16[288,512]{1,0:T(8,128)(2,1)S(1)}, u32[]{:S(2)}, u32[]{:S(2)}) collective-permute-start(bf16[288,512]{1,0:T(8,128)(2,1)S(1)} %get-tuple-element.20), channel_id=1, source_target_pairs={{0,1},{1,0},{2,3},{3,2},{4,5},{5,4},{6,7},{7,6},{8,9},{9,8},{10,11... | collective-permute-start | bytes 884744 | tf_op jit(solution)/shard_map/ppermute | solution.py:252
  34.1 1.6 %collective-permute-start.5 = (bf16[288,512]{1,0:T(8,128)(2,1)S(1)}, bf16[288,512]{1,0:T(8,128)(2,1)S(1)}, u32[]{:S(2)}, u32[]{:S(2)}) collective-permute-start(bf16[288,512]{1,0:T(8,128)(2,1)S(1)} %get-tuple-element.18), channel_id=1, source_target_pairs={{0,1},{1,0},{2,3},{3,2},{4,5},{5,4},{6,7},{7,6},{8,9},{9,8},{10,11... | collective-permute-start | bytes 884744 | tf_op jit(solution)/shard_map/ppermute | solution.py:259
  34.3 9.3 %collective-permute-start.6 = (bf16[288,512]{1,0:T(8,128)(2,1)S(1)}, bf16[288,512]{1,0:T(8,128)(2,1)S(1)}, u32[]{:S(2)}, u32[]{:S(2)}) collective-permute-start(bf16[288,512]{1,0:T(8,128)(2,1)S(1)} %fusion), channel_id=1, source_target_pairs={{0,2},{2,0},{1,3},{3,1},{4,6},{6,4},{5,7},{7,5},{8,10},{10,8},{9,1... | collective-permute-start | bytes 884744 | tf_op jit(solution)/shard_map/ppermute | solution.py:257
